TPU v7x, 32 devices: a whole 2x2x4 slice. The times are simulated.
32 devices in a mesh: dom: 4 (over y, x), grp: 8 (over z, core).
Axes of the slice: x: 2, y: 2, z: 4, core: 2. Of those that a mesh axis runs over, the one named last changes fastest.
Arguments:
- features: bfloat16 [40960, 128], P(('dom', 'grp')), may hold values from -6 to 6
- send_dom: int32 [32, 4, 32], P(('dom', 'grp')), may hold values from 0 to 1279
- send_grp: int32 [32, 8, 32], P(('dom', 'grp')), may hold values from 0 to 1279
- tile_vals: bfloat16 [1536, 128, 128], P(('dom', 'grp')), may hold values from 0.049804688 to 1
- tile_tgt: int32 [1536], P(('dom', 'grp')), may hold values from 0 to 9, as said below
- tile_src: int32 [1536], P(('dom', 'grp')), may hold values from 0 to 12, as said below
- tile_count: int32 [32], P(('dom', 'grp')), may hold values from 13 to 48, as said below
- w_self: bfloat16 [128, 256], replicated, may hold values from -0.5 to 0.5
- w_neigh: bfloat16 [128, 256], replicated, may hold values from -0.5 to 0.5
- cotangent: bfloat16 [40960, 256], P(('dom', 'grp'))
Outputs:
- output: bfloat16 [40960, 256], P(('dom', 'grp'))
- grad_features: bfloat16 [40960, 128], P(('dom', 'grp'))
- grad_self: float32 [128, 256], replicated
- grad_neigh: float32 [128, 256], replicated
Inputs may be any that keep to these rules, and one draw needn't show every extreme that they name: `tile_tgt`: in every partition, tile slot t for t < 10 has target block t; other slots name any target block. `tile_src`: in every partition, tile slot t for t < 13 has source block t; other slots name any source block. `tile_count`: some partition has all 48 slots live in every draw.
All inputs are finite; a program needn't handle non-finite values.
Results may differ from a plain program's by a relative error of at most 0.0049.
Values may be sent and summed in bfloat16 or wider, within the bound.
No kernel may reach another device: no remote copies, remote signals or barrier semaphores. Data moves between devices by JAX's collectives and lax.ppermute only.
A program may use at most 64 MiB of HBM per device.

v0:
```python
import jax
import jax.numpy as jnp
from jax import lax
from jax.sharding import PartitionSpec as P


def per_device(
    features,
    send_dom,
    send_grp,
    tile_vals,
    tile_tgt,
    tile_src,
    tile_count,
    w_self,
    w_neigh,
    cotangent,
):
    tile_size = tile_vals.shape[1]
    width = features.shape[1]
    node_count = features.shape[0]
    block_count = node_count // tile_size
    dom_index = send_dom[0]
    grp_index = send_grp[0]
    dom_peers = dom_index.shape[0]
    recv_dom = lax.all_to_all(features[dom_index], "dom", split_axis=0, concat_axis=0, tiled=True)
    recv_grp = lax.all_to_all(features[grp_index], "grp", split_axis=0, concat_axis=0, tiled=True)
    source = jnp.concatenate(
        [features, recv_dom.reshape(-1, width), recv_grp.reshape(-1, width)], axis=0
    )
    source = source.reshape(-1, tile_size, width)
    source_count = source.shape[0]
    slot_count = tile_vals.shape[0]
    usable = jnp.arange(slot_count, dtype=jnp.int32) < tile_count[0]
    to_target = (
        (tile_tgt[None, :] == jnp.arange(block_count, dtype=jnp.int32)[:, None]) & usable[None, :]
    ).astype(jnp.float32)
    to_source = (
        (tile_src[None, :] == jnp.arange(source_count, dtype=jnp.int32)[:, None]) & usable[None, :]
    ).astype(jnp.float32)
    products = jnp.einsum(
        "tij,tjf->tif", tile_vals, source[tile_src], preferred_element_type=jnp.float32
    )
    summed = jnp.einsum("bt,tif->bif", to_target, products, precision=lax.Precision.HIGHEST)
    unit_column = jnp.ones((tile_size,), jnp.bfloat16)
    row_sums = jnp.einsum("tij,j->ti", tile_vals, unit_column, preferred_element_type=jnp.float32)
    degree = jnp.dot(to_target, row_sums, precision=lax.Precision.HIGHEST)
    agg = (summed / degree[:, :, None]).reshape(node_count, width).astype(jnp.bfloat16)
    preact = jnp.dot(features, w_self, preferred_element_type=jnp.float32) + jnp.dot(
        agg, w_neigh, preferred_element_type=jnp.float32
    )
    sigm = jax.nn.sigmoid(preact)
    output = (preact * sigm).astype(jnp.bfloat16)
    grad_pre = (cotangent.astype(jnp.float32) * sigm * (1.0 + preact * (1.0 - sigm))).astype(
        jnp.bfloat16
    )
    part_self = jnp.einsum("nf,nh->fh", features, grad_pre, preferred_element_type=jnp.float32)
    part_neigh = jnp.einsum("nf,nh->fh", agg, grad_pre, preferred_element_type=jnp.float32)
    grad_own = jnp.einsum("nh,fh->nf", grad_pre, w_self, preferred_element_type=jnp.float32)
    grad_agg = jnp.einsum("nh,fh->nf", grad_pre, w_neigh, preferred_element_type=jnp.float32)
    grad_agg = (grad_agg / degree.reshape(-1)[:, None]).astype(jnp.bfloat16)
    picked = grad_agg.reshape(block_count, tile_size, width)[tile_tgt]
    backward = jnp.einsum("tij,tif->tjf", tile_vals, picked, preferred_element_type=jnp.float32)
    grad_source = jnp.einsum(
        "st,tjf->sjf", to_source, backward, precision=lax.Precision.HIGHEST
    ).reshape(-1, width)
    dom_rows = dom_peers * dom_index.shape[1]
    back_dom = (
        grad_source[node_count : node_count + dom_rows]
        .reshape(dom_index.shape[0], dom_index.shape[1], width)
        .astype(jnp.bfloat16)
    )
    back_grp = (
        grad_source[node_count + dom_rows :]
        .reshape(grp_index.shape[0], grp_index.shape[1], width)
        .astype(jnp.bfloat16)
    )
    ret_dom = lax.all_to_all(back_dom, "dom", split_axis=0, concat_axis=0, tiled=True)
    ret_grp = lax.all_to_all(back_grp, "grp", split_axis=0, concat_axis=0, tiled=True)
    grad_self, grad_neigh = lax.psum((part_self, part_neigh), ("dom", "grp"))
    grad_total = grad_own + grad_source[:node_count]
    grad_total = grad_total.at[dom_index.reshape(-1)].add(
        ret_dom.reshape(-1, width).astype(jnp.float32)
    )
    grad_total = grad_total.at[grp_index.reshape(-1)].add(
        ret_grp.reshape(-1, width).astype(jnp.float32)
    )
    return (output, grad_total.astype(jnp.bfloat16), grad_self, grad_neigh)


def solution(mesh):
    return jax.shard_map(
        per_device,
        mesh=mesh,
        in_specs=(
            P(("dom", "grp"), None),
            P(("dom", "grp"), None, None),
            P(("dom", "grp"), None, None),
            P(("dom", "grp"), None, None),
            P(("dom", "grp")),
            P(("dom", "grp")),
            P(("dom", "grp")),
            P(),
            P(),
            P(("dom", "grp"), None),
        ),
        out_specs=(P(("dom", "grp"), None), P(("dom", "grp"), None), P(), P()),
        check_vma=False,
    )
```

profile of v0, /device:TPU:0, one launch (start us, length us, event | category | flops | bytes accessed | tf_op | source)
XLA Modules:
  0.0 210.0 jit_solution(4787525386066854471)
XLA Ops:
  7.2 0.0 copy-start
  7.2 0.8 compare_select_fusion.2
  8.0 0.1 reshape.166
  8.1 2.3 %gather_fusion = bf16[128,128]{1,0:T(8,128)(2,1)} fusion(bf16[1280,128]{1,0:T(8,128)(2,1)} %param.10, s32[1024]{0:T(1024)S(1)} %pad_clamp_fusion.3), kind=kCustom, calls=%fused_computation | custom fusion | bytes 66048 | tf_op jit(solution)/shard_map/gather | solution.py:26
  10.4 5.2 %all-to-all-start = ((bf16[4,32,128]{2,1,0:T(8,128)(2,1)}), bf16[4,32,128]{2,1,0:T(8,128)(2,1)S(1)}, u32[]{:S(2)}, u32[]{:S(2)}) async-start(bf16[4,32,128]{2,1,0:T(8,128)(2,1)} %bitcast.3), calls=%async_computation | async-start | bytes 65536 | tf_op jit(solution)/shard_map/all_to_all | solution.py:26
  15.6 0.8 reshape_squeeze.6
  16.3 0.8 reshape_squeeze.7
  17.1 0.7 compare_select_fusion
  18.4 0.7 compare_select_fusion.5
  19.1 0.7 compare_select_fusion.4
  19.8 0.1 reshape.174
  19.9 0.5 fusion.30
  20.4 1.4 fusion.34
  21.8 0.1 fusion.16
  21.9 1.5 gather_fusion.1
  23.4 4.9 %all-to-all-start.1 = ((bf16[8,32,128]{2,1,0:T(8,128)(2,1)}), bf16[8,32,128]{2,1,0:T(8,128)(2,1)S(1)}, u32[]{:S(2)}, u32[]{:S(2)}) async-start(bf16[8,32,128]{2,1,0:T(8,128)(2,1)} %bitcast.6), calls=%async_computation.1 | async-start | bytes 131072 | tf_op jit(solution)/shard_map/all_to_all | solution.py:27
  28.3 0.1 copy.17
  28.4 5.8 %all-to-all-done.1 = bf16[8,32,128]{2,1,0:T(8,128)(2,1)S(1)} async-done(((bf16[8,32,128]{2,1,0:T(8,128)(2,1)}), bf16[8,32,128]{2,1,0:T(8,128)(2,1)S(1)}, u32[]{:S(2)}, u32[]{:S(2)}) %all-to-all-start.1) | async-done | bytes 65568 | tf_op jit(solution)/shard_map/all_to_all | solution.py:27
  34.2 1.9 gather_fusion.2
  36.1 4.3 %fusion.35 = f32[48,128,128]{2,1,0:T(8,128)} fusion(bf16[48,128,128]{2,1,0:T(8,128)(2,1)} %gather_fusion.2, bf16[48,128,128]{2,1,0:T(8,128)(2,1)S(1)} %copy-done), kind=kOutput, calls=%fused_computation.55 | convolution fusion | flops 201326592 | bytes 6291456 | tf_op jit(solution)/shard_map/tij,tjf->tif/dot_general | solution.py:41
  40.4 3.6 %copy.22 = f32[48,128,128]{1,0,2:T(8,128)} copy(f32[48,128,128]{2,1,0:T(8,128)} %fusion.35) | data formatting | bytes 6291456 | tf_op jit(solution)/shard_map/tij,tjf->tif/dot_general | solution.py:41
  44.1 3.3 %fusion.8 = bf16[10,128,128]{2,0,1:T(8,128)(2,1)S(1)} fusion(f32[48,128,128]{1,0,2:T(8,128)} %copy.22, f32[10,128]{0,1:T(8,128)S(1)} %copy.17, s32[48]{0:T(128)S(1)} %copy-done.5, pred[48]{0:T(512)(128)(4,1)S(1)} %iota_compare_fusion.2), kind=kOutput, calls=%fused_computation.18 | convolution fusion | flops 94700480 | bytes 3478768 | tf_op jit(solution)/shard_map/bt,tif->bif/dot_general | solution.py:44
  47.3 0.1 copy.18
  47.4 1.6 multiply_convert_fusion
  49.1 1.0 fusion.37
  50.0 0.3 fusion.4
  50.4 1.9 gather_fusion.3
  52.3 3.7 %fusion.36 = f32[48,128,128]{2,1,0:T(8,128)} fusion(bf16[48,128,128]{2,1,0:T(8,128)(2,1)} %gather_fusion.3, bf16[48,128,128]{2,1,0:T(8,128)(2,1)S(1)} %copy-done), kind=kOutput, calls=%fused_computation.56 | convolution fusion | flops 201326592 | bytes 6291456 | tf_op jit(solution)/shard_map/tij,tif->tjf/dot_general | solution.py:63
  56.1 3.6 %copy.24 = f32[48,128,128]{1,0,2:T(8,128)} copy(f32[48,128,128]{2,1,0:T(8,128)} %fusion.36) | data formatting | bytes 6291456 | tf_op jit(solution)/shard_map/tij,tif->tjf/dot_general | solution.py:63
  59.7 4.0 %fusion.33 = (bf16[13,128,128]{2,0,1:T(8,128)(2,1)S(1)}, f32[13,128,128]{2,0,1:T(8,128)}) fusion(f32[48,128,128]{1,0,2:T(8,128)} %copy.24, s32[48]{0:T(128)S(1)} %copy-done.6, pred[48]{0:T(512)(128)(4,1)S(1)} %iota_compare_fusion.2), kind=kOutput, calls=%fused_computation.53 | convolution fusion | flops 122897632 | bytes 4423920 | tf_op jit(solution)/shard_map/st,tjf->sjf/dot_general | solution.py:64
  63.7 0.1 slice.29
  63.8 0.6 copy.25
  64.4 4.2 %all-to-all-start.2 = ((bf16[4,32,128]{2,1,0:T(8,128)(2,1)}), bf16[4,32,128]{2,1,0:T(8,128)(2,1)S(1)}, u32[]{:S(2)}, u32[]{:S(2)}) async-start(bf16[4,32,128]{2,1,0:T(8,128)(2,1)} %bitcast.26), calls=%async_computation.2 | async-start | bytes 65536 | tf_op jit(solution)/shard_map/all_to_all | solution.py:78
  68.6 1.0 convolution_bitcast_fusion
  69.7 0.1 slice.30
  69.7 1.4 copy.19
  71.2 0.6 copy.20
  71.8 0.0 all-reduce.3.cloned.1.call-update
  71.8 1.5 all-to-all-done.2
  73.4 3.4 %all-to-all-start.3 = ((bf16[8,32,128]{2,1,0:T(8,128)(2,1)}), bf16[8,32,128]{2,1,0:T(8,128)(2,1)S(1)}, u32[]{:S(2)}, u32[]{:S(2)}) async-start(bf16[8,32,128]{2,1,0:T(8,128)(2,1)} %bitcast.21), calls=%async_computation.3 | async-start | bytes 131072 | tf_op jit(solution)/shard_map/all_to_all | solution.py:79
  76.7 1.2 convolution_add_fusion.1
  77.9 3.1 %scatter_custom_fusion = f32[1280,128]{1,0:T(8,128)} fusion(f32[1280,128]{1,0:T(8,128)} %convolution_add_fusion.1, s32[128]{0:T(128)S(1)} %fusion.29, bf16[128,128]{1,0:T(8,128)(2,1)S(1)} %bitcast.80), kind=kCustom, calls=%fused_computation.23 | custom fusion | flops 32768 | bytes 688128 | tf_op jit(solution)/shard_map/scatter-add | solution.py:82
  81.0 1.6 all-to-all-done.3
  82.6 3.7 %scatter_custom_fusion.1 = f32[1280,128]{1,0:T(8,128)} fusion(f32[1280,128]{1,0:T(8,128)} %scatter_custom_fusion, s32[256]{0:T(256)S(1)} %bitcast.83, bf16[256,128]{1,0:T(8,128)(2,1)S(1)} %bitcast.77), kind=kCustom, calls=%fused_computation.21 | custom fusion | flops 65536 | bytes 720896 | tf_op jit(solution)/shard_map/scatter-add | solution.py:85
  86.3 1.8 convert_element_type.55
  88.1 111.8 %all-reduce.3.cloned.1.call-done = (f32[128,256]{0,1:T(8,128)}, f32[128,256]{1,0:T(8,128)}) async-done(((f32[128,256]{0,1:T(8,128)}, f32[128,256]{1,0:T(8,128)}), (f32[128,256]{0,1:T(8,128)}, f32[128,256]{1,0:T(8,128)})) %all-reduce.3.cloned.1.call-update) | async-done | bytes 262160 | tf_op jit(solution)/shard_map/psum | solution.py:80
  199.9 1.7 copy.21
  201.6 1.6 copy.31
  (27 shorter events, 0.1 us)
Async XLA Ops:
  7.2 12.7 %copy-start = (bf16[48,128,128]{2,1,0:T(8,128)(2,1)S(1)}, bf16[48,128,128]{2,1,0:T(8,128)(2,1)}, u32[]{:S(2)}) copy-start(bf16[48,128,128]{2,1,0:T(8,128)(2,1)} %param.13) | copy-start | bytes 4718596
  7.2 13.2 %copy-start.1 = (bf16[1280,128]{1,0:T(8,128)(2,1)S(1)}, bf16[1280,128]{1,0:T(8,128)(2,1)}, u32[]{:S(2)}) copy-start(bf16[1280,128]{1,0:T(8,128)(2,1)} %param.10) | copy-start | bytes 983044
  7.2 13.2 %copy-start.3 = (bf16[128,256]{1,0:T(8,128)(2,1)S(1)}, bf16[128,256]{1,0:T(8,128)(2,1)}, u32[]{:S(2)}) copy-start(bf16[128,256]{1,0:T(8,128)(2,1)} %param.17) | copy-start | bytes 196612
  10.4 13.0 %all-to-all-start = ((bf16[4,32,128]{2,1,0:T(8,128)(2,1)}), bf16[4,32,128]{2,1,0:T(8,128)(2,1)S(1)}, u32[]{:S(2)}, u32[]{:S(2)}) async-start(bf16[4,32,128]{2,1,0:T(8,128)(2,1)} %bitcast.3), calls=%async_computation | async-start | bytes 65536 | tf_op jit(solution)/shard_map/all_to_all | solution.py:26
  19.9 1.9 copy-start.5
  23.4 10.8 %all-to-all-start.1 = ((bf16[8,32,128]{2,1,0:T(8,128)(2,1)}), bf16[8,32,128]{2,1,0:T(8,128)(2,1)S(1)}, u32[]{:S(2)}, u32[]{:S(2)}) async-start(bf16[8,32,128]{2,1,0:T(8,128)(2,1)} %bitcast.6), calls=%async_computation.1 | async-start | bytes 131072 | tf_op jit(solution)/shard_map/all_to_all | solution.py:27
  44.1 3.4 %copy-start.2 = (f32[1280,256]{1,0:T(8,128)S(1)}, f32[1280,256]{1,0:T(8,128)}, u32[]{:S(2)}) copy-start(f32[1280,256]{1,0:T(8,128)} %fusion.34) | copy-start | bytes 3932164
  44.1 3.4 %copy-start.7 = (bf16[1280,256]{1,0:T(8,128)(2,1)S(1)}, bf16[1280,256]{1,0:T(8,128)(2,1)}, u32[]{:S(2)}) copy-start(bf16[1280,256]{1,0:T(8,128)(2,1)} %param.19) | copy-start | bytes 1966084
  44.1 3.4 %copy-start.8 = (bf16[128,256]{1,0:T(8,128)(2,1)S(1)}, bf16[128,256]{1,0:T(8,128)(2,1)}, u32[]{:S(2)}) copy-start(bf16[128,256]{1,0:T(8,128)(2,1)} %param.18) | copy-start | bytes 196612
  56.1 3.6 %copy-start.6 = (s32[48]{0:T(128)S(1)}, s32[48]{0:T(128)}, u32[]{:S(2)}) copy-start(s32[48]{0:T(128)} %param.15) | copy-start | bytes 580
  64.4 9.0 %all-to-all-start.2 = ((bf16[4,32,128]{2,1,0:T(8,128)(2,1)}), bf16[4,32,128]{2,1,0:T(8,128)(2,1)S(1)}, u32[]{:S(2)}, u32[]{:S(2)}) async-start(bf16[4,32,128]{2,1,0:T(8,128)(2,1)} %bitcast.26), calls=%async_computation.2 | async-start | bytes 65536 | tf_op jit(solution)/shard_map/all_to_all | solution.py:78
  68.6 8.1 %copy-start.4 = (bf16[128,256]{1,0:T(8,128)(2,1)S(1)}, bf16[128,256]{1,0:T(8,128)(2,1)}, u32[]{:S(2)}) copy-start(bf16[128,256]{1,0:T(8,128)(2,1)} %param.17) | copy-start | bytes 196612
  68.6 131.3 %all-reduce.3.cloned.1.call-start = ((), (), s32[]{:S(2)}) async-start(), calls=%async_computation.4 | async-start | bytes 524288 | tf_op jit(solution)/shard_map/psum | solution.py:80
  73.4 9.2 %all-to-all-start.3 = ((bf16[8,32,128]{2,1,0:T(8,128)(2,1)}), bf16[8,32,128]{2,1,0:T(8,128)(2,1)S(1)}, u32[]{:S(2)}, u32[]{:S(2)}) async-start(bf16[8,32,128]{2,1,0:T(8,128)(2,1)} %bitcast.21), calls=%async_computation.3 | async-start | bytes 131072 | tf_op jit(solution)/shard_map/all_to_all | solution.py:79
Sparse Core Ops, SparseCore 0:
  75.7 124.1 all-reduce.2
where the time goes:
time: 211 us; the launch traced here: 210 us
  waiting for transfers between devices  121 us (57%)
  local copies, waits for them, and re-layouts  22.9 us (11%)
  matrix products  22.5 us (11%)
  starting transfers between devices  17.6 us (8%)
  between operations  14.8 us (7%)
  other arithmetic  11.5 us (5%)
    psum x1, waiting for transfers between devices, per_device(): grad_self, grad_neigh = lax.psum((part_self, part_neigh), ('dom', 'grp'))  112 us
    all_to_all x1, waiting for transfers between devices, per_device(): lax.all_to_all(features[grp_index], 'grp', split_axis=0, concat_axis=0, t...  5.79 us
    all_to_all x1, starting transfers between devices, per_device(): lax.all_to_all(features[dom_index], 'dom', split_axis=0, concat_axis=0, t...  5.16 us
    all_to_all x1, starting transfers between devices, per_device(): lax.all_to_all(features[grp_index], 'grp', split_axis=0, concat_axis=0, t...  4.88 us
    dot_general x1, matrix products, per_device(): jnp.einsum('tij,tjf->tif', tile_vals, source[tile_src], preferred_element...  4.3 us
  transfers between devices with their start and end apart: 5, of which 4 were waited for; matrix products, arithmetic and copies ran while one was open for 10% of the time, Pallas kernels for 0%

commit v1 on v0

--- a/solution.py
+++ b/solution.py
@@ -2,6 +2,21 @@
 import jax.numpy as jnp
 from jax import lax
 from jax.sharding import PartitionSpec as P
+
+
+def weight_sum(part_self, part_neigh):
+    axes = ("dom", "grp")
+    peers = lax.psum(1, axes)
+    rows = part_self.shape[0]
+    stacked = jnp.concatenate([part_self, part_neigh], axis=0)
+    flat = stacked.reshape(-1)
+    pad = (-flat.shape[0]) % peers
+    chunks = jnp.pad(flat, (0, pad)).reshape(peers, -1)
+    mine = jnp.sum(lax.all_to_all(chunks, axes, 0, 0, tiled=True), axis=0, keepdims=True)
+    spread = jnp.broadcast_to(mine, chunks.shape)
+    total = lax.all_to_all(spread, axes, 0, 0, tiled=True).reshape(-1)
+    total = total[: flat.shape[0]].reshape(stacked.shape)
+    return total[:rows], total[rows:]
 
 
 def per_device(
@@ -77,7 +92,7 @@
     )
     ret_dom = lax.all_to_all(back_dom, "dom", split_axis=0, concat_axis=0, tiled=True)
     ret_grp = lax.all_to_all(back_grp, "grp", split_axis=0, concat_axis=0, tiled=True)
-    grad_self, grad_neigh = lax.psum((part_self, part_neigh), ("dom", "grp"))
+    grad_self, grad_neigh = weight_sum(part_self, part_neigh)
     grad_total = grad_own + grad_source[:node_count]
     grad_total = grad_total.at[dom_index.reshape(-1)].add(
         ret_dom.reshape(-1, width).astype(jnp.float32)

time: 211 us -> 104 us (0.49)
  waiting for transfers between devices: 121 us -> 27.6 us
  between operations: 14.8 us -> 1.55 us
  starting transfers between devices: 17.6 us -> 23.5 us
  matrix products: 22.5 us -> 19.2 us
  other arithmetic: 11.5 us -> 8.48 us
    psum x1 -> x0, waiting for transfers between devices: 112 us -> none  [per_device(): grad_self, grad_neigh = lax.psum((part_self, part_neigh), ('dom', 'grp'))]
    all_to_all x0 -> x2, waiting for transfers between devices: none -> 12.3 us  [the longest x1 8.64 us: weight_sum(): lax.all_to_all(chunks, axes, 0, 0, tiled=True)]
    all_to_all x0 -> x2, starting transfers between devices: none -> 5.17 us  [the longest x1 2.59 us: weight_sum(): lax.all_to_all(chunks, axes, 0, 0, tiled=True)]
    all_to_all x1, waiting for transfers between devices: 1.59 us -> 5.67 us  [per_device(): lax.all_to_all(back_grp, 'grp', split_axis=0, concat_axis=0, tiled=True)]
    all_to_all x1, waiting for transfers between devices: 1.54 us -> 3.76 us  [per_device(): lax.all_to_all(back_dom, 'dom', split_axis=0, concat_axis=0, tiled=True)]
  transfers between devices with their start and end apart: 5 -> 6, of which waited for: 4 -> 5; matrix products, arithmetic and copies ran while one was open for 10% -> 13% of each run, Pallas kernels for 0% -> 0%
where the time goes in v1:
time: 104 us; the launch traced here: 103 us
  waiting for transfers between devices  27.6 us (27%)
  starting transfers between devices  23.5 us (23%)
  local copies, waits for them, and re-layouts  22.8 us (22%)
  matrix products  19.2 us (18%)
  other arithmetic  8.48 us (8%)
  between operations  1.55 us (1%)
    all_to_all x1, waiting for transfers between devices, weight_sum(): lax.all_to_all(chunks, axes, 0, 0, tiled=True)  8.64 us
    all_to_all x1, waiting for transfers between devices, per_device(): lax.all_to_all(features[grp_index], 'grp', split_axis=0, concat_axis=0, t...  5.79 us
    all_to_all x1, waiting for transfers between devices, per_device(): lax.all_to_all(back_grp, 'grp', split_axis=0, concat_axis=0, tiled=True)  5.67 us
    all_to_all x1, starting transfers between devices, per_device(): lax.all_to_all(features[dom_index], 'dom', split_axis=0, concat_axis=0, t...  5.16 us
    all_to_all x1, starting transfers between devices, per_device(): lax.all_to_all(features[grp_index], 'grp', split_axis=0, concat_axis=0, t...  4.88 us
    all_to_all x1, starting transfers between devices, per_device(): lax.all_to_all(back_dom, 'dom', split_axis=0, concat_axis=0, tiled=True)  4.33 us
    dot_general x1, matrix products, per_device(): jnp.einsum('tij,tjf->tif', tile_vals, source[tile_src], preferred_element...  4.3 us
    all_to_all x1, starting transfers between devices, per_device(): lax.all_to_all(back_grp, 'grp', split_axis=0, concat_axis=0, tiled=True)  3.97 us
  transfers between devices with their start and end apart: 6, of which 5 were waited for; matrix products, arithmetic and copies ran while one was open for 13% of the time, Pallas kernels for 0%

profile of v1, /device:TPU:0, one launch (start us, length us, event | category | flops | bytes accessed | tf_op | source)
XLA Modules:
  0.0 103.1 jit_solution(8277247179049573002)
XLA Ops:
  0.7 0.8 compare_select_fusion.2
  1.6 2.3 %gather_fusion = bf16[128,128]{1,0:T(8,128)(2,1)} fusion(bf16[1280,128]{1,0:T(8,128)(2,1)} %param.10, s32[1024]{0:T(1024)S(1)} %pad_clamp_fusion.3), kind=kCustom, calls=%fused_computation | custom fusion | bytes 66048 | tf_op jit(solution)/shard_map/gather | solution.py:41
  3.9 5.2 %all-to-all-start = ((bf16[4,32,128]{2,1,0:T(8,128)(2,1)}), bf16[4,32,128]{2,1,0:T(8,128)(2,1)S(1)}, u32[]{:S(2)}, u32[]{:S(2)}) async-start(bf16[4,32,128]{2,1,0:T(8,128)(2,1)} %bitcast.3), calls=%async_computation | async-start | bytes 65536 | tf_op jit(solution)/shard_map/all_to_all | solution.py:41
  9.7 0.7 compare_select_fusion.5
  10.3 0.7 compare_select_fusion.4
  11.0 0.7 compare_select_fusion
  11.8 0.5 fusion.22
  12.3 1.4 %fusion.26 = f32[1280,256]{1,0:T(8,128)} fusion(bf16[1280,128]{1,0:T(8,128)(2,1)S(1)} %copy-done.1, bf16[128,256]{1,0:T(8,128)(2,1)S(1)} %copy-done.8), kind=kOutput, calls=%fused_computation.56 | convolution fusion | flops 83886080 | bytes 1703936 | tf_op jit(solution)/shard_map/dot_general | solution.py:64
  13.8 1.5 %gather_fusion.1 = bf16[256,128]{1,0:T(8,128)(2,1)} fusion(bf16[1280,128]{1,0:T(8,128)(2,1)S(1)} %copy-done.1, s32[1024]{0:T(1024)S(1)} %pad_clamp_fusion.2), kind=kCustom, calls=%fused_computation.1 | custom fusion | bytes 132096 | tf_op jit(solution)/shard_map/gather | solution.py:42
  15.3 4.9 %all-to-all-start.1 = ((bf16[8,32,128]{2,1,0:T(8,128)(2,1)}), bf16[8,32,128]{2,1,0:T(8,128)(2,1)S(1)}, u32[]{:S(2)}, u32[]{:S(2)}) async-start(bf16[8,32,128]{2,1,0:T(8,128)(2,1)} %bitcast.6), calls=%async_computation.1 | async-start | bytes 131072 | tf_op jit(solution)/shard_map/all_to_all | solution.py:42
  20.3 5.8 %all-to-all-done.1 = bf16[8,32,128]{2,1,0:T(8,128)(2,1)S(1)} async-done(((bf16[8,32,128]{2,1,0:T(8,128)(2,1)}), bf16[8,32,128]{2,1,0:T(8,128)(2,1)S(1)}, u32[]{:S(2)}, u32[]{:S(2)}) %all-to-all-start.1) | async-done | bytes 65568 | tf_op jit(solution)/shard_map/all_to_all | solution.py:42
  26.1 2.0 %gather_fusion.2 = bf16[48,128,128]{2,1,0:T(8,128)(2,1)} fusion(bf16[13,128,128]{2,1,0:T(8,128)(2,1)S(1)} %bitcast.65, s32[1024]{0:T(1024)S(1)} %pad_clamp_fusion.1), kind=kCustom, calls=%fused_computation.2 | custom fusion | bytes 3145920 | tf_op jit(solution)/shard_map/gather | solution.py:57
  28.1 4.3 %convolution_bitcast_fusion.1 = f32[48,128,128]{1,2,0:T(8,128)} fusion(bf16[48,128,128]{2,1,0:T(8,128)(2,1)} %gather_fusion.2, bf16[48,128,128]{2,1,0:T(8,128)(2,1)S(1)} %copy-done), kind=kOutput, calls=%fused_computation.11 | convolution fusion | flops 201326592 | bytes 6291456 | tf_op jit(solution)/shard_map/tij,tjf->tif/dot_general | solution.py:56
  32.4 3.6 %copy.28 = f32[48,128,128]{2,0,1:T(8,128)} copy(f32[48,128,128]{1,2,0:T(8,128)} %convolution_bitcast_fusion.1) | data formatting | bytes 6291456 | tf_op jit(solution)/shard_map/tij,tjf->tif/dot_general | solution.py:56
  36.0 3.3 %fusion.1 = bf16[10,128,128]{2,0,1:T(8,128)(2,1)S(1)} fusion(f32[48,128,128]{2,0,1:T(8,128)} %copy.28, f32[10,128]{0,1:T(8,128)S(1)} %copy.29, s32[48]{0:T(128)S(1)} %copy-done.14, pred[48]{0:T(512)(128)(4,1)S(1)} %iota_compare_fusion.2), kind=kOutput, calls=%fused_computation.16 | convolution fusion | flops 94700480 | bytes 3478768 | tf_op jit(solution)/shard_map/bt,tif->bif/dot_general | solution.py:59
  39.4 1.6 %multiply_convert_fusion = (bf16[1280,256]{1,0:T(8,128)(2,1)S(1)}, bf16[1280,256]{1,0:T(8,128)(2,1)}) fusion(bf16[1280,256]{1,0:T(8,128)(2,1)S(1)} %copy-done.16, f32[1280,256]{1,0:T(8,128)S(1)} %copy-done.4, bf16[1280,128]{1,0:T(8,128)(2,1)S(1)} %bitcast.69, bf16[128,256]{1,0:T(8,128)(2,1)S(1)} %copy-done.17), kind=kOutput, calls=%fused_computation.13 | convolution fusion | flops 88145920 | bytes 3670016 | tf_op jit(solution)/shard_map/dot_general | solution.py:64
  41.0 1.0 fusion.27
  42.0 1.0 convolution_bitcast_fusion.2
  42.9 0.3 fusion
  43.3 0.8 gather_fusion.3
  44.2 2.3 %convolution_bitcast_fusion = f32[48,128,128]{1,2,0:T(8,128)} fusion(bf16[48,128,128]{2,1,0:T(8,128)(2,1)S(1)} %gather_fusion.3, bf16[48,128,128]{2,1,0:T(8,128)(2,1)S(1)} %copy-done), kind=kOutput, calls=%fused_computation.10 | convolution fusion | flops 201326592 | bytes 6291456 | tf_op jit(solution)/shard_map/tij,tif->tjf/dot_general | solution.py:78
  46.5 3.6 %copy.32 = f32[48,128,128]{2,0,1:T(8,128)} copy(f32[48,128,128]{1,2,0:T(8,128)} %convolution_bitcast_fusion) | data formatting | bytes 6291456 | tf_op jit(solution)/shard_map/tij,tif->tjf/dot_general | solution.py:78
  50.1 3.1 %fusion.25 = (bf16[13,128,128]{2,0,1:T(8,128)(2,1)S(1)}, f32[13,128,128]{2,0,1:T(8,128)S(1)}) fusion(f32[48,128,128]{2,0,1:T(8,128)} %copy.32, s32[48]{0:T(128)S(1)} %copy-done.15, pred[48]{0:T(512)(128)(4,1)S(1)} %iota_compare_fusion.2), kind=kOutput, calls=%fused_computation.55 | convolution fusion | flops 122897632 | bytes 4423920 | tf_op jit(solution)/shard_map/st,tjf->sjf/dot_general | solution.py:79
  53.2 0.8 copy-done.5
  54.1 0.6 copy.39
  54.7 4.3 %all-to-all-start.2 = ((bf16[4,32,128]{2,1,0:T(8,128)(2,1)}), bf16[4,32,128]{2,1,0:T(8,128)(2,1)S(1)}, u32[]{:S(2)}, u32[]{:S(2)}) async-start(bf16[4,32,128]{2,1,0:T(8,128)(2,1)} %bitcast.26), calls=%async_computation.2 | async-start | bytes 65536 | tf_op jit(solution)/shard_map/all_to_all | solution.py:93
  59.1 1.0 all_to_all.29
  60.0 3.8 %all-to-all-done.2 = bf16[4,32,128]{2,1,0:T(8,128)(2,1)S(1)} async-done(((bf16[4,32,128]{2,1,0:T(8,128)(2,1)}), bf16[4,32,128]{2,1,0:T(8,128)(2,1)S(1)}, u32[]{:S(2)}, u32[]{:S(2)}) %all-to-all-start.2) | async-done | bytes 32800 | tf_op jit(solution)/shard_map/all_to_all | solution.py:93
  63.8 0.6 copy-done.10
  64.4 2.6 %all-to-all-start.4 = ((f32[32,1,2048]{2,1,0:T(1,128)}), f32[32,1,2048]{2,1,0:T(1,128)S(1)}, u32[]{:S(2)}, u32[]{:S(2)}) async-start(f32[32,1,2048]{2,1,0:T(1,128)} %all_to_all.29), calls=%async_computation.4 | async-start | bytes 524288 | tf_op jit(solution)/shard_map/all_to_all | solution.py:15
  67.0 1.1 %slice.48 = bf16[2,128,128]{2,0,1:T(2,128)(2,1)S(1)} slice(bf16[13,128,128]{2,0,1:T(8,128)(2,1)} %copy-done.5), slice={[11:13], [0:128], [0:128]} | slice | bytes 131072 | tf_op jit(solution)/shard_map/slice | solution.py:89
  68.1 0.6 copy.34
  68.8 8.6 %all-to-all-done.4 = f32[32,1,2048]{2,1,0:T(1,128)S(1)} async-done(((f32[32,1,2048]{2,1,0:T(1,128)}), f32[32,1,2048]{2,1,0:T(1,128)S(1)}, u32[]{:S(2)}, u32[]{:S(2)}) %all-to-all-start.4) | async-done | bytes 262176 | tf_op jit(solution)/shard_map/all_to_all | solution.py:15
  77.4 4.0 %all-to-all-start.3 = ((bf16[8,32,128]{2,1,0:T(8,128)(2,1)}), bf16[8,32,128]{2,1,0:T(8,128)(2,1)}, u32[]{:S(2)}, u32[]{:S(2)}) async-start(bf16[8,32,128]{2,1,0:T(8,128)(2,1)} %bitcast.71), calls=%async_computation.3 | async-start | bytes 131072 | tf_op jit(solution)/shard_map/all_to_all | solution.py:94
  81.6 5.7 %all-to-all-done.3 = bf16[8,32,128]{2,1,0:T(8,128)(2,1)} async-done(((bf16[8,32,128]{2,1,0:T(8,128)(2,1)}), bf16[8,32,128]{2,1,0:T(8,128)(2,1)}, u32[]{:S(2)}, u32[]{:S(2)}) %all-to-all-start.3) | async-done | bytes 65568 | tf_op jit(solution)/shard_map/all_to_all | solution.py:94
  87.3 0.8 broadcast_in_dim.11
  88.1 2.6 %all-to-all-start.5 = ((f32[32,1,2048]{2,1,0:T(1,128)}), f32[32,1,2048]{2,1,0:T(1,128)S(1)}, u32[]{:S(2)}, u32[]{:S(2)}) async-start(f32[32,1,2048]{2,1,0:T(1,128)} %broadcast_in_dim.11), calls=%async_computation.5 | async-start | bytes 524288 | tf_op jit(solution)/shard_map/all_to_all | solution.py:17
  90.7 0.5 fusion.21
  91.3 0.2 copy.33
  91.6 0.6 copy-done.9
  92.2 0.3 convolution_add_fusion.1
  92.5 1.6 %scatter_custom_fusion = f32[1280,128]{1,0:T(8,128)S(1)} fusion(f32[1280,128]{1,0:T(8,128)S(1)} %convolution_add_fusion.1, s32[128]{0:T(128)} %fusion.21, bf16[128,128]{1,0:T(8,128)(2,1)S(1)} %bitcast.73), kind=kCustom, calls=%fused_computation.24 | custom fusion | flops 32768 | bytes 688128 | tf_op jit(solution)/shard_map/scatter-add | solution.py:97
  94.2 2.5 %scatter_custom_fusion.1 = f32[1280,128]{1,0:T(8,128)S(1)} fusion(f32[1280,128]{1,0:T(8,128)S(1)} %scatter_custom_fusion, s32[256]{0:T(256)S(1)} %bitcast.77, bf16[256,128]{1,0:T(8,128)(2,1)} %bitcast.25), kind=kCustom, calls=%fused_computation.22 | custom fusion | flops 65536 | bytes 720896 | tf_op jit(solution)/shard_map/scatter-add | solution.py:100
  96.7 0.8 convert_element_type.55
  97.4 3.7 %all-to-all-done.5 = f32[32,1,2048]{2,1,0:T(1,128)S(1)} async-done(((f32[32,1,2048]{2,1,0:T(1,128)}), f32[32,1,2048]{2,1,0:T(1,128)S(1)}, u32[]{:S(2)}, u32[]{:S(2)}) %all-to-all-start.5) | async-done | bytes 262176 | tf_op jit(solution)/shard_map/all_to_all | solution.py:17
  101.1 0.7 slice_reduce_fusion
  101.8 0.7 slice.37
  102.5 0.7 slice.35
  (51 shorter events, 1.0 us)
Async XLA Ops:
  0.6 11.1 %copy-start = (bf16[48,128,128]{2,1,0:T(8,128)(2,1)S(1)}, bf16[48,128,128]{2,1,0:T(8,128)(2,1)}, u32[]{:S(2)}) copy-start(bf16[48,128,128]{2,1,0:T(8,128)(2,1)} %param.13) | copy-start | bytes 4718596
  0.6 11.6 %copy-start.1 = (bf16[1280,128]{1,0:T(8,128)(2,1)S(1)}, bf16[1280,128]{1,0:T(8,128)(2,1)}, u32[]{:S(2)}) copy-start(bf16[1280,128]{1,0:T(8,128)(2,1)} %param.10) | copy-start | bytes 983044
  0.7 11.6 %copy-start.8 = (bf16[128,256]{1,0:T(8,128)(2,1)S(1)}, bf16[128,256]{1,0:T(8,128)(2,1)}, u32[]{:S(2)}) copy-start(bf16[128,256]{1,0:T(8,128)(2,1)} %param.17) | copy-start | bytes 196612
  3.9 11.4 %all-to-all-start = ((bf16[4,32,128]{2,1,0:T(8,128)(2,1)}), bf16[4,32,128]{2,1,0:T(8,128)(2,1)S(1)}, u32[]{:S(2)}, u32[]{:S(2)}) async-start(bf16[4,32,128]{2,1,0:T(8,128)(2,1)} %bitcast.3), calls=%async_computation | async-start | bytes 65536 | tf_op jit(solution)/shard_map/all_to_all | solution.py:41
  11.8 1.9 %copy-start.14 = (s32[48]{0:T(128)S(1)}, s32[48]{0:T(128)}, u32[]{:S(2)}) copy-start(s32[48]{0:T(128)} %param.14) | copy-start | bytes 580
  15.3 10.8 %all-to-all-start.1 = ((bf16[8,32,128]{2,1,0:T(8,128)(2,1)}), bf16[8,32,128]{2,1,0:T(8,128)(2,1)S(1)}, u32[]{:S(2)}, u32[]{:S(2)}) async-start(bf16[8,32,128]{2,1,0:T(8,128)(2,1)} %bitcast.6), calls=%async_computation.1 | async-start | bytes 131072 | tf_op jit(solution)/shard_map/all_to_all | solution.py:42
  36.0 3.4 %copy-start.4 = (f32[1280,256]{1,0:T(8,128)S(1)}, f32[1280,256]{1,0:T(8,128)}, u32[]{:S(2)}) copy-start(f32[1280,256]{1,0:T(8,128)} %fusion.26) | copy-start | bytes 3932164
  36.0 3.4 %copy-start.16 = (bf16[1280,256]{1,0:T(8,128)(2,1)S(1)}, bf16[1280,256]{1,0:T(8,128)(2,1)}, u32[]{:S(2)}) copy-start(bf16[1280,256]{1,0:T(8,128)(2,1)} %param.19) | copy-start | bytes 1966084
  36.0 3.4 %copy-start.17 = (bf16[128,256]{1,0:T(8,128)(2,1)S(1)}, bf16[128,256]{1,0:T(8,128)(2,1)}, u32[]{:S(2)}) copy-start(bf16[128,256]{1,0:T(8,128)(2,1)} %param.18) | copy-start | bytes 196612
  41.0 2.3 %copy-start.2 = (bf16[1280,256]{1,0:T(8,128)(2,1)}, bf16[1280,256]{1,0:T(8,128)(2,1)S(1)}, u32[]{:S(2)}) copy-start(bf16[1280,256]{1,0:T(8,128)(2,1)S(1)} %get-tuple-element.6) | copy-start | bytes 1966084
  46.5 3.6 %copy-start.15 = (s32[48]{0:T(128)S(1)}, s32[48]{0:T(128)}, u32[]{:S(2)}) copy-start(s32[48]{0:T(128)} %param.15) | copy-start | bytes 580
  50.1 8.9 %copy-start.6 = (f32[128,256]{1,0:T(8,128)S(1)}, f32[128,256]{1,0:T(8,128)}, u32[]{:S(2)}) copy-start(f32[128,256]{1,0:T(8,128)} %fusion.27) | copy-start | bytes 393220
  50.1 8.9 %copy-start.7 = (f32[128,256]{1,0:T(8,128)S(1)}, f32[128,256]{1,0:T(8,128)}, u32[]{:S(2)}) copy-start(f32[128,256]{1,0:T(8,128)} %convolution_bitcast_fusion.2) | copy-start | bytes 393220
  53.2 0.8 copy-start.5
  53.2 28.2 %copy-start.13 = (s32[1,4,32]{2,1,0:T(4,128)S(1)}, s32[1,4,32]{2,1,0:T(4,128)}, u32[]{:S(2)}) copy-start(s32[1,4,32]{2,1,0:T(4,128)} %param.11) | copy-start | bytes 1540
  54.7 36.5 %copy-start.12 = (s32[1,8,32]{2,1,0:T(8,128)S(1)}, s32[1,8,32]{2,1,0:T(8,128)}, u32[]{:S(2)}) copy-start(s32[1,8,32]{2,1,0:T(8,128)} %param.12) | copy-start | bytes 3076
  54.7 9.1 %all-to-all-start.2 = ((bf16[4,32,128]{2,1,0:T(8,128)(2,1)}), bf16[4,32,128]{2,1,0:T(8,128)(2,1)S(1)}, u32[]{:S(2)}, u32[]{:S(2)}) async-start(bf16[4,32,128]{2,1,0:T(8,128)(2,1)} %bitcast.26), calls=%async_computation.2 | async-start | bytes 65536 | tf_op jit(solution)/shard_map/all_to_all | solution.py:93
  63.8 0.6 copy-start.10
  64.4 13.0 %all-to-all-start.4 = ((f32[32,1,2048]{2,1,0:T(1,128)}), f32[32,1,2048]{2,1,0:T(1,128)S(1)}, u32[]{:S(2)}, u32[]{:S(2)}) async-start(f32[32,1,2048]{2,1,0:T(1,128)} %all_to_all.29), calls=%async_computation.4 | async-start | bytes 524288 | tf_op jit(solution)/shard_map/all_to_all | solution.py:15
  67.0 24.6 %copy-start.3 = (bf16[1280,256]{1,0:T(8,128)(2,1)S(1)}, bf16[1280,256]{1,0:T(8,128)(2,1)}, u32[]{:S(2)}) copy-start(bf16[1280,256]{1,0:T(8,128)(2,1)} %copy-done.2) | copy-start | bytes 1966084
  77.4 9.9 %all-to-all-start.3 = ((bf16[8,32,128]{2,1,0:T(8,128)(2,1)}), bf16[8,32,128]{2,1,0:T(8,128)(2,1)}, u32[]{:S(2)}, u32[]{:S(2)}) async-start(bf16[8,32,128]{2,1,0:T(8,128)(2,1)} %bitcast.71), calls=%async_computation.3 | async-start | bytes 131072 | tf_op jit(solution)/shard_map/all_to_all | solution.py:94
  88.1 13.0 %all-to-all-start.5 = ((f32[32,1,2048]{2,1,0:T(1,128)}), f32[32,1,2048]{2,1,0:T(1,128)S(1)}, u32[]{:S(2)}, u32[]{:S(2)}) async-start(f32[32,1,2048]{2,1,0:T(1,128)} %broadcast_in_dim.11), calls=%async_computation.5 | async-start | bytes 524288 | tf_op jit(solution)/shard_map/all_to_all | solution.py:17
  91.3 0.8 copy-start.9
  91.6 1.0 copy-start.11

commit v2 on v1

--- a/solution.py
+++ b/solution.py
@@ -19,6 +19,28 @@
     return total[:rows], total[rows:]
 
 
+def exchange(dom_part, grp_part):
+    axes = ("dom", "grp")
+    n_dom, n_grp = dom_part.shape[0], grp_part.shape[0]
+    a = lax.axis_index("dom")
+    b = lax.axis_index("grp")
+    cell = dom_part.shape[1:]
+    buf = jnp.zeros((n_dom, n_grp) + cell, dom_part.dtype)
+    buf = lax.dynamic_update_slice_in_dim(buf, dom_part[:, None], b, axis=1)
+    buf = lax.dynamic_update_slice_in_dim(buf, grp_part[None], a, axis=0)
+    got = lax.all_to_all(buf.reshape((n_dom * n_grp,) + cell), axes, 0, 0, tiled=True)
+    got = got.reshape((n_dom, n_grp) + cell)
+    from_dom = lax.dynamic_index_in_dim(got, b, axis=1, keepdims=False)
+    own_dom = lax.dynamic_index_in_dim(dom_part, a, axis=0, keepdims=True)
+    from_dom = lax.dynamic_update_slice_in_dim(from_dom, own_dom, a, axis=0)
+    from_grp = lax.dynamic_index_in_dim(got, a, axis=0, keepdims=False)
+    return from_dom, from_grp
+
+
+def one_hot_rows(index, count):
+    return (index.reshape(-1)[:, None] == jnp.arange(count, dtype=jnp.int32)[None, :]).astype(jnp.bfloat16)
+
+
 def per_device(
     features,
     send_dom,
@@ -37,9 +59,13 @@
     block_count = node_count // tile_size
     dom_index = send_dom[0]
     grp_index = send_grp[0]
-    dom_peers = dom_index.shape[0]
-    recv_dom = lax.all_to_all(features[dom_index], "dom", split_axis=0, concat_axis=0, tiled=True)
-    recv_grp = lax.all_to_all(features[grp_index], "grp", split_axis=0, concat_axis=0, tiled=True)
+    n_dom, bnd = dom_index.shape
+    n_grp = grp_index.shape[0]
+    send_index = jnp.concatenate([dom_index.reshape(-1), grp_index.reshape(-1)])
+    pick = one_hot_rows(send_index, node_count)
+    sent = jnp.dot(pick, features, preferred_element_type=jnp.float32).astype(jnp.bfloat16)
+    sent = sent.reshape(n_dom + n_grp, bnd, width)
+    recv_dom, recv_grp = exchange(sent[:n_dom], sent[n_dom:])
     source = jnp.concatenate(
         [features, recv_dom.reshape(-1, width), recv_grp.reshape(-1, width)], axis=0
     )
@@ -79,26 +105,13 @@
     grad_source = jnp.einsum(
         "st,tjf->sjf", to_source, backward, precision=lax.Precision.HIGHEST
     ).reshape(-1, width)
-    dom_rows = dom_peers * dom_index.shape[1]
-    back_dom = (
-        grad_source[node_count : node_count + dom_rows]
-        .reshape(dom_index.shape[0], dom_index.shape[1], width)
-        .astype(jnp.bfloat16)
-    )
-    back_grp = (
-        grad_source[node_count + dom_rows :]
-        .reshape(grp_index.shape[0], grp_index.shape[1], width)
-        .astype(jnp.bfloat16)
-    )
-    ret_dom = lax.all_to_all(back_dom, "dom", split_axis=0, concat_axis=0, tiled=True)
-    ret_grp = lax.all_to_all(back_grp, "grp", split_axis=0, concat_axis=0, tiled=True)
+    remote = grad_source[node_count:].astype(jnp.bfloat16).reshape(n_dom + n_grp, bnd, width)
+    ret_dom, ret_grp = exchange(remote[:n_dom], remote[n_dom:])
     grad_self, grad_neigh = weight_sum(part_self, part_neigh)
+    returned = jnp.concatenate([ret_dom.reshape(-1, width), ret_grp.reshape(-1, width)])
     grad_total = grad_own + grad_source[:node_count]
-    grad_total = grad_total.at[dom_index.reshape(-1)].add(
-        ret_dom.reshape(-1, width).astype(jnp.float32)
-    )
-    grad_total = grad_total.at[grp_index.reshape(-1)].add(
-        ret_grp.reshape(-1, width).astype(jnp.float32)
+    grad_total = grad_total + lax.dot_general(
+        pick, returned, (((0,), (0,)), ((), ())), preferred_element_type=jnp.float32
     )
     return (output, grad_total.astype(jnp.bfloat16), grad_self, grad_neigh)
 

time: 104 us -> 88.5 us (0.85)
  other arithmetic: 8.48 us -> 1.21 us
  starting transfers between devices: 23.5 us -> 18.9 us
  waiting for transfers between devices: 27.6 us -> 23.7 us
  matrix products: 19.2 us -> 20.9 us
  local copies, waits for them, and re-layouts: 22.8 us -> 21.5 us
    all_to_all x1, waiting for transfers between devices: 8.64 us -> 0.01 us  [weight_sum(): lax.all_to_all(chunks, axes, 0, 0, tiled=True)]
    all_to_all x4 -> x2, starting transfers between devices: 18.3 us -> 13.1 us  [exchange(): lax.all_to_all(buf.reshape((n_dom * n_grp,) + cell), axes, 0, 0, tiled=True)]
    all_to_all x1, waiting for transfers between devices: 3.7 us -> 8.09 us  [weight_sum(): total = lax.all_to_all(spread, axes, 0, 0, tiled=True).reshape(-1)]
    scatter-add x2 -> x0, other arithmetic: 4.13 us -> none  [the longest x1 2.5 us: per_device(): grad_total.at[grp_index.reshape(-1)]]
    gather x2 -> x0, local copies, waits for them, and re-layouts: 3.74 us -> none  [the longest x1 2.27 us: per_device(): features[dom_index]]
    dynamic_update_slice x0 -> x6, local copies, waits for them, and re-layouts: none -> 3.23 us  [the longest x2 1.27 us: exchange(): buf = lax.dynamic_update_slice_in_dim(buf, grp_part[None], a, axis=0)]
    dot_general x0 -> x2, matrix products: none -> 3.03 us  [the longest x1 1.56 us: per_device(): lax.dot_general(pick, returned, (((0,), (0,)), ((), ())), preferred_eleme...]
    another operation x2 -> x4, local copies, waits for them, and re-layouts: 0.16 us -> 3.13 us  [the longest x2 1.64 us: per_device(): send_index = jnp.concatenate([dom_index.reshape(-1), grp_index.reshape(-1)])]
  transfers between devices with their start and end apart: 6 -> 4, of which waited for: 5 -> 3; matrix products, arithmetic and copies ran while one was open for 13% -> 21% of each run, Pallas kernels for 0% -> 0%
where the time goes in v2:
time: 88.5 us; the launch traced here: 87.9 us
  waiting for transfers between devices  23.7 us (27%)
  local copies, waits for them, and re-layouts  21.5 us (24%)
  matrix products  20.9 us (24%)
  starting transfers between devices  18.9 us (21%)
  between operations  1.64 us (2%)
  other arithmetic  1.21 us (1%)
    all_to_all x2, waiting for transfers between devices, exchange(): lax.all_to_all(buf.reshape((n_dom * n_grp,) + cell), axes, 0, 0, tiled=True)  15.6 us
    all_to_all x2, starting transfers between devices, exchange(): lax.all_to_all(buf.reshape((n_dom * n_grp,) + cell), axes, 0, 0, tiled=True)  13.1 us
    all_to_all x1, waiting for transfers between devices, weight_sum(): total = lax.all_to_all(spread, axes, 0, 0, tiled=True).reshape(-1)  8.09 us
    dot_general x1, matrix products, per_device(): jnp.einsum('tij,tjf->tif', tile_vals, source[tile_src], preferred_element...  4.3 us
    dot_general x1, local copies, waits for them, and re-layouts, per_device(): jnp.einsum('tij,tif->tjf', tile_vals, picked, preferred_element_type=jnp....  3.61 us
    dot_general x1, local copies, waits for them, and re-layouts, per_device(): jnp.einsum('tij,tjf->tif', tile_vals, source[tile_src], preferred_element...  3.61 us
    all_to_all x1, starting transfers between devices, weight_sum(): lax.all_to_all(chunks, axes, 0, 0, tiled=True)  3.3 us
    dot_general x1, matrix products, per_device(): jnp.einsum('bt,tif->bif', to_target, products, precision=lax.Precision.HI...  3.26 us
  transfers between devices with their start and end apart: 4, of which 3 were waited for; matrix products, arithmetic and copies ran while one was open for 21% of the time, Pallas kernels for 0%

profile of v2, /device:TPU:0, one launch (start us, length us, event | category | flops | bytes accessed | tf_op | source)
XLA Modules:
  0.0 87.9 jit_solution(10371632384816216487)
XLA Ops:
  0.6 0.0 copy-start
  0.6 0.9 %reshape_squeeze.7 = s32[256]{0:T(256)S(1)} reshape(s32[1,8,32]{2,1,0:T(8,128)} %param.12) | data formatting | bytes 2048 | tf_op jit(solution)/shard_map/reshape;squeeze | solution.py:64
  1.5 0.8 reshape_squeeze.6
  2.3 1.5 %fusion.4 = bf16[384,128]{1,0:T(8,128)(2,1)S(1)} fusion(bf16[1280,128]{1,0:T(8,128)(2,1)} %param.10, s32[384]{0:T(512)S(1)} %pad_add_fusion), kind=kOutput, calls=%fused_computation.17 | convolution fusion | flops 126369792 | bytes 427520 | tf_op jit(solution)/shard_map/dot_general | solution.py:66
  3.8 0.0 copy-start.8
  3.9 0.7 broadcast.20.clone
  4.6 0.6 constant_dynamic-update-slice_fusion.3
  5.2 0.6 constant_dynamic-update-slice_fusion.2
  5.9 7.3 %all-to-all-start = ((bf16[32,32,128]{2,1,0:T(8,128)(2,1)}), bf16[32,32,128]{2,1,0:T(8,128)(2,1)S(1)}, u32[]{:S(2)}, u32[]{:S(2)}) async-start(bf16[32,32,128]{2,1,0:T(8,128)(2,1)} %bitcast.5), calls=%async_computation | async-start | bytes 524288 | tf_op jit(solution)/shard_map/all_to_all | solution.py:31
  13.8 0.5 fusion.25
  14.3 0.1 fusion.11
  14.5 0.1 copy.46
  14.7 1.4 %fusion.30 = f32[1280,256]{1,0:T(8,128)} fusion(bf16[1280,128]{1,0:T(8,128)(2,1)S(1)} %copy-done.3, bf16[128,256]{1,0:T(8,128)(2,1)S(1)} %copy-done.5), kind=kOutput, calls=%fused_computation.63 | convolution fusion | flops 83886080 | bytes 1703936 | tf_op jit(solution)/shard_map/dot_general | solution.py:90
  16.0 7.5 %all-to-all-done = bf16[32,32,128]{2,1,0:T(8,128)(2,1)S(1)} async-done(((bf16[32,32,128]{2,1,0:T(8,128)(2,1)}), bf16[32,32,128]{2,1,0:T(8,128)(2,1)S(1)}, u32[]{:S(2)}, u32[]{:S(2)}) %all-to-all-start) | async-done | bytes 262176 | tf_op jit(solution)/shard_map/all_to_all | solution.py:31
  23.6 1.9 %gather_fusion = bf16[48,128,128]{2,1,0:T(8,128)(2,1)} fusion(bf16[13,128,128]{2,1,0:T(8,128)(2,1)S(1)} %bitcast.67, s32[1024]{0:T(1024)S(1)} %pad_clamp_fusion.1), kind=kCustom, calls=%fused_computation | custom fusion | bytes 3145920 | tf_op jit(solution)/shard_map/gather | solution.py:83
  25.6 4.3 %convolution_bitcast_fusion.1 = f32[48,128,128]{1,2,0:T(8,128)} fusion(bf16[48,128,128]{2,1,0:T(8,128)(2,1)} %gather_fusion, bf16[48,128,128]{2,1,0:T(8,128)(2,1)S(1)} %copy-done), kind=kOutput, calls=%fused_computation.11 | convolution fusion | flops 201326592 | bytes 6291456 | tf_op jit(solution)/shard_map/tij,tjf->tif/dot_general | solution.py:82
  29.9 3.6 %copy.45 = f32[48,128,128]{2,0,1:T(8,128)} copy(f32[48,128,128]{1,2,0:T(8,128)} %convolution_bitcast_fusion.1) | data formatting | bytes 6291456 | tf_op jit(solution)/shard_map/tij,tjf->tif/dot_general | solution.py:82
  33.5 3.3 %fusion.3 = bf16[10,128,128]{2,0,1:T(8,128)(2,1)S(1)} fusion(f32[48,128,128]{2,0,1:T(8,128)} %copy.45, f32[10,128]{0,1:T(8,128)S(1)} %copy.46, s32[48]{0:T(128)S(1)} %copy-done.8, pred[48]{0:T(512)(128)(4,1)S(1)} %iota_compare_fusion.7), kind=kOutput, calls=%fused_computation.16 | convolution fusion | flops 94700480 | bytes 3478768 | tf_op jit(solution)/shard_map/bt,tif->bif/dot_general | solution.py:85
  36.7 0.1 copy.47
  36.9 1.6 %multiply_convert_fusion = (bf16[1280,256]{1,0:T(8,128)(2,1)S(1)}, bf16[1280,256]{1,0:T(8,128)(2,1)}) fusion(bf16[1280,256]{1,0:T(8,128)(2,1)S(1)} %copy-done.10, f32[1280,256]{1,0:T(8,128)S(1)} %copy-done.4, bf16[1280,128]{1,0:T(8,128)(2,1)S(1)} %bitcast.71, bf16[128,256]{1,0:T(8,128)(2,1)S(1)} %copy-done.11), kind=kOutput, calls=%fused_computation.13 | convolution fusion | flops 88145920 | bytes 3670016 | tf_op jit(solution)/shard_map/dot_general | solution.py:90
  38.5 0.3 fusion.31
  38.8 0.3 convolution_bitcast_fusion.2
  39.2 1.0 %all_to_all.21 = f32[32,1,2048]{2,1,0:T(1,128)} reshape(f32[256,256]{1,0:T(8,128)S(1)} %pad_maximum_fusion.1) | data formatting | bytes 524288 | tf_op jit(solution)/shard_map/all_to_all | solution.py:15
  40.1 3.3 %all-to-all-start.2 = ((f32[32,1,2048]{2,1,0:T(1,128)}), f32[32,1,2048]{2,1,0:T(1,128)}, u32[]{:S(2)}, u32[]{:S(2)}) async-start(f32[32,1,2048]{2,1,0:T(1,128)} %all_to_all.21), calls=%async_computation.2 | async-start | bytes 524288 | tf_op jit(solution)/shard_map/all_to_all | solution.py:15
  43.4 0.3 fusion
  43.8 0.8 gather_fusion.1
  44.7 2.3 %convolution_bitcast_fusion = f32[48,128,128]{1,2,0:T(8,128)} fusion(bf16[48,128,128]{2,1,0:T(8,128)(2,1)S(1)} %gather_fusion.1, bf16[48,128,128]{2,1,0:T(8,128)(2,1)S(1)} %copy-done), kind=kOutput, calls=%fused_computation.10 | convolution fusion | flops 201326592 | bytes 6291456 | tf_op jit(solution)/shard_map/tij,tif->tjf/dot_general | solution.py:104
  47.0 3.6 %copy.49 = f32[48,128,128]{2,0,1:T(8,128)} copy(f32[48,128,128]{1,2,0:T(8,128)} %convolution_bitcast_fusion) | data formatting | bytes 6291456 | tf_op jit(solution)/shard_map/tij,tif->tjf/dot_general | solution.py:104
  50.6 3.0 %fusion.29 = (bf16[13,128,128]{2,0,1:T(8,128)(2,1)S(1)}, f32[13,128,128]{2,0,1:T(8,128)S(1)}) fusion(f32[48,128,128]{2,0,1:T(8,128)} %copy.49, s32[48]{0:T(128)S(1)} %copy-done.9, pred[48]{0:T(512)(128)(4,1)S(1)} %iota_compare_fusion.7), kind=kOutput, calls=%fused_computation.62 | convolution fusion | flops 122897632 | bytes 4423920 | tf_op jit(solution)/shard_map/st,tjf->sjf/dot_general | solution.py:105
  53.7 0.1 slice.66
  53.7 0.1 slice.67
  53.9 0.7 broadcast.20
  54.6 0.6 constant_dynamic-update-slice_fusion.1
  55.2 0.6 constant_dynamic-update-slice_fusion
  55.9 5.8 %all-to-all-start.1 = ((bf16[32,32,128]{2,1,0:T(8,128)(2,1)}), bf16[32,32,128]{2,1,0:T(8,128)(2,1)S(1)}, u32[]{:S(2)}, u32[]{:S(2)}) async-start(bf16[32,32,128]{2,1,0:T(8,128)(2,1)} %bitcast.23), calls=%async_computation.1 | async-start | bytes 524288 | tf_op jit(solution)/shard_map/all_to_all | solution.py:31
  61.6 0.2 copy.50
  61.9 0.6 copy-done.6
  62.5 0.3 convolution_add_fusion.2
  62.8 1.1 %reduce_sum.9 = f32[2048]{0:T(1024)S(1)} reduce(f32[32,1,2048]{2,1,0:T(1,128)} %all-to-all-done.2, f32[]{:T(128)} %constant.44.clone.1), dimensions={0,1}, to_apply=%region_0.1 | reduce | flops 63488 | bytes 270340 | tf_op jit(solution)/shard_map/reduce_sum | solution.py:15
  63.9 8.1 %all-to-all-done.1 = bf16[32,32,128]{2,1,0:T(8,128)(2,1)S(1)} async-done(((bf16[32,32,128]{2,1,0:T(8,128)(2,1)}), bf16[32,32,128]{2,1,0:T(8,128)(2,1)S(1)}, u32[]{:S(2)}, u32[]{:S(2)}) %all-to-all-start.1) | async-done | bytes 262176 | tf_op jit(solution)/shard_map/all_to_all | solution.py:31
  72.0 0.8 broadcast_in_dim.43
  72.9 2.6 %all-to-all-start.3 = ((f32[32,1,2048]{2,1,0:T(1,128)}), f32[32,1,2048]{2,1,0:T(1,128)S(1)}, u32[]{:S(2)}, u32[]{:S(2)}) async-start(f32[32,1,2048]{2,1,0:T(1,128)} %broadcast_in_dim.43), calls=%async_computation.3 | async-start | bytes 524288 | tf_op jit(solution)/shard_map/all_to_all | solution.py:17
  75.5 0.7 dynamic-slice_dynamic-update-slice_fusion
  76.2 1.6 %fusion.1 = bf16[1280,128]{1,0:T(8,128)(2,1)} fusion(f32[1280,128]{1,0:T(8,128)S(1)} %convolution_add_fusion.2, s32[384]{0:T(512)S(1)} %pad_add_fusion, bf16[256,128]{1,0:T(8,128)(2,1)S(1)} %bitcast.86, bf16[128,128]{1,0:T(8,128)(2,1)S(1)} %bitcast.87), kind=kOutput, calls=%fused_computation.7 | convolution fusion | flops 126844928 | bytes 1082880 | tf_op jit(solution)/shard_map/dot_general | solution.py:113
  77.7 8.1 %all-to-all-done.3 = f32[32,1,2048]{2,1,0:T(1,128)S(1)} async-done(((f32[32,1,2048]{2,1,0:T(1,128)}), f32[32,1,2048]{2,1,0:T(1,128)S(1)}, u32[]{:S(2)}, u32[]{:S(2)}) %all-to-all-start.3) | async-done | bytes 262176 | tf_op jit(solution)/shard_map/all_to_all | solution.py:17
  85.8 0.7 slice_reduce_fusion
  86.5 0.7 slice.56
  87.2 0.7 slice.58
  (38 shorter events, 0.2 us)
Async XLA Ops:
  0.6 13.2 %copy-start = (bf16[48,128,128]{2,1,0:T(8,128)(2,1)S(1)}, bf16[48,128,128]{2,1,0:T(8,128)(2,1)}, u32[]{:S(2)}) copy-start(bf16[48,128,128]{2,1,0:T(8,128)(2,1)} %param.13) | copy-start | bytes 4718596
  3.8 10.6 %copy-start.8 = (s32[48]{0:T(128)S(1)}, s32[48]{0:T(128)}, u32[]{:S(2)}) copy-start(s32[48]{0:T(128)} %param.14) | copy-start | bytes 580
  3.8 10.7 %copy-start.9 = (s32[48]{0:T(128)S(1)}, s32[48]{0:T(128)}, u32[]{:S(2)}) copy-start(s32[48]{0:T(128)} %param.15) | copy-start | bytes 580
  3.8 10.8 %copy-start.3 = (bf16[1280,128]{1,0:T(8,128)(2,1)S(1)}, bf16[1280,128]{1,0:T(8,128)(2,1)}, u32[]{:S(2)}) copy-start(bf16[1280,128]{1,0:T(8,128)(2,1)} %param.10) | copy-start | bytes 983044
  3.8 10.8 %copy-start.5 = (bf16[128,256]{1,0:T(8,128)(2,1)S(1)}, bf16[128,256]{1,0:T(8,128)(2,1)}, u32[]{:S(2)}) copy-start(bf16[128,256]{1,0:T(8,128)(2,1)} %param.17) | copy-start | bytes 196612
  5.9 17.7 %all-to-all-start = ((bf16[32,32,128]{2,1,0:T(8,128)(2,1)}), bf16[32,32,128]{2,1,0:T(8,128)(2,1)S(1)}, u32[]{:S(2)}, u32[]{:S(2)}) async-start(bf16[32,32,128]{2,1,0:T(8,128)(2,1)} %bitcast.5), calls=%async_computation | async-start | bytes 524288 | tf_op jit(solution)/shard_map/all_to_all | solution.py:31
  33.5 3.4 %copy-start.4 = (f32[1280,256]{1,0:T(8,128)S(1)}, f32[1280,256]{1,0:T(8,128)}, u32[]{:S(2)}) copy-start(f32[1280,256]{1,0:T(8,128)} %fusion.30) | copy-start | bytes 3932164
  33.5 3.4 %copy-start.10 = (bf16[1280,256]{1,0:T(8,128)(2,1)S(1)}, bf16[1280,256]{1,0:T(8,128)(2,1)}, u32[]{:S(2)}) copy-start(bf16[1280,256]{1,0:T(8,128)(2,1)} %param.19) | copy-start | bytes 1966084
  33.5 3.4 %copy-start.11 = (bf16[128,256]{1,0:T(8,128)(2,1)S(1)}, bf16[128,256]{1,0:T(8,128)(2,1)}, u32[]{:S(2)}) copy-start(bf16[128,256]{1,0:T(8,128)(2,1)} %param.18) | copy-start | bytes 196612
  38.5 4.9 %copy-start.1 = (bf16[1280,256]{1,0:T(8,128)(2,1)}, bf16[1280,256]{1,0:T(8,128)(2,1)S(1)}, u32[]{:S(2)}) copy-start(bf16[1280,256]{1,0:T(8,128)(2,1)S(1)} %get-tuple-element.6) | copy-start | bytes 1966084
  40.1 15.8 %all-to-all-start.2 = ((f32[32,1,2048]{2,1,0:T(1,128)}), f32[32,1,2048]{2,1,0:T(1,128)}, u32[]{:S(2)}, u32[]{:S(2)}) async-start(f32[32,1,2048]{2,1,0:T(1,128)} %all_to_all.21), calls=%async_computation.2 | async-start | bytes 524288 | tf_op jit(solution)/shard_map/all_to_all | solution.py:15
  53.7 8.2 %copy-start.2 = (bf16[1280,256]{1,0:T(8,128)(2,1)S(1)}, bf16[1280,256]{1,0:T(8,128)(2,1)}, u32[]{:S(2)}) copy-start(bf16[1280,256]{1,0:T(8,128)(2,1)} %copy-done.1) | copy-start | bytes 1966084
  53.8 0.8 copy-start.7
  55.9 16.1 %all-to-all-start.1 = ((bf16[32,32,128]{2,1,0:T(8,128)(2,1)}), bf16[32,32,128]{2,1,0:T(8,128)(2,1)S(1)}, u32[]{:S(2)}, u32[]{:S(2)}) async-start(bf16[32,32,128]{2,1,0:T(8,128)(2,1)} %bitcast.23), calls=%async_computation.1 | async-start | bytes 524288 | tf_op jit(solution)/shard_map/all_to_all | solution.py:31
  61.6 0.8 copy-start.6
  72.9 13.0 %all-to-all-start.3 = ((f32[32,1,2048]{2,1,0:T(1,128)}), f32[32,1,2048]{2,1,0:T(1,128)S(1)}, u32[]{:S(2)}, u32[]{:S(2)}) async-start(f32[32,1,2048]{2,1,0:T(1,128)} %broadcast_in_dim.43), calls=%async_computation.3 | async-start | bytes 524288 | tf_op jit(solution)/shard_map/all_to_all | solution.py:17

commit v3 on v2

--- a/solution.py
+++ b/solution.py
@@ -2,6 +2,8 @@
 import jax.numpy as jnp
 from jax import lax
 from jax.sharding import PartitionSpec as P
+from jax.experimental import pallas as pl
+from jax.experimental.pallas import tpu as pltpu
 
 
 def weight_sum(part_self, part_neigh):
@@ -41,6 +43,47 @@
     return (index.reshape(-1)[:, None] == jnp.arange(count, dtype=jnp.int32)[None, :]).astype(jnp.bfloat16)
 
 
+def tile_pass(tile_tgt, tile_src, tile_count, tile_vals, blocks, out_count, transpose):
+    slots, size, _ = tile_vals.shape
+    in_count, _, wide = blocks.shape
+
+    def kernel(tgt_ref, src_ref, cnt_ref, tiles_ref, blocks_ref, out_ref):
+        out_ref[...] = jnp.zeros_like(out_ref)
+
+        def body(t, carry):
+            @pl.when(t < cnt_ref[0])
+            def _():
+                if transpose:
+                    read, write = tgt_ref[t], src_ref[t]
+                    part = lax.dot_general(
+                        tiles_ref[t], blocks_ref[read], (((0,), (0,)), ((), ())),
+                        preferred_element_type=jnp.float32,
+                    )
+                else:
+                    read, write = src_ref[t], tgt_ref[t]
+                    part = jnp.dot(tiles_ref[t], blocks_ref[read], preferred_element_type=jnp.float32)
+                out_ref[write] += part
+
+            return carry
+
+        lax.fori_loop(0, slots, body, 0)
+
+    whole = lambda i, *_: (0, 0, 0)
+    return pl.pallas_call(
+        kernel,
+        grid_spec=pltpu.PrefetchScalarGridSpec(
+            num_scalar_prefetch=3,
+            grid=(1,),
+            in_specs=[
+                pl.BlockSpec((slots, size, size), whole),
+                pl.BlockSpec((in_count, size, wide), whole),
+            ],
+            out_specs=pl.BlockSpec((out_count, size, wide), whole),
+        ),
+        out_shape=jax.ShapeDtypeStruct((out_count, size, wide), jnp.float32),
+    )(tile_tgt, tile_src, tile_count, tile_vals, blocks)
+
+
 def per_device(
     features,
     send_dom,
@@ -71,22 +114,13 @@
     )
     source = source.reshape(-1, tile_size, width)
     source_count = source.shape[0]
-    slot_count = tile_vals.shape[0]
-    usable = jnp.arange(slot_count, dtype=jnp.int32) < tile_count[0]
-    to_target = (
-        (tile_tgt[None, :] == jnp.arange(block_count, dtype=jnp.int32)[:, None]) & usable[None, :]
-    ).astype(jnp.float32)
-    to_source = (
-        (tile_src[None, :] == jnp.arange(source_count, dtype=jnp.int32)[:, None]) & usable[None, :]
-    ).astype(jnp.float32)
-    products = jnp.einsum(
-        "tij,tjf->tif", tile_vals, source[tile_src], preferred_element_type=jnp.float32
+    ones = jnp.ones(source.shape[:2] + (width,), source.dtype)
+    acc = tile_pass(
+        tile_tgt, tile_src, tile_count, tile_vals, jnp.concatenate([source, ones], axis=2),
+        block_count, False,
     )
-    summed = jnp.einsum("bt,tif->bif", to_target, products, precision=lax.Precision.HIGHEST)
-    unit_column = jnp.ones((tile_size,), jnp.bfloat16)
-    row_sums = jnp.einsum("tij,j->ti", tile_vals, unit_column, preferred_element_type=jnp.float32)
-    degree = jnp.dot(to_target, row_sums, precision=lax.Precision.HIGHEST)
-    agg = (summed / degree[:, :, None]).reshape(node_count, width).astype(jnp.bfloat16)
+    degree = acc[:, :, width]
+    agg = (acc[:, :, :width] / degree[:, :, None]).reshape(node_count, width).astype(jnp.bfloat16)
     preact = jnp.dot(features, w_self, preferred_element_type=jnp.float32) + jnp.dot(
         agg, w_neigh, preferred_element_type=jnp.float32
     )
@@ -100,10 +134,9 @@
     grad_own = jnp.einsum("nh,fh->nf", grad_pre, w_self, preferred_element_type=jnp.float32)
     grad_agg = jnp.einsum("nh,fh->nf", grad_pre, w_neigh, preferred_element_type=jnp.float32)
     grad_agg = (grad_agg / degree.reshape(-1)[:, None]).astype(jnp.bfloat16)
-    picked = grad_agg.reshape(block_count, tile_size, width)[tile_tgt]
-    backward = jnp.einsum("tij,tif->tjf", tile_vals, picked, preferred_element_type=jnp.float32)
-    grad_source = jnp.einsum(
-        "st,tjf->sjf", to_source, backward, precision=lax.Precision.HIGHEST
+    grad_source = tile_pass(
+        tile_tgt, tile_src, tile_count, tile_vals, grad_agg.reshape(block_count, tile_size, width),
+        source_count, True,
     ).reshape(-1, width)
     remote = grad_source[node_count:].astype(jnp.bfloat16).reshape(n_dom + n_grp, bnd, width)
     ret_dom, ret_grp = exchange(remote[:n_dom], remote[n_dom:])

time: 88.5 us -> 91.8 us (1.037)
  Pallas kernels: 0 us -> 18.1 us
  matrix products: 20.9 us -> 6.98 us
  local copies, waits for them, and re-layouts: 21.5 us -> 11.9 us
  waiting for transfers between devices: 23.7 us -> 28 us
  starting transfers between devices: 18.9 us -> 22.5 us
  other arithmetic: 1.21 us -> 2.78 us
    pallas_call x0 -> x2, Pallas kernels: none -> 18.1 us  [tile_pass(): pl.pallas_call(kernel, grid_spec=pltpu.PrefetchScalarGridSpec(num_scalar_...]
    dot_general x6 -> x0, matrix products: 13.6 us -> none  [the longest x1 4.3 us: per_device(): jnp.einsum('tij,tjf->tif', tile_vals, source[tile_src], preferred_element...]
    dot_general x3 -> x0, local copies, waits for them, and re-layouts: 7.34 us -> none  [the longest x1 3.61 us: per_device(): jnp.einsum('tij,tif->tjf', tile_vals, picked, preferred_element_type=jnp....]
    all_to_all x2, waiting for transfers between devices: 15.6 us -> 19.3 us  [exchange(): lax.all_to_all(buf.reshape((n_dom * n_grp,) + cell), axes, 0, 0, tiled=True)]
    gather x2 -> x0, local copies, waits for them, and re-layouts: 2.8 us -> none  [the longest x1 1.95 us: per_device(): source[tile_src]]
    all_to_all x2, starting transfers between devices: 13.1 us -> 15.7 us  [exchange(): lax.all_to_all(buf.reshape((n_dom * n_grp,) + cell), axes, 0, 0, tiled=True)]
    slice x0 -> x1, local copies, waits for them, and re-layouts: none -> 1.39 us  [per_device(): degree = acc[:, :, width]]
    convert_element_type x0 -> x1, other arithmetic: none -> 1.33 us  [per_device(): (acc[:, :, :width] / degree[:, :, None]).reshape(node_count, width)]
  transfers between devices with their start and end apart: 4 -> 4, of which waited for: 3 -> 3; matrix products, arithmetic and copies ran while one was open for 21% -> 7% of each run, Pallas kernels for 0% -> 10%
where the time goes in v3:
time: 91.8 us
  waiting for transfers between devices  28 us (31%)
  starting transfers between devices  22.5 us (25%)
  Pallas kernels  18.1 us (20%)
  local copies, waits for them, and re-layouts  11.9 us (13%)
  matrix products  6.98 us (8%)
  other arithmetic  2.78 us (3%)
  between operations  1.53 us (2%)
    all_to_all x2, waiting for transfers between devices, exchange(): lax.all_to_all(buf.reshape((n_dom * n_grp,) + cell), axes, 0, 0, tiled=True)  19.3 us
    pallas_call x2, Pallas kernels, tile_pass(): pl.pallas_call(kernel, grid_spec=pltpu.PrefetchScalarGridSpec(num_scalar_...  18.1 us
    all_to_all x2, starting transfers between devices, exchange(): lax.all_to_all(buf.reshape((n_dom * n_grp,) + cell), axes, 0, 0, tiled=True)  15.7 us
    all_to_all x1, waiting for transfers between devices, weight_sum(): total = lax.all_to_all(spread, axes, 0, 0, tiled=True).reshape(-1)  8.76 us
    all_to_all x1, starting transfers between devices, weight_sum(): lax.all_to_all(chunks, axes, 0, 0, tiled=True)  4.22 us
    all_to_all x1, starting transfers between devices, weight_sum(): total = lax.all_to_all(spread, axes, 0, 0, tiled=True).reshape(-1)  2.58 us
    slice x3, local copies, waits for them, and re-layouts, weight_sum(): return (total[:rows], total[rows:])  2.02 us
  transfers between devices with their start and end apart: 4, of which 3 were waited for; matrix products, arithmetic and copies ran while one was open for 7% of the time, Pallas kernels for 10%

profile of v3, /device:TPU:0, one launch (start us, length us, event | category | flops | bytes accessed | tf_op | source)
XLA Modules:
  0.0 91.8 jit_solution(15811254186424031125)
XLA Ops:
  0.6 0.0 copy-start
  0.6 0.0 copy-start.1
  0.7 0.0 copy-start.2
  0.7 0.8 reshape_squeeze.7
  1.5 0.8 reshape_squeeze.6
  2.3 1.5 %fusion.3 = bf16[384,128]{1,0:T(8,128)(2,1)S(1)} fusion(bf16[1280,128]{1,0:T(8,128)(2,1)} %param.10, s32[384]{0:T(512)S(1)} %pad_add_fusion), kind=kOutput, calls=%fused_computation.11 | convolution fusion | flops 126369792 | bytes 427520 | tf_op jit(solution)/shard_map/dot_general | solution.py:109
  3.8 0.7 broadcast.12.clone
  4.5 0.6 constant_dynamic-update-slice_fusion.3
  5.1 0.6 constant_dynamic-update-slice_fusion.2
  5.8 7.3 %all-to-all-start = ((bf16[32,32,128]{2,1,0:T(8,128)(2,1)}), bf16[32,32,128]{2,1,0:T(8,128)(2,1)S(1)}, u32[]{:S(2)}, u32[]{:S(2)}) async-start(bf16[32,32,128]{2,1,0:T(8,128)(2,1)} %bitcast.3), calls=%async_computation | async-start | bytes 524288 | tf_op jit(solution)/shard_map/all_to_all | solution.py:33
  13.7 0.0 copy-done.1
  13.7 0.0 copy-done.2
  13.7 0.3 fusion.11
  14.1 9.4 %all-to-all-done = bf16[32,32,128]{2,1,0:T(8,128)(2,1)S(1)} async-done(((bf16[32,32,128]{2,1,0:T(8,128)(2,1)}), bf16[32,32,128]{2,1,0:T(8,128)(2,1)S(1)}, u32[]{:S(2)}, u32[]{:S(2)}) %all-to-all-start) | async-done | bytes 262176 | tf_op jit(solution)/shard_map/all_to_all | solution.py:33
  23.5 1.0 %concatenate.17.blocks_ref = bf16[13,128,256]{2,1,0:T(8,128)(2,1)} pad(bf16[13,128,128]{2,1,0:T(8,128)(2,1)S(1)} %bitcast.43, bf16[]{:T(256)} %constant.37.clone.1), padding=0_0x0_0x0_128 | pad | bytes 1277954 | tf_op jit(solution)/shard_map/concatenate | solution.py:119
  24.6 8.7 %shard_map.129 = f32[10,128,256]{2,1,0:T(8,128)} custom-call(s32[48]{0:T(128)} %tgt_ref.3, s32[48]{0:T(128)} %src_ref.3, s32[1]{0:T(128)S(6)} %copy.27.cnt_ref, bf16[48,128,128]{2,1,0:T(8,128)(2,1)} %tiles_ref.3, bf16[13,128,256]{2,1,0:T(8,128)(2,1)} %concatenate.17.blocks_ref), custom_call_target="tpu_custom_call" | custom-call | tf_op jit(solution)/shard_map/pallas_call | solution.py:72
  33.2 0.0 copy-start.3
  33.2 1.4 %slice_reduce_fusion = f32[10,128]{1,0:T(8,128)S(1)} fusion(f32[10,128,256]{2,1,0:T(8,128)} %shard_map.129), kind=kLoop, calls=%fused_computation.15 | loop fusion | bytes 10240 | tf_op jit(solution)/shard_map/slice | solution.py:122
  34.6 1.3 %fusion.6 = bf16[10,128,128]{2,1,0:T(8,128)(2,1)S(1)} fusion(f32[10,128,256]{2,1,0:T(8,128)} %shard_map.129, f32[10,128]{1,0:T(8,128)S(1)} %slice_reduce_fusion), kind=kLoop, calls=%fused_computation.17 | loop fusion | flops 327680 | bytes 988160 | tf_op jit(solution)/shard_map/convert_element_type | solution.py:123
  36.0 0.0 copy-done
  36.0 0.0 copy-done.3
  36.0 1.6 %multiply_convert_fusion = (bf16[1280,256]{1,0:T(8,128)(2,1)S(1)}, bf16[1280,256]{1,0:T(8,128)(2,1)}) fusion(bf16[1280,256]{1,0:T(8,128)(2,1)S(1)} %copy-done.3, f32[1280,256]{1,0:T(8,128)S(1)} %fusion.11, bf16[1280,128]{1,0:T(8,128)(2,1)S(1)} %bitcast.44, bf16[128,256]{1,0:T(8,128)(2,1)S(1)} %copy-done), kind=kOutput, calls=%fused_computation.8 | convolution fusion | flops 88145920 | bytes 3670016 | tf_op jit(solution)/shard_map/dot_general | solution.py:124
  37.6 0.3 fusion.12
  37.9 0.3 convolution_bitcast_fusion
  38.3 1.0 %all_to_all.21 = f32[32,1,2048]{2,1,0:T(1,128)} reshape(f32[256,256]{1,0:T(8,128)S(1)} %pad_maximum_fusion.1) | data formatting | bytes 524288 | tf_op jit(solution)/shard_map/all_to_all | solution.py:17
  39.2 4.2 %all-to-all-start.2 = ((f32[32,1,2048]{2,1,0:T(1,128)}), f32[32,1,2048]{2,1,0:T(1,128)S(1)}, u32[]{:S(2)}, u32[]{:S(2)}) async-start(f32[32,1,2048]{2,1,0:T(1,128)} %all_to_all.21), calls=%async_computation.2 | async-start | bytes 524288 | tf_op jit(solution)/shard_map/all_to_all | solution.py:17
  43.5 1.1 %fusion = bf16[1280,128]{1,0:T(8,128)(2,1)} fusion(bf16[1280,256]{1,0:T(8,128)(2,1)S(1)} %get-tuple-element.6, bf16[128,256]{1,0:T(8,128)(2,1)S(1)} %copy-done, f32[1280]{0:T(1024)S(1)} %bitcast.60), kind=kOutput, calls=%fused_computation.4 | convolution fusion | flops 84213760 | bytes 1053696 | tf_op jit(solution)/shard_map/nh,fh->nf/dot_general | solution.py:135
  44.5 9.4 %shard_map.130 = f32[13,128,128]{2,1,0:T(8,128)} custom-call(s32[48]{0:T(128)} %tgt_ref.3, s32[48]{0:T(128)} %src_ref.3, s32[1]{0:T(128)S(6)} %copy.27.cnt_ref, bf16[48,128,128]{2,1,0:T(8,128)(2,1)} %tiles_ref.3, bf16[10,128,128]{2,1,0:T(8,128)(2,1)} %bitcast.50), custom_call_target="tpu_custom_call" | custom-call | tf_op jit(solution)/shard_map/pallas_call | solution.py:72
  53.9 1.2 %convert.3 = bf16[13,128,128]{2,1,0:T(8,128)(2,1)S(1)} convert(f32[13,128,128]{2,1,0:T(8,128)} %shard_map.130) | non-fusion elementwise | flops 212992 | bytes 1277952 | tf_op jit(solution)/shard_map/convert
  55.2 0.0 slice-start
  55.2 0.7 broadcast.12
  55.9 0.6 constant_dynamic-update-slice_fusion.1
  56.6 0.6 constant_dynamic-update-slice_fusion
  57.2 0.0 all-to-all-done.2
  57.2 8.4 %all-to-all-start.1 = ((bf16[32,32,128]{2,1,0:T(8,128)(2,1)}), bf16[32,32,128]{2,1,0:T(8,128)(2,1)S(1)}, u32[]{:S(2)}, u32[]{:S(2)}) async-start(bf16[32,32,128]{2,1,0:T(8,128)(2,1)} %bitcast.16), calls=%async_computation.1 | async-start | bytes 524288 | tf_op jit(solution)/shard_map/all_to_all | solution.py:33
  65.6 0.0 slice-done
  65.6 0.3 convolution_add_fusion.2
  66.0 0.2 reduce_sum.9
  66.1 9.9 %all-to-all-done.1 = bf16[32,32,128]{2,1,0:T(8,128)(2,1)S(1)} async-done(((bf16[32,32,128]{2,1,0:T(8,128)(2,1)}), bf16[32,32,128]{2,1,0:T(8,128)(2,1)S(1)}, u32[]{:S(2)}, u32[]{:S(2)}) %all-to-all-start.1) | async-done | bytes 262176 | tf_op jit(solution)/shard_map/all_to_all | solution.py:33
  76.0 0.8 broadcast_in_dim.25
  76.8 2.6 %all-to-all-start.3 = ((f32[32,1,2048]{2,1,0:T(1,128)}), f32[32,1,2048]{2,1,0:T(1,128)S(1)}, u32[]{:S(2)}, u32[]{:S(2)}) async-start(f32[32,1,2048]{2,1,0:T(1,128)} %broadcast_in_dim.25), calls=%async_computation.3 | async-start | bytes 524288 | tf_op jit(solution)/shard_map/all_to_all | solution.py:19
  79.5 1.6 %fusion.1 = bf16[1280,128]{1,0:T(8,128)(2,1)} fusion(f32[1280,128]{1,0:T(8,128)S(1)} %convolution_add_fusion.2, s32[384]{0:T(512)S(1)} %pad_add_fusion, bf16[256,128]{1,0:T(8,128)(2,1)S(1)} %bitcast.59, bf16[128,128]{1,0:T(8,128)(2,1)S(1)} %bitcast.61), kind=kOutput, calls=%fused_computation.5 | convolution fusion | flops 126844928 | bytes 1082880 | tf_op jit(solution)/shard_map/dot_general | solution.py:146
  81.0 8.8 %all-to-all-done.3 = f32[32,1,2048]{2,1,0:T(1,128)S(1)} async-done(((f32[32,1,2048]{2,1,0:T(1,128)}), f32[32,1,2048]{2,1,0:T(1,128)S(1)}, u32[]{:S(2)}, u32[]{:S(2)}) %all-to-all-start.3) | async-done | bytes 262176 | tf_op jit(solution)/shard_map/all_to_all | solution.py:19
  89.8 0.7 slice_reduce_fusion.1
  90.5 0.7 slice.64
  91.1 0.7 slice.66
  (13 shorter events, 0.1 us)
Async XLA Ops:
  0.6 35.3 %copy-start = (bf16[128,256]{1,0:T(8,128)(2,1)S(1)}, bf16[128,256]{1,0:T(8,128)(2,1)}, u32[]{:S(2)}) copy-start(bf16[128,256]{1,0:T(8,128)(2,1)} %param.18) | copy-start | bytes 196612
  0.6 13.1 %copy-start.1 = (bf16[1280,128]{1,0:T(8,128)(2,1)S(1)}, bf16[1280,128]{1,0:T(8,128)(2,1)}, u32[]{:S(2)}) copy-start(bf16[1280,128]{1,0:T(8,128)(2,1)} %param.10) | copy-start | bytes 983044
  0.7 13.1 %copy-start.2 = (bf16[128,256]{1,0:T(8,128)(2,1)S(1)}, bf16[128,256]{1,0:T(8,128)(2,1)}, u32[]{:S(2)}) copy-start(bf16[128,256]{1,0:T(8,128)(2,1)} %param.17) | copy-start | bytes 196612
  5.8 17.7 %all-to-all-start = ((bf16[32,32,128]{2,1,0:T(8,128)(2,1)}), bf16[32,32,128]{2,1,0:T(8,128)(2,1)S(1)}, u32[]{:S(2)}, u32[]{:S(2)}) async-start(bf16[32,32,128]{2,1,0:T(8,128)(2,1)} %bitcast.3), calls=%async_computation | async-start | bytes 524288 | tf_op jit(solution)/shard_map/all_to_all | solution.py:33
  33.2 2.7 %copy-start.3 = (bf16[1280,256]{1,0:T(8,128)(2,1)S(1)}, bf16[1280,256]{1,0:T(8,128)(2,1)}, u32[]{:S(2)}) copy-start(bf16[1280,256]{1,0:T(8,128)(2,1)} %param.19) | copy-start | bytes 1966084
  39.2 18.0 %all-to-all-start.2 = ((f32[32,1,2048]{2,1,0:T(1,128)}), f32[32,1,2048]{2,1,0:T(1,128)S(1)}, u32[]{:S(2)}, u32[]{:S(2)}) async-start(f32[32,1,2048]{2,1,0:T(1,128)} %all_to_all.21), calls=%async_computation.2 | async-start | bytes 524288 | tf_op jit(solution)/shard_map/all_to_all | solution.py:17
  55.2 10.5 %slice-start = ((f32[13,128,128]{2,1,0:T(8,128)}), f32[10,128,128]{2,1,0:T(8,128)S(1)}, s32[]{:S(2)}) async-start(f32[13,128,128]{2,1,0:T(8,128)} %shard_map.130), calls=%async_computation.4 | async-start | bytes 1310720 | tf_op jit(solution)/shard_map/slice | solution.py:145
  57.2 18.8 %all-to-all-start.1 = ((bf16[32,32,128]{2,1,0:T(8,128)(2,1)}), bf16[32,32,128]{2,1,0:T(8,128)(2,1)S(1)}, u32[]{:S(2)}, u32[]{:S(2)}) async-start(bf16[32,32,128]{2,1,0:T(8,128)(2,1)} %bitcast.16), calls=%async_computation.1 | async-start | bytes 524288 | tf_op jit(solution)/shard_map/all_to_all | solution.py:33
  76.8 13.0 %all-to-all-start.3 = ((f32[32,1,2048]{2,1,0:T(1,128)}), f32[32,1,2048]{2,1,0:T(1,128)S(1)}, u32[]{:S(2)}, u32[]{:S(2)}) async-start(f32[32,1,2048]{2,1,0:T(1,128)} %broadcast_in_dim.25), calls=%async_computation.3 | async-start | bytes 524288 | tf_op jit(solution)/shard_map/all_to_all | solution.py:19

commit v4 on v3

--- a/solution.py
+++ b/solution.py
@@ -6,22 +6,26 @@
 from jax.experimental.pallas import tpu as pltpu
 
 
-def weight_sum(part_self, part_neigh):
+MERGE_LIMIT = 4 << 20
+
+
+def weight_chunks(part_self, part_neigh, peers):
+    flat = jnp.concatenate([part_self, part_neigh], axis=0).reshape(-1)
+    pad = (-flat.shape[0]) % peers
+    return jnp.pad(flat, (0, pad)).reshape(peers, -1)
+
+
+def weight_spread(received, part_self, part_neigh):
     axes = ("dom", "grp")
-    peers = lax.psum(1, axes)
     rows = part_self.shape[0]
-    stacked = jnp.concatenate([part_self, part_neigh], axis=0)
-    flat = stacked.reshape(-1)
-    pad = (-flat.shape[0]) % peers
-    chunks = jnp.pad(flat, (0, pad)).reshape(peers, -1)
-    mine = jnp.sum(lax.all_to_all(chunks, axes, 0, 0, tiled=True), axis=0, keepdims=True)
-    spread = jnp.broadcast_to(mine, chunks.shape)
+    mine = jnp.sum(received, axis=0, keepdims=True)
+    spread = jnp.broadcast_to(mine, received.shape)
     total = lax.all_to_all(spread, axes, 0, 0, tiled=True).reshape(-1)
-    total = total[: flat.shape[0]].reshape(stacked.shape)
+    total = total[: 2 * part_self.size].reshape(2 * rows, -1)
     return total[:rows], total[rows:]
 
 
-def exchange(dom_part, grp_part):
+def exchange(dom_part, grp_part, extra=None):
     axes = ("dom", "grp")
     n_dom, n_grp = dom_part.shape[0], grp_part.shape[0]
     a = lax.axis_index("dom")
@@ -30,13 +34,19 @@
     buf = jnp.zeros((n_dom, n_grp) + cell, dom_part.dtype)
     buf = lax.dynamic_update_slice_in_dim(buf, dom_part[:, None], b, axis=1)
     buf = lax.dynamic_update_slice_in_dim(buf, grp_part[None], a, axis=0)
-    got = lax.all_to_all(buf.reshape((n_dom * n_grp,) + cell), axes, 0, 0, tiled=True)
-    got = got.reshape((n_dom, n_grp) + cell)
-    from_dom = lax.dynamic_index_in_dim(got, b, axis=1, keepdims=False)
+    if extra is not None:
+        extra = extra.reshape((n_dom, n_grp, -1) + cell[1:]).astype(buf.dtype)
+        buf = jnp.concatenate([buf, extra], axis=2)
+    got = lax.all_to_all(buf.reshape((n_dom * n_grp,) + buf.shape[2:]), axes, 0, 0, tiled=True)
+    got = got.reshape((n_dom, n_grp) + buf.shape[2:])
+    rows = got[:, :, : cell[0]]
+    from_dom = lax.dynamic_index_in_dim(rows, b, axis=1, keepdims=False)
     own_dom = lax.dynamic_index_in_dim(dom_part, a, axis=0, keepdims=True)
     from_dom = lax.dynamic_update_slice_in_dim(from_dom, own_dom, a, axis=0)
-    from_grp = lax.dynamic_index_in_dim(got, a, axis=0, keepdims=False)
-    return from_dom, from_grp
+    from_grp = lax.dynamic_index_in_dim(rows, a, axis=0, keepdims=False)
+    if extra is None:
+        return from_dom, from_grp
+    return from_dom, from_grp, got[:, :, cell[0] :].reshape(n_dom * n_grp, -1)
 
 
 def one_hot_rows(index, count):
@@ -139,9 +149,19 @@
         source_count, True,
     ).reshape(-1, width)
     remote = grad_source[node_count:].astype(jnp.bfloat16).reshape(n_dom + n_grp, bnd, width)
-    ret_dom, ret_grp = exchange(remote[:n_dom], remote[n_dom:])
-    grad_self, grad_neigh = weight_sum(part_self, part_neigh)
+    peers = n_dom * n_grp
+    chunks = weight_chunks(part_self, part_neigh, peers)
+    merged_bytes = peers * (bnd * width + chunks.shape[1]) * 4
+    if merged_bytes <= MERGE_LIMIT and chunks.shape[1] % width == 0:
+        ret_dom, ret_grp, received = exchange(
+            remote[:n_dom].astype(jnp.float32), remote[n_dom:].astype(jnp.float32), chunks
+        )
+    else:
+        ret_dom, ret_grp = exchange(remote[:n_dom], remote[n_dom:])
+        received = lax.all_to_all(chunks, ("dom", "grp"), 0, 0, tiled=True)
+    grad_self, grad_neigh = weight_spread(received, part_self, part_neigh)
     returned = jnp.concatenate([ret_dom.reshape(-1, width), ret_grp.reshape(-1, width)])
+    returned = returned.astype(jnp.bfloat16)
     grad_total = grad_own + grad_source[:node_count]
     grad_total = grad_total + lax.dot_general(
         pick, returned, (((0,), (0,)), ((), ())), preferred_element_type=jnp.float32

time: 91.8 us -> 96.2 us (1.048)
  waiting for transfers between devices: 28 us -> 39.8 us
  starting transfers between devices: 22.5 us -> 14.1 us
  local copies, waits for them, and re-layouts: 11.9 us -> 9.1 us
  Pallas kernels: 18.1 us -> 20.6 us
    all_to_all x4 -> x3, waiting for transfers between devices: 28 us -> 39.8 us  [the longest x2 31 us: exchange(): lax.all_to_all(buf.reshape((n_dom * n_grp,) + buf.shape[2:]), axes, 0, 0,...]
    all_to_all x4 -> x3, starting transfers between devices: 22.5 us -> 14.1 us  [the longest x2 11.5 us: exchange(): lax.all_to_all(buf.reshape((n_dom * n_grp,) + buf.shape[2:]), axes, 0, 0,...]
    pallas_call x2, Pallas kernels: 18.1 us -> 20.6 us  [tile_pass(): pl.pallas_call(kernel, grid_spec=pltpu.PrefetchScalarGridSpec(num_scalar_...]
    another operation x2 -> x1, local copies, waits for them, and re-layouts: 1.49 us -> 0.01 us
    all_to_all x1 -> x0, local copies, waits for them, and re-layouts: 0.97 us -> none  [weight_sum(): lax.all_to_all(chunks, axes, 0, 0, tiled=True)]
  transfers between devices with their start and end apart: 4 -> 3, of which waited for: 3 -> 3; matrix products, arithmetic and copies ran while one was open for 7% -> 2% of each run, Pallas kernels for 10% -> 0%
where the time goes in v4:
time: 96.2 us; the launch traced here: 95.7 us
  waiting for transfers between devices  39.8 us (41%)
  Pallas kernels  20.6 us (21%)
  starting transfers between devices  14.1 us (15%)
  local copies, waits for them, and re-layouts  9.1 us (9%)
  matrix products  6.96 us (7%)
  other arithmetic  3.61 us (4%)
  between operations  1.55 us (2%)
    all_to_all x2, waiting for transfers between devices, exchange(): lax.all_to_all(buf.reshape((n_dom * n_grp,) + buf.shape[2:]), axes, 0, 0,...  31 us
    pallas_call x2, Pallas kernels, tile_pass(): pl.pallas_call(kernel, grid_spec=pltpu.PrefetchScalarGridSpec(num_scalar_...  20.6 us
    all_to_all x2, starting transfers between devices, exchange(): lax.all_to_all(buf.reshape((n_dom * n_grp,) + buf.shape[2:]), axes, 0, 0,...  11.5 us
    all_to_all x1, waiting for transfers between devices, weight_spread(): total = lax.all_to_all(spread, axes, 0, 0, tiled=True).reshape(-1)  8.76 us
    all_to_all x1, starting transfers between devices, weight_spread(): total = lax.all_to_all(spread, axes, 0, 0, tiled=True).reshape(-1)  2.58 us
    slice x3, local copies, waits for them, and re-layouts, weight_spread(): return (total[:rows], total[rows:])  2.02 us
  transfers between devices with their start and end apart: 3, of which 3 were waited for; matrix products, arithmetic and copies ran while one was open for 2% of the time, Pallas kernels for 0%

profile of v4, /device:TPU:0, one launch (start us, length us, event | category | flops | bytes accessed | tf_op | source)
XLA Modules:
  0.0 95.7 jit_solution(202542297160256365)
XLA Ops:
  0.6 0.0 copy-start
  0.6 0.0 copy-start.1
  0.7 0.0 copy-start.2
  0.7 0.8 reshape_squeeze.7
  1.5 0.8 reshape_squeeze.6
  2.3 1.5 %fusion.3 = bf16[384,128]{1,0:T(8,128)(2,1)S(1)} fusion(bf16[1280,128]{1,0:T(8,128)(2,1)} %param.10, s32[384]{0:T(512)S(1)} %pad_add_fusion), kind=kOutput, calls=%fused_computation.11 | convolution fusion | flops 126369792 | bytes 427520 | tf_op jit(solution)/shard_map/dot_general | solution.py:119
  3.8 0.7 broadcast_in_dim.12
  4.5 0.6 constant_dynamic-update-slice_fusion.2
  5.1 0.6 constant_dynamic-update-slice_fusion.1
  5.8 7.3 %all-to-all-start = ((bf16[32,32,128]{2,1,0:T(8,128)(2,1)}), bf16[32,32,128]{2,1,0:T(8,128)(2,1)S(1)}, u32[]{:S(2)}, u32[]{:S(2)}) async-start(bf16[32,32,128]{2,1,0:T(8,128)(2,1)} %bitcast.3), calls=%async_computation | async-start | bytes 524288 | tf_op jit(solution)/shard_map/all_to_all | solution.py:40
  13.7 0.0 copy-done.1
  13.7 0.0 copy-done.2
  13.7 0.3 fusion.11
  14.0 9.4 %all-to-all-done = bf16[32,32,128]{2,1,0:T(8,128)(2,1)S(1)} async-done(((bf16[32,32,128]{2,1,0:T(8,128)(2,1)}), bf16[32,32,128]{2,1,0:T(8,128)(2,1)S(1)}, u32[]{:S(2)}, u32[]{:S(2)}) %all-to-all-start) | async-done | bytes 262176 | tf_op jit(solution)/shard_map/all_to_all | solution.py:40
  23.5 1.1 %concatenate.26.blocks_ref = bf16[13,128,256]{2,1,0:T(8,128)(2,1)} pad(bf16[13,128,128]{2,1,0:T(8,128)(2,1)S(1)} %bitcast.48, bf16[]{:T(256)} %constant.31.clone.1), padding=0_0x0_0x0_128 | pad | bytes 1277954 | tf_op jit(solution)/shard_map/concatenate | solution.py:129
  24.6 9.8 %shard_map.129 = f32[10,128,256]{2,1,0:T(8,128)} custom-call(s32[48]{0:T(128)} %tgt_ref.3, s32[48]{0:T(128)} %src_ref.3, s32[1]{0:T(128)S(6)} %copy.26.cnt_ref, bf16[48,128,128]{2,1,0:T(8,128)(2,1)} %tiles_ref.3, bf16[13,128,256]{2,1,0:T(8,128)(2,1)} %concatenate.26.blocks_ref), custom_call_target="tpu_custom_call" | custom-call | tf_op jit(solution)/shard_map/pallas_call | solution.py:82
  34.4 0.0 copy-start.3
  34.4 1.4 %slice_reduce_fusion = f32[10,128]{1,0:T(8,128)S(1)} fusion(f32[10,128,256]{2,1,0:T(8,128)} %shard_map.129), kind=kLoop, calls=%fused_computation.16 | loop fusion | bytes 10240 | tf_op jit(solution)/shard_map/slice | solution.py:132
  35.8 1.3 %fusion.6 = bf16[10,128,128]{2,1,0:T(8,128)(2,1)S(1)} fusion(f32[10,128,256]{2,1,0:T(8,128)} %shard_map.129, f32[10,128]{1,0:T(8,128)S(1)} %slice_reduce_fusion), kind=kLoop, calls=%fused_computation.18 | loop fusion | flops 327680 | bytes 988160 | tf_op jit(solution)/shard_map/convert_element_type | solution.py:133
  37.1 0.0 copy-done
  37.1 0.0 copy-done.3
  37.1 1.6 %multiply_convert_fusion = (bf16[1280,256]{1,0:T(8,128)(2,1)S(1)}, bf16[1280,256]{1,0:T(8,128)(2,1)}) fusion(bf16[1280,256]{1,0:T(8,128)(2,1)S(1)} %copy-done.3, f32[1280,256]{1,0:T(8,128)S(1)} %fusion.11, bf16[1280,128]{1,0:T(8,128)(2,1)S(1)} %bitcast.49, bf16[128,256]{1,0:T(8,128)(2,1)S(1)} %copy-done), kind=kOutput, calls=%fused_computation.8 | convolution fusion | flops 88145920 | bytes 3670016 | tf_op jit(solution)/shard_map/dot_general | solution.py:134
  38.7 0.3 fusion.12
  39.0 0.3 convolution_bitcast_fusion
  39.4 1.1 %fusion = bf16[1280,128]{1,0:T(8,128)(2,1)} fusion(bf16[1280,256]{1,0:T(8,128)(2,1)S(1)} %get-tuple-element.6, bf16[128,256]{1,0:T(8,128)(2,1)S(1)} %copy-done, f32[1280]{0:T(1024)S(1)} %bitcast.63), kind=kOutput, calls=%fused_computation.4 | convolution fusion | flops 84213760 | bytes 1053696 | tf_op jit(solution)/shard_map/nh,fh->nf/dot_general | solution.py:145
  40.4 10.8 %shard_map.130 = f32[13,128,128]{2,1,0:T(8,128)} custom-call(s32[48]{0:T(128)} %tgt_ref.3, s32[48]{0:T(128)} %src_ref.3, s32[1]{0:T(128)S(6)} %copy.26.cnt_ref, bf16[48,128,128]{2,1,0:T(8,128)(2,1)} %tiles_ref.3, bf16[10,128,128]{2,1,0:T(8,128)(2,1)} %bitcast.53), custom_call_target="tpu_custom_call" | custom-call | tf_op jit(solution)/shard_map/pallas_call | solution.py:82
  51.2 1.2 %convert.14 = bf16[13,128,128]{2,1,0:T(8,128)(2,1)S(1)} convert(f32[13,128,128]{2,1,0:T(8,128)} %shard_map.130) | non-fusion elementwise | flops 212992 | bytes 1277952 | tf_op jit(solution)/shard_map/convert.7
  52.6 0.1 broadcast_in_dim.28
  52.7 0.9 pad_maximum_fusion
  53.6 0.0 slice-start
  53.6 4.2 %all-to-all-start.1 = ((f32[32,48,128]{2,1,0:T(8,128)}), f32[32,48,128]{2,1,0:T(8,128)S(1)}, u32[]{:S(2)}, u32[]{:S(2)}) async-start(f32[32,48,128]{2,1,0:T(8,128)} %pad_maximum_fusion), calls=%async_computation.1 | async-start | bytes 1572864 | tf_op jit(solution)/shard_map/all_to_all | solution.py:40
  57.8 0.0 slice-done
  57.8 0.3 convolution_add_fusion.2
  58.1 21.6 %all-to-all-done.1 = f32[32,48,128]{2,1,0:T(8,128)S(1)} async-done(((f32[32,48,128]{2,1,0:T(8,128)}), f32[32,48,128]{2,1,0:T(8,128)S(1)}, u32[]{:S(2)}, u32[]{:S(2)}) %all-to-all-start.1) | async-done | bytes 786464 | tf_op jit(solution)/shard_map/all_to_all | solution.py:40
  79.8 0.8 broadcast_in_dim.30
  80.7 2.6 %all-to-all-start.2 = ((f32[32,1,2048]{2,1,0:T(1,128)}), f32[32,1,2048]{2,1,0:T(1,128)S(1)}, u32[]{:S(2)}, u32[]{:S(2)}) async-start(f32[32,1,2048]{2,1,0:T(1,128)} %broadcast_in_dim.30), calls=%async_computation.2 | async-start | bytes 524288 | tf_op jit(solution)/shard_map/all_to_all | solution.py:23
  83.3 1.6 %fusion.1 = bf16[1280,128]{1,0:T(8,128)(2,1)} fusion(f32[1280,128]{1,0:T(8,128)S(1)} %convolution_add_fusion.2, s32[384]{0:T(512)S(1)} %pad_add_fusion, bf16[256,128]{1,0:T(8,128)(2,1)S(1)} %bitcast.62, bf16[128,128]{1,0:T(8,128)(2,1)S(1)} %bitcast.65), kind=kOutput, calls=%fused_computation.5 | convolution fusion | flops 126844928 | bytes 1082880 | tf_op jit(solution)/shard_map/dot_general | solution.py:166
  84.9 8.8 %all-to-all-done.2 = f32[32,1,2048]{2,1,0:T(1,128)S(1)} async-done(((f32[32,1,2048]{2,1,0:T(1,128)}), f32[32,1,2048]{2,1,0:T(1,128)S(1)}, u32[]{:S(2)}, u32[]{:S(2)}) %all-to-all-start.2) | async-done | bytes 262176 | tf_op jit(solution)/shard_map/all_to_all | solution.py:23
  93.6 0.7 slice_reduce_fusion.2
  94.3 0.7 slice.69
  95.0 0.7 slice.71
  (18 shorter events, 0.3 us)
Async XLA Ops:
  0.6 36.5 %copy-start = (bf16[128,256]{1,0:T(8,128)(2,1)S(1)}, bf16[128,256]{1,0:T(8,128)(2,1)}, u32[]{:S(2)}) copy-start(bf16[128,256]{1,0:T(8,128)(2,1)} %param.18) | copy-start | bytes 196612
  0.6 13.1 %copy-start.1 = (bf16[1280,128]{1,0:T(8,128)(2,1)S(1)}, bf16[1280,128]{1,0:T(8,128)(2,1)}, u32[]{:S(2)}) copy-start(bf16[1280,128]{1,0:T(8,128)(2,1)} %param.10) | copy-start | bytes 983044
  0.7 13.1 %copy-start.2 = (bf16[128,256]{1,0:T(8,128)(2,1)S(1)}, bf16[128,256]{1,0:T(8,128)(2,1)}, u32[]{:S(2)}) copy-start(bf16[128,256]{1,0:T(8,128)(2,1)} %param.17) | copy-start | bytes 196612
  5.8 17.7 %all-to-all-start = ((bf16[32,32,128]{2,1,0:T(8,128)(2,1)}), bf16[32,32,128]{2,1,0:T(8,128)(2,1)S(1)}, u32[]{:S(2)}, u32[]{:S(2)}) async-start(bf16[32,32,128]{2,1,0:T(8,128)(2,1)} %bitcast.3), calls=%async_computation | async-start | bytes 524288 | tf_op jit(solution)/shard_map/all_to_all | solution.py:40
  34.4 2.7 %copy-start.3 = (bf16[1280,256]{1,0:T(8,128)(2,1)S(1)}, bf16[1280,256]{1,0:T(8,128)(2,1)}, u32[]{:S(2)}) copy-start(bf16[1280,256]{1,0:T(8,128)(2,1)} %param.19) | copy-start | bytes 1966084
  53.6 4.2 %slice-start = ((f32[13,128,128]{2,1,0:T(8,128)}), f32[10,128,128]{2,1,0:T(8,128)S(1)}, s32[]{:S(2)}) async-start(f32[13,128,128]{2,1,0:T(8,128)} %shard_map.130), calls=%async_computation.3 | async-start | bytes 1310720 | tf_op jit(solution)/shard_map/slice | solution.py:165
  53.6 26.2 %all-to-all-start.1 = ((f32[32,48,128]{2,1,0:T(8,128)}), f32[32,48,128]{2,1,0:T(8,128)S(1)}, u32[]{:S(2)}, u32[]{:S(2)}) async-start(f32[32,48,128]{2,1,0:T(8,128)} %pad_maximum_fusion), calls=%async_computation.1 | async-start | bytes 1572864 | tf_op jit(solution)/shard_map/all_to_all | solution.py:40
  80.7 13.0 %all-to-all-start.2 = ((f32[32,1,2048]{2,1,0:T(1,128)}), f32[32,1,2048]{2,1,0:T(1,128)S(1)}, u32[]{:S(2)}, u32[]{:S(2)}) async-start(f32[32,1,2048]{2,1,0:T(1,128)} %broadcast_in_dim.30), calls=%async_computation.2 | async-start | bytes 524288 | tf_op jit(solution)/shard_map/all_to_all | solution.py:23

commit v5 on v2

--- a/solution.py
+++ b/solution.py
@@ -73,19 +73,15 @@
     source_count = source.shape[0]
     slot_count = tile_vals.shape[0]
     usable = jnp.arange(slot_count, dtype=jnp.int32) < tile_count[0]
-    to_target = (
-        (tile_tgt[None, :] == jnp.arange(block_count, dtype=jnp.int32)[:, None]) & usable[None, :]
-    ).astype(jnp.float32)
-    to_source = (
-        (tile_src[None, :] == jnp.arange(source_count, dtype=jnp.int32)[:, None]) & usable[None, :]
-    ).astype(jnp.float32)
+    target_id = jnp.where(usable, tile_tgt, block_count)
+    source_id = jnp.where(usable, tile_src, source_count)
     products = jnp.einsum(
         "tij,tjf->tif", tile_vals, source[tile_src], preferred_element_type=jnp.float32
     )
-    summed = jnp.einsum("bt,tif->bif", to_target, products, precision=lax.Precision.HIGHEST)
+    summed = jax.ops.segment_sum(products, target_id, num_segments=block_count)
     unit_column = jnp.ones((tile_size,), jnp.bfloat16)
     row_sums = jnp.einsum("tij,j->ti", tile_vals, unit_column, preferred_element_type=jnp.float32)
-    degree = jnp.dot(to_target, row_sums, precision=lax.Precision.HIGHEST)
+    degree = jax.ops.segment_sum(row_sums, target_id, num_segments=block_count)
     agg = (summed / degree[:, :, None]).reshape(node_count, width).astype(jnp.bfloat16)
     preact = jnp.dot(features, w_self, preferred_element_type=jnp.float32) + jnp.dot(
         agg, w_neigh, preferred_element_type=jnp.float32
@@ -102,9 +98,7 @@
     grad_agg = (grad_agg / degree.reshape(-1)[:, None]).astype(jnp.bfloat16)
     picked = grad_agg.reshape(block_count, tile_size, width)[tile_tgt]
     backward = jnp.einsum("tij,tif->tjf", tile_vals, picked, preferred_element_type=jnp.float32)
-    grad_source = jnp.einsum(
-        "st,tjf->sjf", to_source, backward, precision=lax.Precision.HIGHEST
-    ).reshape(-1, width)
+    grad_source = jax.ops.segment_sum(backward, source_id, num_segments=source_count).reshape(-1, width)
     remote = grad_source[node_count:].astype(jnp.bfloat16).reshape(n_dom + n_grp, bnd, width)
     ret_dom, ret_grp = exchange(remote[:n_dom], remote[n_dom:])
     grad_self, grad_neigh = weight_sum(part_self, part_neigh)

time: 88.5 us -> 97.4 us (1.10)
  other arithmetic: 1.21 us -> 15.7 us
  matrix products: 20.9 us -> 18 us
  local copies, waits for them, and re-layouts: 21.5 us -> 19.7 us
  waiting for transfers between devices: 23.7 us -> 22.7 us
    scatter-add x0 -> x3, other arithmetic: none -> 14.2 us  [the longest x1 6.73 us: per_device(): jax.ops.segment_sum(backward, source_id, num_segments=source_count)]
    dot_general x3 -> x0, matrix products: 6.44 us -> none  [the longest x1 3.26 us: per_device(): jnp.einsum('bt,tif->bif', to_target, products, precision=lax.Precision.HI...]
    dot_general x1, matrix products: 1.64 us -> 3.15 us  [per_device(): jnp.dot(agg, w_neigh, preferred_element_type=jnp.float32)]
    dot_general x1, matrix products: 1.56 us -> 2.65 us  [per_device(): lax.dot_general(pick, returned, (((0,), (0,)), ((), ())), preferred_eleme...]
  transfers between devices with their start and end apart: 4 -> 4, of which waited for: 3 -> 3; matrix products, arithmetic and copies ran while one was open for 21% -> 25% of each run, Pallas kernels for 0% -> 0%
where the time goes in v5:
time: 97.4 us; the launch traced here: 96.6 us
  waiting for transfers between devices  22.7 us (23%)
  local copies, waits for them, and re-layouts  19.7 us (20%)
  starting transfers between devices  18.9 us (19%)
  matrix products  18 us (18%)
  other arithmetic  15.7 us (16%)
  between operations  1.63 us (2%)
    all_to_all x2, waiting for transfers between devices, exchange(): lax.all_to_all(buf.reshape((n_dom * n_grp,) + cell), axes, 0, 0, tiled=True)  15 us
    all_to_all x2, starting transfers between devices, exchange(): lax.all_to_all(buf.reshape((n_dom * n_grp,) + cell), axes, 0, 0, tiled=True)  13.1 us
    all_to_all x1, waiting for transfers between devices, weight_sum(): total = lax.all_to_all(spread, axes, 0, 0, tiled=True).reshape(-1)  7.67 us
    scatter-add x1, other arithmetic, per_device(): jax.ops.segment_sum(backward, source_id, num_segments=source_count)  6.73 us
    scatter-add x1, other arithmetic, per_device(): summed = jax.ops.segment_sum(products, target_id, num_segments=block_count)  6.72 us
    dot_general x1, matrix products, per_device(): jnp.einsum('tij,tjf->tif', tile_vals, source[tile_src], preferred_element...  4.31 us
    dot_general x1, local copies, waits for them, and re-layouts, per_device(): jnp.einsum('tij,tjf->tif', tile_vals, source[tile_src], preferred_element...  3.56 us
    dot_general x1, local copies, waits for them, and re-layouts, per_device(): jnp.einsum('tij,tif->tjf', tile_vals, picked, preferred_element_type=jnp....  3.56 us
  transfers between devices with their start and end apart: 4, of which 3 were waited for; matrix products, arithmetic and copies ran while one was open for 25% of the time, Pallas kernels for 0%

profile of v5, /device:TPU:0, one launch (start us, length us, event | category | flops | bytes accessed | tf_op | source)
XLA Modules:
  0.0 96.6 jit_solution(8372356854995357027)
XLA Ops:
  0.6 0.0 copy-start
  0.6 0.9 reshape_squeeze.7
  1.5 0.8 reshape_squeeze.6
  2.3 1.5 %fusion.3 = bf16[384,128]{1,0:T(8,128)(2,1)S(1)} fusion(bf16[1280,128]{1,0:T(8,128)(2,1)} %param.10, s32[384]{0:T(512)S(1)} %pad_add_fusion), kind=kOutput, calls=%fused_computation.18 | convolution fusion | flops 126369792 | bytes 427520 | tf_op jit(solution)/shard_map/dot_general | solution.py:66
  3.8 0.0 copy-start.5
  3.8 0.0 copy-start.6
  3.8 0.0 copy-start.3
  3.8 0.0 copy-start.4
  3.9 0.7 broadcast.14.clone
  4.6 0.6 constant_dynamic-update-slice_fusion.3
  5.2 0.6 constant_dynamic-update-slice_fusion.2
  5.9 7.3 %all-to-all-start = ((bf16[32,32,128]{2,1,0:T(8,128)(2,1)}), bf16[32,32,128]{2,1,0:T(8,128)(2,1)S(1)}, u32[]{:S(2)}, u32[]{:S(2)}) async-start(bf16[32,32,128]{2,1,0:T(8,128)(2,1)} %bitcast.4), calls=%async_computation | async-start | bytes 524288 | tf_op jit(solution)/shard_map/all_to_all | solution.py:31
  13.8 0.5 fusion.11
  14.4 0.8 scatter_custom_fusion.1
  15.2 1.4 %fusion.15 = f32[1280,256]{1,0:T(8,128)} fusion(bf16[1280,128]{1,0:T(8,128)(2,1)S(1)} %copy-done.3, bf16[128,256]{1,0:T(8,128)(2,1)S(1)} %copy-done.4), kind=kOutput, calls=%fused_computation.53 | convolution fusion | flops 83886080 | bytes 1703936 | tf_op jit(solution)/shard_map/dot_general | solution.py:86
  16.6 7.0 %all-to-all-done = bf16[32,32,128]{2,1,0:T(8,128)(2,1)S(1)} async-done(((bf16[32,32,128]{2,1,0:T(8,128)(2,1)}), bf16[32,32,128]{2,1,0:T(8,128)(2,1)S(1)}, u32[]{:S(2)}, u32[]{:S(2)}) %all-to-all-start) | async-done | bytes 262176 | tf_op jit(solution)/shard_map/all_to_all | solution.py:31
  23.6 1.9 %gather_fusion = bf16[48,128,128]{2,1,0:T(8,128)(2,1)} fusion(bf16[13,128,128]{2,1,0:T(8,128)(2,1)S(1)} %bitcast.57, s32[1024]{0:T(1024)S(1)} %pad_clamp_fusion.1), kind=kCustom, calls=%fused_computation | custom fusion | bytes 3145920 | tf_op jit(solution)/shard_map/gather | solution.py:79
  25.6 4.3 %convolution_bitcast_fusion.1 = f32[48,128,128]{1,2,0:T(8,128)} fusion(bf16[48,128,128]{2,1,0:T(8,128)(2,1)} %gather_fusion, bf16[48,128,128]{2,1,0:T(8,128)(2,1)S(1)} %copy-done), kind=kOutput, calls=%fused_computation.14 | convolution fusion | flops 201326592 | bytes 6291456 | tf_op jit(solution)/shard_map/tij,tjf->tif/dot_general | solution.py:78
  29.9 3.6 %copy.28 = f32[48,128,128]{2,1,0:T(8,128)} copy(f32[48,128,128]{1,2,0:T(8,128)} %convolution_bitcast_fusion.1) | data formatting | bytes 6291456 | tf_op jit(solution)/shard_map/tij,tjf->tif/dot_general | solution.py:78
  33.5 0.0 copy-start.7
  33.5 6.7 %scatter_fusion = f32[10,128,128]{2,1,0:T(8,128)S(1)} fusion(f32[10,128,128]{2,1,0:T(8,128)S(1)} %broadcast_in_dim.51, s32[48]{0:T(128)S(1)} %get-tuple-element.9, f32[48,128,128]{2,1,0:T(8,128)} %copy.28), kind=kCustom, calls=%fused_computation.2 | custom fusion | flops 786432 | bytes 9437376 | tf_op jit(solution)/shard_map/scatter-add | solution.py:81
  40.2 0.2 divide_convert_fusion
  40.5 3.1 %multiply_convert_fusion = (bf16[1280,256]{1,0:T(8,128)(2,1)S(1)}, bf16[1280,256]{1,0:T(8,128)(2,1)}) fusion(bf16[1280,256]{1,0:T(8,128)(2,1)} %param.19, f32[1280,256]{1,0:T(8,128)} %fusion.15, bf16[1280,128]{1,0:T(8,128)(2,1)S(1)} %bitcast.60, bf16[128,256]{1,0:T(8,128)(2,1)S(1)} %copy-done.7), kind=kOutput, calls=%fused_computation.15 | convolution fusion | flops 88145920 | bytes 3670016 | tf_op jit(solution)/shard_map/dot_general | solution.py:86
  43.6 0.3 fusion.16
  43.9 0.3 convolution_bitcast_fusion.2
  44.3 1.0 %all_to_all.21 = f32[32,1,2048]{2,1,0:T(1,128)} reshape(f32[256,256]{1,0:T(8,128)S(1)} %pad_maximum_fusion.1) | data formatting | bytes 524288 | tf_op jit(solution)/shard_map/all_to_all | solution.py:15
  45.3 3.3 %all-to-all-start.2 = ((f32[32,1,2048]{2,1,0:T(1,128)}), f32[32,1,2048]{2,1,0:T(1,128)}, u32[]{:S(2)}, u32[]{:S(2)}) async-start(f32[32,1,2048]{2,1,0:T(1,128)} %all_to_all.21), calls=%async_computation.2 | async-start | bytes 524288 | tf_op jit(solution)/shard_map/all_to_all | solution.py:15
  48.6 0.3 fusion
  48.9 0.8 gather_fusion.1
  49.8 2.3 %convolution_bitcast_fusion = f32[48,128,128]{1,2,0:T(8,128)} fusion(bf16[48,128,128]{2,1,0:T(8,128)(2,1)S(1)} %gather_fusion.1, bf16[48,128,128]{2,1,0:T(8,128)(2,1)S(1)} %copy-done), kind=kOutput, calls=%fused_computation.13 | convolution fusion | flops 201326592 | bytes 6291456 | tf_op jit(solution)/shard_map/tij,tif->tjf/dot_general | solution.py:100
  52.1 3.6 %copy.30 = f32[48,128,128]{2,1,0:T(8,128)} copy(f32[48,128,128]{1,2,0:T(8,128)} %convolution_bitcast_fusion) | data formatting | bytes 6291456 | tf_op jit(solution)/shard_map/tij,tif->tjf/dot_general | solution.py:100
  55.7 0.1 broadcast_in_dim.59
  55.8 6.7 %scatter_fusion.1 = f32[13,128,128]{2,1,0:T(8,128)S(1)} fusion(f32[13,128,128]{2,1,0:T(8,128)S(1)} %broadcast_in_dim.59, s32[48]{0:T(128)S(1)} %get-tuple-element.13, f32[48,128,128]{2,1,0:T(8,128)} %copy.30), kind=kCustom, calls=%fused_computation.4 | custom fusion | flops 786432 | bytes 9437376 | tf_op jit(solution)/shard_map/scatter-add | solution.py:101
  62.5 0.1 convert.3
  62.6 0.7 broadcast.14
  63.4 0.6 constant_dynamic-update-slice_fusion.1
  64.0 0.6 constant_dynamic-update-slice_fusion
  64.6 5.8 %all-to-all-start.1 = ((bf16[32,32,128]{2,1,0:T(8,128)(2,1)}), bf16[32,32,128]{2,1,0:T(8,128)(2,1)S(1)}, u32[]{:S(2)}, u32[]{:S(2)}) async-start(bf16[32,32,128]{2,1,0:T(8,128)(2,1)} %bitcast.22), calls=%async_computation.1 | async-start | bytes 524288 | tf_op jit(solution)/shard_map/all_to_all | solution.py:31
  70.5 1.2 %convolution_add_fusion.2 = f32[1280,128]{1,0:T(8,128)} fusion(f32[1280,128]{1,0:T(8,128)S(1)} %bitcast.59, bf16[1280,256]{1,0:T(8,128)(2,1)S(1)} %copy-done.2, bf16[128,256]{1,0:T(8,128)(2,1)S(1)} %copy-done.4), kind=kOutput, calls=%fused_computation.8 | convolution fusion | flops 84049920 | bytes 2031616 | tf_op jit(solution)/shard_map/nh,fh->nf/dot_general | solution.py:96
  71.7 1.1 %reduce_sum.9 = f32[2048]{0:T(1024)S(1)} reduce(f32[32,1,2048]{2,1,0:T(1,128)} %all-to-all-done.2, f32[]{:T(128)} %constant.15.clone.1), dimensions={0,1}, to_apply=%region_3.4 | reduce | flops 63488 | bytes 270340 | tf_op jit(solution)/shard_map/reduce_sum | solution.py:15
  72.8 8.0 %all-to-all-done.1 = bf16[32,32,128]{2,1,0:T(8,128)(2,1)S(1)} async-done(((bf16[32,32,128]{2,1,0:T(8,128)(2,1)}), bf16[32,32,128]{2,1,0:T(8,128)(2,1)S(1)}, u32[]{:S(2)}, u32[]{:S(2)}) %all-to-all-start.1) | async-done | bytes 262176 | tf_op jit(solution)/shard_map/all_to_all | solution.py:31
  80.8 0.8 broadcast_in_dim.64
  81.6 2.6 %all-to-all-start.3 = ((f32[32,1,2048]{2,1,0:T(1,128)}), f32[32,1,2048]{2,1,0:T(1,128)S(1)}, u32[]{:S(2)}, u32[]{:S(2)}) async-start(f32[32,1,2048]{2,1,0:T(1,128)} %broadcast_in_dim.64), calls=%async_computation.3 | async-start | bytes 524288 | tf_op jit(solution)/shard_map/all_to_all | solution.py:17
  84.3 2.6 %fusion.1 = bf16[1280,128]{1,0:T(8,128)(2,1)} fusion(f32[1280,128]{1,0:T(8,128)} %convolution_add_fusion.2, s32[384]{0:T(512)S(1)} %pad_add_fusion, bf16[256,128]{1,0:T(8,128)(2,1)S(1)} %bitcast.74, bf16[128,128]{1,0:T(8,128)(2,1)S(1)} %bitcast.76), kind=kOutput, calls=%fused_computation.10 | convolution fusion | flops 126844928 | bytes 1082880 | tf_op jit(solution)/shard_map/dot_general | solution.py:107
  86.9 7.7 %all-to-all-done.3 = f32[32,1,2048]{2,1,0:T(1,128)S(1)} async-done(((f32[32,1,2048]{2,1,0:T(1,128)}), f32[32,1,2048]{2,1,0:T(1,128)S(1)}, u32[]{:S(2)}, u32[]{:S(2)}) %all-to-all-start.3) | async-done | bytes 262176 | tf_op jit(solution)/shard_map/all_to_all | solution.py:17
  94.6 0.7 slice_reduce_fusion
  95.3 0.7 slice.56
  96.0 0.7 slice.58
  (29 shorter events, 0.3 us)
Async XLA Ops:
  0.6 13.2 %copy-start = (bf16[48,128,128]{2,1,0:T(8,128)(2,1)S(1)}, bf16[48,128,128]{2,1,0:T(8,128)(2,1)}, u32[]{:S(2)}) copy-start(bf16[48,128,128]{2,1,0:T(8,128)(2,1)} %param.13) | copy-start | bytes 4718596
  3.8 10.5 %copy-start.5 = (s32[48]{0:T(128)S(1)}, s32[48]{0:T(128)}, u32[]{:S(2)}) copy-start(s32[48]{0:T(128)} %param.14) | copy-start | bytes 580
  3.8 10.5 %copy-start.6 = (s32[48]{0:T(128)S(1)}, s32[48]{0:T(128)}, u32[]{:S(2)}) copy-start(s32[48]{0:T(128)} %param.15) | copy-start | bytes 580
  3.8 11.4 %copy-start.3 = (bf16[1280,128]{1,0:T(8,128)(2,1)S(1)}, bf16[1280,128]{1,0:T(8,128)(2,1)}, u32[]{:S(2)}) copy-start(bf16[1280,128]{1,0:T(8,128)(2,1)} %param.10) | copy-start | bytes 983044
  3.8 11.4 %copy-start.4 = (bf16[128,256]{1,0:T(8,128)(2,1)S(1)}, bf16[128,256]{1,0:T(8,128)(2,1)}, u32[]{:S(2)}) copy-start(bf16[128,256]{1,0:T(8,128)(2,1)} %param.17) | copy-start | bytes 196612
  5.9 17.7 %all-to-all-start = ((bf16[32,32,128]{2,1,0:T(8,128)(2,1)}), bf16[32,32,128]{2,1,0:T(8,128)(2,1)S(1)}, u32[]{:S(2)}, u32[]{:S(2)}) async-start(bf16[32,32,128]{2,1,0:T(8,128)(2,1)} %bitcast.4), calls=%async_computation | async-start | bytes 524288 | tf_op jit(solution)/shard_map/all_to_all | solution.py:31
  33.5 7.0 %copy-start.7 = (bf16[128,256]{1,0:T(8,128)(2,1)S(1)}, bf16[128,256]{1,0:T(8,128)(2,1)}, u32[]{:S(2)}) copy-start(bf16[128,256]{1,0:T(8,128)(2,1)} %param.18) | copy-start | bytes 196612
  43.6 5.0 %copy-start.1 = (bf16[1280,256]{1,0:T(8,128)(2,1)}, bf16[1280,256]{1,0:T(8,128)(2,1)S(1)}, u32[]{:S(2)}) copy-start(bf16[1280,256]{1,0:T(8,128)(2,1)S(1)} %get-tuple-element.6) | copy-start | bytes 1966084
  45.3 19.4 %all-to-all-start.2 = ((f32[32,1,2048]{2,1,0:T(1,128)}), f32[32,1,2048]{2,1,0:T(1,128)}, u32[]{:S(2)}, u32[]{:S(2)}) async-start(f32[32,1,2048]{2,1,0:T(1,128)} %all_to_all.21), calls=%async_computation.2 | async-start | bytes 524288 | tf_op jit(solution)/shard_map/all_to_all | solution.py:15
  62.5 7.9 %copy-start.2 = (bf16[1280,256]{1,0:T(8,128)(2,1)S(1)}, bf16[1280,256]{1,0:T(8,128)(2,1)}, u32[]{:S(2)}) copy-start(bf16[1280,256]{1,0:T(8,128)(2,1)} %copy-done.1) | copy-start | bytes 1966084
  64.6 16.2 %all-to-all-start.1 = ((bf16[32,32,128]{2,1,0:T(8,128)(2,1)}), bf16[32,32,128]{2,1,0:T(8,128)(2,1)S(1)}, u32[]{:S(2)}, u32[]{:S(2)}) async-start(bf16[32,32,128]{2,1,0:T(8,128)(2,1)} %bitcast.22), calls=%async_computation.1 | async-start | bytes 524288 | tf_op jit(solution)/shard_map/all_to_all | solution.py:31
  81.6 13.0 %all-to-all-start.3 = ((f32[32,1,2048]{2,1,0:T(1,128)}), f32[32,1,2048]{2,1,0:T(1,128)S(1)}, u32[]{:S(2)}, u32[]{:S(2)}) async-start(f32[32,1,2048]{2,1,0:T(1,128)} %broadcast_in_dim.64), calls=%async_computation.3 | async-start | bytes 524288 | tf_op jit(solution)/shard_map/all_to_all | solution.py:17

commit v6 on v2

--- a/solution.py
+++ b/solution.py
@@ -37,6 +37,17 @@
     return from_dom, from_grp
 
 
+ADJ_LIMIT = 4 << 20
+
+
+def split_bf16(value):
+    hi = value.astype(jnp.bfloat16)
+    rest = value - hi.astype(jnp.float32)
+    mid = rest.astype(jnp.bfloat16)
+    low = (rest - mid.astype(jnp.float32)).astype(jnp.bfloat16)
+    return hi, mid, low
+
+
 def one_hot_rows(index, count):
     return (index.reshape(-1)[:, None] == jnp.arange(count, dtype=jnp.int32)[None, :]).astype(jnp.bfloat16)
 
@@ -65,28 +76,53 @@
     pick = one_hot_rows(send_index, node_count)
     sent = jnp.dot(pick, features, preferred_element_type=jnp.float32).astype(jnp.bfloat16)
     sent = sent.reshape(n_dom + n_grp, bnd, width)
-    recv_dom, recv_grp = exchange(sent[:n_dom], sent[n_dom:])
-    source = jnp.concatenate(
-        [features, recv_dom.reshape(-1, width), recv_grp.reshape(-1, width)], axis=0
-    )
-    source = source.reshape(-1, tile_size, width)
-    source_count = source.shape[0]
     slot_count = tile_vals.shape[0]
+    source_count = block_count + (n_dom + n_grp) * bnd // tile_size
+    remote_count = source_count - block_count
     usable = jnp.arange(slot_count, dtype=jnp.int32) < tile_count[0]
     to_target = (
         (tile_tgt[None, :] == jnp.arange(block_count, dtype=jnp.int32)[:, None]) & usable[None, :]
     ).astype(jnp.float32)
-    to_source = (
-        (tile_src[None, :] == jnp.arange(source_count, dtype=jnp.int32)[:, None]) & usable[None, :]
-    ).astype(jnp.float32)
-    products = jnp.einsum(
-        "tij,tjf->tif", tile_vals, source[tile_src], preferred_element_type=jnp.float32
-    )
-    summed = jnp.einsum("bt,tif->bif", to_target, products, precision=lax.Precision.HIGHEST)
     unit_column = jnp.ones((tile_size,), jnp.bfloat16)
     row_sums = jnp.einsum("tij,j->ti", tile_vals, unit_column, preferred_element_type=jnp.float32)
     degree = jnp.dot(to_target, row_sums, precision=lax.Precision.HIGHEST)
-    agg = (summed / degree[:, :, None]).reshape(node_count, width).astype(jnp.bfloat16)
+    split = block_count * remote_count * tile_size * tile_size * 4 <= ADJ_LIMIT
+    if split:
+        is_own = tile_src < block_count
+        own_src = jnp.where(is_own, tile_src, 0)
+        own_target = to_target * is_own.astype(jnp.float32)[None, :]
+        remote_of = (
+            tile_src[None, :] == block_count + jnp.arange(remote_count, dtype=jnp.int32)[:, None]
+        ).astype(jnp.float32)
+        pair = (to_target[:, None, :] * remote_of[None, :, :]).reshape(-1, slot_count)
+        adj = jnp.dot(
+            pair.astype(jnp.bfloat16), tile_vals.reshape(slot_count, -1),
+            preferred_element_type=jnp.float32,
+        )
+        adj = adj.reshape(block_count, remote_count, tile_size, tile_size).transpose(0, 2, 1, 3)
+        adj = adj.reshape(node_count, remote_count * tile_size)
+        pieces = split_bf16(adj)
+        own_blocks = features.reshape(block_count, tile_size, width)
+        products = jnp.einsum(
+            "tij,tjf->tif", tile_vals, own_blocks[own_src], preferred_element_type=jnp.float32
+        )
+        summed = jnp.einsum("bt,tif->bif", own_target, products, precision=lax.Precision.HIGHEST)
+        recv_dom, recv_grp = exchange(sent[:n_dom], sent[n_dom:])
+        received = jnp.concatenate([recv_dom.reshape(-1, width), recv_grp.reshape(-1, width)], axis=0)
+        far = sum(jnp.dot(p, received, preferred_element_type=jnp.float32) for p in pieces)
+        summed = summed.reshape(node_count, width) + far
+    else:
+        recv_dom, recv_grp = exchange(sent[:n_dom], sent[n_dom:])
+        source = jnp.concatenate(
+            [features, recv_dom.reshape(-1, width), recv_grp.reshape(-1, width)], axis=0
+        )
+        source = source.reshape(-1, tile_size, width)
+        products = jnp.einsum(
+            "tij,tjf->tif", tile_vals, source[tile_src], preferred_element_type=jnp.float32
+        )
+        summed = jnp.einsum("bt,tif->bif", to_target, products, precision=lax.Precision.HIGHEST)
+        summed = summed.reshape(node_count, width)
+    agg = (summed / degree.reshape(-1)[:, None]).astype(jnp.bfloat16)
     preact = jnp.dot(features, w_self, preferred_element_type=jnp.float32) + jnp.dot(
         agg, w_neigh, preferred_element_type=jnp.float32
     )
@@ -102,14 +138,31 @@
     grad_agg = (grad_agg / degree.reshape(-1)[:, None]).astype(jnp.bfloat16)
     picked = grad_agg.reshape(block_count, tile_size, width)[tile_tgt]
     backward = jnp.einsum("tij,tif->tjf", tile_vals, picked, preferred_element_type=jnp.float32)
-    grad_source = jnp.einsum(
-        "st,tjf->sjf", to_source, backward, precision=lax.Precision.HIGHEST
-    ).reshape(-1, width)
-    remote = grad_source[node_count:].astype(jnp.bfloat16).reshape(n_dom + n_grp, bnd, width)
+    if split:
+        near = sum(
+            lax.dot_general(p, grad_agg, (((0,), (0,)), ((), ())), preferred_element_type=jnp.float32)
+            for p in pieces
+        )
+        to_own = (
+            (own_src[None, :] == jnp.arange(block_count, dtype=jnp.int32)[:, None])
+            & (usable & is_own)[None, :]
+        ).astype(jnp.float32)
+        grad_near = jnp.einsum("st,tjf->sjf", to_own, backward, precision=lax.Precision.HIGHEST)
+        grad_near = grad_near.reshape(-1, width)
+        remote = near.astype(jnp.bfloat16).reshape(n_dom + n_grp, bnd, width)
+    else:
+        to_source = (
+            (tile_src[None, :] == jnp.arange(source_count, dtype=jnp.int32)[:, None]) & usable[None, :]
+        ).astype(jnp.float32)
+        grad_source = jnp.einsum(
+            "st,tjf->sjf", to_source, backward, precision=lax.Precision.HIGHEST
+        ).reshape(-1, width)
+        grad_near = grad_source[:node_count]
+        remote = grad_source[node_count:].astype(jnp.bfloat16).reshape(n_dom + n_grp, bnd, width)
     ret_dom, ret_grp = exchange(remote[:n_dom], remote[n_dom:])
     grad_self, grad_neigh = weight_sum(part_self, part_neigh)
     returned = jnp.concatenate([ret_dom.reshape(-1, width), ret_grp.reshape(-1, width)])
-    grad_total = grad_own + grad_source[:node_count]
+    grad_total = grad_own + grad_near
     grad_total = grad_total + lax.dot_general(
         pick, returned, (((0,), (0,)), ((), ())), preferred_element_type=jnp.float32
     )

time: 88.5 us -> 90.6 us (1.024)
  waiting for transfers between devices: 23.7 us -> 13.2 us
  local copies, waits for them, and re-layouts: 21.5 us -> 29.4 us
  starting transfers between devices: 18.9 us -> 21.8 us
  matrix products: 20.9 us -> 22.4 us
    all_to_all x2, waiting for transfers between devices: 15.6 us -> 6.66 us  [exchange(): lax.all_to_all(buf.reshape((n_dom * n_grp,) + cell), axes, 0, 0, tiled=True)]
    all_to_all x1, starting transfers between devices: 3.3 us -> 6.07 us  [weight_sum(): lax.all_to_all(chunks, axes, 0, 0, tiled=True)]
    unnamed x25 -> x26, local copies, waits for them, and re-layouts: 0.67 us -> 3.09 us
    dynamic_slice x2, local copies, waits for them, and re-layouts: 0.01 us -> 1.69 us  [exchange(): from_grp = lax.dynamic_index_in_dim(got, a, axis=0, keepdims=False)]
    all_to_all x1, waiting for transfers between devices: 8.09 us -> 6.5 us  [weight_sum(): total = lax.all_to_all(spread, axes, 0, 0, tiled=True).reshape(-1)]
    squeeze x2, local copies, waits for them, and re-layouts: 0.01 us -> 1.53 us  [exchange(): from_dom = lax.dynamic_index_in_dim(got, b, axis=1, keepdims=False)]
    dot_general x1, matrix products: 2.33 us -> 3.75 us  [per_device(): jnp.einsum('tij,tif->tjf', tile_vals, picked, preferred_element_type=jnp....]
    transpose x0 -> x1, local copies, waits for them, and re-layouts: none -> 1.35 us  [per_device(): adj.reshape(block_count, remote_count, tile_size, tile_size)]
  transfers between devices with their start and end apart: 4 -> 4, of which waited for: 3 -> 2; matrix products, arithmetic and copies ran while one was open for 21% -> 38% of each run, Pallas kernels for 0% -> 0%
where the time goes in v6:
time: 90.6 us; the launch traced here: 89.7 us
  local copies, waits for them, and re-layouts  29.4 us (32%)
  matrix products  22.4 us (25%)
  starting transfers between devices  21.8 us (24%)
  waiting for transfers between devices  13.2 us (15%)
  between operations  1.6 us (2%)
  other arithmetic  1.26 us (1%)
    all_to_all x2, starting transfers between devices, exchange(): lax.all_to_all(buf.reshape((n_dom * n_grp,) + cell), axes, 0, 0, tiled=True)  13.1 us
    all_to_all x2, waiting for transfers between devices, exchange(): lax.all_to_all(buf.reshape((n_dom * n_grp,) + cell), axes, 0, 0, tiled=True)  6.66 us
    all_to_all x1, waiting for transfers between devices, weight_sum(): total = lax.all_to_all(spread, axes, 0, 0, tiled=True).reshape(-1)  6.5 us
    all_to_all x1, starting transfers between devices, weight_sum(): lax.all_to_all(chunks, axes, 0, 0, tiled=True)  6.07 us
    dot_general x1, matrix products, per_device(): jnp.einsum('tij,tif->tjf', tile_vals, picked, preferred_element_type=jnp....  3.75 us
    dot_general x1, local copies, waits for them, and re-layouts, per_device(): jnp.einsum('tij,tjf->tif', tile_vals, own_blocks[own_src], preferred_elem...  3.61 us
    dot_general x1, matrix products, per_device(): jnp.einsum('bt,tif->bif', own_target, products, precision=lax.Precision.H...  3.49 us
    unnamed x26, local copies, waits for them, and re-layouts  3.09 us
  transfers between devices with their start and end apart: 4, of which 2 were waited for; matrix products, arithmetic and copies ran while one was open for 38% of the time, Pallas kernels for 0%

profile of v6, /device:TPU:0, one launch (start us, length us, event | category | flops | bytes accessed | tf_op | source)
XLA Modules:
  0.0 89.7 jit_solution(9253874691385172271)
XLA Ops:
  0.7 0.8 reshape_squeeze.6
  1.5 0.8 reshape_squeeze.7
  2.3 0.5 fusion.8
  2.8 0.7 broadcast.74.clone
  3.5 0.6 constant_dynamic-update-slice_fusion.3
  4.2 0.6 constant_dynamic-update-slice_fusion.2
  4.8 7.4 %all-to-all-start = ((bf16[32,32,128]{2,1,0:T(8,128)(2,1)}), bf16[32,32,128]{2,1,0:T(8,128)(2,1)}, u32[]{:S(2)}, u32[]{:S(2)}) async-start(bf16[32,32,128]{2,1,0:T(8,128)(2,1)} %bitcast.13), calls=%async_computation | async-start | bytes 524288 | tf_op jit(solution)/shard_map/all_to_all | solution.py:31
  13.0 0.8 gather_fusion
  13.9 0.5 copy-done.1
  14.4 2.9 %convolution_bitcast_fusion.1 = f32[48,128,128]{1,2,0:T(8,128)} fusion(bf16[48,128,128]{2,1,0:T(8,128)(2,1)S(1)} %gather_fusion, bf16[48,128,128]{2,1,0:T(8,128)(2,1)S(1)} %copy-done.1), kind=kOutput, calls=%fused_computation.19 | convolution fusion | flops 201326592 | bytes 6291456 | tf_op jit(solution)/shard_map/tij,tjf->tif/dot_general | solution.py:106
  17.3 3.6 %copy.36 = f32[48,128,128]{2,0,1:T(8,128)} copy(f32[48,128,128]{1,2,0:T(8,128)} %convolution_bitcast_fusion.1) | data formatting | bytes 6291456 | tf_op jit(solution)/shard_map/tij,tjf->tif/dot_general | solution.py:106
  20.9 3.5 %fusion.21 = f32[10,128,128]{2,0,1:T(8,128)S(1)} fusion(f32[48,128,128]{2,0,1:T(8,128)} %copy.36, f32[48]{0:T(128)S(1)} %get-tuple-element.9, s32[48]{0:T(128)S(1)} %copy-done.9, pred[48]{0:T(512)(128)(4,1)S(1)} %iota_compare_fusion.7), kind=kOutput, calls=%fused_computation.53 | convolution fusion | flops 94373280 | bytes 3801520 | tf_op jit(solution)/shard_map/bt,tif->bif/dot_general | solution.py:109
  24.4 1.4 %convolution_bitcast_fusion.2 = f32[10,128,3,128]{3,0,1,2:T(8,128)S(1)} fusion(f32[3,48]{1,0:T(4,128)S(1)} %compare_convert_fusion, f32[10,48]{1,0:T(8,128)S(1)} %fusion.26, bf16[6,8,128,128]{3,2,1,0:T(8,128)(2,1)S(1)} %bitcast.122), kind=kOutput, calls=%fused_computation.20 | convolution fusion | flops 47188800 | bytes 3541440 | tf_op jit(solution)/shard_map/dot_general | solution.py:98
  25.8 0.5 fusion.40
  26.3 1.1 %copy.37 = f32[10,128,128]{2,1,0:T(8,128)} copy(f32[10,128,128]{2,0,1:T(8,128)S(1)} %fusion.21) | data formatting | bytes 1310720 | tf_op jit(solution)/shard_map/bt,tif->bif/dot_general | solution.py:109
  27.4 1.3 %copy.39 = f32[10,128,3,128]{3,2,1,0:T(4,128)S(1)} copy(f32[10,128,3,128]{3,0,1,2:T(8,128)S(1)} %convolution_bitcast_fusion.2) | data formatting | bytes 3932160 | tf_op jit(solution)/shard_map/transpose | solution.py:102
  28.9 1.4 %fusion.50 = f32[1280,256]{1,0:T(8,128)} fusion(bf16[1280,128]{1,0:T(8,128)(2,1)S(1)} %copy-done, bf16[128,256]{1,0:T(8,128)(2,1)S(1)} %copy-done.7), kind=kOutput, calls=%fused_computation.96 | convolution fusion | flops 83886080 | bytes 1703936 | tf_op jit(solution)/shard_map/dot_general | solution.py:126
  30.3 0.8 dynamic-slice_bitcast_fusion.1
  31.0 0.8 constant_dynamic-slice_fusion.1
  32.8 0.6 copy-done.6
  33.9 0.8 copy-done.5
  34.9 1.6 %multiply_convert_fusion = (bf16[1280,256]{1,0:T(8,128)(2,1)S(1)}, bf16[1280,256]{1,0:T(8,128)(2,1)}) fusion(bf16[1280,256]{1,0:T(8,128)(2,1)S(1)} %copy-done.11, f32[1280,256]{1,0:T(8,128)S(1)} %copy-done.5, bf16[1280,128]{1,0:T(8,128)(2,1)S(1)} %fusion.2, bf16[128,256]{1,0:T(8,128)(2,1)S(1)} %copy-done.12), kind=kOutput, calls=%fused_computation.24 | convolution fusion | flops 88145920 | bytes 3670016 | tf_op jit(solution)/shard_map/dot_general | solution.py:126
  38.0 0.5 convolution_add_fusion.6
  38.5 0.5 fusion.7
  39.0 0.6 slice.50
  39.6 1.0 %all_to_all.21 = f32[32,1,2048]{2,1,0:T(1,128)} reshape(f32[256,256]{1,0:T(8,128)S(1)} %pad_maximum_fusion) | data formatting | bytes 524288 | tf_op jit(solution)/shard_map/all_to_all | solution.py:15
  40.6 6.1 %all-to-all-start.2 = ((f32[32,1,2048]{2,1,0:T(1,128)}), f32[32,1,2048]{2,1,0:T(1,128)}, u32[]{:S(2)}, u32[]{:S(2)}) async-start(f32[32,1,2048]{2,1,0:T(1,128)} %all_to_all.21), calls=%async_computation.2 | async-start | bytes 524288 | tf_op jit(solution)/shard_map/all_to_all | solution.py:15
  46.7 2.0 %gather_fusion.1 = bf16[48,128,128]{2,1,0:T(8,128)(2,1)} fusion(bf16[10,128,128]{2,1,0:T(8,128)(2,1)S(1)} %bitcast.123, s32[1024]{0:T(1024)S(1)} %pad_clamp_fusion), kind=kCustom, calls=%fused_computation.1 | custom fusion | bytes 3145920 | tf_op jit(solution)/shard_map/gather | solution.py:139
  48.6 3.8 %convolution_bitcast_fusion = f32[48,128,128]{1,2,0:T(8,128)} fusion(bf16[48,128,128]{2,1,0:T(8,128)(2,1)} %gather_fusion.1, bf16[48,128,128]{2,1,0:T(8,128)(2,1)S(1)} %copy-done.2), kind=kOutput, calls=%fused_computation.18 | convolution fusion | flops 201326592 | bytes 6291456 | tf_op jit(solution)/shard_map/tij,tif->tjf/dot_general | solution.py:140
  52.4 2.6 %copy.42 = f32[48,128,128]{2,0,1:T(8,128)S(1)} copy(f32[48,128,128]{1,2,0:T(8,128)} %convolution_bitcast_fusion) | data formatting | bytes 6291456 | tf_op jit(solution)/shard_map/tij,tif->tjf/dot_general | solution.py:140
  55.0 0.7 broadcast.74
  55.7 1.4 %constant_dynamic-update-slice_fusion.1 = bf16[4,8,32,128]{3,2,1,0:T(8,128)(2,1)} fusion(bf16[4,8,32,128]{3,2,1,0:T(8,128)(2,1)} %broadcast.74, bf16[4,1,32,128]{3,2,1,0:T(8,128)(2,1)} %bitcast.136, s32[]{:T(128)S(6)} %select_n.31), kind=kLoop, calls=%fused_computation.75 | loop fusion | bytes 65540 | tf_op jit(solution)/shard_map/dynamic_update_slice | solution.py:29
  57.1 0.6 constant_dynamic-update-slice_fusion
  57.8 5.7 %all-to-all-start.1 = ((bf16[32,32,128]{2,1,0:T(8,128)(2,1)}), bf16[32,32,128]{2,1,0:T(8,128)(2,1)}, u32[]{:S(2)}, u32[]{:S(2)}) async-start(bf16[32,32,128]{2,1,0:T(8,128)(2,1)} %bitcast.29), calls=%async_computation.1 | async-start | bytes 524288 | tf_op jit(solution)/shard_map/all_to_all | solution.py:31
  63.5 1.2 %fusion.30 = f32[10,128,128]{2,0,1:T(8,128)S(1)} fusion(f32[48,128,128]{2,0,1:T(8,128)S(1)} %copy.42, s32[48]{0:T(128)S(1)} %get-tuple-element.10, pred[48]{0:T(512)(128)(4,1)S(1)} %get-tuple-element.8), kind=kOutput, calls=%fused_computation.62 | convolution fusion | flops 94372800 | bytes 3801328 | tf_op jit(solution)/shard_map/st,tjf->sjf/dot_general | solution.py:150
  64.9 0.8 copy-done.4
  66.1 1.1 %reduce_sum.9 = f32[2048]{0:T(1024)S(1)} reduce(f32[32,1,2048]{2,1,0:T(1,128)} %all-to-all-done.2, f32[]{:T(128)} %constant.21.clone.1), dimensions={0,1}, to_apply=%region_0.1 | reduce | flops 63488 | bytes 270340 | tf_op jit(solution)/shard_map/reduce_sum | solution.py:15
  67.2 6.7 %all-to-all-done.1 = bf16[32,32,128]{2,1,0:T(8,128)(2,1)} async-done(((bf16[32,32,128]{2,1,0:T(8,128)(2,1)}), bf16[32,32,128]{2,1,0:T(8,128)(2,1)}, u32[]{:S(2)}, u32[]{:S(2)}) %all-to-all-start.1) | async-done | bytes 262176 | tf_op jit(solution)/shard_map/all_to_all | solution.py:31
  73.8 0.8 broadcast_in_dim.52
  74.7 2.6 %all-to-all-start.3 = ((f32[32,1,2048]{2,1,0:T(1,128)}), f32[32,1,2048]{2,1,0:T(1,128)S(1)}, u32[]{:S(2)}, u32[]{:S(2)}) async-start(f32[32,1,2048]{2,1,0:T(1,128)} %broadcast_in_dim.52), calls=%async_computation.3 | async-start | bytes 524288 | tf_op jit(solution)/shard_map/all_to_all | solution.py:17
  77.3 0.8 dynamic-slice_bitcast_fusion
  78.0 0.7 dynamic-slice_dynamic-update-slice_fusion
  78.7 0.8 constant_dynamic-slice_fusion
  79.6 1.6 %fusion.4 = bf16[1280,128]{1,0:T(8,128)(2,1)} fusion(f32[1280,128]{1,0:T(8,128)S(1)} %convolution_add_fusion.2, s32[384]{0:T(512)S(1)} %pad_add_fusion, bf16[256,128]{1,0:T(8,128)(2,1)S(1)} %bitcast.139, bf16[128,128]{1,0:T(8,128)(2,1)S(1)} %bitcast.140), kind=kOutput, calls=%fused_computation.12 | convolution fusion | flops 126844928 | bytes 1082880 | tf_op jit(solution)/shard_map/dot_general | solution.py:166
  81.1 6.5 %all-to-all-done.3 = f32[32,1,2048]{2,1,0:T(1,128)S(1)} async-done(((f32[32,1,2048]{2,1,0:T(1,128)}), f32[32,1,2048]{2,1,0:T(1,128)S(1)}, u32[]{:S(2)}, u32[]{:S(2)}) %all-to-all-start.3) | async-done | bytes 262176 | tf_op jit(solution)/shard_map/all_to_all | solution.py:17
  87.6 0.7 slice_reduce_fusion
  88.3 0.7 slice.43
  89.0 0.7 slice.41
  (48 shorter events, 3.8 us)
Async XLA Ops:
  0.6 1.6 %copy-start = (bf16[1280,128]{1,0:T(8,128)(2,1)S(1)}, bf16[1280,128]{1,0:T(8,128)(2,1)}, u32[]{:S(2)}) copy-start(bf16[1280,128]{1,0:T(8,128)(2,1)} %param.10) | copy-start | bytes 983044
  0.6 12.2 %copy-start.10 = (s32[48]{0:T(128)S(1)}, s32[48]{0:T(128)}, u32[]{:S(2)}) copy-start(s32[48]{0:T(128)} %param.15) | copy-start | bytes 580
  0.7 12.3 %copy-start.9 = (s32[48]{0:T(128)S(1)}, s32[48]{0:T(128)}, u32[]{:S(2)}) copy-start(s32[48]{0:T(128)} %param.14) | copy-start | bytes 580
  4.8 25.5 %all-to-all-start = ((bf16[32,32,128]{2,1,0:T(8,128)(2,1)}), bf16[32,32,128]{2,1,0:T(8,128)(2,1)}, u32[]{:S(2)}, u32[]{:S(2)}) async-start(bf16[32,32,128]{2,1,0:T(8,128)(2,1)} %bitcast.13), calls=%async_computation | async-start | bytes 524288 | tf_op jit(solution)/shard_map/all_to_all | solution.py:31
  13.0 1.4 %copy-start.1 = (bf16[48,128,128]{2,1,0:T(8,128)(2,1)S(1)}, bf16[48,128,128]{2,1,0:T(8,128)(2,1)}, u32[]{:S(2)}) copy-start(bf16[48,128,128]{2,1,0:T(8,128)(2,1)} %param.13) | copy-start | bytes 4718596
  27.4 1.5 %copy-start.7 = (bf16[128,256]{1,0:T(8,128)(2,1)S(1)}, bf16[128,256]{1,0:T(8,128)(2,1)}, u32[]{:S(2)}) copy-start(bf16[128,256]{1,0:T(8,128)(2,1)} %param.17) | copy-start | bytes 196612
  32.3 1.1 %copy-start.6 = (f32[10,128,128]{2,1,0:T(8,128)S(1)}, f32[10,128,128]{2,1,0:T(8,128)}, u32[]{:S(2)}) copy-start(f32[10,128,128]{2,1,0:T(8,128)} %copy.37) | copy-start | bytes 1966084
  33.4 1.3 %copy-start.5 = (f32[1280,256]{1,0:T(8,128)S(1)}, f32[1280,256]{1,0:T(8,128)}, u32[]{:S(2)}) copy-start(f32[1280,256]{1,0:T(8,128)} %fusion.50) | copy-start | bytes 3932164
  33.4 1.5 %copy-start.11 = (bf16[1280,256]{1,0:T(8,128)(2,1)S(1)}, bf16[1280,256]{1,0:T(8,128)(2,1)}, u32[]{:S(2)}) copy-start(bf16[1280,256]{1,0:T(8,128)(2,1)} %param.19) | copy-start | bytes 1966084
  33.4 1.5 %copy-start.12 = (bf16[128,256]{1,0:T(8,128)(2,1)S(1)}, bf16[128,256]{1,0:T(8,128)(2,1)}, u32[]{:S(2)}) copy-start(bf16[128,256]{1,0:T(8,128)(2,1)} %param.18) | copy-start | bytes 196612
  36.5 1.0 %copy-start.3 = (bf16[1280,256]{1,0:T(8,128)(2,1)}, bf16[1280,256]{1,0:T(8,128)(2,1)S(1)}, u32[]{:S(2)}) copy-start(bf16[1280,256]{1,0:T(8,128)(2,1)S(1)} %get-tuple-element.6) | copy-start | bytes 1966084
  40.6 17.2 %all-to-all-start.2 = ((f32[32,1,2048]{2,1,0:T(1,128)}), f32[32,1,2048]{2,1,0:T(1,128)}, u32[]{:S(2)}, u32[]{:S(2)}) async-start(f32[32,1,2048]{2,1,0:T(1,128)} %all_to_all.21), calls=%async_computation.2 | async-start | bytes 524288 | tf_op jit(solution)/shard_map/all_to_all | solution.py:15
  46.7 2.0 %copy-start.2 = (bf16[48,128,128]{2,1,0:T(8,128)(2,1)S(1)}, bf16[48,128,128]{2,1,0:T(8,128)(2,1)}, u32[]{:S(2)}) copy-start(bf16[48,128,128]{2,1,0:T(8,128)(2,1)} %param.13) | copy-start | bytes 4718596
  57.8 16.1 %all-to-all-start.1 = ((bf16[32,32,128]{2,1,0:T(8,128)(2,1)}), bf16[32,32,128]{2,1,0:T(8,128)(2,1)}, u32[]{:S(2)}, u32[]{:S(2)}) async-start(bf16[32,32,128]{2,1,0:T(8,128)(2,1)} %bitcast.29), calls=%async_computation.1 | async-start | bytes 524288 | tf_op jit(solution)/shard_map/all_to_all | solution.py:31
  64.6 1.1 %copy-start.4 = (bf16[1280,256]{1,0:T(8,128)(2,1)S(1)}, bf16[1280,256]{1,0:T(8,128)(2,1)}, u32[]{:S(2)}) copy-start(bf16[1280,256]{1,0:T(8,128)(2,1)} %copy-done.3) | copy-start | bytes 1966084
  64.7 1.1 %copy-start.8 = (bf16[128,256]{1,0:T(8,128)(2,1)S(1)}, bf16[128,256]{1,0:T(8,128)(2,1)}, u32[]{:S(2)}) copy-start(bf16[128,256]{1,0:T(8,128)(2,1)} %param.17) | copy-start | bytes 196612
  74.7 13.0 %all-to-all-start.3 = ((f32[32,1,2048]{2,1,0:T(1,128)}), f32[32,1,2048]{2,1,0:T(1,128)S(1)}, u32[]{:S(2)}, u32[]{:S(2)}) async-start(f32[32,1,2048]{2,1,0:T(1,128)} %broadcast_in_dim.52), calls=%async_computation.3 | async-start | bytes 524288 | tf_op jit(solution)/shard_map/all_to_all | solution.py:17

commit v7 on v2

--- a/solution.py
+++ b/solution.py
@@ -38,7 +38,33 @@
 
 
 def one_hot_rows(index, count):
-    return (index.reshape(-1)[:, None] == jnp.arange(count, dtype=jnp.int32)[None, :]).astype(jnp.bfloat16)
+    hot = index[..., None] == jnp.arange(count, dtype=jnp.int32)
+    return hot.astype(jnp.bfloat16).reshape(-1, count)
+
+
+PLACE_LIMIT = 4 << 20
+
+
+def placement(n_dom, n_grp, bnd):
+    a = lax.axis_index("dom")
+    b = lax.axis_index("grp")
+    blk = jnp.arange(n_dom + n_grp, dtype=jnp.int32)
+    cell = jnp.where(blk < n_dom, blk * n_grp + b, a * n_grp + (blk - n_dom))
+    local = blk == a
+    cell = jnp.where(local, -1, cell)
+    col = cell[:, None] * bnd + jnp.arange(bnd, dtype=jnp.int32)[None, :]
+    place = one_hot_rows(col, n_dom * n_grp * bnd)
+    keep = jnp.broadcast_to(local[:, None], (n_dom + n_grp, bnd)).reshape(-1, 1)
+    return place, keep
+
+
+def swap(table, place, keep):
+    peers = lax.psum(1, ("dom", "grp"))
+    buf = lax.dot_general(place, table, (((0,), (0,)), ((), ())), preferred_element_type=jnp.float32)
+    buf = buf.astype(table.dtype).reshape(peers, -1, table.shape[1])
+    got = lax.all_to_all(buf, ("dom", "grp"), 0, 0, tiled=True).reshape(-1, table.shape[1])
+    back = jnp.dot(place, got, preferred_element_type=jnp.float32).astype(table.dtype)
+    return jnp.where(keep, table, back)
 
 
 def per_device(
@@ -61,11 +87,16 @@
     grp_index = send_grp[0]
     n_dom, bnd = dom_index.shape
     n_grp = grp_index.shape[0]
-    send_index = jnp.concatenate([dom_index.reshape(-1), grp_index.reshape(-1)])
-    pick = one_hot_rows(send_index, node_count)
+    pick = one_hot_rows(jnp.concatenate([dom_index, grp_index], axis=0), node_count)
     sent = jnp.dot(pick, features, preferred_element_type=jnp.float32).astype(jnp.bfloat16)
-    sent = sent.reshape(n_dom + n_grp, bnd, width)
-    recv_dom, recv_grp = exchange(sent[:n_dom], sent[n_dom:])
+    table_bytes = n_dom * n_grp * bnd * (n_dom + n_grp) * bnd * 2
+    if table_bytes <= PLACE_LIMIT:
+        place, keep = placement(n_dom, n_grp, bnd)
+        got = swap(sent, place, keep)
+        recv_dom, recv_grp = got[: n_dom * bnd], got[n_dom * bnd :]
+    else:
+        sent = sent.reshape(n_dom + n_grp, bnd, width)
+        recv_dom, recv_grp = exchange(sent[:n_dom], sent[n_dom:])
     source = jnp.concatenate(
         [features, recv_dom.reshape(-1, width), recv_grp.reshape(-1, width)], axis=0
     )
@@ -105,10 +136,14 @@
     grad_source = jnp.einsum(
         "st,tjf->sjf", to_source, backward, precision=lax.Precision.HIGHEST
     ).reshape(-1, width)
-    remote = grad_source[node_count:].astype(jnp.bfloat16).reshape(n_dom + n_grp, bnd, width)
-    ret_dom, ret_grp = exchange(remote[:n_dom], remote[n_dom:])
+    remote = grad_source[node_count:].astype(jnp.bfloat16)
+    if table_bytes <= PLACE_LIMIT:
+        returned = swap(remote, place, keep)
+    else:
+        remote = remote.reshape(n_dom + n_grp, bnd, width)
+        ret_dom, ret_grp = exchange(remote[:n_dom], remote[n_dom:])
+        returned = jnp.concatenate([ret_dom.reshape(-1, width), ret_grp.reshape(-1, width)])
     grad_self, grad_neigh = weight_sum(part_self, part_neigh)
-    returned = jnp.concatenate([ret_dom.reshape(-1, width), ret_grp.reshape(-1, width)])
     grad_total = grad_own + grad_source[:node_count]
     grad_total = grad_total + lax.dot_general(
         pick, returned, (((0,), (0,)), ((), ())), preferred_element_type=jnp.float32

time: 88.5 us -> 87.3 us (0.986)
  local copies, waits for them, and re-layouts: 21.5 us -> 16.2 us
  matrix products: 20.9 us -> 25.6 us
  waiting for transfers between devices: 23.7 us -> 22.5 us
    dot_general x0 -> x3, matrix products: none -> 3.25 us  [the longest x2 2.82 us: swap(): lax.dot_general(place, table, (((0,), (0,)), ((), ())), preferred_element...]
    dynamic_update_slice x6 -> x0, local copies, waits for them, and re-layouts: 3.23 us -> none  [the longest x2 1.27 us: exchange(): buf = lax.dynamic_update_slice_in_dim(buf, grp_part[None], a, axis=0)]
    another operation x4 -> x0, local copies, waits for them, and re-layouts: 3.13 us -> none  [the longest x2 1.64 us: per_device(): send_index = jnp.concatenate([dom_index.reshape(-1), grp_index.reshape(-1)])]
    dot_general x1, matrix products: 0.33 us -> 1.45 us  [per_device(): jnp.einsum('nh,fh->nf', grad_pre, w_self, preferred_element_type=jnp.floa...]
    all_to_all x1, waiting for transfers between devices: 8.09 us -> 7.05 us  [weight_sum(): total = lax.all_to_all(spread, axes, 0, 0, tiled=True).reshape(-1)]
  transfers between devices with their start and end apart: 4 -> 4, of which waited for: 3 -> 3; matrix products, arithmetic and copies ran while one was open for 21% -> 22% of each run, Pallas kernels for 0% -> 0%
where the time goes in v7:
time: 87.3 us; the launch traced here: 86.8 us
  matrix products  25.6 us (29%)
  waiting for transfers between devices  22.5 us (26%)
  starting transfers between devices  18.9 us (22%)
  local copies, waits for them, and re-layouts  16.2 us (19%)
  other arithmetic  2.01 us (2%)
  between operations  1.62 us (2%)
    all_to_all x2, waiting for transfers between devices, swap(): lax.all_to_all(buf, ('dom', 'grp'), 0, 0, tiled=True)  15.5 us
    all_to_all x2, starting transfers between devices, swap(): lax.all_to_all(buf, ('dom', 'grp'), 0, 0, tiled=True)  13.1 us
    all_to_all x1, waiting for transfers between devices, weight_sum(): total = lax.all_to_all(spread, axes, 0, 0, tiled=True).reshape(-1)  7.05 us
    dot_general x1, matrix products, per_device(): jnp.einsum('tij,tjf->tif', tile_vals, source[tile_src], preferred_element...  4.29 us
    dot_general x1, local copies, waits for them, and re-layouts, per_device(): jnp.einsum('tij,tif->tjf', tile_vals, picked, preferred_element_type=jnp....  3.59 us
    dot_general x1, local copies, waits for them, and re-layouts, per_device(): jnp.einsum('tij,tjf->tif', tile_vals, source[tile_src], preferred_element...  3.59 us
    all_to_all x1, starting transfers between devices, weight_sum(): lax.all_to_all(chunks, axes, 0, 0, tiled=True)  3.31 us
    dot_general x1, matrix products, per_device(): jnp.einsum('bt,tif->bif', to_target, products, precision=lax.Precision.HI...  3.26 us
  transfers between devices with their start and end apart: 4, of which 3 were waited for; matrix products, arithmetic and copies ran while one was open for 22% of the time, Pallas kernels for 0%

profile of v7, /device:TPU:0, one launch (start us, length us, event | category | flops | bytes accessed | tf_op | source)
XLA Modules:
  0.0 86.8 jit_solution(1500943652722512581)
XLA Ops:
  0.6 0.0 copy-start
  0.7 0.1 iota_add_fusion
  0.8 0.1 add.79
  0.8 0.7 pad_add_fusion
  1.5 0.1 eq.74
  1.6 1.5 %fusion.12 = bf16[384,128]{1,0:T(8,128)(2,1)S(1)} fusion(bf16[1280,128]{1,0:T(8,128)(2,1)} %param.10, s32[384]{0:T(512)S(1)} %eq.74), kind=kOutput, calls=%fused_computation.26 | convolution fusion | flops 126369792 | bytes 427520 | tf_op jit(solution)/shard_map/dot_general | solution.py:91
  3.1 0.0 copy-start.3
  3.1 0.0 copy-start.5
  3.1 1.4 %fusion.8 = bf16[1024,128]{1,0:T(8,128)(2,1)} fusion(bf16[384,128]{1,0:T(8,128)(2,1)S(1)} %fusion.12, s32[384]{0:T(512)S(1)} %add.79), kind=kOutput, calls=%fused_computation.22 | convolution fusion | flops 101187584 | bytes 361984 | tf_op jit(solution)/shard_map/dot_general | solution.py:63
  4.5 7.3 %all-to-all-start = ((bf16[32,32,128]{2,1,0:T(8,128)(2,1)}), bf16[32,32,128]{2,1,0:T(8,128)(2,1)S(1)}, u32[]{:S(2)}, u32[]{:S(2)}) async-start(bf16[32,32,128]{2,1,0:T(8,128)(2,1)} %bitcast.4), calls=%async_computation | async-start | bytes 524288 | tf_op jit(solution)/shard_map/all_to_all | solution.py:65
  12.6 0.5 fusion.40
  13.1 0.1 fusion.24
  13.2 0.1 broadcast_in_dim.27
  13.3 0.1 broadcast_in_dim.28
  13.4 0.1 copy.30
  13.5 1.4 %fusion.43 = f32[1280,256]{1,0:T(8,128)} fusion(bf16[1280,128]{1,0:T(8,128)(2,1)S(1)} %copy-done.3, bf16[128,256]{1,0:T(8,128)(2,1)S(1)} %copy-done.5), kind=kOutput, calls=%fused_computation.70 | convolution fusion | flops 83886080 | bytes 1703936 | tf_op jit(solution)/shard_map/dot_general | solution.py:121
  14.9 7.3 %all-to-all-done = bf16[32,32,128]{2,1,0:T(8,128)(2,1)S(1)} async-done(((bf16[32,32,128]{2,1,0:T(8,128)(2,1)}), bf16[32,32,128]{2,1,0:T(8,128)(2,1)S(1)}, u32[]{:S(2)}, u32[]{:S(2)}) %all-to-all-start) | async-done | bytes 262176 | tf_op jit(solution)/shard_map/all_to_all | solution.py:65
  22.2 0.4 fusion.14
  22.7 2.0 %gather_fusion = bf16[48,128,128]{2,1,0:T(8,128)(2,1)} fusion(bf16[13,128,128]{2,1,0:T(8,128)(2,1)S(1)} %bitcast.54, s32[1024]{0:T(1024)S(1)} %pad_clamp_fusion.1), kind=kCustom, calls=%fused_computation | custom fusion | bytes 3145920 | tf_op jit(solution)/shard_map/gather | solution.py:114
  24.7 4.3 %convolution_bitcast_fusion.1 = f32[48,128,128]{1,2,0:T(8,128)} fusion(bf16[48,128,128]{2,1,0:T(8,128)(2,1)} %gather_fusion, bf16[48,128,128]{2,1,0:T(8,128)(2,1)S(1)} %copy-done), kind=kOutput, calls=%fused_computation.11 | convolution fusion | flops 201326592 | bytes 6291456 | tf_op jit(solution)/shard_map/tij,tjf->tif/dot_general | solution.py:113
  28.9 3.6 %copy.29 = f32[48,128,128]{2,0,1:T(8,128)} copy(f32[48,128,128]{1,2,0:T(8,128)} %convolution_bitcast_fusion.1) | data formatting | bytes 6291456 | tf_op jit(solution)/shard_map/tij,tjf->tif/dot_general | solution.py:113
  32.5 3.3 %fusion.7 = bf16[10,128,128]{2,0,1:T(8,128)(2,1)S(1)} fusion(f32[48,128,128]{2,0,1:T(8,128)} %copy.29, f32[10,128]{0,1:T(8,128)S(1)} %copy.30, s32[48]{0:T(128)S(1)} %copy-done.8, pred[48]{0:T(512)(128)(4,1)S(1)} %iota_compare_fusion.27), kind=kOutput, calls=%fused_computation.21 | convolution fusion | flops 94700480 | bytes 3478768 | tf_op jit(solution)/shard_map/bt,tif->bif/dot_general | solution.py:116
  35.8 0.1 copy.31
  35.9 1.6 %multiply_convert_fusion = (bf16[1280,256]{1,0:T(8,128)(2,1)S(1)}, bf16[1280,256]{1,0:T(8,128)(2,1)}) fusion(bf16[1280,256]{1,0:T(8,128)(2,1)S(1)} %copy-done.10, f32[1280,256]{1,0:T(8,128)S(1)} %copy-done.4, bf16[1280,128]{1,0:T(8,128)(2,1)S(1)} %bitcast.58, bf16[128,256]{1,0:T(8,128)(2,1)S(1)} %copy-done.11), kind=kOutput, calls=%fused_computation.18 | convolution fusion | flops 88145920 | bytes 3670016 | tf_op jit(solution)/shard_map/dot_general | solution.py:121
  37.6 0.3 fusion.44
  37.9 0.3 convolution_bitcast_fusion.2
  38.2 1.0 %all_to_all.21 = f32[32,1,2048]{2,1,0:T(1,128)} reshape(f32[256,256]{1,0:T(8,128)S(1)} %pad_maximum_fusion.1) | data formatting | bytes 524288 | tf_op jit(solution)/shard_map/all_to_all | solution.py:15
  39.2 3.3 %all-to-all-start.2 = ((f32[32,1,2048]{2,1,0:T(1,128)}), f32[32,1,2048]{2,1,0:T(1,128)}, u32[]{:S(2)}, u32[]{:S(2)}) async-start(f32[32,1,2048]{2,1,0:T(1,128)} %all_to_all.21), calls=%async_computation.2 | async-start | bytes 524288 | tf_op jit(solution)/shard_map/all_to_all | solution.py:15
  42.5 0.3 fusion
  42.9 0.8 gather_fusion.1
  43.7 2.3 %convolution_bitcast_fusion = f32[48,128,128]{1,2,0:T(8,128)} fusion(bf16[48,128,128]{2,1,0:T(8,128)(2,1)S(1)} %gather_fusion.1, bf16[48,128,128]{2,1,0:T(8,128)(2,1)S(1)} %copy-done), kind=kOutput, calls=%fused_computation.10 | convolution fusion | flops 201326592 | bytes 6291456 | tf_op jit(solution)/shard_map/tij,tif->tjf/dot_general | solution.py:135
  46.1 3.6 %copy.33 = f32[48,128,128]{2,0,1:T(8,128)} copy(f32[48,128,128]{1,2,0:T(8,128)} %convolution_bitcast_fusion) | data formatting | bytes 6291456 | tf_op jit(solution)/shard_map/tij,tif->tjf/dot_general | solution.py:135
  49.6 3.0 %fusion.30 = f32[13,128,128]{2,0,1:T(8,128)S(1)} fusion(f32[48,128,128]{2,0,1:T(8,128)} %copy.33, s32[48]{0:T(128)S(1)} %copy-done.9, pred[48]{0:T(512)(128)(4,1)S(1)} %iota_compare_fusion.27), kind=kOutput, calls=%fused_computation.51 | convolution fusion | flops 122684640 | bytes 3997936 | tf_op jit(solution)/shard_map/st,tjf->sjf/dot_general | solution.py:136
  52.7 0.1 slice.46
  52.8 0.6 copy-done.6
  53.4 1.4 %fusion.9 = bf16[1024,128]{1,0:T(8,128)(2,1)} fusion(bf16[384,128]{1,0:T(8,128)(2,1)S(1)} %bitcast.63, s32[384]{0:T(512)S(1)} %add.79), kind=kOutput, calls=%fused_computation.23 | convolution fusion | flops 101187584 | bytes 361984 | tf_op jit(solution)/shard_map/dot_general | solution.py:63
  54.8 5.8 %all-to-all-start.1 = ((bf16[32,32,128]{2,1,0:T(8,128)(2,1)}), bf16[32,32,128]{2,1,0:T(8,128)(2,1)S(1)}, u32[]{:S(2)}, u32[]{:S(2)}) async-start(bf16[32,32,128]{2,1,0:T(8,128)(2,1)} %bitcast.62), calls=%async_computation.1 | async-start | bytes 524288 | tf_op jit(solution)/shard_map/all_to_all | solution.py:65
  60.6 1.1 %copy.34 = f32[10,128,128]{2,1,0:T(8,128)} copy(f32[10,128,128]{2,0,1:T(8,128)S(1)} %bitcast.56) | data formatting | bytes 1310720 | tf_op jit(solution)/shard_map/slice | solution.py:147
  61.6 1.1 %reduce_sum.9 = f32[2048]{0:T(1024)S(1)} reduce(f32[32,1,2048]{2,1,0:T(1,128)} %all-to-all-done.2, f32[]{:T(128)} %constant.31.clone.1), dimensions={0,1}, to_apply=%region_0.1 | reduce | flops 63488 | bytes 270340 | tf_op jit(solution)/shard_map/reduce_sum | solution.py:15
  62.8 8.2 %all-to-all-done.1 = bf16[32,32,128]{2,1,0:T(8,128)(2,1)S(1)} async-done(((bf16[32,32,128]{2,1,0:T(8,128)(2,1)}), bf16[32,32,128]{2,1,0:T(8,128)(2,1)S(1)}, u32[]{:S(2)}, u32[]{:S(2)}) %all-to-all-start.1) | async-done | bytes 262176 | tf_op jit(solution)/shard_map/all_to_all | solution.py:65
  71.0 0.8 broadcast_in_dim.58
  71.8 2.6 %all-to-all-start.3 = ((f32[32,1,2048]{2,1,0:T(1,128)}), f32[32,1,2048]{2,1,0:T(1,128)S(1)}, u32[]{:S(2)}, u32[]{:S(2)}) async-start(f32[32,1,2048]{2,1,0:T(1,128)} %broadcast_in_dim.58), calls=%async_computation.3 | async-start | bytes 524288 | tf_op jit(solution)/shard_map/all_to_all | solution.py:17
  74.4 1.5 %convolution_add_fusion.2 = f32[1280,128]{1,0:T(8,128)S(1)} fusion(f32[1280,128]{1,0:T(8,128)} %bitcast.57, bf16[1280,256]{1,0:T(8,128)(2,1)S(1)} %copy-done.2, bf16[128,256]{1,0:T(8,128)(2,1)} %param.17), kind=kOutput, calls=%fused_computation.5 | convolution fusion | flops 84049920 | bytes 2031616 | tf_op jit(solution)/shard_map/nh,fh->nf/dot_general | solution.py:131
  75.9 1.9 %fusion.1 = bf16[1280,128]{1,0:T(8,128)(2,1)} fusion(f32[1280,128]{1,0:T(8,128)S(1)} %convolution_add_fusion.2, bf16[384,128]{1,0:T(8,128)(2,1)S(1)} %bitcast.64, bf16[1024,128]{1,0:T(8,128)(2,1)S(1)} %bitcast.61, s32[384]{0:T(512)S(1)} %eq.74, s32[384]{0:T(512)S(1)} %add.79, pred[384]{0:T(512)(128)(4,1)S(1)} %broadcast_in_dim.28), kind=kOutput, calls=%fused_computation.7 | convolution fusion | flops 227803136 | bytes 1346944 | tf_op jit(solution)/shard_map/dot_general | solution.py:148
  77.7 7.0 %all-to-all-done.3 = f32[32,1,2048]{2,1,0:T(1,128)S(1)} async-done(((f32[32,1,2048]{2,1,0:T(1,128)}), f32[32,1,2048]{2,1,0:T(1,128)S(1)}, u32[]{:S(2)}, u32[]{:S(2)}) %all-to-all-start.3) | async-done | bytes 262176 | tf_op jit(solution)/shard_map/all_to_all | solution.py:17
  84.8 0.7 slice_reduce_fusion
  85.5 0.7 slice.34
  86.1 0.7 slice.32
  (31 shorter events, 0.1 us)
Async XLA Ops:
  0.6 11.9 %copy-start = (bf16[48,128,128]{2,1,0:T(8,128)(2,1)S(1)}, bf16[48,128,128]{2,1,0:T(8,128)(2,1)}, u32[]{:S(2)}) copy-start(bf16[48,128,128]{2,1,0:T(8,128)(2,1)} %param.13) | copy-start | bytes 4718596
  0.6 11.9 %copy-start.9 = (s32[48]{0:T(128)S(1)}, s32[48]{0:T(128)}, u32[]{:S(2)}) copy-start(s32[48]{0:T(128)} %param.15) | copy-start | bytes 580
  0.7 11.9 %copy-start.8 = (s32[48]{0:T(128)S(1)}, s32[48]{0:T(128)}, u32[]{:S(2)}) copy-start(s32[48]{0:T(128)} %param.14) | copy-start | bytes 580
  3.1 10.4 %copy-start.3 = (bf16[1280,128]{1,0:T(8,128)(2,1)S(1)}, bf16[1280,128]{1,0:T(8,128)(2,1)}, u32[]{:S(2)}) copy-start(bf16[1280,128]{1,0:T(8,128)(2,1)} %param.10) | copy-start | bytes 983044
  3.1 10.4 %copy-start.5 = (bf16[128,256]{1,0:T(8,128)(2,1)S(1)}, bf16[128,256]{1,0:T(8,128)(2,1)}, u32[]{:S(2)}) copy-start(bf16[128,256]{1,0:T(8,128)(2,1)} %param.17) | copy-start | bytes 196612
  4.5 17.7 %all-to-all-start = ((bf16[32,32,128]{2,1,0:T(8,128)(2,1)}), bf16[32,32,128]{2,1,0:T(8,128)(2,1)S(1)}, u32[]{:S(2)}, u32[]{:S(2)}) async-start(bf16[32,32,128]{2,1,0:T(8,128)(2,1)} %bitcast.4), calls=%async_computation | async-start | bytes 524288 | tf_op jit(solution)/shard_map/all_to_all | solution.py:65
  32.5 3.4 %copy-start.4 = (f32[1280,256]{1,0:T(8,128)S(1)}, f32[1280,256]{1,0:T(8,128)}, u32[]{:S(2)}) copy-start(f32[1280,256]{1,0:T(8,128)} %fusion.43) | copy-start | bytes 3932164
  32.5 3.4 %copy-start.10 = (bf16[1280,256]{1,0:T(8,128)(2,1)S(1)}, bf16[1280,256]{1,0:T(8,128)(2,1)}, u32[]{:S(2)}) copy-start(bf16[1280,256]{1,0:T(8,128)(2,1)} %param.19) | copy-start | bytes 1966084
  32.5 3.4 %copy-start.11 = (bf16[128,256]{1,0:T(8,128)(2,1)S(1)}, bf16[128,256]{1,0:T(8,128)(2,1)}, u32[]{:S(2)}) copy-start(bf16[128,256]{1,0:T(8,128)(2,1)} %param.18) | copy-start | bytes 196612
  37.6 4.9 %copy-start.1 = (bf16[1280,256]{1,0:T(8,128)(2,1)}, bf16[1280,256]{1,0:T(8,128)(2,1)S(1)}, u32[]{:S(2)}) copy-start(bf16[1280,256]{1,0:T(8,128)(2,1)S(1)} %get-tuple-element.6) | copy-start | bytes 1966084
  39.2 15.6 %all-to-all-start.2 = ((f32[32,1,2048]{2,1,0:T(1,128)}), f32[32,1,2048]{2,1,0:T(1,128)}, u32[]{:S(2)}, u32[]{:S(2)}) async-start(f32[32,1,2048]{2,1,0:T(1,128)} %all_to_all.21), calls=%async_computation.2 | async-start | bytes 524288 | tf_op jit(solution)/shard_map/all_to_all | solution.py:15
  52.8 0.6 copy-start.6
  54.8 19.6 %copy-start.2 = (bf16[1280,256]{1,0:T(8,128)(2,1)S(1)}, bf16[1280,256]{1,0:T(8,128)(2,1)}, u32[]{:S(2)}) copy-start(bf16[1280,256]{1,0:T(8,128)(2,1)} %copy-done.1) | copy-start | bytes 1966084
  54.8 16.1 %all-to-all-start.1 = ((bf16[32,32,128]{2,1,0:T(8,128)(2,1)}), bf16[32,32,128]{2,1,0:T(8,128)(2,1)S(1)}, u32[]{:S(2)}, u32[]{:S(2)}) async-start(bf16[32,32,128]{2,1,0:T(8,128)(2,1)} %bitcast.62), calls=%async_computation.1 | async-start | bytes 524288 | tf_op jit(solution)/shard_map/all_to_all | solution.py:65
  61.6 14.2 %copy-start.7 = (bf16[3,128,128]{2,1,0:T(8,128)(2,1)S(1)}, bf16[3,128,128]{2,1,0:T(8,128)(2,1)}, u32[]{:S(2)}) copy-start(bf16[3,128,128]{2,1,0:T(8,128)(2,1)} %copy-done.6) | copy-start | bytes 294916
  71.8 13.0 %all-to-all-start.3 = ((f32[32,1,2048]{2,1,0:T(1,128)}), f32[32,1,2048]{2,1,0:T(1,128)S(1)}, u32[]{:S(2)}, u32[]{:S(2)}) async-start(f32[32,1,2048]{2,1,0:T(1,128)} %broadcast_in_dim.58), calls=%async_computation.3 | async-start | bytes 524288 | tf_op jit(solution)/shard_map/all_to_all | solution.py:17

commit v8 on v7

--- a/solution.py
+++ b/solution.py
@@ -4,11 +4,18 @@
 from jax.sharding import PartitionSpec as P
 
 
-def weight_sum(part_self, part_neigh):
+def weight_sum(part_self, part_neigh, stacked=None):
     axes = ("dom", "grp")
     peers = lax.psum(1, axes)
     rows = part_self.shape[0]
-    stacked = jnp.concatenate([part_self, part_neigh], axis=0)
+    if stacked is None:
+        stacked = jnp.concatenate([part_self, part_neigh], axis=0)
+    if stacked.shape[0] % (8 * peers) == 0:
+        chunks = stacked.reshape(peers, -1, stacked.shape[1])
+        mine = jnp.sum(lax.all_to_all(chunks, axes, 0, 0, tiled=True), axis=0, keepdims=True)
+        total = lax.all_to_all(jnp.broadcast_to(mine, chunks.shape), axes, 0, 0, tiled=True)
+        total = total.reshape(stacked.shape)
+        return total[:rows], total[rows:]
     flat = stacked.reshape(-1)
     pad = (-flat.shape[0]) % peers
     chunks = jnp.pad(flat, (0, pad)).reshape(peers, -1)
@@ -58,13 +65,24 @@
     return place, keep
 
 
-def swap(table, place, keep):
+def swap(table, place, keep, buf=None):
     peers = lax.psum(1, ("dom", "grp"))
-    buf = lax.dot_general(place, table, (((0,), (0,)), ((), ())), preferred_element_type=jnp.float32)
-    buf = buf.astype(table.dtype).reshape(peers, -1, table.shape[1])
+    if buf is None:
+        buf = lax.dot_general(place, table, (((0,), (0,)), ((), ())), preferred_element_type=jnp.float32)
+        buf = buf.astype(table.dtype)
+    buf = buf.reshape(peers, -1, table.shape[1])
     got = lax.all_to_all(buf, ("dom", "grp"), 0, 0, tiled=True).reshape(-1, table.shape[1])
     back = jnp.dot(place, got, preferred_element_type=jnp.float32).astype(table.dtype)
     return jnp.where(keep, table, back)
+
+
+def send_rows(dom_index, grp_index):
+    a = lax.axis_index("dom")
+    b = lax.axis_index("grp")
+    n_dom, n_grp = dom_index.shape[0], grp_index.shape[0]
+    p = jnp.arange(n_dom, dtype=jnp.int32)[:, None, None]
+    q = jnp.arange(n_grp, dtype=jnp.int32)[None, :, None]
+    return jnp.where(p == a, grp_index[None], jnp.where(q == b, dom_index[:, None], -1))
 
 
 def per_device(
@@ -88,13 +106,19 @@
     n_dom, bnd = dom_index.shape
     n_grp = grp_index.shape[0]
     pick = one_hot_rows(jnp.concatenate([dom_index, grp_index], axis=0), node_count)
-    sent = jnp.dot(pick, features, preferred_element_type=jnp.float32).astype(jnp.bfloat16)
     table_bytes = n_dom * n_grp * bnd * (n_dom + n_grp) * bnd * 2
     if table_bytes <= PLACE_LIMIT:
         place, keep = placement(n_dom, n_grp, bnd)
-        got = swap(sent, place, keep)
+        direct = one_hot_rows(send_rows(dom_index, grp_index), node_count)
+        buf = jnp.dot(direct, features, preferred_element_type=jnp.float32).astype(jnp.bfloat16)
+        own_rows = one_hot_rows(lax.dynamic_index_in_dim(dom_index, lax.axis_index("dom"), 0), node_count)
+        own_sent = jnp.dot(own_rows, features, preferred_element_type=jnp.float32).astype(jnp.bfloat16)
+        table = jnp.zeros(((n_dom + n_grp) * bnd, width), jnp.bfloat16)
+        table = lax.dynamic_update_slice_in_dim(table, own_sent, lax.axis_index("dom") * bnd, 0)
+        got = swap(table, place, keep, buf)
         recv_dom, recv_grp = got[: n_dom * bnd], got[n_dom * bnd :]
     else:
+        sent = jnp.dot(pick, features, preferred_element_type=jnp.float32).astype(jnp.bfloat16)
         sent = sent.reshape(n_dom + n_grp, bnd, width)
         recv_dom, recv_grp = exchange(sent[:n_dom], sent[n_dom:])
     source = jnp.concatenate(
@@ -126,8 +150,11 @@
     grad_pre = (cotangent.astype(jnp.float32) * sigm * (1.0 + preact * (1.0 - sigm))).astype(
         jnp.bfloat16
     )
-    part_self = jnp.einsum("nf,nh->fh", features, grad_pre, preferred_element_type=jnp.float32)
-    part_neigh = jnp.einsum("nf,nh->fh", agg, grad_pre, preferred_element_type=jnp.float32)
+    stacked = jnp.einsum(
+        "nf,nh->fh", jnp.concatenate([features, agg], axis=1), grad_pre,
+        preferred_element_type=jnp.float32,
+    )
+    part_self, part_neigh = stacked[:width], stacked[width:]
     grad_own = jnp.einsum("nh,fh->nf", grad_pre, w_self, preferred_element_type=jnp.float32)
     grad_agg = jnp.einsum("nh,fh->nf", grad_pre, w_neigh, preferred_element_type=jnp.float32)
     grad_agg = (grad_agg / degree.reshape(-1)[:, None]).astype(jnp.bfloat16)
@@ -143,7 +170,7 @@
         remote = remote.reshape(n_dom + n_grp, bnd, width)
         ret_dom, ret_grp = exchange(remote[:n_dom], remote[n_dom:])
         returned = jnp.concatenate([ret_dom.reshape(-1, width), ret_grp.reshape(-1, width)])
-    grad_self, grad_neigh = weight_sum(part_self, part_neigh)
+    grad_self, grad_neigh = weight_sum(part_self, part_neigh, stacked)
     grad_total = grad_own + grad_source[:node_count]
     grad_total = grad_total + lax.dot_general(
         pick, returned, (((0,), (0,)), ((), ())), preferred_element_type=jnp.float32

time: 87.3 us -> 89.3 us (1.023)
  local copies, waits for them, and re-layouts: 16.2 us -> 13.9 us
  waiting for transfers between devices: 22.5 us -> 24 us
  matrix products: 25.6 us -> 27 us
  other arithmetic: 2.01 us -> 3.05 us
    dot_general x3, matrix products: 2.08 us -> 4.01 us  [the longest x1 2.72 us: per_device(): jnp.dot(direct, features, preferred_element_type=jnp.float32)]
    all_to_all x2, waiting for transfers between devices: 15.5 us -> 16.9 us  [swap(): lax.all_to_all(buf, ('dom', 'grp'), 0, 0, tiled=True)]
    dot_general x2 -> x1, matrix products: 2.82 us -> 1.41 us  [swap(): lax.dot_general(place, table, (((0,), (0,)), ((), ())), preferred_element...]
    slice x3 -> x1, local copies, waits for them, and re-layouts: 2.02 us -> 0.72 us  [weight_sum(): return (total[:rows], total[rows:])]
    dot_general x1, matrix products: 0.34 us -> 1.43 us  [per_device(): jnp.einsum('nh,fh->nf', grad_pre, w_neigh, preferred_element_type=jnp.flo...]
    dot_general x1, matrix products: 1.39 us -> 0.31 us  [per_device(): jnp.dot(features, w_self, preferred_element_type=jnp.float32)]
    concatenate x1, other arithmetic: 0.03 us -> 1 us  [per_device(): jnp.concatenate([features, recv_dom.reshape(-1, width), recv_grp.reshape(...]
    all_to_all x1 -> x0, local copies, waits for them, and re-layouts: 0.97 us -> none  [weight_sum(): lax.all_to_all(chunks, axes, 0, 0, tiled=True)]
  transfers between devices with their start and end apart: 4 -> 4, of which waited for: 3 -> 3; matrix products, arithmetic and copies ran while one was open for 22% -> 21% of each run, Pallas kernels for 0% -> 0%
where the time goes in v8:
time: 89.3 us; the launch traced here: 88.6 us
  matrix products  27 us (30%)
  waiting for transfers between devices  24 us (27%)
  starting transfers between devices  19.1 us (21%)
  local copies, waits for them, and re-layouts  13.9 us (16%)
  other arithmetic  3.05 us (3%)
  between operations  1.6 us (2%)
    all_to_all x2, waiting for transfers between devices, swap(): lax.all_to_all(buf, ('dom', 'grp'), 0, 0, tiled=True)  16.9 us
    all_to_all x2, starting transfers between devices, swap(): lax.all_to_all(buf, ('dom', 'grp'), 0, 0, tiled=True)  13.2 us
    all_to_all x1, waiting for transfers between devices, weight_sum(): lax.all_to_all(jnp.broadcast_to(mine, chunks.shape), axes, 0, 0, tiled=True)  7.09 us
    dot_general x1, matrix products, per_device(): jnp.einsum('tij,tjf->tif', tile_vals, source[tile_src], preferred_element...  4.3 us
    dot_general x1, local copies, waits for them, and re-layouts, per_device(): jnp.einsum('tij,tjf->tif', tile_vals, source[tile_src], preferred_element...  3.6 us
    dot_general x1, local copies, waits for them, and re-layouts, per_device(): jnp.einsum('tij,tif->tjf', tile_vals, picked, preferred_element_type=jnp....  3.6 us
    all_to_all x1, starting transfers between devices, weight_sum(): lax.all_to_all(chunks, axes, 0, 0, tiled=True)  3.31 us
    dot_general x1, matrix products, per_device(): jnp.einsum('bt,tif->bif', to_target, products, precision=lax.Precision.HI...  3.18 us
  transfers between devices with their start and end apart: 4, of which 3 were waited for; matrix products, arithmetic and copies ran while one was open for 21% of the time, Pallas kernels for 0%

profile of v8, /device:TPU:0, one launch (start us, length us, event | category | flops | bytes accessed | tf_op | source)
XLA Modules:
  0.0 88.6 jit_solution(3244638618937672127)
XLA Ops:
  0.6 0.0 copy-start
  0.7 0.9 %select_select_fusion = s32[4,8,32]{2,1,0:T(8,128)S(1)} fusion(s32[4,32]{1,0:T(4,128)} %bitcast.74, s32[8,32]{1,0:T(8,128)} %bitcast.72, pred[8]{0:T(512)(128)(4,1)S(1)} %iota_compare_fusion.26, pred[4]{0:T(512)(128)(4,1)S(1)} %iota_compare_fusion.27), kind=kLoop, calls=%fused_computation.48 | loop fusion | flops 2048 | bytes 5644 | tf_op jit(solution)/shard_map/jit(_where)/select_n | solution.py:85
  1.6 0.1 select_n.62
  1.7 2.7 %fusion.18 = bf16[1024,128]{1,0:T(8,128)(2,1)} fusion(bf16[1280,128]{1,0:T(8,128)(2,1)} %param.10, s32[1024]{0:T(1024)S(1)} %select_n.62), kind=kOutput, calls=%fused_computation.26 | convolution fusion | flops 336986112 | bytes 593920 | tf_op jit(solution)/shard_map/dot_general | solution.py:113
  4.4 7.4 %all-to-all-start = ((bf16[32,32,128]{2,1,0:T(8,128)(2,1)}), bf16[32,32,128]{2,1,0:T(8,128)(2,1)}, u32[]{:S(2)}, u32[]{:S(2)}) async-start(bf16[32,32,128]{2,1,0:T(8,128)(2,1)} %bitcast.5), calls=%async_computation | async-start | bytes 524288 | tf_op jit(solution)/shard_map/all_to_all | solution.py:74
  12.6 0.1 iota_add_fusion
  12.6 0.5 fusion.50
  13.2 0.1 fusion.35
  13.3 0.1 broadcast_in_dim.100
  13.4 0.1 broadcast_in_dim.101
  13.5 0.1 add.88
  13.6 0.1 copy.17
  13.7 0.2 fusion.23
  13.9 0.3 fusion.54
  14.3 7.9 %all-to-all-done = bf16[32,32,128]{2,1,0:T(8,128)(2,1)} async-done(((bf16[32,32,128]{2,1,0:T(8,128)(2,1)}), bf16[32,32,128]{2,1,0:T(8,128)(2,1)}, u32[]{:S(2)}, u32[]{:S(2)}) %all-to-all-start) | async-done | bytes 262176 | tf_op jit(solution)/shard_map/all_to_all | solution.py:74
  22.2 1.4 %fusion.22 = bf16[384,128]{1,0:T(8,128)(2,1)S(1)} fusion(bf16[384,128]{1,0:T(8,128)(2,1)S(1)} %fusion.23, bf16[1024,128]{1,0:T(8,128)(2,1)} %bitcast.6, s32[384]{0:T(512)S(1)} %add.88, pred[384]{0:T(512)(128)(4,1)S(1)} %broadcast_in_dim.101), kind=kOutput, calls=%fused_computation.31 | convolution fusion | flops 101154816 | bytes 460672 | tf_op jit(solution)/shard_map/dot_general | solution.py:75
  23.6 1.0 %pad_maximum_fusion = bf16[1664,128]{1,0:T(8,128)(2,1)S(1)} fusion(bf16[384,128]{1,0:T(8,128)(2,1)S(1)} %fusion.22, bf16[1280,128]{1,0:T(8,128)(2,1)} %param.10), kind=kLoop, calls=%fused_computation.41 | loop fusion | flops 851968 | bytes 851968 | tf_op jit(solution)/shard_map/concatenate | solution.py:124
  24.6 2.0 %gather_fusion = bf16[48,128,128]{2,1,0:T(8,128)(2,1)} fusion(bf16[13,128,128]{2,1,0:T(8,128)(2,1)S(1)} %bitcast.61, s32[1024]{0:T(1024)S(1)} %pad_clamp_fusion.1), kind=kCustom, calls=%fused_computation | custom fusion | bytes 3145920 | tf_op jit(solution)/shard_map/gather | solution.py:138
  26.5 4.3 %fusion.55 = f32[48,128,128]{2,1,0:T(8,128)} fusion(bf16[48,128,128]{2,1,0:T(8,128)(2,1)} %gather_fusion, bf16[48,128,128]{2,1,0:T(8,128)(2,1)S(1)} %copy-done), kind=kOutput, calls=%fused_computation.81 | convolution fusion | flops 201326592 | bytes 6291456 | tf_op jit(solution)/shard_map/tij,tjf->tif/dot_general | solution.py:137
  30.8 3.6 %copy.21 = f32[48,128,128]{1,0,2:T(8,128)} copy(f32[48,128,128]{2,1,0:T(8,128)} %fusion.55) | data formatting | bytes 6291456 | tf_op jit(solution)/shard_map/tij,tjf->tif/dot_general | solution.py:137
  34.4 3.2 %fusion.14 = bf16[10,128,128]{2,0,1:T(8,128)(2,1)S(1)} fusion(f32[48,128,128]{1,0,2:T(8,128)} %copy.21, f32[10,128]{0,1:T(8,128)S(1)} %copy.17, s32[48]{0:T(128)S(1)} %copy-done.9, pred[48]{0:T(512)(128)(4,1)S(1)} %iota_compare_fusion.29), kind=kOutput, calls=%fused_computation.24 | convolution fusion | flops 94700480 | bytes 3478768 | tf_op jit(solution)/shard_map/bt,tif->bif/dot_general | solution.py:140
  37.6 0.1 copy.18
  37.8 1.6 %multiply_convert_fusion = (bf16[1280,256]{1,0:T(8,128)(2,1)S(1)}, bf16[1280,256]{1,0:T(8,128)(2,1)}) fusion(bf16[1280,256]{1,0:T(8,128)(2,1)S(1)} %copy-done.11, f32[1280,256]{1,0:T(8,128)S(1)} %fusion.54, bf16[1280,128]{1,0:T(8,128)(2,1)S(1)} %bitcast.65, bf16[128,256]{1,0:T(8,128)(2,1)S(1)} %copy-done.12), kind=kOutput, calls=%fused_computation.21 | convolution fusion | flops 88145920 | bytes 3670016 | tf_op jit(solution)/shard_map/dot_general | solution.py:145
  39.4 0.9 copy-done.3
  40.3 1.1 %convolution_bitcast_fusion = f32[32,8,256]{2,1,0:T(8,128)} fusion(bf16[1280,256]{1,0:T(8,128)(2,1)S(1)} %get-tuple-element.4, bf16[1280,128]{1,0:T(8,128)(2,1)S(1)} %bitcast.66, bf16[1280,128]{1,0:T(8,128)(2,1)S(1)} %copy-done.2), kind=kOutput, calls=%fused_computation.27 | convolution fusion | flops 169082880 | bytes 1572864 | tf_op jit(solution)/shard_map/nf,nh->fh/dot_general | solution.py:153
  41.3 3.3 %all-to-all-start.2 = ((f32[32,8,256]{2,1,0:T(8,128)}), f32[32,8,256]{2,1,0:T(8,128)}, u32[]{:S(2)}, u32[]{:S(2)}) async-start(f32[32,8,256]{2,1,0:T(8,128)} %convolution_bitcast_fusion), calls=%async_computation.2 | async-start | bytes 524288 | tf_op jit(solution)/shard_map/all_to_all | solution.py:15
  44.6 1.4 %fusion.6 = bf16[1280,128]{1,0:T(8,128)(2,1)S(1)} fusion(bf16[1280,256]{1,0:T(8,128)(2,1)} %copy-done.3, bf16[128,256]{1,0:T(8,128)(2,1)S(1)} %copy-done.12, f32[1280]{0:T(1024)S(1)} %bitcast.71), kind=kOutput, calls=%fused_computation.13 | convolution fusion | flops 84213760 | bytes 1053696 | tf_op jit(solution)/shard_map/nh,fh->nf/dot_general | solution.py:159
  46.1 0.8 gather_fusion.1
  46.9 2.3 %fusion.56 = f32[48,128,128]{2,1,0:T(8,128)} fusion(bf16[48,128,128]{2,1,0:T(8,128)(2,1)S(1)} %gather_fusion.1, bf16[48,128,128]{2,1,0:T(8,128)(2,1)S(1)} %copy-done), kind=kOutput, calls=%fused_computation.82 | convolution fusion | flops 201326592 | bytes 6291456 | tf_op jit(solution)/shard_map/tij,tif->tjf/dot_general | solution.py:162
  49.3 3.6 %copy.23 = f32[48,128,128]{1,0,2:T(8,128)} copy(f32[48,128,128]{2,1,0:T(8,128)} %fusion.56) | data formatting | bytes 6291456 | tf_op jit(solution)/shard_map/tij,tif->tjf/dot_general | solution.py:162
  52.9 3.0 %fusion.1 = f32[13,128,128]{2,0,1:T(8,128)S(1)} fusion(f32[48,128,128]{1,0,2:T(8,128)} %copy.23, s32[48]{0:T(128)S(1)} %copy-done.10, pred[48]{0:T(512)(128)(4,1)S(1)} %iota_compare_fusion.29), kind=kOutput, calls=%fused_computation.4 | convolution fusion | flops 122684640 | bytes 3997936 | tf_op jit(solution)/shard_map/st,tjf->sjf/dot_general | solution.py:163
  55.9 0.0 copy-start.7
  55.9 0.1 slice.44
  56.0 0.0 copy-start.5
  56.0 0.6 copy-done.5
  56.7 1.4 %fusion.17 = bf16[1024,128]{1,0:T(8,128)(2,1)} fusion(bf16[384,128]{1,0:T(8,128)(2,1)S(1)} %bitcast.68, s32[384]{0:T(512)S(1)} %add.88), kind=kOutput, calls=%fused_computation.25 | convolution fusion | flops 101187584 | bytes 361984 | tf_op jit(solution)/shard_map/dot_general | solution.py:71
  58.1 5.8 %all-to-all-start.1 = ((bf16[32,32,128]{2,1,0:T(8,128)(2,1)}), bf16[32,32,128]{2,1,0:T(8,128)(2,1)S(1)}, u32[]{:S(2)}, u32[]{:S(2)}) async-start(bf16[32,32,128]{2,1,0:T(8,128)(2,1)} %bitcast.18), calls=%async_computation.1 | async-start | bytes 524288 | tf_op jit(solution)/shard_map/all_to_all | solution.py:74
  63.9 0.1 eq.145
  63.9 0.2 copy.19
  64.2 0.0 copy-start.6
  64.2 1.0 %reduce_sum.9 = f32[8,256]{1,0:T(8,128)S(1)} reduce(f32[32,8,256]{2,1,0:T(8,128)} %all-to-all-done.2, f32[]{:T(128)} %constant.41.clone.1), dimensions={0}, to_apply=%region_0.1 | reduce | flops 63488 | bytes 270340 | tf_op jit(solution)/shard_map/reduce_sum | solution.py:15
  65.2 9.0 %all-to-all-done.1 = bf16[32,32,128]{2,1,0:T(8,128)(2,1)S(1)} async-done(((bf16[32,32,128]{2,1,0:T(8,128)(2,1)}), bf16[32,32,128]{2,1,0:T(8,128)(2,1)S(1)}, u32[]{:S(2)}, u32[]{:S(2)}) %all-to-all-start.1) | async-done | bytes 262176 | tf_op jit(solution)/shard_map/all_to_all | solution.py:74
  74.2 0.7 broadcast_in_dim.115
  74.9 2.6 %all-to-all-start.3 = ((f32[32,8,256]{2,1,0:T(8,128)}), f32[32,8,256]{2,1,0:T(8,128)S(1)}, u32[]{:S(2)}, u32[]{:S(2)}) async-start(f32[32,8,256]{2,1,0:T(8,128)} %broadcast_in_dim.115), calls=%async_computation.3 | async-start | bytes 524288 | tf_op jit(solution)/shard_map/all_to_all | solution.py:16
  77.5 1.4 %convolution_add_fusion.2 = f32[1280,128]{1,0:T(8,128)S(1)} fusion(f32[1280,128]{1,0:T(8,128)S(1)} %bitcast.64, bf16[1280,256]{1,0:T(8,128)(2,1)} %copy-done.3, bf16[128,256]{1,0:T(8,128)(2,1)} %param.17), kind=kOutput, calls=%fused_computation.12 | convolution fusion | flops 84049920 | bytes 2031616 | tf_op jit(solution)/shard_map/nh,fh->nf/dot_general | solution.py:158
  79.0 1.9 %fusion.7 = bf16[1280,128]{1,0:T(8,128)(2,1)} fusion(f32[1280,128]{1,0:T(8,128)S(1)} %convolution_add_fusion.2, bf16[384,128]{1,0:T(8,128)(2,1)S(1)} %bitcast.69, bf16[1024,128]{1,0:T(8,128)(2,1)S(1)} %bitcast.67, s32[384]{0:T(512)S(1)} %eq.145, s32[384]{0:T(512)S(1)} %add.88, pred[384]{0:T(512)(128)(4,1)S(1)} %broadcast_in_dim.101), kind=kOutput, calls=%fused_computation.14 | convolution fusion | flops 227803136 | bytes 1346944 | tf_op jit(solution)/shard_map/dot_general | solution.py:175
  80.8 7.1 %all-to-all-done.3 = f32[32,8,256]{2,1,0:T(8,128)S(1)} async-done(((f32[32,8,256]{2,1,0:T(8,128)}), f32[32,8,256]{2,1,0:T(8,128)S(1)}, u32[]{:S(2)}, u32[]{:S(2)}) %all-to-all-start.3) | async-done | bytes 262176 | tf_op jit(solution)/shard_map/all_to_all | solution.py:16
  87.9 0.7 slice_bitcast_fusion
  (33 shorter events, 0.2 us)
Async XLA Ops:
  0.6 12.0 %copy-start = (bf16[48,128,128]{2,1,0:T(8,128)(2,1)S(1)}, bf16[48,128,128]{2,1,0:T(8,128)(2,1)}, u32[]{:S(2)}) copy-start(bf16[48,128,128]{2,1,0:T(8,128)(2,1)} %param.13) | copy-start | bytes 4718596
  1.6 10.9 %copy-start.9 = (s32[48]{0:T(128)S(1)}, s32[48]{0:T(128)}, u32[]{:S(2)}) copy-start(s32[48]{0:T(128)} %param.14) | copy-start | bytes 580
  1.6 10.9 %copy-start.10 = (s32[48]{0:T(128)S(1)}, s32[48]{0:T(128)}, u32[]{:S(2)}) copy-start(s32[48]{0:T(128)} %param.15) | copy-start | bytes 580
  4.4 8.9 %copy-start.8 = (s32[1,4,32]{2,1,0:T(4,128)S(1)}, s32[1,4,32]{2,1,0:T(4,128)}, u32[]{:S(2)}) copy-start(s32[1,4,32]{2,1,0:T(4,128)} %param.11) | copy-start | bytes 1540
  4.4 9.3 %copy-start.1 = (bf16[1280,128]{1,0:T(8,128)(2,1)S(1)}, bf16[1280,128]{1,0:T(8,128)(2,1)}, u32[]{:S(2)}) copy-start(bf16[1280,128]{1,0:T(8,128)(2,1)} %param.10) | copy-start | bytes 983044
  4.4 9.6 %copy-start.4 = (bf16[128,256]{1,0:T(8,128)(2,1)S(1)}, bf16[128,256]{1,0:T(8,128)(2,1)}, u32[]{:S(2)}) copy-start(bf16[128,256]{1,0:T(8,128)(2,1)} %param.17) | copy-start | bytes 196612
  4.4 17.8 %all-to-all-start = ((bf16[32,32,128]{2,1,0:T(8,128)(2,1)}), bf16[32,32,128]{2,1,0:T(8,128)(2,1)}, u32[]{:S(2)}, u32[]{:S(2)}) async-start(bf16[32,32,128]{2,1,0:T(8,128)(2,1)} %bitcast.5), calls=%async_computation | async-start | bytes 524288 | tf_op jit(solution)/shard_map/all_to_all | solution.py:74
  34.4 3.3 %copy-start.11 = (bf16[1280,256]{1,0:T(8,128)(2,1)S(1)}, bf16[1280,256]{1,0:T(8,128)(2,1)}, u32[]{:S(2)}) copy-start(bf16[1280,256]{1,0:T(8,128)(2,1)} %param.19) | copy-start | bytes 1966084
  34.4 3.3 %copy-start.12 = (bf16[128,256]{1,0:T(8,128)(2,1)S(1)}, bf16[128,256]{1,0:T(8,128)(2,1)}, u32[]{:S(2)}) copy-start(bf16[128,256]{1,0:T(8,128)(2,1)} %param.18) | copy-start | bytes 196612
  37.7 2.5 %copy-start.2 = (bf16[1280,128]{1,0:T(8,128)(2,1)S(1)}, bf16[1280,128]{1,0:T(8,128)(2,1)}, u32[]{:S(2)}) copy-start(bf16[1280,128]{1,0:T(8,128)(2,1)} %param.10) | copy-start | bytes 983044
  39.4 0.9 copy-start.3
  41.3 16.8 %all-to-all-start.2 = ((f32[32,8,256]{2,1,0:T(8,128)}), f32[32,8,256]{2,1,0:T(8,128)}, u32[]{:S(2)}, u32[]{:S(2)}) async-start(f32[32,8,256]{2,1,0:T(8,128)} %convolution_bitcast_fusion), calls=%async_computation.2 | async-start | bytes 524288 | tf_op jit(solution)/shard_map/all_to_all | solution.py:15
  55.9 7.9 %copy-start.7 = (s32[1,8,32]{2,1,0:T(8,128)S(1)}, s32[1,8,32]{2,1,0:T(8,128)}, u32[]{:S(2)}) copy-start(s32[1,8,32]{2,1,0:T(8,128)} %param.12) | copy-start | bytes 3076
  56.0 0.6 copy-start.5
  58.1 16.1 %all-to-all-start.1 = ((bf16[32,32,128]{2,1,0:T(8,128)(2,1)}), bf16[32,32,128]{2,1,0:T(8,128)(2,1)S(1)}, u32[]{:S(2)}, u32[]{:S(2)}) async-start(bf16[32,32,128]{2,1,0:T(8,128)(2,1)} %bitcast.18), calls=%async_computation.1 | async-start | bytes 524288 | tf_op jit(solution)/shard_map/all_to_all | solution.py:74
  64.2 14.8 %copy-start.6 = (bf16[3,128,128]{2,1,0:T(8,128)(2,1)S(1)}, bf16[3,128,128]{2,1,0:T(8,128)(2,1)}, u32[]{:S(2)}) copy-start(bf16[3,128,128]{2,1,0:T(8,128)(2,1)} %copy-done.5) | copy-start | bytes 294916
  74.9 13.0 %all-to-all-start.3 = ((f32[32,8,256]{2,1,0:T(8,128)}), f32[32,8,256]{2,1,0:T(8,128)S(1)}, u32[]{:S(2)}, u32[]{:S(2)}) async-start(f32[32,8,256]{2,1,0:T(8,128)} %broadcast_in_dim.115), calls=%async_computation.3 | async-start | bytes 524288 | tf_op jit(solution)/shard_map/all_to_all | solution.py:16

commit v9 on v7

--- a/solution.py
+++ b/solution.py
@@ -4,11 +4,18 @@
 from jax.sharding import PartitionSpec as P
 
 
-def weight_sum(part_self, part_neigh):
+def weight_sum(part_self, part_neigh, stacked=None):
     axes = ("dom", "grp")
     peers = lax.psum(1, axes)
     rows = part_self.shape[0]
-    stacked = jnp.concatenate([part_self, part_neigh], axis=0)
+    if stacked is None:
+        stacked = jnp.concatenate([part_self, part_neigh], axis=0)
+    if stacked.shape[0] % (8 * peers) == 0:
+        chunks = stacked.reshape(peers, -1, stacked.shape[1])
+        mine = jnp.sum(lax.all_to_all(chunks, axes, 0, 0, tiled=True), axis=0, keepdims=True)
+        total = lax.all_to_all(jnp.broadcast_to(mine, chunks.shape), axes, 0, 0, tiled=True)
+        total = total.reshape(stacked.shape)
+        return total[:rows], total[rows:]
     flat = stacked.reshape(-1)
     pad = (-flat.shape[0]) % peers
     chunks = jnp.pad(flat, (0, pad)).reshape(peers, -1)
@@ -126,8 +133,11 @@
     grad_pre = (cotangent.astype(jnp.float32) * sigm * (1.0 + preact * (1.0 - sigm))).astype(
         jnp.bfloat16
     )
-    part_self = jnp.einsum("nf,nh->fh", features, grad_pre, preferred_element_type=jnp.float32)
-    part_neigh = jnp.einsum("nf,nh->fh", agg, grad_pre, preferred_element_type=jnp.float32)
+    stacked = jnp.einsum(
+        "nf,nh->fh", jnp.concatenate([features, agg], axis=1), grad_pre,
+        preferred_element_type=jnp.float32,
+    )
+    part_self, part_neigh = stacked[:width], stacked[width:]
     grad_own = jnp.einsum("nh,fh->nf", grad_pre, w_self, preferred_element_type=jnp.float32)
     grad_agg = jnp.einsum("nh,fh->nf", grad_pre, w_neigh, preferred_element_type=jnp.float32)
     grad_agg = (grad_agg / degree.reshape(-1)[:, None]).astype(jnp.bfloat16)
@@ -143,7 +153,7 @@
         remote = remote.reshape(n_dom + n_grp, bnd, width)
         ret_dom, ret_grp = exchange(remote[:n_dom], remote[n_dom:])
         returned = jnp.concatenate([ret_dom.reshape(-1, width), ret_grp.reshape(-1, width)])
-    grad_self, grad_neigh = weight_sum(part_self, part_neigh)
+    grad_self, grad_neigh = weight_sum(part_self, part_neigh, stacked)
     grad_total = grad_own + grad_source[:node_count]
     grad_total = grad_total + lax.dot_general(
         pick, returned, (((0,), (0,)), ((), ())), preferred_element_type=jnp.float32

time: 87.3 us -> 89.4 us (1.024)
  local copies, waits for them, and re-layouts: 16.2 us -> 13.8 us
  waiting for transfers between devices: 22.5 us -> 24.6 us
  matrix products: 25.6 us -> 26.9 us
    all_to_all x2, waiting for transfers between devices: 15.5 us -> 17.5 us  [swap(): lax.all_to_all(buf, ('dom', 'grp'), 0, 0, tiled=True)]
    slice x3 -> x1, local copies, waits for them, and re-layouts: 2.02 us -> 0.72 us  [weight_sum(): return (total[:rows], total[rows:])]
    dot_general x1, matrix products: 0.34 us -> 1.44 us  [per_device(): jnp.einsum('nh,fh->nf', grad_pre, w_neigh, preferred_element_type=jnp.flo...]
    dot_general x1, matrix products: 1.39 us -> 0.31 us  [per_device(): jnp.dot(features, w_self, preferred_element_type=jnp.float32)]
    concatenate x1, other arithmetic: 0.03 us -> 1 us  [per_device(): jnp.concatenate([features, recv_dom.reshape(-1, width), recv_grp.reshape(...]
    dot_general x1, matrix products: 0.43 us -> 1.4 us  [swap(): jnp.dot(place, got, preferred_element_type=jnp.float32).astype(table.dtype)]
    all_to_all x1 -> x0, local copies, waits for them, and re-layouts: 0.97 us -> none  [weight_sum(): lax.all_to_all(chunks, axes, 0, 0, tiled=True)]
  transfers between devices with their start and end apart: 4 -> 4, of which waited for: 3 -> 3; matrix products, arithmetic and copies ran while one was open for 22% -> 21% of each run, Pallas kernels for 0% -> 0%
where the time goes in v9:
time: 89.4 us; the launch traced here: 88.8 us
  matrix products  26.9 us (30%)
  waiting for transfers between devices  24.6 us (28%)
  starting transfers between devices  19.1 us (21%)
  local copies, waits for them, and re-layouts  13.8 us (15%)
  other arithmetic  2.85 us (3%)
  between operations  1.6 us (2%)
    all_to_all x2, waiting for transfers between devices, swap(): lax.all_to_all(buf, ('dom', 'grp'), 0, 0, tiled=True)  17.5 us
    all_to_all x2, starting transfers between devices, swap(): lax.all_to_all(buf, ('dom', 'grp'), 0, 0, tiled=True)  13.2 us
    all_to_all x1, waiting for transfers between devices, weight_sum(): lax.all_to_all(jnp.broadcast_to(mine, chunks.shape), axes, 0, 0, tiled=True)  7.09 us
    dot_general x1, matrix products, per_device(): jnp.einsum('tij,tjf->tif', tile_vals, source[tile_src], preferred_element...  4.3 us
    dot_general x1, local copies, waits for them, and re-layouts, per_device(): jnp.einsum('tij,tjf->tif', tile_vals, source[tile_src], preferred_element...  3.58 us
    dot_general x1, local copies, waits for them, and re-layouts, per_device(): jnp.einsum('tij,tif->tjf', tile_vals, picked, preferred_element_type=jnp....  3.58 us
    all_to_all x1, starting transfers between devices, weight_sum(): lax.all_to_all(chunks, axes, 0, 0, tiled=True)  3.31 us
    dot_general x1, matrix products, per_device(): jnp.einsum('bt,tif->bif', to_target, products, precision=lax.Precision.HI...  3.18 us
  transfers between devices with their start and end apart: 4, of which 3 were waited for; matrix products, arithmetic and copies ran while one was open for 21% of the time, Pallas kernels for 0%

profile of v9, /device:TPU:0, one launch (start us, length us, event | category | flops | bytes accessed | tf_op | source)
XLA Modules:
  0.0 88.8 jit_solution(13238996438224821868)
XLA Ops:
  0.6 0.0 copy-start
  0.7 0.1 iota_add_fusion
  0.8 0.1 add.79
  0.8 0.7 pad_add_fusion
  1.5 0.1 eq.74
  1.6 1.5 %fusion.21 = bf16[384,128]{1,0:T(8,128)(2,1)S(1)} fusion(bf16[1280,128]{1,0:T(8,128)(2,1)} %param.10, s32[384]{0:T(512)S(1)} %eq.74), kind=kOutput, calls=%fused_computation.29 | convolution fusion | flops 126369792 | bytes 427520 | tf_op jit(solution)/shard_map/dot_general | solution.py:98
  3.1 0.0 copy-start.11
  3.1 0.0 copy-start.1
  3.1 0.0 copy-start.4
  3.1 1.4 %fusion.17 = bf16[1024,128]{1,0:T(8,128)(2,1)} fusion(bf16[384,128]{1,0:T(8,128)(2,1)S(1)} %fusion.21, s32[384]{0:T(512)S(1)} %add.79), kind=kOutput, calls=%fused_computation.24 | convolution fusion | flops 101187584 | bytes 361984 | tf_op jit(solution)/shard_map/dot_general | solution.py:70
  4.6 7.4 %all-to-all-start = ((bf16[32,32,128]{2,1,0:T(8,128)(2,1)}), bf16[32,32,128]{2,1,0:T(8,128)(2,1)}, u32[]{:S(2)}, u32[]{:S(2)}) async-start(bf16[32,32,128]{2,1,0:T(8,128)(2,1)} %bitcast.4), calls=%async_computation | async-start | bytes 524288 | tf_op jit(solution)/shard_map/all_to_all | solution.py:72
  12.7 0.5 fusion.51
  13.2 0.1 fusion.36
  13.4 0.1 broadcast_in_dim.27
  13.4 0.1 broadcast_in_dim.28
  13.5 0.1 copy.17
  13.7 0.3 fusion.55
  14.0 8.3 %all-to-all-done = bf16[32,32,128]{2,1,0:T(8,128)(2,1)} async-done(((bf16[32,32,128]{2,1,0:T(8,128)(2,1)}), bf16[32,32,128]{2,1,0:T(8,128)(2,1)}, u32[]{:S(2)}, u32[]{:S(2)}) %all-to-all-start) | async-done | bytes 262176 | tf_op jit(solution)/shard_map/all_to_all | solution.py:72
  22.3 1.4 %fusion.23 = bf16[384,128]{1,0:T(8,128)(2,1)S(1)} fusion(bf16[384,128]{1,0:T(8,128)(2,1)} %copy-done.11, bf16[1024,128]{1,0:T(8,128)(2,1)} %bitcast.5, s32[384]{0:T(512)S(1)} %add.79, pred[384]{0:T(512)(128)(4,1)S(1)} %broadcast_in_dim.28), kind=kOutput, calls=%fused_computation.31 | convolution fusion | flops 101154816 | bytes 460672 | tf_op jit(solution)/shard_map/dot_general | solution.py:73
  23.7 1.0 %pad_maximum_fusion = bf16[1664,128]{1,0:T(8,128)(2,1)S(1)} fusion(bf16[384,128]{1,0:T(8,128)(2,1)S(1)} %fusion.23, bf16[1280,128]{1,0:T(8,128)(2,1)} %param.10), kind=kLoop, calls=%fused_computation.41 | loop fusion | flops 851968 | bytes 851968 | tf_op jit(solution)/shard_map/concatenate | solution.py:107
  24.8 2.0 %gather_fusion = bf16[48,128,128]{2,1,0:T(8,128)(2,1)} fusion(bf16[13,128,128]{2,1,0:T(8,128)(2,1)S(1)} %bitcast.59, s32[1024]{0:T(1024)S(1)} %pad_clamp_fusion.1), kind=kCustom, calls=%fused_computation | custom fusion | bytes 3145920 | tf_op jit(solution)/shard_map/gather | solution.py:121
  26.7 4.3 %fusion.56 = f32[48,128,128]{2,1,0:T(8,128)} fusion(bf16[48,128,128]{2,1,0:T(8,128)(2,1)} %gather_fusion, bf16[48,128,128]{2,1,0:T(8,128)(2,1)S(1)} %copy-done), kind=kOutput, calls=%fused_computation.75 | convolution fusion | flops 201326592 | bytes 6291456 | tf_op jit(solution)/shard_map/tij,tjf->tif/dot_general | solution.py:120
  31.0 3.6 %copy.21 = f32[48,128,128]{1,0,2:T(8,128)} copy(f32[48,128,128]{2,1,0:T(8,128)} %fusion.56) | data formatting | bytes 6291456 | tf_op jit(solution)/shard_map/tij,tjf->tif/dot_general | solution.py:120
  34.6 3.2 %fusion.14 = bf16[10,128,128]{2,0,1:T(8,128)(2,1)S(1)} fusion(f32[48,128,128]{1,0,2:T(8,128)} %copy.21, f32[10,128]{0,1:T(8,128)S(1)} %copy.17, s32[48]{0:T(128)S(1)} %copy-done.7, pred[48]{0:T(512)(128)(4,1)S(1)} %iota_compare_fusion.27), kind=kOutput, calls=%fused_computation.23 | convolution fusion | flops 94700480 | bytes 3478768 | tf_op jit(solution)/shard_map/bt,tif->bif/dot_general | solution.py:123
  37.8 0.1 copy.18
  37.9 1.6 %multiply_convert_fusion = (bf16[1280,256]{1,0:T(8,128)(2,1)S(1)}, bf16[1280,256]{1,0:T(8,128)(2,1)}) fusion(bf16[1280,256]{1,0:T(8,128)(2,1)S(1)} %copy-done.9, f32[1280,256]{1,0:T(8,128)S(1)} %fusion.55, bf16[1280,128]{1,0:T(8,128)(2,1)S(1)} %bitcast.63, bf16[128,256]{1,0:T(8,128)(2,1)S(1)} %copy-done.10), kind=kOutput, calls=%fused_computation.20 | convolution fusion | flops 88145920 | bytes 3670016 | tf_op jit(solution)/shard_map/dot_general | solution.py:128
  39.6 0.9 copy-done.3
  40.4 1.1 %convolution_bitcast_fusion = f32[32,8,256]{2,1,0:T(8,128)} fusion(bf16[1280,256]{1,0:T(8,128)(2,1)S(1)} %get-tuple-element.4, bf16[1280,128]{1,0:T(8,128)(2,1)S(1)} %bitcast.64, bf16[1280,128]{1,0:T(8,128)(2,1)S(1)} %copy-done.2), kind=kOutput, calls=%fused_computation.26 | convolution fusion | flops 169082880 | bytes 1572864 | tf_op jit(solution)/shard_map/nf,nh->fh/dot_general | solution.py:136
  41.5 3.3 %all-to-all-start.2 = ((f32[32,8,256]{2,1,0:T(8,128)}), f32[32,8,256]{2,1,0:T(8,128)}, u32[]{:S(2)}, u32[]{:S(2)}) async-start(f32[32,8,256]{2,1,0:T(8,128)} %convolution_bitcast_fusion), calls=%async_computation.2 | async-start | bytes 524288 | tf_op jit(solution)/shard_map/all_to_all | solution.py:15
  44.8 1.4 %fusion.4 = bf16[1280,128]{1,0:T(8,128)(2,1)S(1)} fusion(bf16[1280,256]{1,0:T(8,128)(2,1)} %copy-done.3, bf16[128,256]{1,0:T(8,128)(2,1)S(1)} %copy-done.10, f32[1280]{0:T(1024)S(1)} %bitcast.69), kind=kOutput, calls=%fused_computation.10 | convolution fusion | flops 84213760 | bytes 1053696 | tf_op jit(solution)/shard_map/nh,fh->nf/dot_general | solution.py:142
  46.2 0.8 gather_fusion.1
  47.1 2.3 %fusion.57 = f32[48,128,128]{2,1,0:T(8,128)} fusion(bf16[48,128,128]{2,1,0:T(8,128)(2,1)S(1)} %gather_fusion.1, bf16[48,128,128]{2,1,0:T(8,128)(2,1)S(1)} %copy-done), kind=kOutput, calls=%fused_computation.76 | convolution fusion | flops 201326592 | bytes 6291456 | tf_op jit(solution)/shard_map/tij,tif->tjf/dot_general | solution.py:145
  49.4 3.6 %copy.23 = f32[48,128,128]{1,0,2:T(8,128)} copy(f32[48,128,128]{2,1,0:T(8,128)} %fusion.57) | data formatting | bytes 6291456 | tf_op jit(solution)/shard_map/tij,tif->tjf/dot_general | solution.py:145
  53.0 3.0 %fusion = f32[13,128,128]{2,0,1:T(8,128)S(1)} fusion(f32[48,128,128]{1,0,2:T(8,128)} %copy.23, s32[48]{0:T(128)S(1)} %copy-done.8, pred[48]{0:T(512)(128)(4,1)S(1)} %iota_compare_fusion.27), kind=kOutput, calls=%fused_computation.2 | convolution fusion | flops 122684640 | bytes 3997936 | tf_op jit(solution)/shard_map/st,tjf->sjf/dot_general | solution.py:146
  56.1 0.1 slice.44
  56.2 0.6 copy-done.5
  56.8 1.4 %fusion.18 = bf16[1024,128]{1,0:T(8,128)(2,1)} fusion(bf16[384,128]{1,0:T(8,128)(2,1)S(1)} %bitcast.66, s32[384]{0:T(512)S(1)} %add.79), kind=kOutput, calls=%fused_computation.25 | convolution fusion | flops 101187584 | bytes 361984 | tf_op jit(solution)/shard_map/dot_general | solution.py:70
  58.2 5.8 %all-to-all-start.1 = ((bf16[32,32,128]{2,1,0:T(8,128)(2,1)}), bf16[32,32,128]{2,1,0:T(8,128)(2,1)S(1)}, u32[]{:S(2)}, u32[]{:S(2)}) async-start(bf16[32,32,128]{2,1,0:T(8,128)(2,1)} %bitcast.17), calls=%async_computation.1 | async-start | bytes 524288 | tf_op jit(solution)/shard_map/all_to_all | solution.py:72
  64.0 0.2 copy.19
  64.2 0.0 copy-start.6
  64.2 1.0 %reduce_sum.9 = f32[8,256]{1,0:T(8,128)S(1)} reduce(f32[32,8,256]{2,1,0:T(8,128)} %all-to-all-done.2, f32[]{:T(128)} %constant.30.clone.1), dimensions={0}, to_apply=%region_0.1 | reduce | flops 63488 | bytes 270340 | tf_op jit(solution)/shard_map/reduce_sum | solution.py:15
  65.2 9.1 %all-to-all-done.1 = bf16[32,32,128]{2,1,0:T(8,128)(2,1)S(1)} async-done(((bf16[32,32,128]{2,1,0:T(8,128)(2,1)}), bf16[32,32,128]{2,1,0:T(8,128)(2,1)S(1)}, u32[]{:S(2)}, u32[]{:S(2)}) %all-to-all-start.1) | async-done | bytes 262176 | tf_op jit(solution)/shard_map/all_to_all | solution.py:72
  74.4 0.7 broadcast_in_dim.58
  75.1 2.6 %all-to-all-start.3 = ((f32[32,8,256]{2,1,0:T(8,128)}), f32[32,8,256]{2,1,0:T(8,128)S(1)}, u32[]{:S(2)}, u32[]{:S(2)}) async-start(f32[32,8,256]{2,1,0:T(8,128)} %broadcast_in_dim.58), calls=%async_computation.3 | async-start | bytes 524288 | tf_op jit(solution)/shard_map/all_to_all | solution.py:16
  77.7 1.4 %convolution_add_fusion.2 = f32[1280,128]{1,0:T(8,128)S(1)} fusion(f32[1280,128]{1,0:T(8,128)S(1)} %bitcast.62, bf16[1280,256]{1,0:T(8,128)(2,1)} %copy-done.3, bf16[128,256]{1,0:T(8,128)(2,1)} %param.17), kind=kOutput, calls=%fused_computation.9 | convolution fusion | flops 84049920 | bytes 2031616 | tf_op jit(solution)/shard_map/nh,fh->nf/dot_general | solution.py:141
  79.1 1.9 %fusion.5 = bf16[1280,128]{1,0:T(8,128)(2,1)} fusion(f32[1280,128]{1,0:T(8,128)S(1)} %convolution_add_fusion.2, bf16[384,128]{1,0:T(8,128)(2,1)S(1)} %bitcast.67, bf16[1024,128]{1,0:T(8,128)(2,1)S(1)} %bitcast.65, s32[384]{0:T(512)S(1)} %eq.74, s32[384]{0:T(512)S(1)} %add.79, pred[384]{0:T(512)(128)(4,1)S(1)} %broadcast_in_dim.28), kind=kOutput, calls=%fused_computation.11 | convolution fusion | flops 227803136 | bytes 1346944 | tf_op jit(solution)/shard_map/dot_general | solution.py:158
  81.0 7.1 %all-to-all-done.3 = f32[32,8,256]{2,1,0:T(8,128)S(1)} async-done(((f32[32,8,256]{2,1,0:T(8,128)}), f32[32,8,256]{2,1,0:T(8,128)S(1)}, u32[]{:S(2)}, u32[]{:S(2)}) %all-to-all-start.3) | async-done | bytes 262176 | tf_op jit(solution)/shard_map/all_to_all | solution.py:16
  88.0 0.7 slice_bitcast_fusion
  (26 shorter events, 0.1 us)
Async XLA Ops:
  0.6 12.1 %copy-start = (bf16[48,128,128]{2,1,0:T(8,128)(2,1)S(1)}, bf16[48,128,128]{2,1,0:T(8,128)(2,1)}, u32[]{:S(2)}) copy-start(bf16[48,128,128]{2,1,0:T(8,128)(2,1)} %param.13) | copy-start | bytes 4718596
  0.6 12.0 %copy-start.8 = (s32[48]{0:T(128)S(1)}, s32[48]{0:T(128)}, u32[]{:S(2)}) copy-start(s32[48]{0:T(128)} %param.15) | copy-start | bytes 580
  0.7 12.0 %copy-start.7 = (s32[48]{0:T(128)S(1)}, s32[48]{0:T(128)}, u32[]{:S(2)}) copy-start(s32[48]{0:T(128)} %param.14) | copy-start | bytes 580
  3.1 10.2 %copy-start.11 = (bf16[384,128]{1,0:T(8,128)(2,1)}, bf16[384,128]{1,0:T(8,128)(2,1)S(1)}, u32[]{:S(2)}) copy-start(bf16[384,128]{1,0:T(8,128)(2,1)S(1)} %fusion.21) | copy-start | bytes 294916
  3.1 10.6 %copy-start.1 = (bf16[1280,128]{1,0:T(8,128)(2,1)S(1)}, bf16[1280,128]{1,0:T(8,128)(2,1)}, u32[]{:S(2)}) copy-start(bf16[1280,128]{1,0:T(8,128)(2,1)} %param.10) | copy-start | bytes 983044
  3.1 10.6 %copy-start.4 = (bf16[128,256]{1,0:T(8,128)(2,1)S(1)}, bf16[128,256]{1,0:T(8,128)(2,1)}, u32[]{:S(2)}) copy-start(bf16[128,256]{1,0:T(8,128)(2,1)} %param.17) | copy-start | bytes 196612
  4.6 17.8 %all-to-all-start = ((bf16[32,32,128]{2,1,0:T(8,128)(2,1)}), bf16[32,32,128]{2,1,0:T(8,128)(2,1)}, u32[]{:S(2)}, u32[]{:S(2)}) async-start(bf16[32,32,128]{2,1,0:T(8,128)(2,1)} %bitcast.4), calls=%async_computation | async-start | bytes 524288 | tf_op jit(solution)/shard_map/all_to_all | solution.py:72
  34.6 3.3 %copy-start.9 = (bf16[1280,256]{1,0:T(8,128)(2,1)S(1)}, bf16[1280,256]{1,0:T(8,128)(2,1)}, u32[]{:S(2)}) copy-start(bf16[1280,256]{1,0:T(8,128)(2,1)} %param.19) | copy-start | bytes 1966084
  34.6 3.3 %copy-start.10 = (bf16[128,256]{1,0:T(8,128)(2,1)S(1)}, bf16[128,256]{1,0:T(8,128)(2,1)}, u32[]{:S(2)}) copy-start(bf16[128,256]{1,0:T(8,128)(2,1)} %param.18) | copy-start | bytes 196612
  37.9 2.5 %copy-start.2 = (bf16[1280,128]{1,0:T(8,128)(2,1)S(1)}, bf16[1280,128]{1,0:T(8,128)(2,1)}, u32[]{:S(2)}) copy-start(bf16[1280,128]{1,0:T(8,128)(2,1)} %param.10) | copy-start | bytes 983044
  39.6 0.9 copy-start.3
  41.5 16.7 %all-to-all-start.2 = ((f32[32,8,256]{2,1,0:T(8,128)}), f32[32,8,256]{2,1,0:T(8,128)}, u32[]{:S(2)}, u32[]{:S(2)}) async-start(f32[32,8,256]{2,1,0:T(8,128)} %convolution_bitcast_fusion), calls=%async_computation.2 | async-start | bytes 524288 | tf_op jit(solution)/shard_map/all_to_all | solution.py:15
  56.2 0.6 copy-start.5
  58.2 16.1 %all-to-all-start.1 = ((bf16[32,32,128]{2,1,0:T(8,128)(2,1)}), bf16[32,32,128]{2,1,0:T(8,128)(2,1)S(1)}, u32[]{:S(2)}, u32[]{:S(2)}) async-start(bf16[32,32,128]{2,1,0:T(8,128)(2,1)} %bitcast.17), calls=%async_computation.1 | async-start | bytes 524288 | tf_op jit(solution)/shard_map/all_to_all | solution.py:72
  64.2 14.9 %copy-start.6 = (bf16[3,128,128]{2,1,0:T(8,128)(2,1)S(1)}, bf16[3,128,128]{2,1,0:T(8,128)(2,1)}, u32[]{:S(2)}) copy-start(bf16[3,128,128]{2,1,0:T(8,128)(2,1)} %copy-done.5) | copy-start | bytes 294916
  75.1 13.0 %all-to-all-start.3 = ((f32[32,8,256]{2,1,0:T(8,128)}), f32[32,8,256]{2,1,0:T(8,128)S(1)}, u32[]{:S(2)}, u32[]{:S(2)}) async-start(f32[32,8,256]{2,1,0:T(8,128)} %broadcast_in_dim.58), calls=%async_computation.3 | async-start | bytes 524288 | tf_op jit(solution)/shard_map/all_to_all | solution.py:16

commit v10 on v7

--- a/solution.py
+++ b/solution.py
@@ -35,6 +35,14 @@
     from_dom = lax.dynamic_update_slice_in_dim(from_dom, own_dom, a, axis=0)
     from_grp = lax.dynamic_index_in_dim(got, a, axis=0, keepdims=False)
     return from_dom, from_grp
+
+
+def segment_matmul(hot, values):
+    hi = values.astype(jnp.bfloat16)
+    lo = (values - hi.astype(jnp.float32)).astype(jnp.bfloat16)
+    hot = hot.astype(jnp.bfloat16)
+    first = jnp.einsum("bt,t...->b...", hot, hi, preferred_element_type=jnp.float32)
+    return first + jnp.einsum("bt,t...->b...", hot, lo, preferred_element_type=jnp.float32)
 
 
 def one_hot_rows(index, count):
@@ -113,7 +121,7 @@
     products = jnp.einsum(
         "tij,tjf->tif", tile_vals, source[tile_src], preferred_element_type=jnp.float32
     )
-    summed = jnp.einsum("bt,tif->bif", to_target, products, precision=lax.Precision.HIGHEST)
+    summed = segment_matmul(to_target, products)
     unit_column = jnp.ones((tile_size,), jnp.bfloat16)
     row_sums = jnp.einsum("tij,j->ti", tile_vals, unit_column, preferred_element_type=jnp.float32)
     degree = jnp.dot(to_target, row_sums, precision=lax.Precision.HIGHEST)
@@ -133,9 +141,7 @@
     grad_agg = (grad_agg / degree.reshape(-1)[:, None]).astype(jnp.bfloat16)
     picked = grad_agg.reshape(block_count, tile_size, width)[tile_tgt]
     backward = jnp.einsum("tij,tif->tjf", tile_vals, picked, preferred_element_type=jnp.float32)
-    grad_source = jnp.einsum(
-        "st,tjf->sjf", to_source, backward, precision=lax.Precision.HIGHEST
-    ).reshape(-1, width)
+    grad_source = segment_matmul(to_source, backward).reshape(-1, width)
     remote = grad_source[node_count:].astype(jnp.bfloat16)
     if table_bytes <= PLACE_LIMIT:
         returned = swap(remote, place, keep)

time: 87.3 us -> 88.3 us (1.011)
  local copies, waits for them, and re-layouts: 16.2 us -> 20.1 us
  matrix products: 25.6 us -> 22.5 us
    convert_element_type x0 -> x4, local copies, waits for them, and re-layouts: none -> 8.75 us  [the longest x2 4.88 us: segment_matmul(): hi = values.astype(jnp.bfloat16)]
    dot_general x2 -> x0, local copies, waits for them, and re-layouts: 7.18 us -> none  [the longest x1 3.59 us: per_device(): jnp.einsum('tij,tif->tjf', tile_vals, picked, preferred_element_type=jnp....]
    dot_general x2 -> x4, matrix products: 6.29 us -> 3.61 us  [the longest x2 2.9 us: segment_matmul(): jnp.einsum('bt,t...->b...', hot, hi, preferred_element_type=jnp.float32)]
    unnamed x24 -> x48, local copies, waits for them, and re-layouts: 0.69 us -> 3.03 us
  transfers between devices with their start and end apart: 4 -> 4, of which waited for: 3 -> 3; matrix products, arithmetic and copies ran while one was open for 22% -> 23% of each run, Pallas kernels for 0% -> 0%
where the time goes in v10:
time: 88.3 us; the launch traced here: 87.7 us
  matrix products  22.5 us (25%)
  waiting for transfers between devices  22.5 us (25%)
  local copies, waits for them, and re-layouts  20.1 us (23%)
  starting transfers between devices  18.9 us (21%)
  other arithmetic  2.02 us (2%)
  between operations  1.7 us (2%)
    all_to_all x2, waiting for transfers between devices, swap(): lax.all_to_all(buf, ('dom', 'grp'), 0, 0, tiled=True)  15.5 us
    all_to_all x2, starting transfers between devices, swap(): lax.all_to_all(buf, ('dom', 'grp'), 0, 0, tiled=True)  13.1 us
    all_to_all x1, waiting for transfers between devices, weight_sum(): total = lax.all_to_all(spread, axes, 0, 0, tiled=True).reshape(-1)  7.02 us
    convert_element_type x2, local copies, waits for them, and re-layouts, segment_matmul(): hi = values.astype(jnp.bfloat16)  4.88 us
    convert_element_type x2, local copies, waits for them, and re-layouts, segment_matmul(): lo = (values - hi.astype(jnp.float32)).astype(jnp.bfloat16)  3.86 us
    dot_general x1, matrix products, per_device(): jnp.einsum('tij,tjf->tif', tile_vals, source[tile_src], preferred_element...  3.8 us
    all_to_all x1, starting transfers between devices, weight_sum(): lax.all_to_all(chunks, axes, 0, 0, tiled=True)  3.3 us
    unnamed x48, local copies, waits for them, and re-layouts  3.03 us
  transfers between devices with their start and end apart: 4, of which 3 were waited for; matrix products, arithmetic and copies ran while one was open for 23% of the time, Pallas kernels for 0%

profile of v10, /device:TPU:0, one launch (start us, length us, event | category | flops | bytes accessed | tf_op | source)
XLA Modules:
  0.0 87.7 jit_solution(6642498548139910577)
XLA Ops:
  0.8 0.7 pad_add_fusion
  1.6 1.5 %fusion.15 = bf16[384,128]{1,0:T(8,128)(2,1)S(1)} fusion(bf16[1280,128]{1,0:T(8,128)(2,1)} %param.10, s32[384]{0:T(512)S(1)} %eq.74), kind=kOutput, calls=%fused_computation.32 | convolution fusion | flops 126369792 | bytes 427520 | tf_op jit(solution)/shard_map/dot_general | solution.py:99
  3.1 1.4 %fusion.11 = bf16[1024,128]{1,0:T(8,128)(2,1)} fusion(bf16[384,128]{1,0:T(8,128)(2,1)S(1)} %fusion.15, s32[384]{0:T(512)S(1)} %add.85), kind=kOutput, calls=%fused_computation.28 | convolution fusion | flops 101187584 | bytes 361984 | tf_op jit(solution)/shard_map/dot_general | solution.py:71
  4.6 7.3 %all-to-all-start = ((bf16[32,32,128]{2,1,0:T(8,128)(2,1)}), bf16[32,32,128]{2,1,0:T(8,128)(2,1)S(1)}, u32[]{:S(2)}, u32[]{:S(2)}) async-start(bf16[32,32,128]{2,1,0:T(8,128)(2,1)} %bitcast.4), calls=%async_computation | async-start | bytes 524288 | tf_op jit(solution)/shard_map/all_to_all | solution.py:73
  12.6 0.5 fusion.50
  13.1 0.1 fusion.27
  13.3 0.1 broadcast_in_dim.28
  13.4 0.1 copy.34
  13.6 1.4 %fusion.53 = f32[1280,256]{1,0:T(8,128)} fusion(bf16[1280,128]{1,0:T(8,128)(2,1)S(1)} %copy-done.5, bf16[128,256]{1,0:T(8,128)(2,1)S(1)} %copy-done.8), kind=kOutput, calls=%fused_computation.83 | convolution fusion | flops 83886080 | bytes 1703936 | tf_op jit(solution)/shard_map/dot_general | solution.py:129
  14.9 7.3 %all-to-all-done = bf16[32,32,128]{2,1,0:T(8,128)(2,1)S(1)} async-done(((bf16[32,32,128]{2,1,0:T(8,128)(2,1)}), bf16[32,32,128]{2,1,0:T(8,128)(2,1)S(1)}, u32[]{:S(2)}, u32[]{:S(2)}) %all-to-all-start) | async-done | bytes 262176 | tf_op jit(solution)/shard_map/all_to_all | solution.py:73
  22.2 0.4 fusion.17
  22.7 2.0 %gather_fusion = bf16[48,128,128]{2,1,0:T(8,128)(2,1)} fusion(bf16[13,128,128]{2,1,0:T(8,128)(2,1)S(1)} %bitcast.66, s32[1024]{0:T(1024)S(1)} %pad_clamp_fusion.1), kind=kCustom, calls=%fused_computation | custom fusion | bytes 3145920 | tf_op jit(solution)/shard_map/gather | solution.py:122
  24.7 3.8 %fusion.1 = (bf16[48,128,128]{1,2,0:T(8,128)(2,1)S(1)}, bf16[48,128,128]{1,2,0:T(8,128)(2,1)}) fusion(bf16[48,128,128]{2,1,0:T(8,128)(2,1)} %gather_fusion, bf16[48,128,128]{2,1,0:T(8,128)(2,1)S(1)} %copy-done), kind=kOutput, calls=%fused_computation.7 | convolution fusion | flops 204472320 | bytes 6291456 | tf_op jit(solution)/shard_map/tij,tjf->tif/dot_general | solution.py:121
  28.5 1.8 %copy.33 = bf16[48,128,128]{2,0,1:T(8,128)(2,1)} copy(bf16[48,128,128]{1,2,0:T(8,128)(2,1)S(1)} %get-tuple-element.8) | data formatting | bytes 3145728 | tf_op jit(solution)/shard_map/convert_element_type | solution.py:42
  30.3 2.0 %copy.32 = bf16[48,128,128]{2,0,1:T(8,128)(2,1)S(1)} copy(bf16[48,128,128]{1,2,0:T(8,128)(2,1)} %get-tuple-element.9) | data formatting | bytes 3145728 | tf_op jit(solution)/shard_map/convert_element_type | solution.py:41
  32.4 1.1 %fusion.32 = f32[10,128,128]{2,0,1:T(8,128)S(1)} fusion(bf16[48,128,128]{2,0,1:T(8,128)(2,1)S(1)} %copy.32, s32[48]{0:T(128)} %param.14, pred[48]{0:T(512)(128)(4,1)S(1)} %iota_compare_fusion.27), kind=kOutput, calls=%fused_computation.58 | convolution fusion | flops 15730560 | bytes 2228464 | tf_op jit(solution)/shard_map/bt,t...->b.../dot_general | solution.py:44
  33.5 0.3 copy-done.6
  33.8 0.4 fusion.10
  34.2 0.1 copy.35
  34.3 0.8 copy-done.7
  35.1 0.2 copy-done.21
  35.3 1.6 %multiply_convert_fusion = (bf16[1280,256]{1,0:T(8,128)(2,1)S(1)}, bf16[1280,256]{1,0:T(8,128)(2,1)}) fusion(bf16[1280,256]{1,0:T(8,128)(2,1)S(1)} %copy-done.21, f32[1280,256]{1,0:T(8,128)S(1)} %copy-done.7, bf16[1280,128]{1,0:T(8,128)(2,1)S(1)} %bitcast.70, bf16[128,256]{1,0:T(8,128)(2,1)S(1)} %copy-done.22), kind=kOutput, calls=%fused_computation.24 | convolution fusion | flops 88145920 | bytes 3670016 | tf_op jit(solution)/shard_map/dot_general | solution.py:129
  36.9 0.3 fusion.54
  37.2 0.3 convolution_bitcast_fusion
  37.6 1.0 %all_to_all.21 = f32[32,1,2048]{2,1,0:T(1,128)} reshape(f32[256,256]{1,0:T(8,128)S(1)} %pad_maximum_fusion.1) | data formatting | bytes 524288 | tf_op jit(solution)/shard_map/all_to_all | solution.py:15
  38.5 3.3 %all-to-all-start.2 = ((f32[32,1,2048]{2,1,0:T(1,128)}), f32[32,1,2048]{2,1,0:T(1,128)}, u32[]{:S(2)}, u32[]{:S(2)}) async-start(f32[32,1,2048]{2,1,0:T(1,128)} %all_to_all.21), calls=%async_computation.2 | async-start | bytes 524288 | tf_op jit(solution)/shard_map/all_to_all | solution.py:15
  41.9 0.3 fusion.2
  42.2 0.8 gather_fusion.1
  43.1 2.4 %fusion = (bf16[48,128,128]{1,2,0:T(8,128)(2,1)}, bf16[48,128,128]{1,2,0:T(8,128)(2,1)}) fusion(bf16[48,128,128]{2,1,0:T(8,128)(2,1)S(1)} %gather_fusion.1, bf16[48,128,128]{2,1,0:T(8,128)(2,1)S(1)} %copy-done), kind=kOutput, calls=%fused_computation.4 | convolution fusion | flops 204472320 | bytes 6291456 | tf_op jit(solution)/shard_map/tij,tif->tjf/dot_general | solution.py:143
  45.5 2.0 %copy.38 = bf16[48,128,128]{2,0,1:T(8,128)(2,1)S(1)} copy(bf16[48,128,128]{1,2,0:T(8,128)(2,1)} %get-tuple-element.6) | data formatting | bytes 3145728 | tf_op jit(solution)/shard_map/convert_element_type | solution.py:42
  47.5 2.9 %copy.37 = bf16[48,128,128]{2,0,1:T(8,128)(2,1)} copy(bf16[48,128,128]{1,2,0:T(8,128)(2,1)} %get-tuple-element.7) | data formatting | bytes 3145728 | tf_op jit(solution)/shard_map/convert_element_type | solution.py:41
  50.4 1.8 %fusion.36 = f32[13,128,128]{2,0,1:T(8,128)S(1)} fusion(bf16[48,128,128]{2,0,1:T(8,128)(2,1)} %copy.37, s32[48]{0:T(128)S(1)} %copy-done.14, pred[48]{0:T(512)(128)(4,1)S(1)} %iota_compare_fusion.27), kind=kOutput, calls=%fused_computation.60 | convolution fusion | flops 20449728 | bytes 2425072 | tf_op jit(solution)/shard_map/bt,t...->b.../dot_general | solution.py:44
  52.2 0.3 convolution_add_fusion.3
  52.5 1.0 %copy-done.3 = f32[13,128,128]{2,0,1:T(8,128)} copy-done((f32[13,128,128]{2,0,1:T(8,128)}, f32[13,128,128]{2,0,1:T(8,128)S(1)}, u32[]{:S(2)}) %copy-start.3) | copy-done | bytes 851992
  53.6 0.6 copy-done.9
  54.3 1.4 %fusion.12 = bf16[1024,128]{1,0:T(8,128)(2,1)} fusion(bf16[384,128]{1,0:T(8,128)(2,1)S(1)} %bitcast.75, s32[384]{0:T(512)S(1)} %copy-done.16), kind=kOutput, calls=%fused_computation.29 | convolution fusion | flops 101187584 | bytes 361984 | tf_op jit(solution)/shard_map/dot_general | solution.py:71
  55.7 5.8 %all-to-all-start.1 = ((bf16[32,32,128]{2,1,0:T(8,128)(2,1)}), bf16[32,32,128]{2,1,0:T(8,128)(2,1)S(1)}, u32[]{:S(2)}, u32[]{:S(2)}) async-start(bf16[32,32,128]{2,1,0:T(8,128)(2,1)} %bitcast.74), calls=%async_computation.1 | async-start | bytes 524288 | tf_op jit(solution)/shard_map/all_to_all | solution.py:73
  61.5 1.1 %copy.39 = f32[10,128,128]{2,1,0:T(8,128)} copy(f32[10,128,128]{2,0,1:T(8,128)S(1)} %bitcast.68) | data formatting | bytes 1310720 | tf_op jit(solution)/shard_map/slice | solution.py:153
  62.5 1.1 %reduce_sum.9 = f32[2048]{0:T(1024)S(1)} reduce(f32[32,1,2048]{2,1,0:T(1,128)} %all-to-all-done.2, f32[]{:T(128)} %constant.31.clone.1), dimensions={0,1}, to_apply=%region_0.1 | reduce | flops 63488 | bytes 270340 | tf_op jit(solution)/shard_map/reduce_sum | solution.py:15
  63.7 8.2 %all-to-all-done.1 = bf16[32,32,128]{2,1,0:T(8,128)(2,1)S(1)} async-done(((bf16[32,32,128]{2,1,0:T(8,128)(2,1)}), bf16[32,32,128]{2,1,0:T(8,128)(2,1)S(1)}, u32[]{:S(2)}, u32[]{:S(2)}) %all-to-all-start.1) | async-done | bytes 262176 | tf_op jit(solution)/shard_map/all_to_all | solution.py:73
  71.8 0.8 broadcast_in_dim.58
  72.7 2.6 %all-to-all-start.3 = ((f32[32,1,2048]{2,1,0:T(1,128)}), f32[32,1,2048]{2,1,0:T(1,128)S(1)}, u32[]{:S(2)}, u32[]{:S(2)}) async-start(f32[32,1,2048]{2,1,0:T(1,128)} %broadcast_in_dim.58), calls=%async_computation.3 | async-start | bytes 524288 | tf_op jit(solution)/shard_map/all_to_all | solution.py:17
  75.3 1.5 %convolution_add_fusion.2 = f32[1280,128]{1,0:T(8,128)S(1)} fusion(f32[1280,128]{1,0:T(8,128)} %bitcast.69, bf16[1280,256]{1,0:T(8,128)(2,1)S(1)} %copy-done.2, bf16[128,256]{1,0:T(8,128)(2,1)} %param.17), kind=kOutput, calls=%fused_computation.11 | convolution fusion | flops 84049920 | bytes 2031616 | tf_op jit(solution)/shard_map/nh,fh->nf/dot_general | solution.py:139
  76.8 1.9 %fusion.3 = bf16[1280,128]{1,0:T(8,128)(2,1)} fusion(f32[1280,128]{1,0:T(8,128)S(1)} %convolution_add_fusion.2, bf16[384,128]{1,0:T(8,128)(2,1)S(1)} %bitcast.76, bf16[1024,128]{1,0:T(8,128)(2,1)S(1)} %bitcast.73, s32[384]{0:T(512)S(1)} %copy-done.18, s32[384]{0:T(512)S(1)} %copy-done.16, pred[384]{0:T(512)(128)(4,1)S(1)} %copy-done.20), kind=kOutput, calls=%fused_computation.13 | convolution fusion | flops 227803136 | bytes 1346944 | tf_op jit(solution)/shard_map/dot_general | solution.py:154
  78.6 7.0 %all-to-all-done.3 = f32[32,1,2048]{2,1,0:T(1,128)S(1)} async-done(((f32[32,1,2048]{2,1,0:T(1,128)}), f32[32,1,2048]{2,1,0:T(1,128)S(1)}, u32[]{:S(2)}, u32[]{:S(2)}) %all-to-all-start.3) | async-done | bytes 262176 | tf_op jit(solution)/shard_map/all_to_all | solution.py:17
  85.6 0.7 slice_reduce_fusion
  86.3 0.7 slice.34
  87.0 0.7 slice.32
  (59 shorter events, 0.6 us)
Async XLA Ops:
  0.6 11.9 %copy-start = (bf16[48,128,128]{2,1,0:T(8,128)(2,1)S(1)}, bf16[48,128,128]{2,1,0:T(8,128)(2,1)}, u32[]{:S(2)}) copy-start(bf16[48,128,128]{2,1,0:T(8,128)(2,1)} %param.13) | copy-start | bytes 4718596
  0.6 11.9 %copy-start.13 = (s32[48]{0:T(128)S(1)}, s32[48]{0:T(128)}, u32[]{:S(2)}) copy-start(s32[48]{0:T(128)} %param.15) | copy-start | bytes 580
  0.7 11.9 %copy-start.11 = (s32[48]{0:T(128)S(1)}, s32[48]{0:T(128)}, u32[]{:S(2)}) copy-start(s32[48]{0:T(128)} %param.14) | copy-start | bytes 580
  0.8 21.4 %copy-start.15 = (s32[384]{0:T(512)}, s32[384]{0:T(512)S(1)}, u32[]{:S(2)}) copy-start(s32[384]{0:T(512)S(1)} %add.85) | copy-start | bytes 4612
  1.6 2.9 %copy-start.17 = (s32[384]{0:T(512)}, s32[384]{0:T(512)S(1)}, u32[]{:S(2)}) copy-start(s32[384]{0:T(512)S(1)} %eq.74) | copy-start | bytes 4612
  3.1 10.4 %copy-start.5 = (bf16[1280,128]{1,0:T(8,128)(2,1)S(1)}, bf16[1280,128]{1,0:T(8,128)(2,1)}, u32[]{:S(2)}) copy-start(bf16[1280,128]{1,0:T(8,128)(2,1)} %param.10) | copy-start | bytes 983044
  3.1 10.4 %copy-start.8 = (bf16[128,256]{1,0:T(8,128)(2,1)S(1)}, bf16[128,256]{1,0:T(8,128)(2,1)}, u32[]{:S(2)}) copy-start(bf16[128,256]{1,0:T(8,128)(2,1)} %param.17) | copy-start | bytes 196612
  4.6 17.7 %all-to-all-start = ((bf16[32,32,128]{2,1,0:T(8,128)(2,1)}), bf16[32,32,128]{2,1,0:T(8,128)(2,1)S(1)}, u32[]{:S(2)}, u32[]{:S(2)}) async-start(bf16[32,32,128]{2,1,0:T(8,128)(2,1)} %bitcast.4), calls=%async_computation | async-start | bytes 524288 | tf_op jit(solution)/shard_map/all_to_all | solution.py:73
  13.4 8.9 %copy-start.19 = (pred[384]{0:T(512)(128)(4,1)}, pred[384]{0:T(512)(128)(4,1)S(1)}, u32[]{:S(2)}) copy-start(pred[384]{0:T(512)(128)(4,1)S(1)} %broadcast_in_dim.28) | copy-start | bytes 1156
  32.3 1.4 %copy-start.6 = (bf16[48,128,128]{2,0,1:T(8,128)(2,1)S(1)}, bf16[48,128,128]{2,0,1:T(8,128)(2,1)}, u32[]{:S(2)}) copy-start(bf16[48,128,128]{2,0,1:T(8,128)(2,1)} %copy.33) | copy-start | bytes 4718596
  32.4 1.4 %copy-start.12 = (s32[48]{0:T(128)S(1)}, s32[48]{0:T(128)}, u32[]{:S(2)}) copy-start(s32[48]{0:T(128)} %param.14) | copy-start | bytes 580
  33.8 1.3 %copy-start.7 = (f32[1280,256]{1,0:T(8,128)S(1)}, f32[1280,256]{1,0:T(8,128)}, u32[]{:S(2)}) copy-start(f32[1280,256]{1,0:T(8,128)} %fusion.53) | copy-start | bytes 3932164
  33.8 1.5 %copy-start.21 = (bf16[1280,256]{1,0:T(8,128)(2,1)S(1)}, bf16[1280,256]{1,0:T(8,128)(2,1)}, u32[]{:S(2)}) copy-start(bf16[1280,256]{1,0:T(8,128)(2,1)} %param.19) | copy-start | bytes 1966084
  33.8 1.5 %copy-start.22 = (bf16[128,256]{1,0:T(8,128)(2,1)S(1)}, bf16[128,256]{1,0:T(8,128)(2,1)}, u32[]{:S(2)}) copy-start(bf16[128,256]{1,0:T(8,128)(2,1)} %param.18) | copy-start | bytes 196612
  36.9 5.0 %copy-start.1 = (bf16[1280,256]{1,0:T(8,128)(2,1)}, bf16[1280,256]{1,0:T(8,128)(2,1)S(1)}, u32[]{:S(2)}) copy-start(bf16[1280,256]{1,0:T(8,128)(2,1)S(1)} %get-tuple-element.10) | copy-start | bytes 1966084
  37.2 4.7 %copy-start.23 = (bf16[128,256]{1,0:T(8,128)(2,1)S(1)}, bf16[128,256]{1,0:T(8,128)(2,1)}, u32[]{:S(2)}) copy-start(bf16[128,256]{1,0:T(8,128)(2,1)} %param.18) | copy-start | bytes 196612
  38.5 17.1 %all-to-all-start.2 = ((f32[32,1,2048]{2,1,0:T(1,128)}), f32[32,1,2048]{2,1,0:T(1,128)}, u32[]{:S(2)}, u32[]{:S(2)}) async-start(f32[32,1,2048]{2,1,0:T(1,128)} %all_to_all.21), calls=%async_computation.2 | async-start | bytes 524288 | tf_op jit(solution)/shard_map/all_to_all | solution.py:15
  47.5 2.9 %copy-start.14 = (s32[48]{0:T(128)S(1)}, s32[48]{0:T(128)}, u32[]{:S(2)}) copy-start(s32[48]{0:T(128)} %param.15) | copy-start | bytes 580
  52.2 2.1 %copy-start.16 = (s32[384]{0:T(512)S(1)}, s32[384]{0:T(512)}, u32[]{:S(2)}) copy-start(s32[384]{0:T(512)} %copy-done.15) | copy-start | bytes 4612
  52.5 1.0 %copy-start.3 = (f32[13,128,128]{2,0,1:T(8,128)}, f32[13,128,128]{2,0,1:T(8,128)S(1)}, u32[]{:S(2)}) copy-start(f32[13,128,128]{2,0,1:T(8,128)S(1)} %convolution_add_fusion.3) | copy-start | bytes 2555908
  53.6 7.9 %copy-start.4 = (f32[13,128,128]{2,0,1:T(8,128)S(1)}, f32[13,128,128]{2,0,1:T(8,128)}, u32[]{:S(2)}) copy-start(f32[13,128,128]{2,0,1:T(8,128)} %copy-done.3) | copy-start | bytes 2555908
  53.6 0.6 copy-start.9
  55.7 19.6 %copy-start.2 = (bf16[1280,256]{1,0:T(8,128)(2,1)S(1)}, bf16[1280,256]{1,0:T(8,128)(2,1)}, u32[]{:S(2)}) copy-start(bf16[1280,256]{1,0:T(8,128)(2,1)} %copy-done.1) | copy-start | bytes 1966084
  55.7 16.1 %all-to-all-start.1 = ((bf16[32,32,128]{2,1,0:T(8,128)(2,1)}), bf16[32,32,128]{2,1,0:T(8,128)(2,1)S(1)}, u32[]{:S(2)}, u32[]{:S(2)}) async-start(bf16[32,32,128]{2,1,0:T(8,128)(2,1)} %bitcast.74), calls=%async_computation.1 | async-start | bytes 524288 | tf_op jit(solution)/shard_map/all_to_all | solution.py:73
  62.5 14.2 %copy-start.10 = (bf16[3,128,128]{2,1,0:T(8,128)(2,1)S(1)}, bf16[3,128,128]{2,1,0:T(8,128)(2,1)}, u32[]{:S(2)}) copy-start(bf16[3,128,128]{2,1,0:T(8,128)(2,1)} %copy-done.9) | copy-start | bytes 294916
  62.5 14.2 %copy-start.18 = (s32[384]{0:T(512)S(1)}, s32[384]{0:T(512)}, u32[]{:S(2)}) copy-start(s32[384]{0:T(512)} %copy-done.17) | copy-start | bytes 4612
  62.5 14.2 %copy-start.20 = (pred[384]{0:T(512)(128)(4,1)S(1)}, pred[384]{0:T(512)(128)(4,1)}, u32[]{:S(2)}) copy-start(pred[384]{0:T(512)(128)(4,1)} %copy-done.19) | copy-start | bytes 1156
  72.7 13.0 %all-to-all-start.3 = ((f32[32,1,2048]{2,1,0:T(1,128)}), f32[32,1,2048]{2,1,0:T(1,128)S(1)}, u32[]{:S(2)}, u32[]{:S(2)}) async-start(f32[32,1,2048]{2,1,0:T(1,128)} %broadcast_in_dim.58), calls=%async_computation.3 | async-start | bytes 524288 | tf_op jit(solution)/shard_map/all_to_all | solution.py:17

commit v11 on v7

--- a/solution.py
+++ b/solution.py
@@ -111,9 +111,9 @@
         (tile_src[None, :] == jnp.arange(source_count, dtype=jnp.int32)[:, None]) & usable[None, :]
     ).astype(jnp.float32)
     products = jnp.einsum(
-        "tij,tjf->tif", tile_vals, source[tile_src], preferred_element_type=jnp.float32
+        "tjf,tij->tfi", source[tile_src], tile_vals, preferred_element_type=jnp.float32
     )
-    summed = jnp.einsum("bt,tif->bif", to_target, products, precision=lax.Precision.HIGHEST)
+    summed = jnp.einsum("bt,tfi->bif", to_target, products, precision=lax.Precision.HIGHEST)
     unit_column = jnp.ones((tile_size,), jnp.bfloat16)
     row_sums = jnp.einsum("tij,j->ti", tile_vals, unit_column, preferred_element_type=jnp.float32)
     degree = jnp.dot(to_target, row_sums, precision=lax.Precision.HIGHEST)
@@ -132,9 +132,9 @@
     grad_agg = jnp.einsum("nh,fh->nf", grad_pre, w_neigh, preferred_element_type=jnp.float32)
     grad_agg = (grad_agg / degree.reshape(-1)[:, None]).astype(jnp.bfloat16)
     picked = grad_agg.reshape(block_count, tile_size, width)[tile_tgt]
-    backward = jnp.einsum("tij,tif->tjf", tile_vals, picked, preferred_element_type=jnp.float32)
+    backward = jnp.einsum("tif,tij->tfj", picked, tile_vals, preferred_element_type=jnp.float32)
     grad_source = jnp.einsum(
-        "st,tjf->sjf", to_source, backward, precision=lax.Precision.HIGHEST
+        "st,tfj->sjf", to_source, backward, precision=lax.Precision.HIGHEST
     ).reshape(-1, width)
     remote = grad_source[node_count:].astype(jnp.bfloat16)
     if table_bytes <= PLACE_LIMIT:

time: 87.3 us -> 78.5 us (0.90)
  local copies, waits for them, and re-layouts: 16.2 us -> 8.77 us
  waiting for transfers between devices: 22.5 us -> 26.2 us
  starting transfers between devices: 18.9 us -> 16.1 us
  matrix products: 25.6 us -> 23.3 us
    dot_general x3 -> x0, local copies, waits for them, and re-layouts: 7.29 us -> none  [the longest x1 3.59 us: per_device(): jnp.einsum('tij,tif->tjf', tile_vals, picked, preferred_element_type=jnp....]
    dot_general x4, matrix products: 12.9 us -> 9.19 us  [the longest x1 2.94 us: per_device(): jnp.einsum('bt,tfi->bif', to_target, products, precision=lax.Precision.HI...]
    all_to_all x1, waiting for transfers between devices: 0.01 us -> 3.71 us  [weight_sum(): lax.all_to_all(chunks, axes, 0, 0, tiled=True)]
    all_to_all x2, starting transfers between devices: 13.1 us -> 10 us  [swap(): lax.all_to_all(buf, ('dom', 'grp'), 0, 0, tiled=True)]
    dot_general x1, matrix products: 1.64 us -> 3.14 us  [per_device(): jnp.dot(agg, w_neigh, preferred_element_type=jnp.float32)]
  transfers between devices with their start and end apart: 4 -> 4, of which waited for: 3 -> 4; matrix products, arithmetic and copies ran while one was open for 22% -> 18% of each run, Pallas kernels for 0% -> 0%
where the time goes in v11:
time: 78.5 us; the launch traced here: 78 us
  waiting for transfers between devices  26.2 us (33%)
  matrix products  23.3 us (30%)
  starting transfers between devices  16.1 us (21%)
  local copies, waits for them, and re-layouts  8.77 us (11%)
  other arithmetic  2.01 us (3%)
  between operations  1.61 us (2%)
    all_to_all x2, waiting for transfers between devices, swap(): lax.all_to_all(buf, ('dom', 'grp'), 0, 0, tiled=True)  15.5 us
    all_to_all x2, starting transfers between devices, swap(): lax.all_to_all(buf, ('dom', 'grp'), 0, 0, tiled=True)  10 us
    all_to_all x1, waiting for transfers between devices, weight_sum(): total = lax.all_to_all(spread, axes, 0, 0, tiled=True).reshape(-1)  7.03 us
    all_to_all x1, waiting for transfers between devices, weight_sum(): lax.all_to_all(chunks, axes, 0, 0, tiled=True)  3.71 us
    all_to_all x1, starting transfers between devices, weight_sum(): lax.all_to_all(chunks, axes, 0, 0, tiled=True)  3.48 us
    dot_general x1, matrix products, per_device(): jnp.dot(agg, w_neigh, preferred_element_type=jnp.float32)  3.14 us
    dot_general x1, matrix products, per_device(): jnp.einsum('bt,tfi->bif', to_target, products, precision=lax.Precision.HI...  2.94 us
    dot_general x1, matrix products, per_device(): jnp.einsum('st,tfj->sjf', to_source, backward, precision=lax.Precision.HI...  2.91 us
  transfers between devices with their start and end apart: 4, of which 4 were waited for; matrix products, arithmetic and copies ran while one was open for 18% of the time, Pallas kernels for 0%

profile of v11, /device:TPU:0, one launch (start us, length us, event | category | flops | bytes accessed | tf_op | source)
XLA Modules:
  0.0 78.0 jit_solution(14554120736940898893)
XLA Ops:
  0.6 0.0 copy-start
  0.7 0.1 iota_add_fusion
  0.8 0.1 add.79
  0.8 0.7 pad_add_fusion
  1.5 0.1 eq.71
  1.6 1.5 %fusion.27 = bf16[384,128]{1,0:T(8,128)(2,1)S(1)} fusion(bf16[1280,128]{1,0:T(8,128)(2,1)} %param.10, s32[384]{0:T(512)S(1)} %eq.71), kind=kOutput, calls=%fused_computation.30 | convolution fusion | flops 126369792 | bytes 427520 | tf_op jit(solution)/shard_map/dot_general | solution.py:91
  3.1 0.0 copy-start.3
  3.1 0.0 copy-start.4
  3.1 1.4 %fusion.23 = bf16[1024,128]{1,0:T(8,128)(2,1)} fusion(bf16[384,128]{1,0:T(8,128)(2,1)S(1)} %fusion.27, s32[384]{0:T(512)S(1)} %add.79), kind=kOutput, calls=%fused_computation.26 | convolution fusion | flops 101187584 | bytes 361984 | tf_op jit(solution)/shard_map/dot_general | solution.py:63
  4.5 7.3 %all-to-all-start = ((bf16[32,32,128]{2,1,0:T(8,128)(2,1)}), bf16[32,32,128]{2,1,0:T(8,128)(2,1)S(1)}, u32[]{:S(2)}, u32[]{:S(2)}) async-start(bf16[32,32,128]{2,1,0:T(8,128)(2,1)} %bitcast.2), calls=%async_computation | async-start | bytes 524288 | tf_op jit(solution)/shard_map/all_to_all | solution.py:65
  12.6 0.5 fusion.54
  13.1 0.1 broadcast_in_dim.27
  13.2 0.1 broadcast_in_dim.28
  13.3 0.1 fusion.39
  13.4 0.0 copy-done.4
  13.4 1.4 %fusion.57 = f32[1280,256]{1,0:T(8,128)} fusion(bf16[1280,128]{1,0:T(8,128)(2,1)S(1)} %copy-done.3, bf16[128,256]{1,0:T(8,128)(2,1)S(1)} %copy-done.4), kind=kOutput, calls=%fused_computation.73 | convolution fusion | flops 83886080 | bytes 1703936 | tf_op jit(solution)/shard_map/dot_general | solution.py:121
  14.8 7.4 %all-to-all-done = bf16[32,32,128]{2,1,0:T(8,128)(2,1)S(1)} async-done(((bf16[32,32,128]{2,1,0:T(8,128)(2,1)}), bf16[32,32,128]{2,1,0:T(8,128)(2,1)S(1)}, u32[]{:S(2)}, u32[]{:S(2)}) %all-to-all-start) | async-done | bytes 262176 | tf_op jit(solution)/shard_map/all_to_all | solution.py:65
  22.2 0.4 fusion.29
  22.7 2.0 %gather_fusion = bf16[48,128,128]{2,1,0:T(8,128)(2,1)} fusion(bf16[13,128,128]{2,1,0:T(8,128)(2,1)S(1)} %bitcast.56, s32[1024]{0:T(1024)S(1)} %pad_clamp_fusion.1), kind=kCustom, calls=%fused_computation | custom fusion | bytes 3145920 | tf_op jit(solution)/shard_map/gather | solution.py:114
  24.7 2.6 %fusion.58 = f32[48,128,128]{2,1,0:T(8,128)S(1)} fusion(bf16[48,128,128]{2,1,0:T(8,128)(2,1)} %gather_fusion, bf16[48,128,128]{2,1,0:T(8,128)(2,1)S(1)} %copy-done), kind=kOutput, calls=%fused_computation.74 | convolution fusion | flops 201326592 | bytes 6291456 | tf_op jit(solution)/shard_map/tjf,tij->tfi/dot_general | solution.py:113
  27.3 2.9 %fusion.20 = bf16[10,128,128]{1,0,2:T(8,128)(2,1)S(1)} fusion(f32[48,128,128]{2,1,0:T(8,128)S(1)} %fusion.58, f32[10,128]{1,0:T(8,128)S(1)} %fusion.39, s32[48]{0:T(128)S(1)} %copy-done.7, pred[48]{0:T(512)(128)(4,1)S(1)} %iota_compare_fusion.26), kind=kOutput, calls=%fused_computation.25 | convolution fusion | flops 94700480 | bytes 3478768 | tf_op jit(solution)/shard_map/bt,tfi->bif/dot_general | solution.py:116
  30.3 0.4 copy.27
  30.6 3.1 %multiply_convert_fusion = (bf16[1280,256]{1,0:T(8,128)(2,1)S(1)}, bf16[1280,256]{1,0:T(8,128)(2,1)}) fusion(bf16[1280,256]{1,0:T(8,128)(2,1)} %param.19, f32[1280,256]{1,0:T(8,128)} %fusion.57, bf16[1280,128]{1,0:T(8,128)(2,1)S(1)} %bitcast.60, bf16[128,256]{1,0:T(8,128)(2,1)S(1)} %copy-done.11), kind=kOutput, calls=%fused_computation.22 | convolution fusion | flops 88145920 | bytes 3670016 | tf_op jit(solution)/shard_map/dot_general | solution.py:121
  33.8 0.3 fusion.60
  34.1 0.3 convolution_bitcast_fusion
  34.4 1.0 %all_to_all.21 = f32[32,1,2048]{2,1,0:T(1,128)} reshape(f32[256,256]{1,0:T(8,128)S(1)} %pad_maximum_fusion.1) | data formatting | bytes 524288 | tf_op jit(solution)/shard_map/all_to_all | solution.py:15
  35.4 3.5 %all-to-all-start.2 = ((f32[32,1,2048]{2,1,0:T(1,128)}), f32[32,1,2048]{2,1,0:T(1,128)}, u32[]{:S(2)}, u32[]{:S(2)}) async-start(f32[32,1,2048]{2,1,0:T(1,128)} %all_to_all.21), calls=%async_computation.2 | async-start | bytes 524288 | tf_op jit(solution)/shard_map/all_to_all | solution.py:15
  38.9 0.3 fusion.4
  39.3 0.8 %gather_fusion.1 = bf16[48,128,128]{2,1,0:T(8,128)(2,1)S(1)} fusion(bf16[10,128,128]{2,1,0:T(8,128)(2,1)S(1)} %bitcast.57, s32[1024]{0:T(1024)S(1)} %pad_clamp_fusion), kind=kCustom, calls=%fused_computation.1 | custom fusion | bytes 3145920 | tf_op jit(solution)/shard_map/gather | solution.py:134
  40.1 0.7 fusion.59
  40.8 2.9 %fusion.17 = f32[13,128,128]{1,0,2:T(8,128)S(1)} fusion(f32[48,128,128]{2,1,0:T(8,128)S(1)} %fusion.59, s32[48]{0:T(128)S(1)} %copy-done.8, pred[48]{0:T(512)(128)(4,1)S(1)} %iota_compare_fusion.26), kind=kOutput, calls=%fused_computation.21 | convolution fusion | flops 122684640 | bytes 3997936 | tf_op jit(solution)/shard_map/st,tfj->sjf/dot_general | solution.py:136
  43.7 0.1 slice.46
  43.8 0.1 copy.31
  43.9 0.0 copy-start.5
  44.0 1.4 %fusion.24 = bf16[1024,128]{1,0:T(8,128)(2,1)} fusion(bf16[384,128]{1,0:T(8,128)(2,1)S(1)} %bitcast.65, s32[384]{0:T(512)S(1)} %add.79), kind=kOutput, calls=%fused_computation.27 | convolution fusion | flops 101187584 | bytes 361984 | tf_op jit(solution)/shard_map/dot_general | solution.py:63
  45.4 3.7 %all-to-all-done.2 = f32[32,1,2048]{2,1,0:T(1,128)} async-done(((f32[32,1,2048]{2,1,0:T(1,128)}), f32[32,1,2048]{2,1,0:T(1,128)}, u32[]{:S(2)}, u32[]{:S(2)}) %all-to-all-start.2) | async-done | bytes 262176 | tf_op jit(solution)/shard_map/all_to_all | solution.py:15
  49.1 2.7 %all-to-all-start.1 = ((bf16[32,32,128]{2,1,0:T(8,128)(2,1)}), bf16[32,32,128]{2,1,0:T(8,128)(2,1)S(1)}, u32[]{:S(2)}, u32[]{:S(2)}) async-start(bf16[32,32,128]{2,1,0:T(8,128)(2,1)} %bitcast.64), calls=%async_computation.1 | async-start | bytes 524288 | tf_op jit(solution)/shard_map/all_to_all | solution.py:65
  51.8 1.2 %copy.30 = f32[10,128,128]{2,1,0:T(8,128)} copy(f32[10,128,128]{1,0,2:T(8,128)S(1)} %bitcast.58) | data formatting | bytes 1310720 | tf_op jit(solution)/shard_map/slice | solution.py:147
  53.0 1.1 %reduce_sum.9 = f32[2048]{0:T(1024)S(1)} reduce(f32[32,1,2048]{2,1,0:T(1,128)} %all-to-all-done.2, f32[]{:T(128)} %constant.31.clone.1), dimensions={0,1}, to_apply=%region_0.1 | reduce | flops 63488 | bytes 270340 | tf_op jit(solution)/shard_map/reduce_sum | solution.py:15
  54.1 8.1 %all-to-all-done.1 = bf16[32,32,128]{2,1,0:T(8,128)(2,1)S(1)} async-done(((bf16[32,32,128]{2,1,0:T(8,128)(2,1)}), bf16[32,32,128]{2,1,0:T(8,128)(2,1)S(1)}, u32[]{:S(2)}, u32[]{:S(2)}) %all-to-all-start.1) | async-done | bytes 262176 | tf_op jit(solution)/shard_map/all_to_all | solution.py:65
  62.2 0.8 %broadcast_in_dim.58 = f32[32,1,2048]{2,1,0:T(1,128)} broadcast(f32[2048]{0:T(1024)S(1)} %reduce_sum.9), dimensions={2} | broadcast | bytes 270336 | tf_op jit(solution)/shard_map/broadcast_in_dim | solution.py:16
  63.0 2.6 %all-to-all-start.3 = ((f32[32,1,2048]{2,1,0:T(1,128)}), f32[32,1,2048]{2,1,0:T(1,128)S(1)}, u32[]{:S(2)}, u32[]{:S(2)}) async-start(f32[32,1,2048]{2,1,0:T(1,128)} %broadcast_in_dim.58), calls=%async_computation.3 | async-start | bytes 524288 | tf_op jit(solution)/shard_map/all_to_all | solution.py:17
  65.6 1.5 %convolution_add_fusion.2 = f32[1280,128]{1,0:T(8,128)S(1)} fusion(f32[1280,128]{1,0:T(8,128)} %bitcast.59, bf16[1280,256]{1,0:T(8,128)(2,1)S(1)} %copy-done.2, bf16[128,256]{1,0:T(8,128)(2,1)} %param.17), kind=kOutput, calls=%fused_computation.9 | convolution fusion | flops 84049920 | bytes 2031616 | tf_op jit(solution)/shard_map/nh,fh->nf/dot_general | solution.py:131
  67.1 1.9 %fusion.5 = bf16[1280,128]{1,0:T(8,128)(2,1)} fusion(f32[1280,128]{1,0:T(8,128)S(1)} %convolution_add_fusion.2, bf16[384,128]{1,0:T(8,128)(2,1)S(1)} %bitcast.66, bf16[1024,128]{1,0:T(8,128)(2,1)S(1)} %bitcast.63, s32[384]{0:T(512)S(1)} %eq.71, s32[384]{0:T(512)S(1)} %add.79, pred[384]{0:T(512)(128)(4,1)S(1)} %copy-done.10), kind=kOutput, calls=%fused_computation.11 | convolution fusion | flops 227803136 | bytes 1346944 | tf_op jit(solution)/shard_map/dot_general | solution.py:148
  69.0 7.0 %all-to-all-done.3 = f32[32,1,2048]{2,1,0:T(1,128)S(1)} async-done(((f32[32,1,2048]{2,1,0:T(1,128)}), f32[32,1,2048]{2,1,0:T(1,128)S(1)}, u32[]{:S(2)}, u32[]{:S(2)}) %all-to-all-start.3) | async-done | bytes 262176 | tf_op jit(solution)/shard_map/all_to_all | solution.py:17
  76.0 0.7 slice_reduce_fusion
  76.7 0.7 slice.34
  77.3 0.7 slice.32
  (28 shorter events, 0.1 us)
Async XLA Ops:
  0.6 11.9 %copy-start = (bf16[48,128,128]{2,1,0:T(8,128)(2,1)S(1)}, bf16[48,128,128]{2,1,0:T(8,128)(2,1)}, u32[]{:S(2)}) copy-start(bf16[48,128,128]{2,1,0:T(8,128)(2,1)} %param.13) | copy-start | bytes 4718596
  0.6 11.9 %copy-start.8 = (s32[48]{0:T(128)S(1)}, s32[48]{0:T(128)}, u32[]{:S(2)}) copy-start(s32[48]{0:T(128)} %param.15) | copy-start | bytes 580
  0.7 11.9 %copy-start.7 = (s32[48]{0:T(128)S(1)}, s32[48]{0:T(128)}, u32[]{:S(2)}) copy-start(s32[48]{0:T(128)} %param.14) | copy-start | bytes 580
  3.1 10.3 %copy-start.3 = (bf16[1280,128]{1,0:T(8,128)(2,1)S(1)}, bf16[1280,128]{1,0:T(8,128)(2,1)}, u32[]{:S(2)}) copy-start(bf16[1280,128]{1,0:T(8,128)(2,1)} %param.10) | copy-start | bytes 983044
  3.1 10.3 %copy-start.4 = (bf16[128,256]{1,0:T(8,128)(2,1)S(1)}, bf16[128,256]{1,0:T(8,128)(2,1)}, u32[]{:S(2)}) copy-start(bf16[128,256]{1,0:T(8,128)(2,1)} %param.17) | copy-start | bytes 196612
  4.5 17.7 %all-to-all-start = ((bf16[32,32,128]{2,1,0:T(8,128)(2,1)}), bf16[32,32,128]{2,1,0:T(8,128)(2,1)S(1)}, u32[]{:S(2)}, u32[]{:S(2)}) async-start(bf16[32,32,128]{2,1,0:T(8,128)(2,1)} %bitcast.2), calls=%async_computation | async-start | bytes 524288 | tf_op jit(solution)/shard_map/all_to_all | solution.py:65
  13.3 9.4 %copy-start.9 = (pred[384]{0:T(512)(128)(4,1)}, pred[384]{0:T(512)(128)(4,1)S(1)}, u32[]{:S(2)}) copy-start(pred[384]{0:T(512)(128)(4,1)S(1)} %broadcast_in_dim.28) | copy-start | bytes 1156
  27.3 3.3 %copy-start.11 = (bf16[128,256]{1,0:T(8,128)(2,1)S(1)}, bf16[128,256]{1,0:T(8,128)(2,1)}, u32[]{:S(2)}) copy-start(bf16[128,256]{1,0:T(8,128)(2,1)} %param.18) | copy-start | bytes 196612
  33.8 5.1 %copy-start.1 = (bf16[1280,256]{1,0:T(8,128)(2,1)}, bf16[1280,256]{1,0:T(8,128)(2,1)S(1)}, u32[]{:S(2)}) copy-start(bf16[1280,256]{1,0:T(8,128)(2,1)S(1)} %get-tuple-element.6) | copy-start | bytes 1966084
  35.4 13.7 %all-to-all-start.2 = ((f32[32,1,2048]{2,1,0:T(1,128)}), f32[32,1,2048]{2,1,0:T(1,128)}, u32[]{:S(2)}, u32[]{:S(2)}) async-start(f32[32,1,2048]{2,1,0:T(1,128)} %all_to_all.21), calls=%async_computation.2 | async-start | bytes 524288 | tf_op jit(solution)/shard_map/all_to_all | solution.py:15
  43.9 5.1 %copy-start.5 = (bf16[3,128,128]{2,1,0:T(8,128)(2,1)}, bf16[3,128,128]{2,1,0:T(8,128)(2,1)S(1)}, u32[]{:S(2)}) copy-start(bf16[3,128,128]{2,1,0:T(8,128)(2,1)S(1)} %copy.31) | copy-start | bytes 294916
  49.1 16.5 %copy-start.2 = (bf16[1280,256]{1,0:T(8,128)(2,1)S(1)}, bf16[1280,256]{1,0:T(8,128)(2,1)}, u32[]{:S(2)}) copy-start(bf16[1280,256]{1,0:T(8,128)(2,1)} %copy-done.1) | copy-start | bytes 1966084
  49.1 13.1 %all-to-all-start.1 = ((bf16[32,32,128]{2,1,0:T(8,128)(2,1)}), bf16[32,32,128]{2,1,0:T(8,128)(2,1)S(1)}, u32[]{:S(2)}, u32[]{:S(2)}) async-start(bf16[32,32,128]{2,1,0:T(8,128)(2,1)} %bitcast.64), calls=%async_computation.1 | async-start | bytes 524288 | tf_op jit(solution)/shard_map/all_to_all | solution.py:65
  53.0 14.1 %copy-start.6 = (bf16[3,128,128]{2,1,0:T(8,128)(2,1)S(1)}, bf16[3,128,128]{2,1,0:T(8,128)(2,1)}, u32[]{:S(2)}) copy-start(bf16[3,128,128]{2,1,0:T(8,128)(2,1)} %copy-done.5) | copy-start | bytes 294916
  53.0 14.1 %copy-start.10 = (pred[384]{0:T(512)(128)(4,1)S(1)}, pred[384]{0:T(512)(128)(4,1)}, u32[]{:S(2)}) copy-start(pred[384]{0:T(512)(128)(4,1)} %copy-done.9) | copy-start | bytes 1156
  63.0 13.0 %all-to-all-start.3 = ((f32[32,1,2048]{2,1,0:T(1,128)}), f32[32,1,2048]{2,1,0:T(1,128)S(1)}, u32[]{:S(2)}, u32[]{:S(2)}) async-start(f32[32,1,2048]{2,1,0:T(1,128)} %broadcast_in_dim.58), calls=%async_computation.3 | async-start | bytes 524288 | tf_op jit(solution)/shard_map/all_to_all | solution.py:17

commit v12 on v9

--- a/solution.py
+++ b/solution.py
@@ -118,9 +118,9 @@
         (tile_src[None, :] == jnp.arange(source_count, dtype=jnp.int32)[:, None]) & usable[None, :]
     ).astype(jnp.float32)
     products = jnp.einsum(
-        "tij,tjf->tif", tile_vals, source[tile_src], preferred_element_type=jnp.float32
+        "tjf,tij->tfi", source[tile_src], tile_vals, preferred_element_type=jnp.float32
     )
-    summed = jnp.einsum("bt,tif->bif", to_target, products, precision=lax.Precision.HIGHEST)
+    summed = jnp.einsum("bt,tfi->bif", to_target, products, precision=lax.Precision.HIGHEST)
     unit_column = jnp.ones((tile_size,), jnp.bfloat16)
     row_sums = jnp.einsum("tij,j->ti", tile_vals, unit_column, preferred_element_type=jnp.float32)
     degree = jnp.dot(to_target, row_sums, precision=lax.Precision.HIGHEST)
@@ -142,9 +142,9 @@
     grad_agg = jnp.einsum("nh,fh->nf", grad_pre, w_neigh, preferred_element_type=jnp.float32)
     grad_agg = (grad_agg / degree.reshape(-1)[:, None]).astype(jnp.bfloat16)
     picked = grad_agg.reshape(block_count, tile_size, width)[tile_tgt]
-    backward = jnp.einsum("tij,tif->tjf", tile_vals, picked, preferred_element_type=jnp.float32)
+    backward = jnp.einsum("tif,tij->tfj", picked, tile_vals, preferred_element_type=jnp.float32)
     grad_source = jnp.einsum(
-        "st,tjf->sjf", to_source, backward, precision=lax.Precision.HIGHEST
+        "st,tfj->sjf", to_source, backward, precision=lax.Precision.HIGHEST
     ).reshape(-1, width)
     remote = grad_source[node_count:].astype(jnp.bfloat16)
     if table_bytes <= PLACE_LIMIT:

time: 89.4 us -> 78.9 us (0.88)
  local copies, waits for them, and re-layouts: 13.8 us -> 6.87 us
  matrix products: 26.9 us -> 23.4 us
  starting transfers between devices: 19.1 us -> 16 us
  waiting for transfers between devices: 24.6 us -> 27.6 us
    dot_general x3 -> x0, local copies, waits for them, and re-layouts: 7.28 us -> none  [the longest x1 3.58 us: per_device(): jnp.einsum('tij,tjf->tif', tile_vals, source[tile_src], preferred_element...]
    all_to_all x1, waiting for transfers between devices: 0.01 us -> 3.66 us  [weight_sum(): lax.all_to_all(chunks, axes, 0, 0, tiled=True)]
    dot_general x4, matrix products: 12.8 us -> 9.21 us  [the longest x1 2.94 us: per_device(): jnp.einsum('bt,tfi->bif', to_target, products, precision=lax.Precision.HI...]
    all_to_all x2, starting transfers between devices: 13.2 us -> 9.88 us  [swap(): lax.all_to_all(buf, ('dom', 'grp'), 0, 0, tiled=True)]
    unnamed x24 -> x42, local copies, waits for them, and re-layouts: 1.55 us -> 0.11 us
    dot_general x1, matrix products: 1.65 us -> 2.92 us  [per_device(): jnp.dot(agg, w_neigh, preferred_element_type=jnp.float32)]
    dot_general x1, matrix products: 1.44 us -> 0.34 us  [per_device(): jnp.einsum('nh,fh->nf', grad_pre, w_neigh, preferred_element_type=jnp.flo...]
    convert_element_type x1, local copies, waits for them, and re-layouts: 0.09 us -> 1.07 us  [per_device(): (summed / degree[:, :, None]).reshape(node_count, width)]
  transfers between devices with their start and end apart: 4 -> 4, of which waited for: 3 -> 4; matrix products, arithmetic and copies ran while one was open for 21% -> 16% of each run, Pallas kernels for 0% -> 0%
where the time goes in v12:
time: 78.9 us; the launch traced here: 78.4 us
  waiting for transfers between devices  27.6 us (35%)
  matrix products  23.4 us (30%)
  starting transfers between devices  16 us (20%)
  local copies, waits for them, and re-layouts  6.87 us (9%)
  other arithmetic  2.84 us (4%)
  between operations  1.66 us (2%)
    all_to_all x2, waiting for transfers between devices, swap(): lax.all_to_all(buf, ('dom', 'grp'), 0, 0, tiled=True)  16.9 us
    all_to_all x2, starting transfers between devices, swap(): lax.all_to_all(buf, ('dom', 'grp'), 0, 0, tiled=True)  9.88 us
    all_to_all x1, waiting for transfers between devices, weight_sum(): lax.all_to_all(jnp.broadcast_to(mine, chunks.shape), axes, 0, 0, tiled=True)  7.07 us
    all_to_all x1, waiting for transfers between devices, weight_sum(): lax.all_to_all(chunks, axes, 0, 0, tiled=True)  3.66 us
    all_to_all x1, starting transfers between devices, weight_sum(): lax.all_to_all(chunks, axes, 0, 0, tiled=True)  3.49 us
    dot_general x1, matrix products, per_device(): jnp.einsum('bt,tfi->bif', to_target, products, precision=lax.Precision.HI...  2.94 us
    dot_general x1, matrix products, per_device(): jnp.dot(agg, w_neigh, preferred_element_type=jnp.float32)  2.92 us
    dot_general x1, matrix products, per_device(): jnp.einsum('st,tfj->sjf', to_source, backward, precision=lax.Precision.HI...  2.91 us
  transfers between devices with their start and end apart: 4, of which 4 were waited for; matrix products, arithmetic and copies ran while one was open for 16% of the time, Pallas kernels for 0%

profile of v12, /device:TPU:0, one launch (start us, length us, event | category | flops | bytes accessed | tf_op | source)
XLA Modules:
  0.0 78.4 jit_solution(6871025572937926541)
XLA Ops:
  0.6 0.0 copy-start
  0.6 0.0 copy-start.16
  0.7 0.0 copy-start.14
  0.7 0.1 iota_add_fusion
  0.8 0.1 add.79
  0.8 0.7 pad_add_fusion
  1.6 0.1 eq.71
  1.6 1.5 %fusion.27 = bf16[384,128]{1,0:T(8,128)(2,1)S(1)} fusion(bf16[1280,128]{1,0:T(8,128)(2,1)} %param.10, s32[384]{0:T(512)S(1)} %eq.71), kind=kOutput, calls=%fused_computation.31 | convolution fusion | flops 126369792 | bytes 427520 | tf_op jit(solution)/shard_map/dot_general | solution.py:98
  3.1 0.0 copy-start.20
  3.1 0.0 copy-start.1
  3.2 1.4 %fusion.23 = bf16[1024,128]{1,0:T(8,128)(2,1)} fusion(bf16[384,128]{1,0:T(8,128)(2,1)S(1)} %fusion.27, s32[384]{0:T(512)S(1)} %add.79), kind=kOutput, calls=%fused_computation.26 | convolution fusion | flops 101187584 | bytes 361984 | tf_op jit(solution)/shard_map/dot_general | solution.py:70
  4.6 7.3 %all-to-all-start = ((bf16[32,32,128]{2,1,0:T(8,128)(2,1)}), bf16[32,32,128]{2,1,0:T(8,128)(2,1)S(1)}, u32[]{:S(2)}, u32[]{:S(2)}) async-start(bf16[32,32,128]{2,1,0:T(8,128)(2,1)} %bitcast.2), calls=%async_computation | async-start | bytes 524288 | tf_op jit(solution)/shard_map/all_to_all | solution.py:72
  12.6 0.5 fusion.57
  13.1 0.1 broadcast_in_dim.27
  13.2 0.7 broadcast_in_dim.28
  13.9 0.1 fusion.42
  14.0 0.3 fusion.61
  14.4 7.9 %all-to-all-done = bf16[32,32,128]{2,1,0:T(8,128)(2,1)S(1)} async-done(((bf16[32,32,128]{2,1,0:T(8,128)(2,1)}), bf16[32,32,128]{2,1,0:T(8,128)(2,1)S(1)}, u32[]{:S(2)}, u32[]{:S(2)}) %all-to-all-start) | async-done | bytes 262176 | tf_op jit(solution)/shard_map/all_to_all | solution.py:72
  22.3 1.3 %fusion.29 = bf16[384,128]{1,0:T(8,128)(2,1)S(1)} fusion(bf16[384,128]{1,0:T(8,128)(2,1)} %copy-done.20, bf16[1024,128]{1,0:T(8,128)(2,1)S(1)} %bitcast.63, s32[384]{0:T(512)} %copy-done.10, pred[384]{0:T(512)(128)(4,1)} %broadcast_in_dim.28), kind=kOutput, calls=%fused_computation.33 | convolution fusion | flops 101154816 | bytes 460672 | tf_op jit(solution)/shard_map/dot_general | solution.py:73
  23.6 1.0 %pad_maximum_fusion = bf16[1664,128]{1,0:T(8,128)(2,1)S(1)} fusion(bf16[384,128]{1,0:T(8,128)(2,1)S(1)} %fusion.29, bf16[1280,128]{1,0:T(8,128)(2,1)} %param.10), kind=kLoop, calls=%fused_computation.43 | loop fusion | flops 851968 | bytes 851968 | tf_op jit(solution)/shard_map/concatenate | solution.py:107
  24.6 2.0 %gather_fusion = bf16[48,128,128]{2,1,0:T(8,128)(2,1)} fusion(bf16[13,128,128]{2,1,0:T(8,128)(2,1)S(1)} %bitcast.57, s32[1024]{0:T(1024)S(1)} %pad_clamp_fusion.1), kind=kCustom, calls=%fused_computation | custom fusion | bytes 3145920 | tf_op jit(solution)/shard_map/gather | solution.py:121
  26.6 2.7 %fusion.62 = f32[48,128,128]{2,1,0:T(8,128)S(1)} fusion(bf16[48,128,128]{2,1,0:T(8,128)(2,1)} %gather_fusion, bf16[48,128,128]{2,1,0:T(8,128)(2,1)S(1)} %copy-done), kind=kOutput, calls=%fused_computation.77 | convolution fusion | flops 201326592 | bytes 6291456 | tf_op jit(solution)/shard_map/tjf,tij->tfi/dot_general | solution.py:120
  29.3 2.9 %fusion.20 = bf16[10,128,128]{1,0,2:T(8,128)(2,1)S(1)} fusion(f32[48,128,128]{2,1,0:T(8,128)S(1)} %fusion.62, f32[10,128]{1,0:T(8,128)S(1)} %fusion.42, s32[48]{0:T(128)S(1)} %copy-done.15, pred[48]{0:T(512)(128)(4,1)S(1)} %copy-done.9), kind=kOutput, calls=%fused_computation.25 | convolution fusion | flops 94700480 | bytes 3478768 | tf_op jit(solution)/shard_map/bt,tfi->bif/dot_general | solution.py:123
  32.2 1.1 %copy.17 = bf16[10,128,128]{2,1,0:T(8,128)(2,1)} copy(bf16[10,128,128]{1,0,2:T(8,128)(2,1)S(1)} %fusion.20) | data formatting | bytes 655360 | tf_op jit(solution)/shard_map/convert_element_type | solution.py:127
  33.3 2.9 %multiply_convert_fusion = (bf16[1280,256]{1,0:T(8,128)(2,1)S(1)}, bf16[1280,256]{1,0:T(8,128)(2,1)}) fusion(bf16[1280,256]{1,0:T(8,128)(2,1)} %param.19, f32[1280,256]{1,0:T(8,128)S(1)} %fusion.61, bf16[1280,128]{1,0:T(8,128)(2,1)} %bitcast.61, bf16[128,256]{1,0:T(8,128)(2,1)} %param.18), kind=kOutput, calls=%fused_computation.22 | convolution fusion | flops 88145920 | bytes 3670016 | tf_op jit(solution)/shard_map/dot_general | solution.py:128
  36.2 1.1 %convolution_bitcast_fusion = f32[32,8,256]{2,1,0:T(8,128)} fusion(bf16[1280,256]{1,0:T(8,128)(2,1)S(1)} %get-tuple-element.4, bf16[1280,128]{1,0:T(8,128)(2,1)S(1)} %bitcast.62, bf16[1280,128]{1,0:T(8,128)(2,1)S(1)} %copy-done.2), kind=kOutput, calls=%fused_computation.28 | convolution fusion | flops 169082880 | bytes 1572864 | tf_op jit(solution)/shard_map/nf,nh->fh/dot_general | solution.py:136
  37.3 3.5 %all-to-all-start.2 = ((f32[32,8,256]{2,1,0:T(8,128)}), f32[32,8,256]{2,1,0:T(8,128)}, u32[]{:S(2)}, u32[]{:S(2)}) async-start(f32[32,8,256]{2,1,0:T(8,128)} %convolution_bitcast_fusion), calls=%async_computation.2 | async-start | bytes 524288 | tf_op jit(solution)/shard_map/all_to_all | solution.py:15
  40.8 0.3 fusion.4
  41.2 0.8 %gather_fusion.1 = bf16[48,128,128]{2,1,0:T(8,128)(2,1)S(1)} fusion(bf16[10,128,128]{2,1,0:T(8,128)(2,1)S(1)} %bitcast.58, s32[1024]{0:T(1024)S(1)} %pad_clamp_fusion), kind=kCustom, calls=%fused_computation.1 | custom fusion | bytes 3145920 | tf_op jit(solution)/shard_map/gather | solution.py:144
  42.0 0.0 copy-start.17
  42.0 0.7 fusion.63
  42.7 0.0 copy-start.11
  42.8 2.9 %fusion.17 = f32[13,128,128]{1,0,2:T(8,128)S(1)} fusion(f32[48,128,128]{2,1,0:T(8,128)S(1)} %fusion.63, s32[48]{0:T(128)S(1)} %copy-done.17, pred[48]{0:T(512)(128)(4,1)S(1)} %copy-done.9), kind=kOutput, calls=%fused_computation.21 | convolution fusion | flops 122684640 | bytes 3997936 | tf_op jit(solution)/shard_map/st,tfj->sjf/dot_general | solution.py:146
  45.7 0.1 slice.44
  45.7 0.1 copy.19
  45.9 0.0 copy-start.6
  45.9 1.4 %fusion.24 = bf16[1024,128]{1,0:T(8,128)(2,1)} fusion(bf16[384,128]{1,0:T(8,128)(2,1)S(1)} %bitcast.65, s32[384]{0:T(512)S(1)} %copy-done.11), kind=kOutput, calls=%fused_computation.27 | convolution fusion | flops 101187584 | bytes 361984 | tf_op jit(solution)/shard_map/dot_general | solution.py:70
  47.3 3.7 %all-to-all-done.2 = f32[32,8,256]{2,1,0:T(8,128)} async-done(((f32[32,8,256]{2,1,0:T(8,128)}), f32[32,8,256]{2,1,0:T(8,128)}, u32[]{:S(2)}, u32[]{:S(2)}) %all-to-all-start.2) | async-done | bytes 262176 | tf_op jit(solution)/shard_map/all_to_all | solution.py:15
  51.0 2.6 %all-to-all-start.1 = ((bf16[32,32,128]{2,1,0:T(8,128)(2,1)}), bf16[32,32,128]{2,1,0:T(8,128)(2,1)S(1)}, u32[]{:S(2)}, u32[]{:S(2)}) async-start(bf16[32,32,128]{2,1,0:T(8,128)(2,1)} %bitcast.17), calls=%async_computation.1 | async-start | bytes 524288 | tf_op jit(solution)/shard_map/all_to_all | solution.py:72
  53.6 0.3 copy.18
  53.9 1.0 %reduce_sum.9 = f32[8,256]{1,0:T(8,128)S(1)} reduce(f32[32,8,256]{2,1,0:T(8,128)} %all-to-all-done.2, f32[]{:T(128)} %constant.30.clone.1), dimensions={0}, to_apply=%region_0.1 | reduce | flops 63488 | bytes 270340 | tf_op jit(solution)/shard_map/reduce_sum | solution.py:15
  54.9 9.0 %all-to-all-done.1 = bf16[32,32,128]{2,1,0:T(8,128)(2,1)S(1)} async-done(((bf16[32,32,128]{2,1,0:T(8,128)(2,1)}), bf16[32,32,128]{2,1,0:T(8,128)(2,1)S(1)}, u32[]{:S(2)}, u32[]{:S(2)}) %all-to-all-start.1) | async-done | bytes 262176 | tf_op jit(solution)/shard_map/all_to_all | solution.py:72
  64.0 0.7 broadcast_in_dim.58
  64.7 2.6 %all-to-all-start.3 = ((f32[32,8,256]{2,1,0:T(8,128)}), f32[32,8,256]{2,1,0:T(8,128)S(1)}, u32[]{:S(2)}, u32[]{:S(2)}) async-start(f32[32,8,256]{2,1,0:T(8,128)} %broadcast_in_dim.58), calls=%async_computation.3 | async-start | bytes 524288 | tf_op jit(solution)/shard_map/all_to_all | solution.py:16
  67.3 1.4 %convolution_add_fusion.2 = f32[1280,128]{1,0:T(8,128)S(1)} fusion(f32[1280,128]{1,0:T(8,128)S(1)} %bitcast.60, bf16[1280,256]{1,0:T(8,128)(2,1)} %copy-done.3, bf16[128,256]{1,0:T(8,128)(2,1)} %param.17), kind=kOutput, calls=%fused_computation.9 | convolution fusion | flops 84049920 | bytes 2031616 | tf_op jit(solution)/shard_map/nh,fh->nf/dot_general | solution.py:141
  68.7 1.9 %fusion.5 = bf16[1280,128]{1,0:T(8,128)(2,1)} fusion(f32[1280,128]{1,0:T(8,128)S(1)} %convolution_add_fusion.2, bf16[384,128]{1,0:T(8,128)(2,1)S(1)} %bitcast.66, bf16[1024,128]{1,0:T(8,128)(2,1)S(1)} %bitcast.64, s32[384]{0:T(512)S(1)} %copy-done.13, s32[384]{0:T(512)S(1)} %copy-done.11, pred[384]{0:T(512)(128)(4,1)S(1)} %copy-done.18), kind=kOutput, calls=%fused_computation.11 | convolution fusion | flops 227803136 | bytes 1346944 | tf_op jit(solution)/shard_map/dot_general | solution.py:158
  70.6 7.1 %all-to-all-done.3 = f32[32,8,256]{2,1,0:T(8,128)S(1)} async-done(((f32[32,8,256]{2,1,0:T(8,128)}), f32[32,8,256]{2,1,0:T(8,128)S(1)}, u32[]{:S(2)}, u32[]{:S(2)}) %all-to-all-start.3) | async-done | bytes 262176 | tf_op jit(solution)/shard_map/all_to_all | solution.py:16
  77.6 0.7 slice_bitcast_fusion
  (41 shorter events, 0.1 us)
Async XLA Ops:
  0.6 12.0 %copy-start = (bf16[48,128,128]{2,1,0:T(8,128)(2,1)S(1)}, bf16[48,128,128]{2,1,0:T(8,128)(2,1)}, u32[]{:S(2)}) copy-start(bf16[48,128,128]{2,1,0:T(8,128)(2,1)} %param.13) | copy-start | bytes 4718596
  0.6 11.9 %copy-start.16 = (s32[48]{0:T(128)S(1)}, s32[48]{0:T(128)}, u32[]{:S(2)}) copy-start(s32[48]{0:T(128)} %param.15) | copy-start | bytes 580
  0.7 11.9 %copy-start.14 = (s32[48]{0:T(128)S(1)}, s32[48]{0:T(128)}, u32[]{:S(2)}) copy-start(s32[48]{0:T(128)} %param.14) | copy-start | bytes 580
  0.8 3.7 %copy-start.10 = (s32[384]{0:T(512)}, s32[384]{0:T(512)S(1)}, u32[]{:S(2)}) copy-start(s32[384]{0:T(512)S(1)} %add.79) | copy-start | bytes 4612
  1.6 11.0 %copy-start.12 = (s32[384]{0:T(512)}, s32[384]{0:T(512)S(1)}, u32[]{:S(2)}) copy-start(s32[384]{0:T(512)S(1)} %eq.71) | copy-start | bytes 4612
  3.1 1.5 %copy-start.20 = (bf16[384,128]{1,0:T(8,128)(2,1)}, bf16[384,128]{1,0:T(8,128)(2,1)S(1)}, u32[]{:S(2)}) copy-start(bf16[384,128]{1,0:T(8,128)(2,1)S(1)} %fusion.27) | copy-start | bytes 294916
  3.1 10.9 %copy-start.1 = (bf16[1280,128]{1,0:T(8,128)(2,1)S(1)}, bf16[1280,128]{1,0:T(8,128)(2,1)}, u32[]{:S(2)}) copy-start(bf16[1280,128]{1,0:T(8,128)(2,1)} %param.10) | copy-start | bytes 983044
  3.1 10.9 %copy-start.5 = (bf16[128,256]{1,0:T(8,128)(2,1)S(1)}, bf16[128,256]{1,0:T(8,128)(2,1)}, u32[]{:S(2)}) copy-start(bf16[128,256]{1,0:T(8,128)(2,1)} %param.17) | copy-start | bytes 196612
  4.6 17.7 %all-to-all-start = ((bf16[32,32,128]{2,1,0:T(8,128)(2,1)}), bf16[32,32,128]{2,1,0:T(8,128)(2,1)S(1)}, u32[]{:S(2)}, u32[]{:S(2)}) async-start(bf16[32,32,128]{2,1,0:T(8,128)(2,1)} %bitcast.2), calls=%async_computation | async-start | bytes 524288 | tf_op jit(solution)/shard_map/all_to_all | solution.py:72
  13.1 0.8 copy-start.8
  26.6 2.7 %copy-start.9 = (pred[48]{0:T(512)(128)(4,1)S(1)}, pred[48]{0:T(512)(128)(4,1)}, u32[]{:S(2)}) copy-start(pred[48]{0:T(512)(128)(4,1)} %copy-done.8) | copy-start | bytes 148
  26.6 2.7 %copy-start.15 = (s32[48]{0:T(128)S(1)}, s32[48]{0:T(128)}, u32[]{:S(2)}) copy-start(s32[48]{0:T(128)} %param.14) | copy-start | bytes 580
  33.3 2.9 %copy-start.2 = (bf16[1280,128]{1,0:T(8,128)(2,1)S(1)}, bf16[1280,128]{1,0:T(8,128)(2,1)}, u32[]{:S(2)}) copy-start(bf16[1280,128]{1,0:T(8,128)(2,1)} %param.10) | copy-start | bytes 983044
  33.3 2.9 %copy-start.4 = (bf16[10,128,128]{2,1,0:T(8,128)(2,1)S(1)}, bf16[10,128,128]{2,1,0:T(8,128)(2,1)}, u32[]{:S(2)}) copy-start(bf16[10,128,128]{2,1,0:T(8,128)(2,1)} %copy.17) | copy-start | bytes 983044
  36.2 5.0 %copy-start.3 = (bf16[1280,256]{1,0:T(8,128)(2,1)}, bf16[1280,256]{1,0:T(8,128)(2,1)S(1)}, u32[]{:S(2)}) copy-start(bf16[1280,256]{1,0:T(8,128)(2,1)S(1)} %get-tuple-element.4) | copy-start | bytes 1966084
  36.2 4.6 %copy-start.19 = (bf16[128,256]{1,0:T(8,128)(2,1)S(1)}, bf16[128,256]{1,0:T(8,128)(2,1)}, u32[]{:S(2)}) copy-start(bf16[128,256]{1,0:T(8,128)(2,1)} %param.18) | copy-start | bytes 196612
  37.3 13.7 %all-to-all-start.2 = ((f32[32,8,256]{2,1,0:T(8,128)}), f32[32,8,256]{2,1,0:T(8,128)}, u32[]{:S(2)}, u32[]{:S(2)}) async-start(f32[32,8,256]{2,1,0:T(8,128)} %convolution_bitcast_fusion), calls=%async_computation.2 | async-start | bytes 524288 | tf_op jit(solution)/shard_map/all_to_all | solution.py:15
  42.0 0.7 copy-start.17
  42.7 3.2 %copy-start.11 = (s32[384]{0:T(512)S(1)}, s32[384]{0:T(512)}, u32[]{:S(2)}) copy-start(s32[384]{0:T(512)} %copy-done.10) | copy-start | bytes 4612
  45.9 7.7 %copy-start.6 = (bf16[3,128,128]{2,1,0:T(8,128)(2,1)}, bf16[3,128,128]{2,1,0:T(8,128)(2,1)S(1)}, u32[]{:S(2)}) copy-start(bf16[3,128,128]{2,1,0:T(8,128)(2,1)S(1)} %copy.19) | copy-start | bytes 294916
  51.0 13.0 %all-to-all-start.1 = ((bf16[32,32,128]{2,1,0:T(8,128)(2,1)}), bf16[32,32,128]{2,1,0:T(8,128)(2,1)S(1)}, u32[]{:S(2)}, u32[]{:S(2)}) async-start(bf16[32,32,128]{2,1,0:T(8,128)(2,1)} %bitcast.17), calls=%async_computation.1 | async-start | bytes 524288 | tf_op jit(solution)/shard_map/all_to_all | solution.py:72
  53.9 14.8 %copy-start.7 = (bf16[3,128,128]{2,1,0:T(8,128)(2,1)S(1)}, bf16[3,128,128]{2,1,0:T(8,128)(2,1)}, u32[]{:S(2)}) copy-start(bf16[3,128,128]{2,1,0:T(8,128)(2,1)} %copy-done.6) | copy-start | bytes 294916
  53.9 14.8 %copy-start.13 = (s32[384]{0:T(512)S(1)}, s32[384]{0:T(512)}, u32[]{:S(2)}) copy-start(s32[384]{0:T(512)} %copy-done.12) | copy-start | bytes 4612
  53.9 14.8 %copy-start.18 = (pred[384]{0:T(512)(128)(4,1)S(1)}, pred[384]{0:T(512)(128)(4,1)}, u32[]{:S(2)}) copy-start(pred[384]{0:T(512)(128)(4,1)} %broadcast_in_dim.28) | copy-start | bytes 1156
  64.7 13.0 %all-to-all-start.3 = ((f32[32,8,256]{2,1,0:T(8,128)}), f32[32,8,256]{2,1,0:T(8,128)S(1)}, u32[]{:S(2)}, u32[]{:S(2)}) async-start(f32[32,8,256]{2,1,0:T(8,128)} %broadcast_in_dim.58), calls=%async_computation.3 | async-start | bytes 524288 | tf_op jit(solution)/shard_map/all_to_all | solution.py:16

commit v13 on v11

--- a/solution.py
+++ b/solution.py
@@ -35,6 +35,17 @@
     from_dom = lax.dynamic_update_slice_in_dim(from_dom, own_dom, a, axis=0)
     from_grp = lax.dynamic_index_in_dim(got, a, axis=0, keepdims=False)
     return from_dom, from_grp
+
+
+ADJ_LIMIT = 4 << 20
+
+
+def split_bf16(value):
+    hi = value.astype(jnp.bfloat16)
+    rest = value - hi.astype(jnp.float32)
+    mid = rest.astype(jnp.bfloat16)
+    low = (rest - mid.astype(jnp.float32)).astype(jnp.bfloat16)
+    return hi, mid, low
 
 
 def one_hot_rows(index, count):
@@ -90,19 +101,9 @@
     pick = one_hot_rows(jnp.concatenate([dom_index, grp_index], axis=0), node_count)
     sent = jnp.dot(pick, features, preferred_element_type=jnp.float32).astype(jnp.bfloat16)
     table_bytes = n_dom * n_grp * bnd * (n_dom + n_grp) * bnd * 2
-    if table_bytes <= PLACE_LIMIT:
-        place, keep = placement(n_dom, n_grp, bnd)
-        got = swap(sent, place, keep)
-        recv_dom, recv_grp = got[: n_dom * bnd], got[n_dom * bnd :]
-    else:
-        sent = sent.reshape(n_dom + n_grp, bnd, width)
-        recv_dom, recv_grp = exchange(sent[:n_dom], sent[n_dom:])
-    source = jnp.concatenate(
-        [features, recv_dom.reshape(-1, width), recv_grp.reshape(-1, width)], axis=0
-    )
-    source = source.reshape(-1, tile_size, width)
-    source_count = source.shape[0]
     slot_count = tile_vals.shape[0]
+    source_count = block_count + (n_dom + n_grp) * bnd // tile_size
+    remote_count = source_count - block_count
     usable = jnp.arange(slot_count, dtype=jnp.int32) < tile_count[0]
     to_target = (
         (tile_tgt[None, :] == jnp.arange(block_count, dtype=jnp.int32)[:, None]) & usable[None, :]
@@ -110,14 +111,49 @@
     to_source = (
         (tile_src[None, :] == jnp.arange(source_count, dtype=jnp.int32)[:, None]) & usable[None, :]
     ).astype(jnp.float32)
-    products = jnp.einsum(
-        "tjf,tij->tfi", source[tile_src], tile_vals, preferred_element_type=jnp.float32
-    )
-    summed = jnp.einsum("bt,tfi->bif", to_target, products, precision=lax.Precision.HIGHEST)
     unit_column = jnp.ones((tile_size,), jnp.bfloat16)
     row_sums = jnp.einsum("tij,j->ti", tile_vals, unit_column, preferred_element_type=jnp.float32)
     degree = jnp.dot(to_target, row_sums, precision=lax.Precision.HIGHEST)
-    agg = (summed / degree[:, :, None]).reshape(node_count, width).astype(jnp.bfloat16)
+    split = table_bytes <= PLACE_LIMIT and (
+        block_count * remote_count * tile_size * tile_size * 4 <= ADJ_LIMIT
+    )
+    if split:
+        is_own = tile_src < block_count
+        own_src = jnp.where(is_own, tile_src, 0)
+        own_target = to_target * is_own.astype(jnp.float32)[None, :]
+        remote_of = (
+            tile_src[None, :] == block_count + jnp.arange(remote_count, dtype=jnp.int32)[:, None]
+        ).astype(jnp.float32)
+        pair = (to_target[:, None, :] * remote_of[None, :, :]).reshape(-1, slot_count)
+        adj = jnp.dot(
+            pair.astype(jnp.bfloat16), tile_vals.reshape(slot_count, -1),
+            preferred_element_type=jnp.float32,
+        )
+        adj = adj.reshape(block_count, remote_count, tile_size, tile_size).transpose(0, 2, 1, 3)
+        adj = adj.reshape(node_count, remote_count * tile_size)
+        pieces = split_bf16(adj)
+        own_blocks = features.reshape(block_count, tile_size, width)
+        products = jnp.einsum(
+            "tjf,tij->tfi", own_blocks[own_src], tile_vals, preferred_element_type=jnp.float32
+        )
+        summed = jnp.einsum("bt,tfi->bif", own_target, products, precision=lax.Precision.HIGHEST)
+        place, keep = placement(n_dom, n_grp, bnd)
+        received = swap(sent, place, keep)
+        far = sum(jnp.dot(p, received, preferred_element_type=jnp.float32) for p in pieces)
+        summed = summed.reshape(node_count, width) + far
+    else:
+        sent = sent.reshape(n_dom + n_grp, bnd, width)
+        recv_dom, recv_grp = exchange(sent[:n_dom], sent[n_dom:])
+        source = jnp.concatenate(
+            [features, recv_dom.reshape(-1, width), recv_grp.reshape(-1, width)], axis=0
+        )
+        source = source.reshape(-1, tile_size, width)
+        products = jnp.einsum(
+            "tjf,tij->tfi", source[tile_src], tile_vals, preferred_element_type=jnp.float32
+        )
+        summed = jnp.einsum("bt,tfi->bif", to_target, products, precision=lax.Precision.HIGHEST)
+        summed = summed.reshape(node_count, width)
+    agg = (summed / degree.reshape(-1)[:, None]).astype(jnp.bfloat16)
     preact = jnp.dot(features, w_self, preferred_element_type=jnp.float32) + jnp.dot(
         agg, w_neigh, preferred_element_type=jnp.float32
     )
@@ -137,7 +173,7 @@
         "st,tfj->sjf", to_source, backward, precision=lax.Precision.HIGHEST
     ).reshape(-1, width)
     remote = grad_source[node_count:].astype(jnp.bfloat16)
-    if table_bytes <= PLACE_LIMIT:
+    if split:
         returned = swap(remote, place, keep)
     else:
         remote = remote.reshape(n_dom + n_grp, bnd, width)

time: 78.5 us -> 90.9 us (1.16)
  matrix products: 23.3 us -> 31 us
  local copies, waits for them, and re-layouts: 8.77 us -> 15.8 us
  waiting for transfers between devices: 26.2 us -> 22.2 us
  starting transfers between devices: 16.1 us -> 18.5 us
    transpose x0 -> x2, local copies, waits for them, and re-layouts: none -> 5.94 us  [the longest x1 4.79 us: per_device(): adj.reshape(block_count, remote_count, tile_size, tile_size)]
    all_to_all x2, waiting for transfers between devices: 15.5 us -> 9.91 us  [swap(): lax.all_to_all(buf, ('dom', 'grp'), 0, 0, tiled=True)]
    dot_general x2 -> x6, matrix products: 5.59 us -> 10.8 us  [the longest x1 3.5 us: per_device(): jnp.einsum('bt,tfi->bif', own_target, products, precision=lax.Precision.H...]
    dot_general x1, matrix products: 0.69 us -> 3.93 us  [per_device(): jnp.einsum('tif,tij->tfj', picked, tile_vals, preferred_element_type=jnp....]
    all_to_all x1, starting transfers between devices: 3.48 us -> 5.79 us  [weight_sum(): lax.all_to_all(chunks, axes, 0, 0, tiled=True)]
    unnamed x24 -> x26, local copies, waits for them, and re-layouts: 0.07 us -> 2.34 us
    dot_general x1, matrix products: 2.91 us -> 4.63 us  [per_device(): jnp.einsum('st,tfj->sjf', to_source, backward, precision=lax.Precision.HI...]
    dot_general x1, matrix products: 3.14 us -> 1.65 us  [per_device(): jnp.dot(agg, w_neigh, preferred_element_type=jnp.float32)]
  transfers between devices with their start and end apart: 4 -> 4, of which waited for: 4 -> 3; matrix products, arithmetic and copies ran while one was open for 18% -> 29% of each run, Pallas kernels for 0% -> 0%
where the time goes in v13:
time: 90.9 us; the launch traced here: 90.3 us
  matrix products  31 us (34%)
  waiting for transfers between devices  22.2 us (24%)
  starting transfers between devices  18.5 us (20%)
  local copies, waits for them, and re-layouts  15.8 us (17%)
  between operations  1.57 us (2%)
  other arithmetic  1.22 us (1%)
    all_to_all x2, starting transfers between devices, swap(): lax.all_to_all(buf, ('dom', 'grp'), 0, 0, tiled=True)  10.1 us
    all_to_all x2, waiting for transfers between devices, swap(): lax.all_to_all(buf, ('dom', 'grp'), 0, 0, tiled=True)  9.91 us
    all_to_all x1, waiting for transfers between devices, weight_sum(): total = lax.all_to_all(spread, axes, 0, 0, tiled=True).reshape(-1)  8.18 us
    all_to_all x1, starting transfers between devices, weight_sum(): lax.all_to_all(chunks, axes, 0, 0, tiled=True)  5.79 us
    transpose x1, local copies, waits for them, and re-layouts, per_device(): adj.reshape(block_count, remote_count, tile_size, tile_size)  4.79 us
    dot_general x1, matrix products, per_device(): jnp.einsum('st,tfj->sjf', to_source, backward, precision=lax.Precision.HI...  4.63 us
    all_to_all x1, waiting for transfers between devices, weight_sum(): lax.all_to_all(chunks, axes, 0, 0, tiled=True)  4.12 us
    dot_general x1, matrix products, per_device(): jnp.einsum('tif,tij->tfj', picked, tile_vals, preferred_element_type=jnp....  3.93 us
  transfers between devices with their start and end apart: 4, of which 3 were waited for; matrix products, arithmetic and copies ran while one was open for 29% of the time, Pallas kernels for 0%

profile of v13, /device:TPU:0, one launch (start us, length us, event | category | flops | bytes accessed | tf_op | source)
XLA Modules:
  0.0 90.3 jit_solution(15721106923542896818)
XLA Ops:
  0.7 0.8 pad_add_fusion
  1.5 0.1 eq.98
  1.7 0.1 add.92
  1.8 0.5 fusion.27
  2.3 0.6 copy-done.11
  2.9 1.4 %fusion.23 = bf16[1024,128]{1,0:T(8,128)(2,1)} fusion(bf16[384,128]{1,0:T(8,128)(2,1)S(1)} %fusion.27, s32[384]{0:T(512)S(1)} %add.92), kind=kOutput, calls=%fused_computation.38 | convolution fusion | flops 101187584 | bytes 361984 | tf_op jit(solution)/shard_map/dot_general | solution.py:74
  4.3 7.4 %all-to-all-start = ((bf16[32,32,128]{2,1,0:T(8,128)(2,1)}), bf16[32,32,128]{2,1,0:T(8,128)(2,1)}, u32[]{:S(2)}, u32[]{:S(2)}) async-start(bf16[32,32,128]{2,1,0:T(8,128)(2,1)} %bitcast.12), calls=%async_computation | async-start | bytes 524288 | tf_op jit(solution)/shard_map/all_to_all | solution.py:76
  11.8 0.5 fusion.62
  12.3 0.9 gather_fusion
  13.2 1.2 %fusion.67 = f32[48,128,128]{2,1,0:T(8,128)S(1)} fusion(bf16[48,128,128]{2,1,0:T(8,128)(2,1)S(1)} %gather_fusion, bf16[48,128,128]{2,1,0:T(8,128)(2,1)S(1)} %copy-done.1), kind=kOutput, calls=%fused_computation.98 | convolution fusion | flops 201326592 | bytes 6291456 | tf_op jit(solution)/shard_map/tjf,tij->tfi/dot_general | solution.py:136
  15.2 3.5 %fusion.15 = f32[10,128,128]{1,0,2:T(8,128)S(1)} fusion(f32[48,128,128]{2,1,0:T(8,128)S(1)} %fusion.67, f32[48]{0:T(128)S(1)} %compare_convert_fusion, s32[48]{0:T(128)S(1)} %copy-done.7, pred[48]{0:T(512)(128)(4,1)S(1)} %iota_compare_fusion.27), kind=kOutput, calls=%fused_computation.31 | convolution fusion | flops 94373280 | bytes 3801520 | tf_op jit(solution)/shard_map/bt,tfi->bif/dot_general | solution.py:139
  18.7 3.0 %convolution_bitcast_fusion = f32[10,128,3,128]{3,0,1,2:T(8,128)} fusion(f32[3,48]{1,0:T(4,128)S(1)} %compare_convert_fusion.1, f32[10,48]{1,0:T(8,128)S(1)} %fusion.47, bf16[6,8,128,128]{3,2,1,0:T(8,128)(2,1)S(1)} %bitcast.96), kind=kOutput, calls=%fused_computation.22 | convolution fusion | flops 47188800 | bytes 3541440 | tf_op jit(solution)/shard_map/dot_general | solution.py:128
  21.7 1.2 %copy.32 = f32[10,128,128]{2,1,0:T(8,128)} copy(f32[10,128,128]{1,0,2:T(8,128)S(1)} %fusion.15) | data formatting | bytes 1310720 | tf_op jit(solution)/shard_map/bt,tfi->bif/transpose | solution.py:139
  23.0 0.1 broadcast_in_dim.34
  23.1 4.8 %copy.34 = f32[10,128,3,128]{3,2,1,0:T(4,128)} copy(f32[10,128,3,128]{3,0,1,2:T(8,128)} %convolution_bitcast_fusion) | data formatting | bytes 3932160 | tf_op jit(solution)/shard_map/transpose | solution.py:132
  27.9 0.1 convolution_bitcast_fusion.2
  28.0 1.4 %fusion.66 = f32[1280,256]{1,0:T(8,128)} fusion(bf16[1280,128]{1,0:T(8,128)(2,1)S(1)} %copy-done, bf16[128,256]{1,0:T(8,128)(2,1)S(1)} %copy-done.5), kind=kOutput, calls=%fused_computation.97 | convolution fusion | flops 83886080 | bytes 1703936 | tf_op jit(solution)/shard_map/dot_general | solution.py:157
  29.4 1.5 %fusion.29 = bf16[384,128]{1,0:T(8,128)(2,1)S(1)} fusion(bf16[384,128]{1,0:T(8,128)(2,1)S(1)} %copy-done.12, bf16[1024,128]{1,0:T(8,128)(2,1)} %bitcast.13, s32[384]{0:T(512)S(1)} %add.92, pred[384]{0:T(512)(128)(4,1)S(1)} %broadcast_in_dim.34), kind=kOutput, calls=%fused_computation.45 | convolution fusion | flops 101154816 | bytes 460672 | tf_op jit(solution)/shard_map/dot_general | solution.py:77
  30.9 2.2 %fusion.21 = f32[1280,128]{1,0:T(8,128)S(1)} fusion(bf16[384,128]{1,0:T(8,128)(2,1)S(1)} %fusion.29, f32[160,8,3,128]{3,2,1,0:T(4,128)} %bitcast.97), kind=kOutput, calls=%fused_computation.33 | convolution fusion | flops 125829120 | bytes 2719744 | tf_op jit(solution)/shard_map/dot_general | solution.py:142
  33.1 0.4 convolution_add_fusion.4
  33.5 0.7 copy-done.4
  34.2 0.5 fusion.6
  34.7 0.8 copy-done.3
  35.5 0.2 copy-done.9
  35.7 1.6 %multiply_convert_fusion = (bf16[1280,256]{1,0:T(8,128)(2,1)S(1)}, bf16[1280,256]{1,0:T(8,128)(2,1)}) fusion(bf16[1280,256]{1,0:T(8,128)(2,1)S(1)} %copy-done.9, f32[1280,256]{1,0:T(8,128)S(1)} %copy-done.3, bf16[1280,128]{1,0:T(8,128)(2,1)S(1)} %fusion.6, bf16[128,256]{1,0:T(8,128)(2,1)S(1)} %copy-done.10), kind=kOutput, calls=%fused_computation.34 | convolution fusion | flops 88145920 | bytes 3670016 | tf_op jit(solution)/shard_map/dot_general | solution.py:157
  37.3 0.3 fusion.7
  37.7 0.3 fusion.69
  38.0 0.3 convolution_bitcast_fusion.1
  38.3 2.0 %gather_fusion.1 = bf16[48,128,128]{2,1,0:T(8,128)(2,1)} fusion(bf16[10,128,128]{2,1,0:T(8,128)(2,1)S(1)} %bitcast.100, s32[1024]{0:T(1024)S(1)} %pad_clamp_fusion), kind=kCustom, calls=%fused_computation.1 | custom fusion | bytes 3145920 | tf_op jit(solution)/shard_map/gather | solution.py:170
  40.2 3.9 %fusion.68 = f32[48,128,128]{2,1,0:T(8,128)} fusion(bf16[48,128,128]{2,1,0:T(8,128)(2,1)} %gather_fusion.1, bf16[48,128,128]{2,1,0:T(8,128)(2,1)S(1)} %copy-done.1), kind=kOutput, calls=%fused_computation.99 | convolution fusion | flops 201326592 | bytes 6291456 | tf_op jit(solution)/shard_map/tif,tij->tfj/dot_general | solution.py:171
  44.2 1.0 %all_to_all.21 = f32[32,1,2048]{2,1,0:T(1,128)} reshape(f32[256,256]{1,0:T(8,128)S(1)} %pad_maximum_fusion) | data formatting | bytes 524288 | tf_op jit(solution)/shard_map/all_to_all | solution.py:15
  45.2 5.8 %all-to-all-start.2 = ((f32[32,1,2048]{2,1,0:T(1,128)}), f32[32,1,2048]{2,1,0:T(1,128)S(1)}, u32[]{:S(2)}, u32[]{:S(2)}) async-start(f32[32,1,2048]{2,1,0:T(1,128)} %all_to_all.21), calls=%async_computation.2 | async-start | bytes 524288 | tf_op jit(solution)/shard_map/all_to_all | solution.py:15
  51.0 4.6 %fusion.18 = f32[13,128,128]{1,0,2:T(8,128)S(1)} fusion(f32[48,128,128]{2,1,0:T(8,128)} %fusion.68, s32[48]{0:T(128)S(1)} %copy-done.8, pred[48]{0:T(512)(128)(4,1)S(1)} %iota_compare_fusion.27), kind=kOutput, calls=%fused_computation.32 | convolution fusion | flops 122684640 | bytes 3997936 | tf_op jit(solution)/shard_map/st,tfj->sjf/dot_general | solution.py:172
  55.7 0.1 copy.38
  55.8 1.4 %fusion.24 = bf16[1024,128]{1,0:T(8,128)(2,1)} fusion(bf16[384,128]{1,0:T(8,128)(2,1)S(1)} %bitcast.105, s32[384]{0:T(512)S(1)} %add.92), kind=kOutput, calls=%fused_computation.39 | convolution fusion | flops 101187584 | bytes 361984 | tf_op jit(solution)/shard_map/dot_general | solution.py:74
  57.2 4.1 %all-to-all-done.2 = f32[32,1,2048]{2,1,0:T(1,128)S(1)} async-done(((f32[32,1,2048]{2,1,0:T(1,128)}), f32[32,1,2048]{2,1,0:T(1,128)S(1)}, u32[]{:S(2)}, u32[]{:S(2)}) %all-to-all-start.2) | async-done | bytes 262176 | tf_op jit(solution)/shard_map/all_to_all | solution.py:15
  61.3 2.7 %all-to-all-start.1 = ((bf16[32,32,128]{2,1,0:T(8,128)(2,1)}), bf16[32,32,128]{2,1,0:T(8,128)(2,1)S(1)}, u32[]{:S(2)}, u32[]{:S(2)}) async-start(bf16[32,32,128]{2,1,0:T(8,128)(2,1)} %bitcast.22), calls=%async_computation.1 | async-start | bytes 524288 | tf_op jit(solution)/shard_map/all_to_all | solution.py:76
  64.1 0.3 copy.37
  64.4 0.2 reduce_sum.9
  64.6 9.9 %all-to-all-done.1 = bf16[32,32,128]{2,1,0:T(8,128)(2,1)S(1)} async-done(((bf16[32,32,128]{2,1,0:T(8,128)(2,1)}), bf16[32,32,128]{2,1,0:T(8,128)(2,1)S(1)}, u32[]{:S(2)}, u32[]{:S(2)}) %all-to-all-start.1) | async-done | bytes 262176 | tf_op jit(solution)/shard_map/all_to_all | solution.py:76
  74.5 0.8 broadcast_in_dim.67
  75.3 2.6 %all-to-all-start.3 = ((f32[32,1,2048]{2,1,0:T(1,128)}), f32[32,1,2048]{2,1,0:T(1,128)S(1)}, u32[]{:S(2)}, u32[]{:S(2)}) async-start(f32[32,1,2048]{2,1,0:T(1,128)} %broadcast_in_dim.67), calls=%async_computation.3 | async-start | bytes 524288 | tf_op jit(solution)/shard_map/all_to_all | solution.py:17
  77.9 0.3 convolution_add_fusion.2
  78.2 1.9 %fusion.8 = bf16[1280,128]{1,0:T(8,128)(2,1)} fusion(f32[1280,128]{1,0:T(8,128)S(1)} %convolution_add_fusion.2, bf16[384,128]{1,0:T(8,128)(2,1)S(1)} %bitcast.106, bf16[1024,128]{1,0:T(8,128)(2,1)S(1)} %bitcast.104, s32[384]{0:T(512)S(1)} %eq.98, s32[384]{0:T(512)S(1)} %add.92, pred[384]{0:T(512)(128)(4,1)S(1)} %broadcast_in_dim.34), kind=kOutput, calls=%fused_computation.16 | convolution fusion | flops 227803136 | bytes 1346944 | tf_op jit(solution)/shard_map/dot_general | solution.py:184
  80.1 8.2 %all-to-all-done.3 = f32[32,1,2048]{2,1,0:T(1,128)S(1)} async-done(((f32[32,1,2048]{2,1,0:T(1,128)}), f32[32,1,2048]{2,1,0:T(1,128)S(1)}, u32[]{:S(2)}, u32[]{:S(2)}) %all-to-all-start.3) | async-done | bytes 262176 | tf_op jit(solution)/shard_map/all_to_all | solution.py:17
  88.3 0.7 slice_reduce_fusion
  88.9 0.7 slice.29
  89.6 0.7 slice.31
  (38 shorter events, 0.4 us)
Async XLA Ops:
  0.6 1.1 %copy-start = (bf16[1280,128]{1,0:T(8,128)(2,1)S(1)}, bf16[1280,128]{1,0:T(8,128)(2,1)}, u32[]{:S(2)}) copy-start(bf16[1280,128]{1,0:T(8,128)(2,1)} %param.10) | copy-start | bytes 983044
  0.6 11.1 %copy-start.8 = (s32[48]{0:T(128)S(1)}, s32[48]{0:T(128)}, u32[]{:S(2)}) copy-start(s32[48]{0:T(128)} %param.15) | copy-start | bytes 580
  0.7 11.2 %copy-start.1 = (bf16[48,128,128]{2,1,0:T(8,128)(2,1)S(1)}, bf16[48,128,128]{2,1,0:T(8,128)(2,1)}, u32[]{:S(2)}) copy-start(bf16[48,128,128]{2,1,0:T(8,128)(2,1)} %param.13) | copy-start | bytes 4718596
  2.3 0.6 copy-start.11
  4.3 25.1 %all-to-all-start = ((bf16[32,32,128]{2,1,0:T(8,128)(2,1)}), bf16[32,32,128]{2,1,0:T(8,128)(2,1)}, u32[]{:S(2)}, u32[]{:S(2)}) async-start(bf16[32,32,128]{2,1,0:T(8,128)(2,1)} %bitcast.12), calls=%async_computation | async-start | bytes 524288 | tf_op jit(solution)/shard_map/all_to_all | solution.py:76
  13.2 2.0 %copy-start.7 = (s32[48]{0:T(128)S(1)}, s32[48]{0:T(128)}, u32[]{:S(2)}) copy-start(s32[48]{0:T(128)} %param.14) | copy-start | bytes 580
  23.1 4.9 %copy-start.5 = (bf16[128,256]{1,0:T(8,128)(2,1)S(1)}, bf16[128,256]{1,0:T(8,128)(2,1)}, u32[]{:S(2)}) copy-start(bf16[128,256]{1,0:T(8,128)(2,1)} %param.17) | copy-start | bytes 196612
  27.8 1.5 %copy-start.12 = (bf16[384,128]{1,0:T(8,128)(2,1)S(1)}, bf16[384,128]{1,0:T(8,128)(2,1)}, u32[]{:S(2)}) copy-start(bf16[384,128]{1,0:T(8,128)(2,1)} %copy-done.11) | copy-start | bytes 294916
  29.4 3.7 %copy-start.2 = (f32[10,128,3,128]{3,2,1,0:T(4,128)S(1)}, f32[10,128,3,128]{3,2,1,0:T(4,128)}, u32[]{:S(2)}) copy-start(f32[10,128,3,128]{3,2,1,0:T(4,128)} %copy.34) | copy-start | bytes 5898244
  33.1 1.1 %copy-start.4 = (f32[10,128,128]{2,1,0:T(8,128)S(1)}, f32[10,128,128]{2,1,0:T(8,128)}, u32[]{:S(2)}) copy-start(f32[10,128,128]{2,1,0:T(8,128)} %copy.32) | copy-start | bytes 1966084
  34.2 1.3 %copy-start.3 = (f32[1280,256]{1,0:T(8,128)S(1)}, f32[1280,256]{1,0:T(8,128)}, u32[]{:S(2)}) copy-start(f32[1280,256]{1,0:T(8,128)} %fusion.66) | copy-start | bytes 3932164
  34.2 1.5 %copy-start.9 = (bf16[1280,256]{1,0:T(8,128)(2,1)S(1)}, bf16[1280,256]{1,0:T(8,128)(2,1)}, u32[]{:S(2)}) copy-start(bf16[1280,256]{1,0:T(8,128)(2,1)} %param.19) | copy-start | bytes 1966084
  34.2 1.5 %copy-start.10 = (bf16[128,256]{1,0:T(8,128)(2,1)S(1)}, bf16[128,256]{1,0:T(8,128)(2,1)}, u32[]{:S(2)}) copy-start(bf16[128,256]{1,0:T(8,128)(2,1)} %param.18) | copy-start | bytes 196612
  45.2 16.2 %all-to-all-start.2 = ((f32[32,1,2048]{2,1,0:T(1,128)}), f32[32,1,2048]{2,1,0:T(1,128)S(1)}, u32[]{:S(2)}, u32[]{:S(2)}) async-start(f32[32,1,2048]{2,1,0:T(1,128)} %all_to_all.21), calls=%async_computation.2 | async-start | bytes 524288 | tf_op jit(solution)/shard_map/all_to_all | solution.py:15
  61.3 16.5 %copy-start.6 = (bf16[128,256]{1,0:T(8,128)(2,1)S(1)}, bf16[128,256]{1,0:T(8,128)(2,1)}, u32[]{:S(2)}) copy-start(bf16[128,256]{1,0:T(8,128)(2,1)} %param.17) | copy-start | bytes 196612
  61.3 13.1 %all-to-all-start.1 = ((bf16[32,32,128]{2,1,0:T(8,128)(2,1)}), bf16[32,32,128]{2,1,0:T(8,128)(2,1)S(1)}, u32[]{:S(2)}, u32[]{:S(2)}) async-start(bf16[32,32,128]{2,1,0:T(8,128)(2,1)} %bitcast.22), calls=%async_computation.1 | async-start | bytes 524288 | tf_op jit(solution)/shard_map/all_to_all | solution.py:76
  75.3 13.0 %all-to-all-start.3 = ((f32[32,1,2048]{2,1,0:T(1,128)}), f32[32,1,2048]{2,1,0:T(1,128)S(1)}, u32[]{:S(2)}, u32[]{:S(2)}) async-start(f32[32,1,2048]{2,1,0:T(1,128)} %broadcast_in_dim.67), calls=%async_computation.3 | async-start | bytes 524288 | tf_op jit(solution)/shard_map/all_to_all | solution.py:17

commit v14 on v11

--- a/solution.py
+++ b/solution.py
@@ -113,7 +113,7 @@
     products = jnp.einsum(
         "tjf,tij->tfi", source[tile_src], tile_vals, preferred_element_type=jnp.float32
     )
-    summed = jnp.einsum("bt,tfi->bif", to_target, products, precision=lax.Precision.HIGHEST)
+    summed = jnp.einsum("bt,tfi->bif", to_target, products, precision=lax.Precision.HIGH)
     unit_column = jnp.ones((tile_size,), jnp.bfloat16)
     row_sums = jnp.einsum("tij,j->ti", tile_vals, unit_column, preferred_element_type=jnp.float32)
     degree = jnp.dot(to_target, row_sums, precision=lax.Precision.HIGHEST)
@@ -134,7 +134,7 @@
     picked = grad_agg.reshape(block_count, tile_size, width)[tile_tgt]
     backward = jnp.einsum("tif,tij->tfj", picked, tile_vals, preferred_element_type=jnp.float32)
     grad_source = jnp.einsum(
-        "st,tfj->sjf", to_source, backward, precision=lax.Precision.HIGHEST
+        "st,tfj->sjf", to_source, backward, precision=lax.Precision.HIGH
     ).reshape(-1, width)
     remote = grad_source[node_count:].astype(jnp.bfloat16)
     if table_bytes <= PLACE_LIMIT:

time: 78.5 us -> 78 us (level)
  matrix products: 23.3 us -> 22.2 us
    dot_general x2, matrix products: 5.85 us -> 4.73 us  [the longest x1 2.38 us: per_device(): jnp.einsum('bt,tfi->bif', to_target, products, precision=lax.Precision.HIGH)]
where the time goes in v14:
time: 78 us; the launch traced here: 77.5 us
  waiting for transfers between devices  26.8 us (34%)
  matrix products  22.2 us (28%)
  starting transfers between devices  16.1 us (21%)
  local copies, waits for them, and re-layouts  8.77 us (11%)
  other arithmetic  2.01 us (3%)
  between operations  1.61 us (2%)
    all_to_all x2, waiting for transfers between devices, swap(): lax.all_to_all(buf, ('dom', 'grp'), 0, 0, tiled=True)  15.5 us
    all_to_all x2, starting transfers between devices, swap(): lax.all_to_all(buf, ('dom', 'grp'), 0, 0, tiled=True)  10 us
    all_to_all x1, waiting for transfers between devices, weight_sum(): total = lax.all_to_all(spread, axes, 0, 0, tiled=True).reshape(-1)  7.04 us
    all_to_all x1, waiting for transfers between devices, weight_sum(): lax.all_to_all(chunks, axes, 0, 0, tiled=True)  4.28 us
    all_to_all x1, starting transfers between devices, weight_sum(): lax.all_to_all(chunks, axes, 0, 0, tiled=True)  3.48 us
    dot_general x1, matrix products, per_device(): jnp.dot(agg, w_neigh, preferred_element_type=jnp.float32)  3.14 us
    dot_general x2, matrix products, swap(): lax.dot_general(place, table, (((0,), (0,)), ((), ())), preferred_element...  2.82 us
    dot_general x1, matrix products, per_device(): jnp.einsum('tjf,tij->tfi', source[tile_src], tile_vals, preferred_element...  2.65 us
  transfers between devices with their start and end apart: 4, of which 4 were waited for; matrix products, arithmetic and copies ran while one was open for 18% of the time, Pallas kernels for 0%

profile of v14, /device:TPU:0, one launch (start us, length us, event | category | flops | bytes accessed | tf_op | source)
XLA Modules:
  0.0 77.5 jit_solution(9890400680005796512)
XLA Ops:
  0.6 0.0 copy-start
  0.7 0.1 iota_add_fusion
  0.8 0.1 add.79
  0.8 0.7 pad_add_fusion
  1.5 0.1 eq.71
  1.6 1.5 %fusion.27 = bf16[384,128]{1,0:T(8,128)(2,1)S(1)} fusion(bf16[1280,128]{1,0:T(8,128)(2,1)} %param.10, s32[384]{0:T(512)S(1)} %eq.71), kind=kOutput, calls=%fused_computation.30 | convolution fusion | flops 126369792 | bytes 427520 | tf_op jit(solution)/shard_map/dot_general | solution.py:91
  3.1 0.0 copy-start.3
  3.1 0.0 copy-start.4
  3.1 1.4 %fusion.23 = bf16[1024,128]{1,0:T(8,128)(2,1)} fusion(bf16[384,128]{1,0:T(8,128)(2,1)S(1)} %fusion.27, s32[384]{0:T(512)S(1)} %add.79), kind=kOutput, calls=%fused_computation.26 | convolution fusion | flops 101187584 | bytes 361984 | tf_op jit(solution)/shard_map/dot_general | solution.py:63
  4.5 7.3 %all-to-all-start = ((bf16[32,32,128]{2,1,0:T(8,128)(2,1)}), bf16[32,32,128]{2,1,0:T(8,128)(2,1)S(1)}, u32[]{:S(2)}, u32[]{:S(2)}) async-start(bf16[32,32,128]{2,1,0:T(8,128)(2,1)} %bitcast.2), calls=%async_computation | async-start | bytes 524288 | tf_op jit(solution)/shard_map/all_to_all | solution.py:65
  12.6 0.5 fusion.54
  13.1 0.1 broadcast_in_dim.27
  13.2 0.1 broadcast_in_dim.28
  13.3 0.1 fusion.39
  13.4 0.0 copy-done.4
  13.4 1.4 %fusion.57 = f32[1280,256]{1,0:T(8,128)} fusion(bf16[1280,128]{1,0:T(8,128)(2,1)S(1)} %copy-done.3, bf16[128,256]{1,0:T(8,128)(2,1)S(1)} %copy-done.4), kind=kOutput, calls=%fused_computation.73 | convolution fusion | flops 83886080 | bytes 1703936 | tf_op jit(solution)/shard_map/dot_general | solution.py:121
  14.8 7.4 %all-to-all-done = bf16[32,32,128]{2,1,0:T(8,128)(2,1)S(1)} async-done(((bf16[32,32,128]{2,1,0:T(8,128)(2,1)}), bf16[32,32,128]{2,1,0:T(8,128)(2,1)S(1)}, u32[]{:S(2)}, u32[]{:S(2)}) %all-to-all-start) | async-done | bytes 262176 | tf_op jit(solution)/shard_map/all_to_all | solution.py:65
  22.2 0.4 fusion.29
  22.7 2.0 %gather_fusion = bf16[48,128,128]{2,1,0:T(8,128)(2,1)} fusion(bf16[13,128,128]{2,1,0:T(8,128)(2,1)S(1)} %bitcast.56, s32[1024]{0:T(1024)S(1)} %pad_clamp_fusion.1), kind=kCustom, calls=%fused_computation | custom fusion | bytes 3145920 | tf_op jit(solution)/shard_map/gather | solution.py:114
  24.7 2.6 %fusion.58 = f32[48,128,128]{2,1,0:T(8,128)S(1)} fusion(bf16[48,128,128]{2,1,0:T(8,128)(2,1)} %gather_fusion, bf16[48,128,128]{2,1,0:T(8,128)(2,1)S(1)} %copy-done), kind=kOutput, calls=%fused_computation.74 | convolution fusion | flops 201326592 | bytes 6291456 | tf_op jit(solution)/shard_map/tjf,tij->tfi/dot_general | solution.py:113
  27.3 2.4 %fusion.20 = bf16[10,128,128]{1,0,2:T(8,128)(2,1)S(1)} fusion(f32[48,128,128]{2,1,0:T(8,128)S(1)} %fusion.58, f32[10,128]{1,0:T(8,128)S(1)} %fusion.39, s32[48]{0:T(128)S(1)} %copy-done.7, pred[48]{0:T(512)(128)(4,1)S(1)} %iota_compare_fusion.26), kind=kOutput, calls=%fused_computation.25 | convolution fusion | flops 47514560 | bytes 3478768 | tf_op jit(solution)/shard_map/bt,tfi->bif/dot_general | solution.py:116
  29.7 0.4 copy.27
  30.1 3.1 %multiply_convert_fusion = (bf16[1280,256]{1,0:T(8,128)(2,1)S(1)}, bf16[1280,256]{1,0:T(8,128)(2,1)}) fusion(bf16[1280,256]{1,0:T(8,128)(2,1)} %param.19, f32[1280,256]{1,0:T(8,128)} %fusion.57, bf16[1280,128]{1,0:T(8,128)(2,1)S(1)} %bitcast.60, bf16[128,256]{1,0:T(8,128)(2,1)S(1)} %copy-done.11), kind=kOutput, calls=%fused_computation.22 | convolution fusion | flops 88145920 | bytes 3670016 | tf_op jit(solution)/shard_map/dot_general | solution.py:121
  33.2 0.3 fusion.60
  33.5 0.3 convolution_bitcast_fusion
  33.9 1.0 %all_to_all.21 = f32[32,1,2048]{2,1,0:T(1,128)} reshape(f32[256,256]{1,0:T(8,128)S(1)} %pad_maximum_fusion.1) | data formatting | bytes 524288 | tf_op jit(solution)/shard_map/all_to_all | solution.py:15
  34.9 3.5 %all-to-all-start.2 = ((f32[32,1,2048]{2,1,0:T(1,128)}), f32[32,1,2048]{2,1,0:T(1,128)}, u32[]{:S(2)}, u32[]{:S(2)}) async-start(f32[32,1,2048]{2,1,0:T(1,128)} %all_to_all.21), calls=%async_computation.2 | async-start | bytes 524288 | tf_op jit(solution)/shard_map/all_to_all | solution.py:15
  38.4 0.3 fusion.4
  38.7 0.8 %gather_fusion.1 = bf16[48,128,128]{2,1,0:T(8,128)(2,1)S(1)} fusion(bf16[10,128,128]{2,1,0:T(8,128)(2,1)S(1)} %bitcast.57, s32[1024]{0:T(1024)S(1)} %pad_clamp_fusion), kind=kCustom, calls=%fused_computation.1 | custom fusion | bytes 3145920 | tf_op jit(solution)/shard_map/gather | solution.py:134
  39.6 0.7 fusion.59
  40.3 2.3 %fusion.17 = f32[13,128,128]{1,0,2:T(8,128)S(1)} fusion(f32[48,128,128]{2,1,0:T(8,128)S(1)} %fusion.59, s32[48]{0:T(128)S(1)} %copy-done.8, pred[48]{0:T(512)(128)(4,1)S(1)} %iota_compare_fusion.26), kind=kOutput, calls=%fused_computation.21 | convolution fusion | flops 61342944 | bytes 3997936 | tf_op jit(solution)/shard_map/st,tfj->sjf/dot_general | solution.py:136
  42.6 0.1 slice.46
  42.7 0.1 copy.31
  42.8 0.0 copy-start.5
  42.8 1.4 %fusion.24 = bf16[1024,128]{1,0:T(8,128)(2,1)} fusion(bf16[384,128]{1,0:T(8,128)(2,1)S(1)} %bitcast.65, s32[384]{0:T(512)S(1)} %add.79), kind=kOutput, calls=%fused_computation.27 | convolution fusion | flops 101187584 | bytes 361984 | tf_op jit(solution)/shard_map/dot_general | solution.py:63
  44.3 4.3 %all-to-all-done.2 = f32[32,1,2048]{2,1,0:T(1,128)} async-done(((f32[32,1,2048]{2,1,0:T(1,128)}), f32[32,1,2048]{2,1,0:T(1,128)}, u32[]{:S(2)}, u32[]{:S(2)}) %all-to-all-start.2) | async-done | bytes 262176 | tf_op jit(solution)/shard_map/all_to_all | solution.py:15
  48.5 2.7 %all-to-all-start.1 = ((bf16[32,32,128]{2,1,0:T(8,128)(2,1)}), bf16[32,32,128]{2,1,0:T(8,128)(2,1)S(1)}, u32[]{:S(2)}, u32[]{:S(2)}) async-start(bf16[32,32,128]{2,1,0:T(8,128)(2,1)} %bitcast.64), calls=%async_computation.1 | async-start | bytes 524288 | tf_op jit(solution)/shard_map/all_to_all | solution.py:65
  51.3 1.2 %copy.30 = f32[10,128,128]{2,1,0:T(8,128)} copy(f32[10,128,128]{1,0,2:T(8,128)S(1)} %bitcast.58) | data formatting | bytes 1310720 | tf_op jit(solution)/shard_map/slice | solution.py:147
  52.4 1.1 %reduce_sum.9 = f32[2048]{0:T(1024)S(1)} reduce(f32[32,1,2048]{2,1,0:T(1,128)} %all-to-all-done.2, f32[]{:T(128)} %constant.31.clone.1), dimensions={0,1}, to_apply=%region_0.1 | reduce | flops 63488 | bytes 270340 | tf_op jit(solution)/shard_map/reduce_sum | solution.py:15
  53.6 8.1 %all-to-all-done.1 = bf16[32,32,128]{2,1,0:T(8,128)(2,1)S(1)} async-done(((bf16[32,32,128]{2,1,0:T(8,128)(2,1)}), bf16[32,32,128]{2,1,0:T(8,128)(2,1)S(1)}, u32[]{:S(2)}, u32[]{:S(2)}) %all-to-all-start.1) | async-done | bytes 262176 | tf_op jit(solution)/shard_map/all_to_all | solution.py:65
  61.6 0.8 %broadcast_in_dim.58 = f32[32,1,2048]{2,1,0:T(1,128)} broadcast(f32[2048]{0:T(1024)S(1)} %reduce_sum.9), dimensions={2} | broadcast | bytes 270336 | tf_op jit(solution)/shard_map/broadcast_in_dim | solution.py:16
  62.5 2.6 %all-to-all-start.3 = ((f32[32,1,2048]{2,1,0:T(1,128)}), f32[32,1,2048]{2,1,0:T(1,128)S(1)}, u32[]{:S(2)}, u32[]{:S(2)}) async-start(f32[32,1,2048]{2,1,0:T(1,128)} %broadcast_in_dim.58), calls=%async_computation.3 | async-start | bytes 524288 | tf_op jit(solution)/shard_map/all_to_all | solution.py:17
  65.1 1.5 %convolution_add_fusion.2 = f32[1280,128]{1,0:T(8,128)S(1)} fusion(f32[1280,128]{1,0:T(8,128)} %bitcast.59, bf16[1280,256]{1,0:T(8,128)(2,1)S(1)} %copy-done.2, bf16[128,256]{1,0:T(8,128)(2,1)} %param.17), kind=kOutput, calls=%fused_computation.9 | convolution fusion | flops 84049920 | bytes 2031616 | tf_op jit(solution)/shard_map/nh,fh->nf/dot_general | solution.py:131
  66.6 1.9 %fusion.5 = bf16[1280,128]{1,0:T(8,128)(2,1)} fusion(f32[1280,128]{1,0:T(8,128)S(1)} %convolution_add_fusion.2, bf16[384,128]{1,0:T(8,128)(2,1)S(1)} %bitcast.66, bf16[1024,128]{1,0:T(8,128)(2,1)S(1)} %bitcast.63, s32[384]{0:T(512)S(1)} %eq.71, s32[384]{0:T(512)S(1)} %add.79, pred[384]{0:T(512)(128)(4,1)S(1)} %copy-done.10), kind=kOutput, calls=%fused_computation.11 | convolution fusion | flops 227803136 | bytes 1346944 | tf_op jit(solution)/shard_map/dot_general | solution.py:148
  68.4 7.0 %all-to-all-done.3 = f32[32,1,2048]{2,1,0:T(1,128)S(1)} async-done(((f32[32,1,2048]{2,1,0:T(1,128)}), f32[32,1,2048]{2,1,0:T(1,128)S(1)}, u32[]{:S(2)}, u32[]{:S(2)}) %all-to-all-start.3) | async-done | bytes 262176 | tf_op jit(solution)/shard_map/all_to_all | solution.py:17
  75.5 0.7 slice_reduce_fusion
  76.1 0.7 slice.34
  76.8 0.7 slice.32
  (28 shorter events, 0.1 us)
Async XLA Ops:
  0.6 11.9 %copy-start = (bf16[48,128,128]{2,1,0:T(8,128)(2,1)S(1)}, bf16[48,128,128]{2,1,0:T(8,128)(2,1)}, u32[]{:S(2)}) copy-start(bf16[48,128,128]{2,1,0:T(8,128)(2,1)} %param.13) | copy-start | bytes 4718596
  0.6 11.9 %copy-start.8 = (s32[48]{0:T(128)S(1)}, s32[48]{0:T(128)}, u32[]{:S(2)}) copy-start(s32[48]{0:T(128)} %param.15) | copy-start | bytes 580
  0.7 11.9 %copy-start.7 = (s32[48]{0:T(128)S(1)}, s32[48]{0:T(128)}, u32[]{:S(2)}) copy-start(s32[48]{0:T(128)} %param.14) | copy-start | bytes 580
  3.1 10.3 %copy-start.3 = (bf16[1280,128]{1,0:T(8,128)(2,1)S(1)}, bf16[1280,128]{1,0:T(8,128)(2,1)}, u32[]{:S(2)}) copy-start(bf16[1280,128]{1,0:T(8,128)(2,1)} %param.10) | copy-start | bytes 983044
  3.1 10.3 %copy-start.4 = (bf16[128,256]{1,0:T(8,128)(2,1)S(1)}, bf16[128,256]{1,0:T(8,128)(2,1)}, u32[]{:S(2)}) copy-start(bf16[128,256]{1,0:T(8,128)(2,1)} %param.17) | copy-start | bytes 196612
  4.5 17.7 %all-to-all-start = ((bf16[32,32,128]{2,1,0:T(8,128)(2,1)}), bf16[32,32,128]{2,1,0:T(8,128)(2,1)S(1)}, u32[]{:S(2)}, u32[]{:S(2)}) async-start(bf16[32,32,128]{2,1,0:T(8,128)(2,1)} %bitcast.2), calls=%async_computation | async-start | bytes 524288 | tf_op jit(solution)/shard_map/all_to_all | solution.py:65
  13.3 9.4 %copy-start.9 = (pred[384]{0:T(512)(128)(4,1)}, pred[384]{0:T(512)(128)(4,1)S(1)}, u32[]{:S(2)}) copy-start(pred[384]{0:T(512)(128)(4,1)S(1)} %broadcast_in_dim.28) | copy-start | bytes 1156
  27.3 2.8 %copy-start.11 = (bf16[128,256]{1,0:T(8,128)(2,1)S(1)}, bf16[128,256]{1,0:T(8,128)(2,1)}, u32[]{:S(2)}) copy-start(bf16[128,256]{1,0:T(8,128)(2,1)} %param.18) | copy-start | bytes 196612
  33.2 5.1 %copy-start.1 = (bf16[1280,256]{1,0:T(8,128)(2,1)}, bf16[1280,256]{1,0:T(8,128)(2,1)S(1)}, u32[]{:S(2)}) copy-start(bf16[1280,256]{1,0:T(8,128)(2,1)S(1)} %get-tuple-element.6) | copy-start | bytes 1966084
  34.9 13.7 %all-to-all-start.2 = ((f32[32,1,2048]{2,1,0:T(1,128)}), f32[32,1,2048]{2,1,0:T(1,128)}, u32[]{:S(2)}, u32[]{:S(2)}) async-start(f32[32,1,2048]{2,1,0:T(1,128)} %all_to_all.21), calls=%async_computation.2 | async-start | bytes 524288 | tf_op jit(solution)/shard_map/all_to_all | solution.py:15
  42.8 5.7 %copy-start.5 = (bf16[3,128,128]{2,1,0:T(8,128)(2,1)}, bf16[3,128,128]{2,1,0:T(8,128)(2,1)S(1)}, u32[]{:S(2)}) copy-start(bf16[3,128,128]{2,1,0:T(8,128)(2,1)S(1)} %copy.31) | copy-start | bytes 294916
  48.5 16.5 %copy-start.2 = (bf16[1280,256]{1,0:T(8,128)(2,1)S(1)}, bf16[1280,256]{1,0:T(8,128)(2,1)}, u32[]{:S(2)}) copy-start(bf16[1280,256]{1,0:T(8,128)(2,1)} %copy-done.1) | copy-start | bytes 1966084
  48.5 13.1 %all-to-all-start.1 = ((bf16[32,32,128]{2,1,0:T(8,128)(2,1)}), bf16[32,32,128]{2,1,0:T(8,128)(2,1)S(1)}, u32[]{:S(2)}, u32[]{:S(2)}) async-start(bf16[32,32,128]{2,1,0:T(8,128)(2,1)} %bitcast.64), calls=%async_computation.1 | async-start | bytes 524288 | tf_op jit(solution)/shard_map/all_to_all | solution.py:65
  52.4 14.1 %copy-start.6 = (bf16[3,128,128]{2,1,0:T(8,128)(2,1)S(1)}, bf16[3,128,128]{2,1,0:T(8,128)(2,1)}, u32[]{:S(2)}) copy-start(bf16[3,128,128]{2,1,0:T(8,128)(2,1)} %copy-done.5) | copy-start | bytes 294916
  52.4 14.1 %copy-start.10 = (pred[384]{0:T(512)(128)(4,1)S(1)}, pred[384]{0:T(512)(128)(4,1)}, u32[]{:S(2)}) copy-start(pred[384]{0:T(512)(128)(4,1)} %copy-done.9) | copy-start | bytes 1156
  62.5 13.0 %all-to-all-start.3 = ((f32[32,1,2048]{2,1,0:T(1,128)}), f32[32,1,2048]{2,1,0:T(1,128)S(1)}, u32[]{:S(2)}, u32[]{:S(2)}) async-start(f32[32,1,2048]{2,1,0:T(1,128)} %broadcast_in_dim.58), calls=%async_computation.3 | async-start | bytes 524288 | tf_op jit(solution)/shard_map/all_to_all | solution.py:17

commit v15 on v12

--- a/solution.py
+++ b/solution.py
@@ -133,11 +133,8 @@
     grad_pre = (cotangent.astype(jnp.float32) * sigm * (1.0 + preact * (1.0 - sigm))).astype(
         jnp.bfloat16
     )
-    stacked = jnp.einsum(
-        "nf,nh->fh", jnp.concatenate([features, agg], axis=1), grad_pre,
-        preferred_element_type=jnp.float32,
-    )
-    part_self, part_neigh = stacked[:width], stacked[width:]
+    part_self = jnp.einsum("nf,nh->fh", features, grad_pre, preferred_element_type=jnp.float32)
+    part_neigh = jnp.einsum("nf,nh->fh", agg, grad_pre, preferred_element_type=jnp.float32)
     grad_own = jnp.einsum("nh,fh->nf", grad_pre, w_self, preferred_element_type=jnp.float32)
     grad_agg = jnp.einsum("nh,fh->nf", grad_pre, w_neigh, preferred_element_type=jnp.float32)
     grad_agg = (grad_agg / degree.reshape(-1)[:, None]).astype(jnp.bfloat16)
@@ -153,7 +150,7 @@
         remote = remote.reshape(n_dom + n_grp, bnd, width)
         ret_dom, ret_grp = exchange(remote[:n_dom], remote[n_dom:])
         returned = jnp.concatenate([ret_dom.reshape(-1, width), ret_grp.reshape(-1, width)])
-    grad_self, grad_neigh = weight_sum(part_self, part_neigh, stacked)
+    grad_self, grad_neigh = weight_sum(part_self, part_neigh)
     grad_total = grad_own + grad_source[:node_count]
     grad_total = grad_total + lax.dot_general(
         pick, returned, (((0,), (0,)), ((), ())), preferred_element_type=jnp.float32

time: 78.9 us -> 76.9 us (0.975)
  waiting for transfers between devices: 27.6 us -> 26.3 us
    all_to_all x2, waiting for transfers between devices: 16.9 us -> 15.6 us  [swap(): lax.all_to_all(buf, ('dom', 'grp'), 0, 0, tiled=True)]
    dot_general x1, matrix products: 0.31 us -> 1.39 us  [per_device(): jnp.dot(features, w_self, preferred_element_type=jnp.float32)]
    concatenate x1, other arithmetic: 1 us -> 0.03 us  [per_device(): jnp.concatenate([features, recv_dom.reshape(-1, width), recv_grp.reshape(...]
    dot_general x1, matrix products: 1.32 us -> 0.43 us  [swap(): jnp.dot(place, got, preferred_element_type=jnp.float32).astype(table.dtype)]
    slice x1, local copies, waits for them, and re-layouts: 0.31 us -> 1.16 us  [per_device(): grad_total = grad_own + grad_source[:node_count]]
  transfers between devices with their start and end apart: 4 -> 4, of which waited for: 4 -> 4; matrix products, arithmetic and copies ran while one was open for 16% -> 19% of each run, Pallas kernels for 0% -> 0%
where the time goes in v15:
time: 76.9 us; the launch traced here: 76.3 us
  waiting for transfers between devices  26.3 us (34%)
  matrix products  23.3 us (30%)
  starting transfers between devices  16.1 us (21%)
  local copies, waits for them, and re-layouts  6.39 us (8%)
  other arithmetic  2.59 us (3%)
  between operations  1.6 us (2%)
    all_to_all x2, waiting for transfers between devices, swap(): lax.all_to_all(buf, ('dom', 'grp'), 0, 0, tiled=True)  15.6 us
    all_to_all x2, starting transfers between devices, swap(): lax.all_to_all(buf, ('dom', 'grp'), 0, 0, tiled=True)  10 us
    all_to_all x1, waiting for transfers between devices, weight_sum(): lax.all_to_all(jnp.broadcast_to(mine, chunks.shape), axes, 0, 0, tiled=True)  7.03 us
    all_to_all x1, waiting for transfers between devices, weight_sum(): lax.all_to_all(chunks, axes, 0, 0, tiled=True)  3.71 us
    all_to_all x1, starting transfers between devices, weight_sum(): lax.all_to_all(chunks, axes, 0, 0, tiled=True)  3.49 us
    dot_general x1, matrix products, per_device(): jnp.dot(agg, w_neigh, preferred_element_type=jnp.float32)  3.14 us
    dot_general x1, matrix products, per_device(): jnp.einsum('bt,tfi->bif', to_target, products, precision=lax.Precision.HI...  2.94 us
    dot_general x1, matrix products, per_device(): jnp.einsum('st,tfj->sjf', to_source, backward, precision=lax.Precision.HI...  2.91 us
  transfers between devices with their start and end apart: 4, of which 4 were waited for; matrix products, arithmetic and copies ran while one was open for 19% of the time, Pallas kernels for 0%

profile of v15, /device:TPU:0, one launch (start us, length us, event | category | flops | bytes accessed | tf_op | source)
XLA Modules:
  0.0 76.3 jit_solution(12839520162757309995)
XLA Ops:
  0.6 0.0 copy-start
  0.7 0.1 iota_add_fusion
  0.8 0.1 add.79
  0.8 0.7 pad_add_fusion
  1.5 0.1 eq.71
  1.6 1.5 %fusion.27 = bf16[384,128]{1,0:T(8,128)(2,1)S(1)} fusion(bf16[1280,128]{1,0:T(8,128)(2,1)} %param.10, s32[384]{0:T(512)S(1)} %eq.71), kind=kOutput, calls=%fused_computation.30 | convolution fusion | flops 126369792 | bytes 427520 | tf_op jit(solution)/shard_map/dot_general | solution.py:98
  3.1 0.0 copy-start.3
  3.1 0.0 copy-start.4
  3.1 1.4 %fusion.23 = bf16[1024,128]{1,0:T(8,128)(2,1)} fusion(bf16[384,128]{1,0:T(8,128)(2,1)S(1)} %fusion.27, s32[384]{0:T(512)S(1)} %add.79), kind=kOutput, calls=%fused_computation.26 | convolution fusion | flops 101187584 | bytes 361984 | tf_op jit(solution)/shard_map/dot_general | solution.py:70
  4.5 7.3 %all-to-all-start = ((bf16[32,32,128]{2,1,0:T(8,128)(2,1)}), bf16[32,32,128]{2,1,0:T(8,128)(2,1)S(1)}, u32[]{:S(2)}, u32[]{:S(2)}) async-start(bf16[32,32,128]{2,1,0:T(8,128)(2,1)} %bitcast.2), calls=%async_computation | async-start | bytes 524288 | tf_op jit(solution)/shard_map/all_to_all | solution.py:72
  12.5 0.0 copy-done.8
  12.5 0.0 copy-done.7
  12.6 0.5 fusion.54
  13.1 0.1 broadcast_in_dim.27
  13.2 0.1 broadcast_in_dim.28
  13.3 0.1 fusion.39
  13.4 0.0 copy-done.4
  13.4 1.4 %fusion.57 = f32[1280,256]{1,0:T(8,128)} fusion(bf16[1280,128]{1,0:T(8,128)(2,1)S(1)} %copy-done.3, bf16[128,256]{1,0:T(8,128)(2,1)S(1)} %copy-done.4), kind=kOutput, calls=%fused_computation.73 | convolution fusion | flops 83886080 | bytes 1703936 | tf_op jit(solution)/shard_map/dot_general | solution.py:128
  14.8 7.4 %all-to-all-done = bf16[32,32,128]{2,1,0:T(8,128)(2,1)S(1)} async-done(((bf16[32,32,128]{2,1,0:T(8,128)(2,1)}), bf16[32,32,128]{2,1,0:T(8,128)(2,1)S(1)}, u32[]{:S(2)}, u32[]{:S(2)}) %all-to-all-start) | async-done | bytes 262176 | tf_op jit(solution)/shard_map/all_to_all | solution.py:72
  22.2 0.4 fusion.29
  22.7 2.0 %gather_fusion = bf16[48,128,128]{2,1,0:T(8,128)(2,1)} fusion(bf16[13,128,128]{2,1,0:T(8,128)(2,1)S(1)} %bitcast.62, s32[1024]{0:T(1024)S(1)} %pad_clamp_fusion.1), kind=kCustom, calls=%fused_computation | custom fusion | bytes 3145920 | tf_op jit(solution)/shard_map/gather | solution.py:121
  24.7 2.6 %fusion.58 = f32[48,128,128]{2,1,0:T(8,128)S(1)} fusion(bf16[48,128,128]{2,1,0:T(8,128)(2,1)} %gather_fusion, bf16[48,128,128]{2,1,0:T(8,128)(2,1)S(1)} %copy-done), kind=kOutput, calls=%fused_computation.74 | convolution fusion | flops 201326592 | bytes 6291456 | tf_op jit(solution)/shard_map/tjf,tij->tfi/dot_general | solution.py:120
  27.3 2.9 %fusion.20 = bf16[10,128,128]{1,0,2:T(8,128)(2,1)S(1)} fusion(f32[48,128,128]{2,1,0:T(8,128)S(1)} %fusion.58, f32[10,128]{1,0:T(8,128)S(1)} %fusion.39, s32[48]{0:T(128)S(1)} %copy-done.7, pred[48]{0:T(512)(128)(4,1)S(1)} %iota_compare_fusion.26), kind=kOutput, calls=%fused_computation.25 | convolution fusion | flops 94700480 | bytes 3478768 | tf_op jit(solution)/shard_map/bt,tfi->bif/dot_general | solution.py:123
  30.3 0.4 copy.16
  30.7 3.1 %multiply_convert_fusion = (bf16[1280,256]{1,0:T(8,128)(2,1)S(1)}, bf16[1280,256]{1,0:T(8,128)(2,1)}) fusion(bf16[1280,256]{1,0:T(8,128)(2,1)} %param.19, f32[1280,256]{1,0:T(8,128)} %fusion.57, bf16[1280,128]{1,0:T(8,128)(2,1)S(1)} %bitcast.66, bf16[128,256]{1,0:T(8,128)(2,1)S(1)} %copy-done.11), kind=kOutput, calls=%fused_computation.22 | convolution fusion | flops 88145920 | bytes 3670016 | tf_op jit(solution)/shard_map/dot_general | solution.py:128
  33.8 0.3 fusion.60
  34.1 0.3 convolution_bitcast_fusion
  34.4 0.7 maximum_bitcast_fusion
  35.1 3.5 %all-to-all-start.2 = ((f32[32,8,256]{2,1,0:T(8,128)}), f32[32,8,256]{2,1,0:T(8,128)}, u32[]{:S(2)}, u32[]{:S(2)}) async-start(f32[32,8,256]{2,1,0:T(8,128)} %maximum_bitcast_fusion), calls=%async_computation.2 | async-start | bytes 524288 | tf_op jit(solution)/shard_map/all_to_all | solution.py:15
  38.6 0.3 fusion.4
  39.0 0.8 %gather_fusion.1 = bf16[48,128,128]{2,1,0:T(8,128)(2,1)S(1)} fusion(bf16[10,128,128]{2,1,0:T(8,128)(2,1)S(1)} %bitcast.63, s32[1024]{0:T(1024)S(1)} %pad_clamp_fusion), kind=kCustom, calls=%fused_computation.1 | custom fusion | bytes 3145920 | tf_op jit(solution)/shard_map/gather | solution.py:141
  39.9 0.7 fusion.59
  40.6 2.9 %fusion.17 = f32[13,128,128]{1,0,2:T(8,128)S(1)} fusion(f32[48,128,128]{2,1,0:T(8,128)S(1)} %fusion.59, s32[48]{0:T(128)S(1)} %copy-done.8, pred[48]{0:T(512)(128)(4,1)S(1)} %iota_compare_fusion.26), kind=kOutput, calls=%fused_computation.21 | convolution fusion | flops 122684640 | bytes 3997936 | tf_op jit(solution)/shard_map/st,tfj->sjf/dot_general | solution.py:143
  43.5 0.1 slice.44
  43.5 0.1 copy.18
  43.7 0.0 copy-start.5
  43.7 1.4 %fusion.24 = bf16[1024,128]{1,0:T(8,128)(2,1)} fusion(bf16[384,128]{1,0:T(8,128)(2,1)S(1)} %bitcast.71, s32[384]{0:T(512)S(1)} %add.79), kind=kOutput, calls=%fused_computation.27 | convolution fusion | flops 101187584 | bytes 361984 | tf_op jit(solution)/shard_map/dot_general | solution.py:70
  45.1 3.7 %all-to-all-done.2 = f32[32,8,256]{2,1,0:T(8,128)} async-done(((f32[32,8,256]{2,1,0:T(8,128)}), f32[32,8,256]{2,1,0:T(8,128)}, u32[]{:S(2)}, u32[]{:S(2)}) %all-to-all-start.2) | async-done | bytes 262176 | tf_op jit(solution)/shard_map/all_to_all | solution.py:15
  48.8 2.7 %all-to-all-start.1 = ((bf16[32,32,128]{2,1,0:T(8,128)(2,1)}), bf16[32,32,128]{2,1,0:T(8,128)(2,1)S(1)}, u32[]{:S(2)}, u32[]{:S(2)}) async-start(bf16[32,32,128]{2,1,0:T(8,128)(2,1)} %bitcast.70), calls=%async_computation.1 | async-start | bytes 524288 | tf_op jit(solution)/shard_map/all_to_all | solution.py:72
  51.5 1.2 %copy.17 = f32[10,128,128]{2,1,0:T(8,128)} copy(f32[10,128,128]{1,0,2:T(8,128)S(1)} %bitcast.64) | data formatting | bytes 1310720 | tf_op jit(solution)/shard_map/slice | solution.py:154
  52.7 1.0 %reduce_sum.9 = f32[8,256]{1,0:T(8,128)S(1)} reduce(f32[32,8,256]{2,1,0:T(8,128)} %all-to-all-done.2, f32[]{:T(128)} %constant.30.clone.1), dimensions={0}, to_apply=%region_0.1 | reduce | flops 63488 | bytes 270340 | tf_op jit(solution)/shard_map/reduce_sum | solution.py:15
  53.7 8.2 %all-to-all-done.1 = bf16[32,32,128]{2,1,0:T(8,128)(2,1)S(1)} async-done(((bf16[32,32,128]{2,1,0:T(8,128)(2,1)}), bf16[32,32,128]{2,1,0:T(8,128)(2,1)S(1)}, u32[]{:S(2)}, u32[]{:S(2)}) %all-to-all-start.1) | async-done | bytes 262176 | tf_op jit(solution)/shard_map/all_to_all | solution.py:72
  61.9 0.7 broadcast_in_dim.58
  62.7 2.6 %all-to-all-start.3 = ((f32[32,8,256]{2,1,0:T(8,128)}), f32[32,8,256]{2,1,0:T(8,128)S(1)}, u32[]{:S(2)}, u32[]{:S(2)}) async-start(f32[32,8,256]{2,1,0:T(8,128)} %broadcast_in_dim.58), calls=%async_computation.3 | async-start | bytes 524288 | tf_op jit(solution)/shard_map/all_to_all | solution.py:16
  65.3 1.5 %convolution_add_fusion.2 = f32[1280,128]{1,0:T(8,128)S(1)} fusion(f32[1280,128]{1,0:T(8,128)} %bitcast.65, bf16[1280,256]{1,0:T(8,128)(2,1)S(1)} %copy-done.2, bf16[128,256]{1,0:T(8,128)(2,1)} %param.17), kind=kOutput, calls=%fused_computation.9 | convolution fusion | flops 84049920 | bytes 2031616 | tf_op jit(solution)/shard_map/nh,fh->nf/dot_general | solution.py:138
  66.7 1.9 %fusion.5 = bf16[1280,128]{1,0:T(8,128)(2,1)} fusion(f32[1280,128]{1,0:T(8,128)S(1)} %convolution_add_fusion.2, bf16[384,128]{1,0:T(8,128)(2,1)S(1)} %bitcast.72, bf16[1024,128]{1,0:T(8,128)(2,1)S(1)} %bitcast.69, s32[384]{0:T(512)S(1)} %eq.71, s32[384]{0:T(512)S(1)} %add.79, pred[384]{0:T(512)(128)(4,1)S(1)} %copy-done.10), kind=kOutput, calls=%fused_computation.11 | convolution fusion | flops 227803136 | bytes 1346944 | tf_op jit(solution)/shard_map/dot_general | solution.py:155
  68.6 7.0 %all-to-all-done.3 = f32[32,8,256]{2,1,0:T(8,128)S(1)} async-done(((f32[32,8,256]{2,1,0:T(8,128)}), f32[32,8,256]{2,1,0:T(8,128)S(1)}, u32[]{:S(2)}, u32[]{:S(2)}) %all-to-all-start.3) | async-done | bytes 262176 | tf_op jit(solution)/shard_map/all_to_all | solution.py:16
  75.6 0.7 slice_bitcast_fusion
  (25 shorter events, 0.1 us)
Async XLA Ops:
  0.6 11.9 %copy-start = (bf16[48,128,128]{2,1,0:T(8,128)(2,1)S(1)}, bf16[48,128,128]{2,1,0:T(8,128)(2,1)}, u32[]{:S(2)}) copy-start(bf16[48,128,128]{2,1,0:T(8,128)(2,1)} %param.13) | copy-start | bytes 4718596
  0.6 11.9 %copy-start.8 = (s32[48]{0:T(128)S(1)}, s32[48]{0:T(128)}, u32[]{:S(2)}) copy-start(s32[48]{0:T(128)} %param.15) | copy-start | bytes 580
  0.7 11.9 %copy-start.7 = (s32[48]{0:T(128)S(1)}, s32[48]{0:T(128)}, u32[]{:S(2)}) copy-start(s32[48]{0:T(128)} %param.14) | copy-start | bytes 580
  3.1 10.3 %copy-start.3 = (bf16[1280,128]{1,0:T(8,128)(2,1)S(1)}, bf16[1280,128]{1,0:T(8,128)(2,1)}, u32[]{:S(2)}) copy-start(bf16[1280,128]{1,0:T(8,128)(2,1)} %param.10) | copy-start | bytes 983044
  3.1 10.3 %copy-start.4 = (bf16[128,256]{1,0:T(8,128)(2,1)S(1)}, bf16[128,256]{1,0:T(8,128)(2,1)}, u32[]{:S(2)}) copy-start(bf16[128,256]{1,0:T(8,128)(2,1)} %param.17) | copy-start | bytes 196612
  4.5 17.7 %all-to-all-start = ((bf16[32,32,128]{2,1,0:T(8,128)(2,1)}), bf16[32,32,128]{2,1,0:T(8,128)(2,1)S(1)}, u32[]{:S(2)}, u32[]{:S(2)}) async-start(bf16[32,32,128]{2,1,0:T(8,128)(2,1)} %bitcast.2), calls=%async_computation | async-start | bytes 524288 | tf_op jit(solution)/shard_map/all_to_all | solution.py:72
  13.3 9.4 %copy-start.9 = (pred[384]{0:T(512)(128)(4,1)}, pred[384]{0:T(512)(128)(4,1)S(1)}, u32[]{:S(2)}) copy-start(pred[384]{0:T(512)(128)(4,1)S(1)} %broadcast_in_dim.28) | copy-start | bytes 1156
  27.3 3.3 %copy-start.11 = (bf16[128,256]{1,0:T(8,128)(2,1)S(1)}, bf16[128,256]{1,0:T(8,128)(2,1)}, u32[]{:S(2)}) copy-start(bf16[128,256]{1,0:T(8,128)(2,1)} %param.18) | copy-start | bytes 196612
  33.8 4.8 %copy-start.1 = (bf16[1280,256]{1,0:T(8,128)(2,1)}, bf16[1280,256]{1,0:T(8,128)(2,1)S(1)}, u32[]{:S(2)}) copy-start(bf16[1280,256]{1,0:T(8,128)(2,1)S(1)} %get-tuple-element.4) | copy-start | bytes 1966084
  35.1 13.7 %all-to-all-start.2 = ((f32[32,8,256]{2,1,0:T(8,128)}), f32[32,8,256]{2,1,0:T(8,128)}, u32[]{:S(2)}, u32[]{:S(2)}) async-start(f32[32,8,256]{2,1,0:T(8,128)} %maximum_bitcast_fusion), calls=%async_computation.2 | async-start | bytes 524288 | tf_op jit(solution)/shard_map/all_to_all | solution.py:15
  43.7 5.1 %copy-start.5 = (bf16[3,128,128]{2,1,0:T(8,128)(2,1)}, bf16[3,128,128]{2,1,0:T(8,128)(2,1)S(1)}, u32[]{:S(2)}) copy-start(bf16[3,128,128]{2,1,0:T(8,128)(2,1)S(1)} %copy.18) | copy-start | bytes 294916
  48.8 16.4 %copy-start.2 = (bf16[1280,256]{1,0:T(8,128)(2,1)S(1)}, bf16[1280,256]{1,0:T(8,128)(2,1)}, u32[]{:S(2)}) copy-start(bf16[1280,256]{1,0:T(8,128)(2,1)} %copy-done.1) | copy-start | bytes 1966084
  48.8 13.1 %all-to-all-start.1 = ((bf16[32,32,128]{2,1,0:T(8,128)(2,1)}), bf16[32,32,128]{2,1,0:T(8,128)(2,1)S(1)}, u32[]{:S(2)}, u32[]{:S(2)}) async-start(bf16[32,32,128]{2,1,0:T(8,128)(2,1)} %bitcast.70), calls=%async_computation.1 | async-start | bytes 524288 | tf_op jit(solution)/shard_map/all_to_all | solution.py:72
  52.7 14.0 %copy-start.6 = (bf16[3,128,128]{2,1,0:T(8,128)(2,1)S(1)}, bf16[3,128,128]{2,1,0:T(8,128)(2,1)}, u32[]{:S(2)}) copy-start(bf16[3,128,128]{2,1,0:T(8,128)(2,1)} %copy-done.5) | copy-start | bytes 294916
  52.7 14.0 %copy-start.10 = (pred[384]{0:T(512)(128)(4,1)S(1)}, pred[384]{0:T(512)(128)(4,1)}, u32[]{:S(2)}) copy-start(pred[384]{0:T(512)(128)(4,1)} %copy-done.9) | copy-start | bytes 1156
  62.7 13.0 %all-to-all-start.3 = ((f32[32,8,256]{2,1,0:T(8,128)}), f32[32,8,256]{2,1,0:T(8,128)S(1)}, u32[]{:S(2)}, u32[]{:S(2)}) async-start(f32[32,8,256]{2,1,0:T(8,128)} %broadcast_in_dim.58), calls=%async_computation.3 | async-start | bytes 524288 | tf_op jit(solution)/shard_map/all_to_all | solution.py:16

commit v16 on v15

--- a/solution.py
+++ b/solution.py
@@ -140,10 +140,8 @@
     grad_agg = (grad_agg / degree.reshape(-1)[:, None]).astype(jnp.bfloat16)
     picked = grad_agg.reshape(block_count, tile_size, width)[tile_tgt]
     backward = jnp.einsum("tif,tij->tfj", picked, tile_vals, preferred_element_type=jnp.float32)
-    grad_source = jnp.einsum(
-        "st,tfj->sjf", to_source, backward, precision=lax.Precision.HIGHEST
-    ).reshape(-1, width)
-    remote = grad_source[node_count:].astype(jnp.bfloat16)
+    grad_source = jnp.einsum("st,tfj->sfj", to_source, backward, precision=lax.Precision.HIGHEST)
+    remote = grad_source[block_count:].transpose(0, 2, 1).reshape(-1, width).astype(jnp.bfloat16)
     if table_bytes <= PLACE_LIMIT:
         returned = swap(remote, place, keep)
     else:
@@ -151,7 +149,7 @@
         ret_dom, ret_grp = exchange(remote[:n_dom], remote[n_dom:])
         returned = jnp.concatenate([ret_dom.reshape(-1, width), ret_grp.reshape(-1, width)])
     grad_self, grad_neigh = weight_sum(part_self, part_neigh)
-    grad_total = grad_own + grad_source[:node_count]
+    grad_total = grad_own + grad_source[:block_count].transpose(0, 2, 1).reshape(node_count, width)
     grad_total = grad_total + lax.dot_general(
         pick, returned, (((0,), (0,)), ((), ())), preferred_element_type=jnp.float32
     )

time: 76.9 us -> 76.7 us (level)
  waiting for transfers between devices: 26.3 us -> 24.1 us
  local copies, waits for them, and re-layouts: 6.39 us -> 7.82 us
  matrix products: 23.3 us -> 24.2 us
    transpose x0 -> x2, local copies, waits for them, and re-layouts: none -> 2.58 us  [per_device(): grad_source[:block_count].transpose(0, 2, 1).reshape(node_count, width)]
    all_to_all x2, waiting for transfers between devices: 15.6 us -> 14.2 us  [swap(): lax.all_to_all(buf, ('dom', 'grp'), 0, 0, tiled=True)]
    slice x3 -> x0, local copies, waits for them, and re-layouts: 1.36 us -> none  [the longest x1 1.16 us: per_device(): grad_total = grad_own + grad_source[:node_count]]
    dot_general x1, matrix products: 1.86 us -> 3 us  [per_device(): lax.dot_general(pick, returned, (((0,), (0,)), ((), ())), preferred_eleme...]
    all_to_all x1, waiting for transfers between devices: 7.03 us -> 6.18 us  [weight_sum(): lax.all_to_all(jnp.broadcast_to(mine, chunks.shape), axes, 0, 0, tiled=True)]
  transfers between devices with their start and end apart: 4 -> 4, of which waited for: 4 -> 4; matrix products, arithmetic and copies ran while one was open for 19% -> 22% of each run, Pallas kernels for 0% -> 0%
where the time goes in v16:
time: 76.7 us; the launch traced here: 76.2 us
  matrix products  24.2 us (32%)
  waiting for transfers between devices  24.1 us (31%)
  starting transfers between devices  15.9 us (21%)
  local copies, waits for them, and re-layouts  7.82 us (10%)
  other arithmetic  2.55 us (3%)
  between operations  1.6 us (2%)
    all_to_all x2, waiting for transfers between devices, swap(): lax.all_to_all(buf, ('dom', 'grp'), 0, 0, tiled=True)  14.2 us
    all_to_all x2, starting transfers between devices, swap(): lax.all_to_all(buf, ('dom', 'grp'), 0, 0, tiled=True)  9.88 us
    all_to_all x1, waiting for transfers between devices, weight_sum(): lax.all_to_all(jnp.broadcast_to(mine, chunks.shape), axes, 0, 0, tiled=True)  6.18 us
    all_to_all x1, waiting for transfers between devices, weight_sum(): lax.all_to_all(chunks, axes, 0, 0, tiled=True)  3.69 us
    all_to_all x1, starting transfers between devices, weight_sum(): lax.all_to_all(chunks, axes, 0, 0, tiled=True)  3.48 us
    dot_general x1, matrix products, per_device(): jnp.dot(agg, w_neigh, preferred_element_type=jnp.float32)  3.15 us
    dot_general x1, matrix products, per_device(): lax.dot_general(pick, returned, (((0,), (0,)), ((), ())), preferred_eleme...  3 us
    dot_general x1, matrix products, per_device(): jnp.einsum('bt,tfi->bif', to_target, products, precision=lax.Precision.HI...  2.94 us
  transfers between devices with their start and end apart: 4, of which 4 were waited for; matrix products, arithmetic and copies ran while one was open for 22% of the time, Pallas kernels for 0%

profile of v16, /device:TPU:0, one launch (start us, length us, event | category | flops | bytes accessed | tf_op | source)
XLA Modules:
  0.0 76.2 jit_solution(9639346946476452444)
XLA Ops:
  0.6 0.0 copy-start
  0.7 0.1 iota_add_fusion
  0.8 0.1 add.79
  0.8 0.7 pad_add_fusion
  1.5 0.1 eq.71
  1.6 1.5 %fusion.24 = bf16[384,128]{1,0:T(8,128)(2,1)S(1)} fusion(bf16[1280,128]{1,0:T(8,128)(2,1)} %param.10, s32[384]{0:T(512)S(1)} %eq.71), kind=kOutput, calls=%fused_computation.29 | convolution fusion | flops 126369792 | bytes 427520 | tf_op jit(solution)/shard_map/dot_general | solution.py:98
  3.1 0.0 copy-start.3
  3.1 0.0 copy-start.4
  3.1 1.4 %fusion.20 = bf16[1024,128]{1,0:T(8,128)(2,1)} fusion(bf16[384,128]{1,0:T(8,128)(2,1)S(1)} %fusion.24, s32[384]{0:T(512)S(1)} %add.79), kind=kOutput, calls=%fused_computation.25 | convolution fusion | flops 101187584 | bytes 361984 | tf_op jit(solution)/shard_map/dot_general | solution.py:70
  4.5 7.3 %all-to-all-start = ((bf16[32,32,128]{2,1,0:T(8,128)(2,1)}), bf16[32,32,128]{2,1,0:T(8,128)(2,1)S(1)}, u32[]{:S(2)}, u32[]{:S(2)}) async-start(bf16[32,32,128]{2,1,0:T(8,128)(2,1)} %bitcast.2), calls=%async_computation | async-start | bytes 524288 | tf_op jit(solution)/shard_map/all_to_all | solution.py:72
  12.6 0.5 fusion.52
  13.1 0.1 broadcast_in_dim.27
  13.2 0.1 broadcast_in_dim.28
  13.3 0.1 fusion.37
  13.4 0.0 copy-done.4
  13.4 1.4 %fusion.55 = f32[1280,256]{1,0:T(8,128)} fusion(bf16[1280,128]{1,0:T(8,128)(2,1)S(1)} %copy-done.3, bf16[128,256]{1,0:T(8,128)(2,1)S(1)} %copy-done.4), kind=kOutput, calls=%fused_computation.74 | convolution fusion | flops 83886080 | bytes 1703936 | tf_op jit(solution)/shard_map/dot_general | solution.py:128
  14.8 7.4 %all-to-all-done = bf16[32,32,128]{2,1,0:T(8,128)(2,1)S(1)} async-done(((bf16[32,32,128]{2,1,0:T(8,128)(2,1)}), bf16[32,32,128]{2,1,0:T(8,128)(2,1)S(1)}, u32[]{:S(2)}, u32[]{:S(2)}) %all-to-all-start) | async-done | bytes 262176 | tf_op jit(solution)/shard_map/all_to_all | solution.py:72
  22.2 0.4 fusion.26
  22.7 2.0 %gather_fusion = bf16[48,128,128]{2,1,0:T(8,128)(2,1)} fusion(bf16[13,128,128]{2,1,0:T(8,128)(2,1)S(1)} %bitcast.63, s32[1024]{0:T(1024)S(1)} %pad_clamp_fusion.1), kind=kCustom, calls=%fused_computation | custom fusion | bytes 3145920 | tf_op jit(solution)/shard_map/gather | solution.py:121
  24.7 2.6 %fusion.56 = f32[48,128,128]{2,1,0:T(8,128)S(1)} fusion(bf16[48,128,128]{2,1,0:T(8,128)(2,1)} %gather_fusion, bf16[48,128,128]{2,1,0:T(8,128)(2,1)S(1)} %copy-done), kind=kOutput, calls=%fused_computation.75 | convolution fusion | flops 201326592 | bytes 6291456 | tf_op jit(solution)/shard_map/tjf,tij->tfi/dot_general | solution.py:120
  27.3 2.9 %fusion.17 = bf16[10,128,128]{1,0,2:T(8,128)(2,1)S(1)} fusion(f32[48,128,128]{2,1,0:T(8,128)S(1)} %fusion.56, f32[10,128]{1,0:T(8,128)S(1)} %fusion.37, s32[48]{0:T(128)S(1)} %copy-done.6, pred[48]{0:T(512)(128)(4,1)S(1)} %iota_compare_fusion.26), kind=kOutput, calls=%fused_computation.24 | convolution fusion | flops 94700480 | bytes 3478768 | tf_op jit(solution)/shard_map/bt,tfi->bif/dot_general | solution.py:123
  30.3 0.4 copy.16
  30.7 3.2 %multiply_convert_fusion = (bf16[1280,256]{1,0:T(8,128)(2,1)S(1)}, bf16[1280,256]{1,0:T(8,128)(2,1)}) fusion(bf16[1280,256]{1,0:T(8,128)(2,1)} %param.19, f32[1280,256]{1,0:T(8,128)} %fusion.55, bf16[1280,128]{1,0:T(8,128)(2,1)S(1)} %bitcast.66, bf16[128,256]{1,0:T(8,128)(2,1)S(1)} %copy-done.11), kind=kOutput, calls=%fused_computation.21 | convolution fusion | flops 88145920 | bytes 3670016 | tf_op jit(solution)/shard_map/dot_general | solution.py:128
  33.8 0.3 fusion.58
  34.1 0.3 convolution_bitcast_fusion
  34.4 0.7 maximum_bitcast_fusion
  35.1 3.5 %all-to-all-start.2 = ((f32[32,8,256]{2,1,0:T(8,128)}), f32[32,8,256]{2,1,0:T(8,128)}, u32[]{:S(2)}, u32[]{:S(2)}) async-start(f32[32,8,256]{2,1,0:T(8,128)} %maximum_bitcast_fusion), calls=%async_computation.2 | async-start | bytes 524288 | tf_op jit(solution)/shard_map/all_to_all | solution.py:15
  38.6 0.3 fusion.4
  39.0 0.8 %gather_fusion.1 = bf16[48,128,128]{2,1,0:T(8,128)(2,1)S(1)} fusion(bf16[10,128,128]{2,1,0:T(8,128)(2,1)S(1)} %bitcast.64, s32[1024]{0:T(1024)S(1)} %pad_clamp_fusion), kind=kCustom, calls=%fused_computation.1 | custom fusion | bytes 3145920 | tf_op jit(solution)/shard_map/gather | solution.py:141
  39.9 0.0 copy-start.8
  39.9 0.7 fusion.57
  40.6 2.9 %fusion = f32[13,128,128]{2,0,1:T(8,128)S(1)} fusion(f32[48,128,128]{2,1,0:T(8,128)S(1)} %fusion.57, s32[48]{0:T(128)S(1)} %copy-done.8, pred[48]{0:T(512)(128)(4,1)S(1)} %iota_compare_fusion.26), kind=kOutput, calls=%fused_computation.2 | convolution fusion | flops 122684640 | bytes 3997936 | tf_op jit(solution)/shard_map/st,tfj->sfj/dot_general | solution.py:143
  43.5 0.1 fusion.34
  43.6 0.1 copy.18
  43.7 0.0 copy-start.5
  43.7 1.4 %fusion.21 = bf16[1024,128]{1,0:T(8,128)(2,1)} fusion(bf16[384,128]{1,0:T(8,128)(2,1)S(1)} %bitcast.70, s32[384]{0:T(512)S(1)} %add.79), kind=kOutput, calls=%fused_computation.26 | convolution fusion | flops 101187584 | bytes 361984 | tf_op jit(solution)/shard_map/dot_general | solution.py:70
  45.1 3.7 %all-to-all-done.2 = f32[32,8,256]{2,1,0:T(8,128)} async-done(((f32[32,8,256]{2,1,0:T(8,128)}), f32[32,8,256]{2,1,0:T(8,128)}, u32[]{:S(2)}, u32[]{:S(2)}) %all-to-all-start.2) | async-done | bytes 262176 | tf_op jit(solution)/shard_map/all_to_all | solution.py:15
  48.8 2.6 %all-to-all-start.1 = ((bf16[32,32,128]{2,1,0:T(8,128)(2,1)}), bf16[32,32,128]{2,1,0:T(8,128)(2,1)S(1)}, u32[]{:S(2)}, u32[]{:S(2)}) async-start(bf16[32,32,128]{2,1,0:T(8,128)(2,1)} %bitcast.18), calls=%async_computation.1 | async-start | bytes 524288 | tf_op jit(solution)/shard_map/all_to_all | solution.py:72
  51.4 1.0 %slice_bitcast_fusion = f32[10,128,128]{1,0,2:T(8,128)} fusion(f32[13,128,128]{2,0,1:T(8,128)S(1)} %fusion), kind=kLoop, calls=%fused_computation.33 | loop fusion | bytes 1310720 | tf_op jit(solution)/shard_map/transpose | solution.py:152
  52.5 1.5 %copy.17 = f32[10,128,128]{2,1,0:T(8,128)S(1)} copy(f32[10,128,128]{1,0,2:T(8,128)} %slice_bitcast_fusion) | data formatting | bytes 1310720 | tf_op jit(solution)/shard_map/transpose | solution.py:152
  54.0 1.0 %reduce_sum.9 = f32[8,256]{1,0:T(8,128)S(1)} reduce(f32[32,8,256]{2,1,0:T(8,128)} %all-to-all-done.2, f32[]{:T(128)} %constant.30.clone.1), dimensions={0}, to_apply=%region_0.1 | reduce | flops 63488 | bytes 270340 | tf_op jit(solution)/shard_map/reduce_sum | solution.py:15
  55.0 6.8 %all-to-all-done.1 = bf16[32,32,128]{2,1,0:T(8,128)(2,1)S(1)} async-done(((bf16[32,32,128]{2,1,0:T(8,128)(2,1)}), bf16[32,32,128]{2,1,0:T(8,128)(2,1)S(1)}, u32[]{:S(2)}, u32[]{:S(2)}) %all-to-all-start.1) | async-done | bytes 262176 | tf_op jit(solution)/shard_map/all_to_all | solution.py:72
  61.8 0.7 broadcast_in_dim.58
  62.5 2.6 %all-to-all-start.3 = ((f32[32,8,256]{2,1,0:T(8,128)}), f32[32,8,256]{2,1,0:T(8,128)S(1)}, u32[]{:S(2)}, u32[]{:S(2)}) async-start(f32[32,8,256]{2,1,0:T(8,128)} %broadcast_in_dim.58), calls=%async_computation.3 | async-start | bytes 524288 | tf_op jit(solution)/shard_map/all_to_all | solution.py:16
  65.1 1.2 %convolution_add_fusion.2 = f32[1280,128]{1,0:T(8,128)} fusion(f32[1280,128]{1,0:T(8,128)S(1)} %bitcast.65, bf16[1280,256]{1,0:T(8,128)(2,1)S(1)} %copy-done.2, bf16[128,256]{1,0:T(8,128)(2,1)S(1)} %copy-done.4), kind=kOutput, calls=%fused_computation.9 | convolution fusion | flops 84049920 | bytes 2031616 | tf_op jit(solution)/shard_map/nh,fh->nf/dot_general | solution.py:138
  66.3 3.0 %fusion.5 = bf16[1280,128]{1,0:T(8,128)(2,1)} fusion(f32[1280,128]{1,0:T(8,128)} %convolution_add_fusion.2, bf16[384,128]{1,0:T(8,128)(2,1)} %bitcast.71, bf16[1024,128]{1,0:T(8,128)(2,1)S(1)} %bitcast.68, s32[384]{0:T(512)S(1)} %eq.71, s32[384]{0:T(512)S(1)} %add.79, pred[384]{0:T(512)(128)(4,1)S(1)} %copy-done.10), kind=kOutput, calls=%fused_computation.11 | convolution fusion | flops 227803136 | bytes 1346944 | tf_op jit(solution)/shard_map/dot_general | solution.py:153
  69.3 6.2 %all-to-all-done.3 = f32[32,8,256]{2,1,0:T(8,128)S(1)} async-done(((f32[32,8,256]{2,1,0:T(8,128)}), f32[32,8,256]{2,1,0:T(8,128)S(1)}, u32[]{:S(2)}, u32[]{:S(2)}) %all-to-all-start.3) | async-done | bytes 262176 | tf_op jit(solution)/shard_map/all_to_all | solution.py:16
  75.5 0.7 slice_bitcast_fusion.1
  (26 shorter events, 0.1 us)
Async XLA Ops:
  0.6 11.9 %copy-start = (bf16[48,128,128]{2,1,0:T(8,128)(2,1)S(1)}, bf16[48,128,128]{2,1,0:T(8,128)(2,1)}, u32[]{:S(2)}) copy-start(bf16[48,128,128]{2,1,0:T(8,128)(2,1)} %param.13) | copy-start | bytes 4718596
  0.6 11.9 %copy-start.7 = (s32[48]{0:T(128)S(1)}, s32[48]{0:T(128)}, u32[]{:S(2)}) copy-start(s32[48]{0:T(128)} %param.15) | copy-start | bytes 580
  0.7 11.9 %copy-start.6 = (s32[48]{0:T(128)S(1)}, s32[48]{0:T(128)}, u32[]{:S(2)}) copy-start(s32[48]{0:T(128)} %param.14) | copy-start | bytes 580
  3.1 10.3 %copy-start.3 = (bf16[1280,128]{1,0:T(8,128)(2,1)S(1)}, bf16[1280,128]{1,0:T(8,128)(2,1)}, u32[]{:S(2)}) copy-start(bf16[1280,128]{1,0:T(8,128)(2,1)} %param.10) | copy-start | bytes 983044
  3.1 10.3 %copy-start.4 = (bf16[128,256]{1,0:T(8,128)(2,1)S(1)}, bf16[128,256]{1,0:T(8,128)(2,1)}, u32[]{:S(2)}) copy-start(bf16[128,256]{1,0:T(8,128)(2,1)} %param.17) | copy-start | bytes 196612
  4.5 17.7 %all-to-all-start = ((bf16[32,32,128]{2,1,0:T(8,128)(2,1)}), bf16[32,32,128]{2,1,0:T(8,128)(2,1)S(1)}, u32[]{:S(2)}, u32[]{:S(2)}) async-start(bf16[32,32,128]{2,1,0:T(8,128)(2,1)} %bitcast.2), calls=%async_computation | async-start | bytes 524288 | tf_op jit(solution)/shard_map/all_to_all | solution.py:72
  13.3 9.0 %copy-start.9 = (pred[384]{0:T(512)(128)(4,1)}, pred[384]{0:T(512)(128)(4,1)S(1)}, u32[]{:S(2)}) copy-start(pred[384]{0:T(512)(128)(4,1)S(1)} %broadcast_in_dim.28) | copy-start | bytes 1156
  27.3 3.3 %copy-start.11 = (bf16[128,256]{1,0:T(8,128)(2,1)S(1)}, bf16[128,256]{1,0:T(8,128)(2,1)}, u32[]{:S(2)}) copy-start(bf16[128,256]{1,0:T(8,128)(2,1)} %param.18) | copy-start | bytes 196612
  33.8 4.8 %copy-start.1 = (bf16[1280,256]{1,0:T(8,128)(2,1)}, bf16[1280,256]{1,0:T(8,128)(2,1)S(1)}, u32[]{:S(2)}) copy-start(bf16[1280,256]{1,0:T(8,128)(2,1)S(1)} %get-tuple-element.4) | copy-start | bytes 1966084
  35.1 13.7 %all-to-all-start.2 = ((f32[32,8,256]{2,1,0:T(8,128)}), f32[32,8,256]{2,1,0:T(8,128)}, u32[]{:S(2)}, u32[]{:S(2)}) async-start(f32[32,8,256]{2,1,0:T(8,128)} %maximum_bitcast_fusion), calls=%async_computation.2 | async-start | bytes 524288 | tf_op jit(solution)/shard_map/all_to_all | solution.py:15
  39.9 0.7 copy-start.8
  43.7 7.7 %copy-start.5 = (bf16[3,128,128]{2,1,0:T(8,128)(2,1)}, bf16[3,128,128]{2,1,0:T(8,128)(2,1)S(1)}, u32[]{:S(2)}) copy-start(bf16[3,128,128]{2,1,0:T(8,128)(2,1)S(1)} %copy.18) | copy-start | bytes 294916
  48.8 13.0 %all-to-all-start.1 = ((bf16[32,32,128]{2,1,0:T(8,128)(2,1)}), bf16[32,32,128]{2,1,0:T(8,128)(2,1)S(1)}, u32[]{:S(2)}, u32[]{:S(2)}) async-start(bf16[32,32,128]{2,1,0:T(8,128)(2,1)} %bitcast.18), calls=%async_computation.1 | async-start | bytes 524288 | tf_op jit(solution)/shard_map/all_to_all | solution.py:72
  52.5 12.6 %copy-start.2 = (bf16[1280,256]{1,0:T(8,128)(2,1)S(1)}, bf16[1280,256]{1,0:T(8,128)(2,1)}, u32[]{:S(2)}) copy-start(bf16[1280,256]{1,0:T(8,128)(2,1)} %copy-done.1) | copy-start | bytes 1966084
  54.0 12.3 %copy-start.10 = (pred[384]{0:T(512)(128)(4,1)S(1)}, pred[384]{0:T(512)(128)(4,1)}, u32[]{:S(2)}) copy-start(pred[384]{0:T(512)(128)(4,1)} %copy-done.9) | copy-start | bytes 1156
  62.5 13.0 %all-to-all-start.3 = ((f32[32,8,256]{2,1,0:T(8,128)}), f32[32,8,256]{2,1,0:T(8,128)S(1)}, u32[]{:S(2)}, u32[]{:S(2)}) async-start(f32[32,8,256]{2,1,0:T(8,128)} %broadcast_in_dim.58), calls=%async_computation.3 | async-start | bytes 524288 | tf_op jit(solution)/shard_map/all_to_all | solution.py:16

commit v17 on v16

--- a/solution.py
+++ b/solution.py
@@ -109,6 +109,14 @@
     )
     source = source.reshape(-1, tile_size, width)
     source_count = source.shape[0]
+    own_blocks = features.reshape(block_count, tile_size, width)
+    far_blocks = source[block_count:]
+    is_own = (tile_src < block_count)[:, None, None]
+    gathered = jnp.where(
+        is_own,
+        own_blocks[jnp.clip(tile_src, 0, block_count - 1)],
+        far_blocks[jnp.clip(tile_src - block_count, 0, source_count - block_count - 1)],
+    )
     slot_count = tile_vals.shape[0]
     usable = jnp.arange(slot_count, dtype=jnp.int32) < tile_count[0]
     to_target = (
@@ -118,7 +126,7 @@
         (tile_src[None, :] == jnp.arange(source_count, dtype=jnp.int32)[:, None]) & usable[None, :]
     ).astype(jnp.float32)
     products = jnp.einsum(
-        "tjf,tij->tfi", source[tile_src], tile_vals, preferred_element_type=jnp.float32
+        "tjf,tij->tfi", gathered, tile_vals, preferred_element_type=jnp.float32
     )
     summed = jnp.einsum("bt,tfi->bif", to_target, products, precision=lax.Precision.HIGHEST)
     unit_column = jnp.ones((tile_size,), jnp.bfloat16)

time: 76.7 us -> 77.2 us (level)
  waiting for transfers between devices: 24.1 us -> 22.1 us
  local copies, waits for them, and re-layouts: 7.82 us -> 9.74 us
    all_to_all x2, waiting for transfers between devices: 14.2 us -> 12.2 us  [swap(): lax.all_to_all(buf, ('dom', 'grp'), 0, 0, tiled=True)]
    gather x1 -> x2, local copies, waits for them, and re-layouts: 1.98 us -> 3.9 us  [the longest x1 1.97 us: per_device(): own_blocks[jnp.clip(tile_src, 0, block_count - 1)]]
  transfers between devices with their start and end apart: 4 -> 4, of which waited for: 4 -> 4; matrix products, arithmetic and copies ran while one was open for 22% -> 24% of each run, Pallas kernels for 0% -> 0%
where the time goes in v17:
time: 77.2 us; the launch traced here: 76.7 us
  matrix products  24.8 us (32%)
  waiting for transfers between devices  22.1 us (29%)
  starting transfers between devices  16 us (21%)
  local copies, waits for them, and re-layouts  9.74 us (13%)
  other arithmetic  2.55 us (3%)
  between operations  1.58 us (2%)
    all_to_all x2, waiting for transfers between devices, swap(): lax.all_to_all(buf, ('dom', 'grp'), 0, 0, tiled=True)  12.2 us
    all_to_all x2, starting transfers between devices, swap(): lax.all_to_all(buf, ('dom', 'grp'), 0, 0, tiled=True)  9.88 us
    all_to_all x1, waiting for transfers between devices, weight_sum(): lax.all_to_all(jnp.broadcast_to(mine, chunks.shape), axes, 0, 0, tiled=True)  6.18 us
    all_to_all x1, waiting for transfers between devices, weight_sum(): lax.all_to_all(chunks, axes, 0, 0, tiled=True)  3.69 us
    all_to_all x1, starting transfers between devices, weight_sum(): lax.all_to_all(chunks, axes, 0, 0, tiled=True)  3.49 us
    dot_general x1, matrix products, per_device(): jnp.einsum('tjf,tij->tfi', gathered, tile_vals, preferred_element_type=jn...  3.24 us
    dot_general x1, matrix products, per_device(): jnp.dot(agg, w_neigh, preferred_element_type=jnp.float32)  3.14 us
    dot_general x1, matrix products, per_device(): lax.dot_general(pick, returned, (((0,), (0,)), ((), ())), preferred_eleme...  3 us
  transfers between devices with their start and end apart: 4, of which 4 were waited for; matrix products, arithmetic and copies ran while one was open for 24% of the time, Pallas kernels for 0%

profile of v17, /device:TPU:0, one launch (start us, length us, event | category | flops | bytes accessed | tf_op | source)
XLA Modules:
  0.0 76.7 jit_solution(9764810352263953287)
XLA Ops:
  0.6 0.0 copy-start
  0.6 0.0 copy-start.7
  0.7 0.1 iota_add_fusion
  0.7 0.1 add.81
  0.8 0.7 pad_add_fusion
  1.5 0.1 eq.71
  1.6 1.5 %fusion.27 = bf16[384,128]{1,0:T(8,128)(2,1)S(1)} fusion(bf16[1280,128]{1,0:T(8,128)(2,1)} %param.10, s32[384]{0:T(512)S(1)} %eq.71), kind=kOutput, calls=%fused_computation.33 | convolution fusion | flops 126369792 | bytes 427520 | tf_op jit(solution)/shard_map/dot_general | solution.py:98
  3.1 0.0 copy-start.6
  3.1 1.4 %fusion.23 = bf16[1024,128]{1,0:T(8,128)(2,1)} fusion(bf16[384,128]{1,0:T(8,128)(2,1)S(1)} %fusion.27, s32[384]{0:T(512)S(1)} %add.81), kind=kOutput, calls=%fused_computation.29 | convolution fusion | flops 101187584 | bytes 361984 | tf_op jit(solution)/shard_map/dot_general | solution.py:70
  4.5 7.3 %all-to-all-start = ((bf16[32,32,128]{2,1,0:T(8,128)(2,1)}), bf16[32,32,128]{2,1,0:T(8,128)(2,1)S(1)}, u32[]{:S(2)}, u32[]{:S(2)}) async-start(bf16[32,32,128]{2,1,0:T(8,128)(2,1)} %bitcast.3), calls=%async_computation | async-start | bytes 524288 | tf_op jit(solution)/shard_map/all_to_all | solution.py:72
  12.5 0.5 fusion.55
  13.1 0.1 broadcast_in_dim.39
  13.2 0.1 broadcast_in_dim.66
  13.3 2.0 %gather_fusion = bf16[48,128,128]{2,1,0:T(8,128)(2,1)} fusion(bf16[10,128,128]{2,1,0:T(8,128)(2,1)S(1)} %bitcast.64, s32[1024]{0:T(1024)S(1)} %get-tuple-element.11), kind=kCustom, calls=%fused_computation | custom fusion | bytes 3145920 | tf_op jit(solution)/shard_map/gather | solution.py:117
  15.2 0.1 fusion.40
  15.4 1.4 %fusion.58 = f32[1280,256]{1,0:T(8,128)} fusion(bf16[1280,128]{1,0:T(8,128)(2,1)S(1)} %copy-done.1, bf16[128,256]{1,0:T(8,128)(2,1)S(1)} %copy-done.4), kind=kOutput, calls=%fused_computation.80 | convolution fusion | flops 83886080 | bytes 1703936 | tf_op jit(solution)/shard_map/dot_general | solution.py:136
  16.8 5.4 %all-to-all-done = bf16[32,32,128]{2,1,0:T(8,128)(2,1)S(1)} async-done(((bf16[32,32,128]{2,1,0:T(8,128)(2,1)}), bf16[32,32,128]{2,1,0:T(8,128)(2,1)S(1)}, u32[]{:S(2)}, u32[]{:S(2)}) %all-to-all-start) | async-done | bytes 262176 | tf_op jit(solution)/shard_map/all_to_all | solution.py:72
  22.2 0.4 fusion.29
  22.7 1.9 %gather_fusion.1 = bf16[48,128,128]{2,1,0:T(8,128)(2,1)} fusion(bf16[3,128,128]{2,1,0:T(8,128)(2,1)S(1)} %bitcast.63, s32[1024]{0:T(1024)S(1)} %get-tuple-element.10), kind=kCustom, calls=%fused_computation.1 | custom fusion | bytes 3145920 | tf_op jit(solution)/shard_map/gather | solution.py:118
  24.6 3.2 %fusion.7 = f32[48,128,128]{2,1,0:T(8,128)S(1)} fusion(bf16[48,128,128]{2,1,0:T(8,128)(2,1)S(1)} %copy-done, bf16[48,128,128]{2,1,0:T(8,128)(2,1)} %gather_fusion, bf16[48,128,128]{2,1,0:T(8,128)(2,1)} %gather_fusion.1, pred[48]{0:T(512)(128)(4,1)S(1)} %broadcast_compare_fusion), kind=kOutput, calls=%fused_computation.15 | convolution fusion | flops 202113024 | bytes 7864368 | tf_op jit(solution)/shard_map/tjf,tij->tfi/dot_general | solution.py:128
  27.8 2.9 %fusion.20 = bf16[10,128,128]{1,0,2:T(8,128)(2,1)S(1)} fusion(f32[48,128,128]{2,1,0:T(8,128)S(1)} %fusion.7, f32[10,128]{1,0:T(8,128)S(1)} %fusion.40, s32[48]{0:T(128)S(1)} %copy-done.6, pred[48]{0:T(512)(128)(4,1)S(1)} %iota_compare_fusion.26), kind=kOutput, calls=%fused_computation.28 | convolution fusion | flops 94700480 | bytes 3478768 | tf_op jit(solution)/shard_map/bt,tfi->bif/dot_general | solution.py:131
  30.8 0.4 copy.16
  31.2 3.1 %multiply_convert_fusion = (bf16[1280,256]{1,0:T(8,128)(2,1)S(1)}, bf16[1280,256]{1,0:T(8,128)(2,1)}) fusion(bf16[1280,256]{1,0:T(8,128)(2,1)} %param.19, f32[1280,256]{1,0:T(8,128)} %fusion.58, bf16[1280,128]{1,0:T(8,128)(2,1)S(1)} %bitcast.67, bf16[128,256]{1,0:T(8,128)(2,1)S(1)} %copy-done.11), kind=kOutput, calls=%fused_computation.25 | convolution fusion | flops 88145920 | bytes 3670016 | tf_op jit(solution)/shard_map/dot_general | solution.py:136
  34.3 0.3 fusion.60
  34.6 0.3 convolution_bitcast_fusion
  34.9 0.7 maximum_bitcast_fusion
  35.6 3.5 %all-to-all-start.2 = ((f32[32,8,256]{2,1,0:T(8,128)}), f32[32,8,256]{2,1,0:T(8,128)}, u32[]{:S(2)}, u32[]{:S(2)}) async-start(f32[32,8,256]{2,1,0:T(8,128)} %maximum_bitcast_fusion), calls=%async_computation.2 | async-start | bytes 524288 | tf_op jit(solution)/shard_map/all_to_all | solution.py:15
  39.1 0.3 fusion.4
  39.5 0.8 %gather_fusion.2 = bf16[48,128,128]{2,1,0:T(8,128)(2,1)S(1)} fusion(bf16[10,128,128]{2,1,0:T(8,128)(2,1)S(1)} %bitcast.65, s32[1024]{0:T(1024)S(1)} %pad_clamp_fusion), kind=kCustom, calls=%fused_computation.2 | custom fusion | bytes 3145920 | tf_op jit(solution)/shard_map/gather | solution.py:149
  40.4 0.0 copy-start.8
  40.4 0.7 fusion.59
  41.1 2.9 %fusion = f32[13,128,128]{2,0,1:T(8,128)S(1)} fusion(f32[48,128,128]{2,1,0:T(8,128)S(1)} %fusion.59, s32[48]{0:T(128)S(1)} %copy-done.8, pred[48]{0:T(512)(128)(4,1)S(1)} %iota_compare_fusion.26), kind=kOutput, calls=%fused_computation.3 | convolution fusion | flops 122684640 | bytes 3997936 | tf_op jit(solution)/shard_map/st,tfj->sfj/dot_general | solution.py:151
  44.0 0.1 fusion.37
  44.1 0.1 copy.18
  44.2 0.0 copy-start.5
  44.2 1.4 %fusion.24 = bf16[1024,128]{1,0:T(8,128)(2,1)} fusion(bf16[384,128]{1,0:T(8,128)(2,1)S(1)} %bitcast.71, s32[384]{0:T(512)S(1)} %add.81), kind=kOutput, calls=%fused_computation.30 | convolution fusion | flops 101187584 | bytes 361984 | tf_op jit(solution)/shard_map/dot_general | solution.py:70
  45.6 3.7 %all-to-all-done.2 = f32[32,8,256]{2,1,0:T(8,128)} async-done(((f32[32,8,256]{2,1,0:T(8,128)}), f32[32,8,256]{2,1,0:T(8,128)}, u32[]{:S(2)}, u32[]{:S(2)}) %all-to-all-start.2) | async-done | bytes 262176 | tf_op jit(solution)/shard_map/all_to_all | solution.py:15
  49.3 2.6 %all-to-all-start.1 = ((bf16[32,32,128]{2,1,0:T(8,128)(2,1)}), bf16[32,32,128]{2,1,0:T(8,128)(2,1)S(1)}, u32[]{:S(2)}, u32[]{:S(2)}) async-start(bf16[32,32,128]{2,1,0:T(8,128)(2,1)} %bitcast.19), calls=%async_computation.1 | async-start | bytes 524288 | tf_op jit(solution)/shard_map/all_to_all | solution.py:72
  51.9 1.1 %slice_bitcast_fusion = f32[10,128,128]{1,0,2:T(8,128)} fusion(f32[13,128,128]{2,0,1:T(8,128)S(1)} %fusion), kind=kLoop, calls=%fused_computation.37 | loop fusion | bytes 1310720 | tf_op jit(solution)/shard_map/transpose | solution.py:160
  53.0 1.5 %copy.17 = f32[10,128,128]{2,1,0:T(8,128)S(1)} copy(f32[10,128,128]{1,0,2:T(8,128)} %slice_bitcast_fusion) | data formatting | bytes 1310720 | tf_op jit(solution)/shard_map/transpose | solution.py:160
  54.5 1.0 %reduce_sum.9 = f32[8,256]{1,0:T(8,128)S(1)} reduce(f32[32,8,256]{2,1,0:T(8,128)} %all-to-all-done.2, f32[]{:T(128)} %constant.37.clone.1), dimensions={0}, to_apply=%region_0.1 | reduce | flops 63488 | bytes 270340 | tf_op jit(solution)/shard_map/reduce_sum | solution.py:15
  55.5 6.8 %all-to-all-done.1 = bf16[32,32,128]{2,1,0:T(8,128)(2,1)S(1)} async-done(((bf16[32,32,128]{2,1,0:T(8,128)(2,1)}), bf16[32,32,128]{2,1,0:T(8,128)(2,1)S(1)}, u32[]{:S(2)}, u32[]{:S(2)}) %all-to-all-start.1) | async-done | bytes 262176 | tf_op jit(solution)/shard_map/all_to_all | solution.py:72
  62.3 0.7 broadcast_in_dim.72
  63.0 2.6 %all-to-all-start.3 = ((f32[32,8,256]{2,1,0:T(8,128)}), f32[32,8,256]{2,1,0:T(8,128)S(1)}, u32[]{:S(2)}, u32[]{:S(2)}) async-start(f32[32,8,256]{2,1,0:T(8,128)} %broadcast_in_dim.72), calls=%async_computation.3 | async-start | bytes 524288 | tf_op jit(solution)/shard_map/all_to_all | solution.py:16
  65.6 1.2 %convolution_add_fusion.2 = f32[1280,128]{1,0:T(8,128)} fusion(f32[1280,128]{1,0:T(8,128)S(1)} %bitcast.66, bf16[1280,256]{1,0:T(8,128)(2,1)S(1)} %copy-done.3, bf16[128,256]{1,0:T(8,128)(2,1)S(1)} %copy-done.4), kind=kOutput, calls=%fused_computation.10 | convolution fusion | flops 84049920 | bytes 2031616 | tf_op jit(solution)/shard_map/nh,fh->nf/dot_general | solution.py:146
  66.8 3.0 %fusion.5 = bf16[1280,128]{1,0:T(8,128)(2,1)} fusion(f32[1280,128]{1,0:T(8,128)} %convolution_add_fusion.2, bf16[384,128]{1,0:T(8,128)(2,1)} %bitcast.72, bf16[1024,128]{1,0:T(8,128)(2,1)S(1)} %bitcast.70, s32[384]{0:T(512)S(1)} %eq.71, s32[384]{0:T(512)S(1)} %add.81, pred[384]{0:T(512)(128)(4,1)S(1)} %copy-done.10), kind=kOutput, calls=%fused_computation.12 | convolution fusion | flops 227803136 | bytes 1346944 | tf_op jit(solution)/shard_map/dot_general | solution.py:161
  69.8 6.2 %all-to-all-done.3 = f32[32,8,256]{2,1,0:T(8,128)S(1)} async-done(((f32[32,8,256]{2,1,0:T(8,128)}), f32[32,8,256]{2,1,0:T(8,128)S(1)}, u32[]{:S(2)}, u32[]{:S(2)}) %all-to-all-start.3) | async-done | bytes 262176 | tf_op jit(solution)/shard_map/all_to_all | solution.py:16
  76.0 0.7 slice_bitcast_fusion.1
  (27 shorter events, 0.1 us)
Async XLA Ops:
  0.6 11.9 %copy-start = (bf16[48,128,128]{2,1,0:T(8,128)(2,1)S(1)}, bf16[48,128,128]{2,1,0:T(8,128)(2,1)}, u32[]{:S(2)}) copy-start(bf16[48,128,128]{2,1,0:T(8,128)(2,1)} %param.13) | copy-start | bytes 4718596
  0.6 11.2 %copy-start.7 = (s32[48]{0:T(128)S(1)}, s32[48]{0:T(128)}, u32[]{:S(2)}) copy-start(s32[48]{0:T(128)} %param.15) | copy-start | bytes 580
  3.1 10.0 %copy-start.6 = (s32[48]{0:T(128)S(1)}, s32[48]{0:T(128)}, u32[]{:S(2)}) copy-start(s32[48]{0:T(128)} %param.14) | copy-start | bytes 580
  3.1 10.2 %copy-start.1 = (bf16[1280,128]{1,0:T(8,128)(2,1)S(1)}, bf16[1280,128]{1,0:T(8,128)(2,1)}, u32[]{:S(2)}) copy-start(bf16[1280,128]{1,0:T(8,128)(2,1)} %param.10) | copy-start | bytes 983044
  4.5 17.7 %all-to-all-start = ((bf16[32,32,128]{2,1,0:T(8,128)(2,1)}), bf16[32,32,128]{2,1,0:T(8,128)(2,1)S(1)}, u32[]{:S(2)}, u32[]{:S(2)}) async-start(bf16[32,32,128]{2,1,0:T(8,128)(2,1)} %bitcast.3), calls=%async_computation | async-start | bytes 524288 | tf_op jit(solution)/shard_map/all_to_all | solution.py:72
  13.3 9.0 %copy-start.9 = (pred[384]{0:T(512)(128)(4,1)}, pred[384]{0:T(512)(128)(4,1)S(1)}, u32[]{:S(2)}) copy-start(pred[384]{0:T(512)(128)(4,1)S(1)} %broadcast_in_dim.66) | copy-start | bytes 1156
  13.3 2.1 %copy-start.4 = (bf16[128,256]{1,0:T(8,128)(2,1)S(1)}, bf16[128,256]{1,0:T(8,128)(2,1)}, u32[]{:S(2)}) copy-start(bf16[128,256]{1,0:T(8,128)(2,1)} %param.17) | copy-start | bytes 196612
  27.8 3.3 %copy-start.11 = (bf16[128,256]{1,0:T(8,128)(2,1)S(1)}, bf16[128,256]{1,0:T(8,128)(2,1)}, u32[]{:S(2)}) copy-start(bf16[128,256]{1,0:T(8,128)(2,1)} %param.18) | copy-start | bytes 196612
  34.3 4.8 %copy-start.2 = (bf16[1280,256]{1,0:T(8,128)(2,1)}, bf16[1280,256]{1,0:T(8,128)(2,1)S(1)}, u32[]{:S(2)}) copy-start(bf16[1280,256]{1,0:T(8,128)(2,1)S(1)} %get-tuple-element.4) | copy-start | bytes 1966084
  35.6 13.7 %all-to-all-start.2 = ((f32[32,8,256]{2,1,0:T(8,128)}), f32[32,8,256]{2,1,0:T(8,128)}, u32[]{:S(2)}, u32[]{:S(2)}) async-start(f32[32,8,256]{2,1,0:T(8,128)} %maximum_bitcast_fusion), calls=%async_computation.2 | async-start | bytes 524288 | tf_op jit(solution)/shard_map/all_to_all | solution.py:15
  40.4 0.7 copy-start.8
  44.2 7.7 %copy-start.5 = (bf16[3,128,128]{2,1,0:T(8,128)(2,1)}, bf16[3,128,128]{2,1,0:T(8,128)(2,1)S(1)}, u32[]{:S(2)}) copy-start(bf16[3,128,128]{2,1,0:T(8,128)(2,1)S(1)} %copy.18) | copy-start | bytes 294916
  49.3 13.0 %all-to-all-start.1 = ((bf16[32,32,128]{2,1,0:T(8,128)(2,1)}), bf16[32,32,128]{2,1,0:T(8,128)(2,1)S(1)}, u32[]{:S(2)}, u32[]{:S(2)}) async-start(bf16[32,32,128]{2,1,0:T(8,128)(2,1)} %bitcast.19), calls=%async_computation.1 | async-start | bytes 524288 | tf_op jit(solution)/shard_map/all_to_all | solution.py:72
  53.0 12.6 %copy-start.3 = (bf16[1280,256]{1,0:T(8,128)(2,1)S(1)}, bf16[1280,256]{1,0:T(8,128)(2,1)}, u32[]{:S(2)}) copy-start(bf16[1280,256]{1,0:T(8,128)(2,1)} %copy-done.2) | copy-start | bytes 1966084
  54.5 12.3 %copy-start.10 = (pred[384]{0:T(512)(128)(4,1)S(1)}, pred[384]{0:T(512)(128)(4,1)}, u32[]{:S(2)}) copy-start(pred[384]{0:T(512)(128)(4,1)} %copy-done.9) | copy-start | bytes 1156
  63.0 13.0 %all-to-all-start.3 = ((f32[32,8,256]{2,1,0:T(8,128)}), f32[32,8,256]{2,1,0:T(8,128)S(1)}, u32[]{:S(2)}, u32[]{:S(2)}) async-start(f32[32,8,256]{2,1,0:T(8,128)} %broadcast_in_dim.72), calls=%async_computation.3 | async-start | bytes 524288 | tf_op jit(solution)/shard_map/all_to_all | solution.py:16

commit v18 on v16

--- a/solution.py
+++ b/solution.py
@@ -135,8 +135,11 @@
     )
     part_self = jnp.einsum("nf,nh->fh", features, grad_pre, preferred_element_type=jnp.float32)
     part_neigh = jnp.einsum("nf,nh->fh", agg, grad_pre, preferred_element_type=jnp.float32)
-    grad_own = jnp.einsum("nh,fh->nf", grad_pre, w_self, preferred_element_type=jnp.float32)
-    grad_agg = jnp.einsum("nh,fh->nf", grad_pre, w_neigh, preferred_element_type=jnp.float32)
+    both = jnp.einsum(
+        "nh,fh->nf", grad_pre, jnp.concatenate([w_self, w_neigh], axis=0),
+        preferred_element_type=jnp.float32,
+    )
+    grad_own, grad_agg = both[:, :width], both[:, width:]
     grad_agg = (grad_agg / degree.reshape(-1)[:, None]).astype(jnp.bfloat16)
     picked = grad_agg.reshape(block_count, tile_size, width)[tile_tgt]
     backward = jnp.einsum("tif,tij->tfj", picked, tile_vals, preferred_element_type=jnp.float32)

time: 76.7 us -> 79.5 us (1.037)
  local copies, waits for them, and re-layouts: 7.82 us -> 10.5 us
    all_to_all x2, waiting for transfers between devices: 14.2 us -> 16.8 us  [swap(): lax.all_to_all(buf, ('dom', 'grp'), 0, 0, tiled=True)]
    all_to_all x1, waiting for transfers between devices: 6.18 us -> 3.88 us  [weight_sum(): lax.all_to_all(jnp.broadcast_to(mine, chunks.shape), axes, 0, 0, tiled=True)]
    dot_general x2 -> x1, matrix products: 1.54 us -> 0.36 us  [per_device(): jnp.einsum('nh,fh->nf', grad_pre, jnp.concatenate([w_self, w_neigh], axis...]
    convert_element_type x1, local copies, waits for them, and re-layouts: 0.37 us -> 1.35 us  [per_device(): (summed / degree[:, :, None]).reshape(node_count, width)]
    transpose x2, local copies, waits for them, and re-layouts: 2.58 us -> 3.46 us  [per_device(): grad_source[:block_count].transpose(0, 2, 1).reshape(node_count, width)]
    unnamed x24 -> x38, local copies, waits for them, and re-layouts: 0.07 us -> 0.9 us
    dot_general x1, matrix products: 2.94 us -> 3.74 us  [per_device(): jnp.einsum('bt,tfi->bif', to_target, products, precision=lax.Precision.HI...]
  transfers between devices with their start and end apart: 4 -> 4, of which waited for: 4 -> 4; matrix products, arithmetic and copies ran while one was open for 22% -> 20% of each run, Pallas kernels for 0% -> 0%
where the time goes in v18:
time: 79.5 us; the launch traced here: 78.9 us
  waiting for transfers between devices  24.5 us (31%)
  matrix products  23.5 us (30%)
  starting transfers between devices  15.9 us (20%)
  local copies, waits for them, and re-layouts  10.5 us (13%)
  other arithmetic  2.86 us (4%)
  between operations  1.62 us (2%)
    all_to_all x2, waiting for transfers between devices, swap(): lax.all_to_all(buf, ('dom', 'grp'), 0, 0, tiled=True)  16.8 us
    all_to_all x2, starting transfers between devices, swap(): lax.all_to_all(buf, ('dom', 'grp'), 0, 0, tiled=True)  9.88 us
    all_to_all x1, waiting for transfers between devices, weight_sum(): lax.all_to_all(jnp.broadcast_to(mine, chunks.shape), axes, 0, 0, tiled=True)  3.88 us
    all_to_all x1, waiting for transfers between devices, weight_sum(): lax.all_to_all(chunks, axes, 0, 0, tiled=True)  3.77 us
    dot_general x1, matrix products, per_device(): jnp.einsum('bt,tfi->bif', to_target, products, precision=lax.Precision.HI...  3.74 us
    all_to_all x1, starting transfers between devices, weight_sum(): lax.all_to_all(chunks, axes, 0, 0, tiled=True)  3.48 us
    transpose x2, local copies, waits for them, and re-layouts, per_device(): grad_source[:block_count].transpose(0, 2, 1).reshape(node_count, width)  3.46 us
    dot_general x1, matrix products, per_device(): lax.dot_general(pick, returned, (((0,), (0,)), ((), ())), preferred_eleme...  3.01 us
  transfers between devices with their start and end apart: 4, of which 4 were waited for; matrix products, arithmetic and copies ran while one was open for 20% of the time, Pallas kernels for 0%

profile of v18, /device:TPU:0, one launch (start us, length us, event | category | flops | bytes accessed | tf_op | source)
XLA Modules:
  0.0 78.9 jit_solution(13011992138817700689)
XLA Ops:
  0.6 0.0 copy-start
  0.7 0.1 iota_add_fusion
  0.8 0.1 add.79
  0.8 0.7 pad_add_fusion
  1.6 0.1 eq.71
  1.6 0.6 copy-done.11
  2.2 1.5 %fusion.23 = bf16[384,128]{1,0:T(8,128)(2,1)S(1)} fusion(bf16[1280,128]{1,0:T(8,128)(2,1)} %param.10, s32[384]{0:T(512)S(1)} %eq.71), kind=kOutput, calls=%fused_computation.26 | convolution fusion | flops 126369792 | bytes 427520 | tf_op jit(solution)/shard_map/dot_general | solution.py:98
  3.7 1.4 %fusion.19 = bf16[1024,128]{1,0:T(8,128)(2,1)} fusion(bf16[384,128]{1,0:T(8,128)(2,1)S(1)} %fusion.23, s32[384]{0:T(512)S(1)} %add.79), kind=kOutput, calls=%fused_computation.22 | convolution fusion | flops 101187584 | bytes 361984 | tf_op jit(solution)/shard_map/dot_general | solution.py:70
  5.1 7.3 %all-to-all-start = ((bf16[32,32,128]{2,1,0:T(8,128)(2,1)}), bf16[32,32,128]{2,1,0:T(8,128)(2,1)S(1)}, u32[]{:S(2)}, u32[]{:S(2)}) async-start(bf16[32,32,128]{2,1,0:T(8,128)(2,1)} %bitcast.2), calls=%async_computation | async-start | bytes 524288 | tf_op jit(solution)/shard_map/all_to_all | solution.py:72
  13.2 0.5 fusion.56
  13.7 0.1 broadcast_in_dim.27
  13.8 0.1 broadcast_in_dim.28
  13.8 0.1 fusion.41
  14.0 0.0 copy-done.5
  14.0 1.4 %fusion.60 = f32[1280,256]{1,0:T(8,128)} fusion(bf16[1280,128]{1,0:T(8,128)(2,1)S(1)} %copy-done.3, bf16[128,256]{1,0:T(8,128)(2,1)S(1)} %copy-done.5), kind=kOutput, calls=%fused_computation.79 | convolution fusion | flops 83886080 | bytes 1703936 | tf_op jit(solution)/shard_map/dot_general | solution.py:128
  15.4 7.4 %all-to-all-done = bf16[32,32,128]{2,1,0:T(8,128)(2,1)S(1)} async-done(((bf16[32,32,128]{2,1,0:T(8,128)(2,1)}), bf16[32,32,128]{2,1,0:T(8,128)(2,1)S(1)}, u32[]{:S(2)}, u32[]{:S(2)}) %all-to-all-start) | async-done | bytes 262176 | tf_op jit(solution)/shard_map/all_to_all | solution.py:72
  22.8 0.4 fusion.25
  23.3 2.0 %gather_fusion = bf16[48,128,128]{2,1,0:T(8,128)(2,1)} fusion(bf16[13,128,128]{2,1,0:T(8,128)(2,1)S(1)} %bitcast.61, s32[1024]{0:T(1024)S(1)} %pad_clamp_fusion.1), kind=kCustom, calls=%fused_computation | custom fusion | bytes 3145920 | tf_op jit(solution)/shard_map/gather | solution.py:121
  25.3 2.7 %fusion.61 = f32[48,128,128]{2,1,0:T(8,128)S(1)} fusion(bf16[48,128,128]{2,1,0:T(8,128)(2,1)} %gather_fusion, bf16[48,128,128]{2,1,0:T(8,128)(2,1)S(1)} %copy-done), kind=kOutput, calls=%fused_computation.80 | convolution fusion | flops 201326592 | bytes 6291456 | tf_op jit(solution)/shard_map/tjf,tij->tfi/dot_general | solution.py:120
  27.9 3.7 %fusion.16 = bf16[10,128,128]{1,0,2:T(8,128)(2,1)} fusion(f32[48,128,128]{2,1,0:T(8,128)S(1)} %fusion.61, f32[10,128]{1,0:T(8,128)S(1)} %fusion.41, s32[48]{0:T(128)S(1)} %copy-done.14, pred[48]{0:T(512)(128)(4,1)S(1)} %iota_compare_fusion.26), kind=kOutput, calls=%fused_computation.21 | convolution fusion | flops 94700480 | bytes 3478768 | tf_op jit(solution)/shard_map/bt,tfi->bif/dot_general | solution.py:123
  31.7 1.4 %copy.16 = bf16[10,128,128]{2,1,0:T(8,128)(2,1)S(1)} copy(bf16[10,128,128]{1,0,2:T(8,128)(2,1)} %fusion.16) | data formatting | bytes 655360 | tf_op jit(solution)/shard_map/convert_element_type | solution.py:127
  33.0 2.7 %multiply_convert_fusion = (bf16[1280,256]{1,0:T(8,128)(2,1)S(1)}, bf16[1280,256]{1,0:T(8,128)(2,1)}) fusion(bf16[1280,256]{1,0:T(8,128)(2,1)} %param.19, f32[1280,256]{1,0:T(8,128)S(1)} %copy-done.4, bf16[1280,128]{1,0:T(8,128)(2,1)S(1)} %bitcast.62, bf16[128,256]{1,0:T(8,128)(2,1)} %param.18), kind=kOutput, calls=%fused_computation.18 | convolution fusion | flops 88145920 | bytes 3670016 | tf_op jit(solution)/shard_map/dot_general | solution.py:128
  35.8 0.3 fusion.63
  36.1 0.3 convolution_bitcast_fusion
  36.4 0.2 copy-done.6
  36.6 0.0 copy-done.8
  36.7 0.4 fusion.35
  37.0 0.8 maximum_bitcast_fusion
  37.8 3.5 %all-to-all-start.2 = ((f32[32,8,256]{2,1,0:T(8,128)}), f32[32,8,256]{2,1,0:T(8,128)}, u32[]{:S(2)}, u32[]{:S(2)}) async-start(f32[32,8,256]{2,1,0:T(8,128)} %maximum_bitcast_fusion), calls=%async_computation.2 | async-start | bytes 524288 | tf_op jit(solution)/shard_map/all_to_all | solution.py:15
  41.3 0.2 fusion.33
  41.6 0.8 %gather_fusion.1 = bf16[48,128,128]{2,1,0:T(8,128)(2,1)S(1)} fusion(bf16[10,128,128]{2,1,0:T(8,128)(2,1)S(1)} %bitcast.60, s32[1024]{0:T(1024)S(1)} %pad_clamp_fusion), kind=kCustom, calls=%fused_computation.1 | custom fusion | bytes 3145920 | tf_op jit(solution)/shard_map/gather | solution.py:144
  42.4 0.0 copy-start.16
  42.4 0.7 fusion.62
  43.1 2.9 %fusion = f32[13,128,128]{2,0,1:T(8,128)S(1)} fusion(f32[48,128,128]{2,1,0:T(8,128)S(1)} %fusion.62, s32[48]{0:T(128)S(1)} %copy-done.16, pred[48]{0:T(512)(128)(4,1)S(1)} %iota_compare_fusion.26), kind=kOutput, calls=%fused_computation.2 | convolution fusion | flops 122684640 | bytes 3997936 | tf_op jit(solution)/shard_map/st,tfj->sfj/dot_general | solution.py:146
  46.1 0.1 fusion.34
  46.1 0.1 copy.18
  46.3 1.4 %fusion.20 = bf16[1024,128]{1,0:T(8,128)(2,1)} fusion(bf16[384,128]{1,0:T(8,128)(2,1)S(1)} %bitcast.67, s32[384]{0:T(512)S(1)} %copy-done.10), kind=kOutput, calls=%fused_computation.23 | convolution fusion | flops 101187584 | bytes 361984 | tf_op jit(solution)/shard_map/dot_general | solution.py:70
  47.7 3.8 %all-to-all-done.2 = f32[32,8,256]{2,1,0:T(8,128)} async-done(((f32[32,8,256]{2,1,0:T(8,128)}), f32[32,8,256]{2,1,0:T(8,128)}, u32[]{:S(2)}, u32[]{:S(2)}) %all-to-all-start.2) | async-done | bytes 262176 | tf_op jit(solution)/shard_map/all_to_all | solution.py:15
  51.5 2.6 %all-to-all-start.1 = ((bf16[32,32,128]{2,1,0:T(8,128)(2,1)}), bf16[32,32,128]{2,1,0:T(8,128)(2,1)S(1)}, u32[]{:S(2)}, u32[]{:S(2)}) async-start(bf16[32,32,128]{2,1,0:T(8,128)(2,1)} %bitcast.18), calls=%async_computation.1 | async-start | bytes 524288 | tf_op jit(solution)/shard_map/all_to_all | solution.py:72
  54.1 1.0 %reduce_sum.9 = f32[8,256]{1,0:T(8,128)S(1)} reduce(f32[32,8,256]{2,1,0:T(8,128)} %all-to-all-done.2, f32[]{:T(128)} %constant.30.clone.1), dimensions={0}, to_apply=%region_0.1 | reduce | flops 63488 | bytes 270340 | tf_op jit(solution)/shard_map/reduce_sum | solution.py:15
  55.1 9.4 %all-to-all-done.1 = bf16[32,32,128]{2,1,0:T(8,128)(2,1)S(1)} async-done(((bf16[32,32,128]{2,1,0:T(8,128)(2,1)}), bf16[32,32,128]{2,1,0:T(8,128)(2,1)S(1)}, u32[]{:S(2)}, u32[]{:S(2)}) %all-to-all-start.1) | async-done | bytes 262176 | tf_op jit(solution)/shard_map/all_to_all | solution.py:72
  64.5 0.7 broadcast_in_dim.58
  65.2 2.6 %all-to-all-start.3 = ((f32[32,8,256]{2,1,0:T(8,128)}), f32[32,8,256]{2,1,0:T(8,128)S(1)}, u32[]{:S(2)}, u32[]{:S(2)}) async-start(f32[32,8,256]{2,1,0:T(8,128)} %broadcast_in_dim.58), calls=%async_computation.3 | async-start | bytes 524288 | tf_op jit(solution)/shard_map/all_to_all | solution.py:16
  67.8 1.0 %slice_bitcast_fusion = f32[10,128,128]{1,0,2:T(8,128)} fusion(f32[13,128,128]{2,0,1:T(8,128)S(1)} %fusion), kind=kLoop, calls=%fused_computation.30 | loop fusion | bytes 1310720 | tf_op jit(solution)/shard_map/transpose | solution.py:155
  68.9 2.4 %copy.17 = f32[10,128,128]{2,1,0:T(8,128)} copy(f32[10,128,128]{1,0,2:T(8,128)} %slice_bitcast_fusion) | data formatting | bytes 1310720 | tf_op jit(solution)/shard_map/transpose | solution.py:155
  71.3 3.0 %fusion.4 = bf16[1280,128]{1,0:T(8,128)(2,1)} fusion(bf16[384,128]{1,0:T(8,128)(2,1)} %bitcast.68, bf16[1024,128]{1,0:T(8,128)(2,1)S(1)} %bitcast.66, s32[384]{0:T(512)S(1)} %copy-done.12, s32[384]{0:T(512)S(1)} %copy-done.10, f32[1280,128]{1,0:T(8,128)} %bitcast.64, f32[1280,256]{1,0:T(8,128)S(1)} %copy-done.2, pred[384]{0:T(512)(128)(4,1)S(1)} %copy-done.18), kind=kOutput, calls=%fused_computation.8 | convolution fusion | flops 227966976 | bytes 2002304 | tf_op jit(solution)/shard_map/dot_general | solution.py:156
  74.3 3.9 %all-to-all-done.3 = f32[32,8,256]{2,1,0:T(8,128)S(1)} async-done(((f32[32,8,256]{2,1,0:T(8,128)}), f32[32,8,256]{2,1,0:T(8,128)S(1)}, u32[]{:S(2)}, u32[]{:S(2)}) %all-to-all-start.3) | async-done | bytes 262176 | tf_op jit(solution)/shard_map/all_to_all | solution.py:16
  78.2 0.7 slice_bitcast_fusion.1
  (40 shorter events, 0.1 us)
Async XLA Ops:
  0.6 12.5 %copy-start = (bf16[48,128,128]{2,1,0:T(8,128)(2,1)S(1)}, bf16[48,128,128]{2,1,0:T(8,128)(2,1)}, u32[]{:S(2)}) copy-start(bf16[48,128,128]{2,1,0:T(8,128)(2,1)} %param.13) | copy-start | bytes 4718596
  0.6 12.4 %copy-start.15 = (s32[48]{0:T(128)S(1)}, s32[48]{0:T(128)}, u32[]{:S(2)}) copy-start(s32[48]{0:T(128)} %param.15) | copy-start | bytes 580
  0.7 12.4 %copy-start.13 = (s32[48]{0:T(128)S(1)}, s32[48]{0:T(128)}, u32[]{:S(2)}) copy-start(s32[48]{0:T(128)} %param.14) | copy-start | bytes 580
  0.8 22.0 %copy-start.9 = (s32[384]{0:T(512)}, s32[384]{0:T(512)S(1)}, u32[]{:S(2)}) copy-start(s32[384]{0:T(512)S(1)} %add.79) | copy-start | bytes 4612
  1.6 0.6 copy-start.11
  3.7 10.3 %copy-start.3 = (bf16[1280,128]{1,0:T(8,128)(2,1)S(1)}, bf16[1280,128]{1,0:T(8,128)(2,1)}, u32[]{:S(2)}) copy-start(bf16[1280,128]{1,0:T(8,128)(2,1)} %param.10) | copy-start | bytes 983044
  3.7 10.3 %copy-start.5 = (bf16[128,256]{1,0:T(8,128)(2,1)S(1)}, bf16[128,256]{1,0:T(8,128)(2,1)}, u32[]{:S(2)}) copy-start(bf16[128,256]{1,0:T(8,128)(2,1)} %param.17) | copy-start | bytes 196612
  5.1 17.7 %all-to-all-start = ((bf16[32,32,128]{2,1,0:T(8,128)(2,1)}), bf16[32,32,128]{2,1,0:T(8,128)(2,1)S(1)}, u32[]{:S(2)}, u32[]{:S(2)}) async-start(bf16[32,32,128]{2,1,0:T(8,128)(2,1)} %bitcast.2), calls=%async_computation | async-start | bytes 524288 | tf_op jit(solution)/shard_map/all_to_all | solution.py:72
  13.8 9.0 %copy-start.17 = (pred[384]{0:T(512)(128)(4,1)}, pred[384]{0:T(512)(128)(4,1)S(1)}, u32[]{:S(2)}) copy-start(pred[384]{0:T(512)(128)(4,1)S(1)} %broadcast_in_dim.28) | copy-start | bytes 1156
  25.3 2.7 %copy-start.14 = (s32[48]{0:T(128)S(1)}, s32[48]{0:T(128)}, u32[]{:S(2)}) copy-start(s32[48]{0:T(128)} %param.14) | copy-start | bytes 580
  27.9 5.1 %copy-start.4 = (f32[1280,256]{1,0:T(8,128)S(1)}, f32[1280,256]{1,0:T(8,128)}, u32[]{:S(2)}) copy-start(f32[1280,256]{1,0:T(8,128)} %fusion.60) | copy-start | bytes 3932164
  35.8 0.8 %copy-start.6 = (bf16[128,256]{1,0:T(8,128)(2,1)S(1)}, bf16[128,256]{1,0:T(8,128)(2,1)}, u32[]{:S(2)}) copy-start(bf16[128,256]{1,0:T(8,128)(2,1)} %param.17) | copy-start | bytes 196612
  35.8 0.9 %copy-start.8 = (bf16[128,256]{1,0:T(8,128)(2,1)S(1)}, bf16[128,256]{1,0:T(8,128)(2,1)}, u32[]{:S(2)}) copy-start(bf16[128,256]{1,0:T(8,128)(2,1)} %param.18) | copy-start | bytes 196612
  37.0 4.5 %copy-start.1 = (f32[1280,256]{1,0:T(8,128)}, f32[1280,256]{1,0:T(8,128)S(1)}, u32[]{:S(2)}) copy-start(f32[1280,256]{1,0:T(8,128)S(1)} %fusion.35) | copy-start | bytes 3932164
  37.8 13.7 %all-to-all-start.2 = ((f32[32,8,256]{2,1,0:T(8,128)}), f32[32,8,256]{2,1,0:T(8,128)}, u32[]{:S(2)}, u32[]{:S(2)}) async-start(f32[32,8,256]{2,1,0:T(8,128)} %maximum_bitcast_fusion), calls=%async_computation.2 | async-start | bytes 524288 | tf_op jit(solution)/shard_map/all_to_all | solution.py:15
  42.4 0.7 copy-start.16
  43.1 3.2 %copy-start.10 = (s32[384]{0:T(512)S(1)}, s32[384]{0:T(512)}, u32[]{:S(2)}) copy-start(s32[384]{0:T(512)} %copy-done.9) | copy-start | bytes 4612
  46.3 18.9 %copy-start.7 = (bf16[3,128,128]{2,1,0:T(8,128)(2,1)}, bf16[3,128,128]{2,1,0:T(8,128)(2,1)S(1)}, u32[]{:S(2)}) copy-start(bf16[3,128,128]{2,1,0:T(8,128)(2,1)S(1)} %copy.18) | copy-start | bytes 294916
  51.5 13.0 %all-to-all-start.1 = ((bf16[32,32,128]{2,1,0:T(8,128)(2,1)}), bf16[32,32,128]{2,1,0:T(8,128)(2,1)S(1)}, u32[]{:S(2)}, u32[]{:S(2)}) async-start(bf16[32,32,128]{2,1,0:T(8,128)(2,1)} %bitcast.18), calls=%async_computation.1 | async-start | bytes 524288 | tf_op jit(solution)/shard_map/all_to_all | solution.py:72
  65.2 13.0 %all-to-all-start.3 = ((f32[32,8,256]{2,1,0:T(8,128)}), f32[32,8,256]{2,1,0:T(8,128)S(1)}, u32[]{:S(2)}, u32[]{:S(2)}) async-start(f32[32,8,256]{2,1,0:T(8,128)} %broadcast_in_dim.58), calls=%async_computation.3 | async-start | bytes 524288 | tf_op jit(solution)/shard_map/all_to_all | solution.py:16
  67.8 3.5 %copy-start.12 = (s32[384]{0:T(512)S(1)}, s32[384]{0:T(512)}, u32[]{:S(2)}) copy-start(s32[384]{0:T(512)} %copy-done.11) | copy-start | bytes 4612
  67.8 3.5 %copy-start.18 = (pred[384]{0:T(512)(128)(4,1)S(1)}, pred[384]{0:T(512)(128)(4,1)}, u32[]{:S(2)}) copy-start(pred[384]{0:T(512)(128)(4,1)} %copy-done.17) | copy-start | bytes 1156
  68.9 2.4 %copy-start.2 = (f32[1280,256]{1,0:T(8,128)S(1)}, f32[1280,256]{1,0:T(8,128)}, u32[]{:S(2)}) copy-start(f32[1280,256]{1,0:T(8,128)} %copy-done.1) | copy-start | bytes 3932164
